TPU v7x, 32 devices: a whole 2x2x4 slice. The times are simulated.
32 devices in a mesh: blk: 8 (over z, y), corpus: 4 (over x, core).
Axes of the slice: x: 2, y: 2, z: 4, core: 2. Of those that a mesh axis runs over, the one named last changes fastest.
Arguments:
- queries: bfloat16 [1024, 4096], P('blk', 'corpus'), may hold values from -12 to 12
- passages: bfloat16 [1024, 4096], P('blk', 'corpus'), may hold values from -4 to 4
- table: bfloat16 [1024, 4096], P('corpus'), may hold values from -4 to 4
- neg_owner: int32 [1024, 7], P('blk'), may hold values from 0 to 3, as said below
- neg_row: int32 [1024, 7], P('blk'), may hold values from 0 to 255
- positive: int32 [1024], P('blk'), may hold values from 0 to 1023, each once
- loss_weight: float32 [1024], P('blk'), may hold values from 32 to 256
Outputs:
- losses: float32 [1024], P(('blk', 'corpus'))
- query_grad: float32 [1024, 4096], P('blk', 'corpus')
- passage_grad: float32 [1024, 4096], P('blk', 'corpus')
- table_grad: float32 [1024, 4096], P('corpus', 'blk')
Inputs may be any that keep to these rules, and one draw needn't show every extreme that they name: `neg_owner`: among the 896 references of the queries of one index of blk (aligned blocks of 128 queries), one shard is named exactly 448 times and no shard more often.
All inputs are finite; a program needn't handle non-finite values.
Results may differ from a plain program's by a relative error of at most 0.0065.
Values may be sent and summed in bfloat16 or wider, within the bound.
No kernel may reach another device: no remote copies, remote signals or barrier semaphores. Data moves between devices by JAX's collectives and lax.ppermute only.
A program may use at most 128 MiB of HBM per device.

v0:
```python
import jax
import jax.numpy as jnp
from jax import lax
from jax.sharding import PartitionSpec as P

CAP = 448


def split_product(mixing, right_side):
    upper = mixing.astype(jnp.bfloat16)
    lower = (mixing - upper.astype(jnp.float32)).astype(jnp.bfloat16)
    return jnp.dot(upper, right_side, preferred_element_type=jnp.float32) + jnp.dot(
        lower, right_side, preferred_element_type=jnp.float32
    )


def per_device(queries, passages, table, neg_owner, neg_row, positive, loss_weight):
    q_rows, col_width = queries.shape
    owner_count = lax.axis_size("corpus")
    factor = (col_width * owner_count) ** (-0.5)
    rows_shard = table.shape[0]
    negs = neg_owner.shape[1]
    ref_count = q_rows * negs
    owners = neg_owner.reshape(ref_count)
    neg_rows = neg_row.reshape(ref_count)
    owner_index = lax.axis_index("corpus")
    all_passages = lax.all_gather(passages, "blk", axis=0, tiled=True)
    all_rows = all_passages.shape[0]
    owner_marks = (owners[:, None] == jnp.arange(owner_count, dtype=jnp.int32)[None, :]).astype(
        jnp.int32
    )
    slot_ranks = jnp.sum(jnp.cumsum(owner_marks, axis=0) * owner_marks, axis=1) - 1
    slot_index = owners * CAP + slot_ranks
    target = jnp.where(owners == owner_index, slot_ranks, CAP)
    wanted = jnp.zeros((CAP,), jnp.int32).at[target].set(neg_rows, mode="drop")
    outgoing = table[wanted]
    arrived = lax.all_to_all(outgoing, "corpus", split_axis=1, concat_axis=0, tiled=True)
    picked = arrived[slot_index]
    hard_rows = picked.reshape(q_rows, negs, col_width)
    logits = lax.dot_general(
        queries, all_passages, (((1,), (1,)), ((), ())), preferred_element_type=jnp.float32
    )
    hard_logits = jnp.einsum("qd,qkd->qk", queries, hard_rows, preferred_element_type=jnp.float32)
    logits, hard_logits = lax.psum((logits, hard_logits), "corpus")
    logits = logits * factor
    hard_logits = hard_logits * factor
    row_top = jnp.maximum(jnp.max(logits, axis=1), jnp.max(hard_logits, axis=1))
    log_total = row_top + jnp.log(
        jnp.sum(jnp.exp(logits - row_top[:, None]), axis=1)
        + jnp.sum(jnp.exp(hard_logits - row_top[:, None]), axis=1)
    )
    one_hot = positive[:, None] == jnp.arange(all_rows, dtype=jnp.int32)[None, :]
    losses = log_total - jnp.sum(jnp.where(one_hot, logits, 0.0), axis=1)
    share = q_rows // owner_count
    loss_share = lax.dynamic_slice_in_dim(losses, owner_index * share, share)
    weighting = (loss_weight * factor)[:, None]
    soft_grad = (
        weighting * (jnp.exp(logits - log_total[:, None]) - one_hot.astype(jnp.float32))
    ).astype(jnp.bfloat16)
    hard_grad = (weighting * jnp.exp(hard_logits - log_total[:, None])).astype(jnp.bfloat16)
    query_grad = jnp.dot(soft_grad, all_passages, preferred_element_type=jnp.float32)
    query_grad = query_grad + jnp.einsum(
        "qk,qkd->qd", hard_grad, hard_rows, preferred_element_type=jnp.float32
    )
    passage_grad = lax.psum_scatter(
        lax.dot_general(
            soft_grad, queries, (((0,), (0,)), ((), ())), preferred_element_type=jnp.float32
        ),
        "blk",
        scatter_dimension=0,
        tiled=True,
    )
    table_rows = owner_count * rows_shard
    flat_ids = owners * rows_shard + neg_rows
    query_of = jnp.arange(ref_count, dtype=jnp.int32) // negs
    mixing = (
        jnp.zeros((table_rows, q_rows), jnp.float32)
        .at[flat_ids, query_of]
        .add(hard_grad.reshape(ref_count).astype(jnp.float32))
    )
    dense_grad = split_product(mixing, queries)
    owned_grad = lax.all_to_all(dense_grad, "corpus", split_axis=0, concat_axis=1, tiled=True)
    table_grad = lax.psum_scatter(owned_grad, "blk", scatter_dimension=1, tiled=True)
    return (loss_share, query_grad, passage_grad, table_grad)


def solution(mesh):
    placed = (
        P("blk", "corpus"),
        P("blk", "corpus"),
        P("corpus", None),
        P("blk", None),
        P("blk", None),
        P("blk"),
        P("blk"),
    )
    return jax.shard_map(
        per_device,
        mesh=mesh,
        in_specs=placed,
        out_specs=(
            P(("blk", "corpus")),
            P("blk", "corpus"),
            P("blk", "corpus"),
            P("corpus", "blk"),
        ),
        check_vma=False,
    )
```

profile of v0, /device:TPU:2, one launch (start us, length us, event | category | flops | bytes accessed | tf_op | source)
XLA Modules:
  0.0 326.0 jit_solution(15712247112752684754)
XLA Ops:
  7.2 0.0 copy-start
  7.2 0.0 all-gather.2.cloned.1.call-start
  7.2 0.7 all-gather.2.cloned.1.call-update
  7.9 0.8 copy.30
  8.7 0.2 eq.61
  8.9 0.2 eq.57
  9.1 0.7 multiply_add_fusion
  9.8 0.8 copy.32
  10.6 0.1 copy.34
  10.7 0.2 mul.71
  11.0 1.1 reduce-window.6
  12.1 0.2 slice_reduce_fusion
  12.3 0.2 reduce-window.9
  12.5 0.7 broadcast_compare_fusion
  13.2 0.1 copy.29
  13.3 0.2 eq.56
  13.6 0.2 reshape.219
  13.8 0.1 add_bitcast_fusion
  13.9 5.3 %scatter_custom_fusion = s32[448]{0:T(512)S(1)} fusion(s32[896]{0:T(1024)S(1)} %get-tuple-element.7, s32[896]{0:T(1024)S(1)} %reshape.219, s32[]{:T(128)} %constant.16.clone.1), kind=kCustom, calls=%fused_computation.51 | custom fusion | bytes 1796 | tf_op jit(solution)/shard_map/scatter | solution.py:35
  19.2 0.0 copy-done
  19.2 4.2 %gather_fusion = bf16[448,4096]{1,0:T(8,128)(2,1)} fusion(bf16[256,4096]{1,0:T(8,128)(2,1)S(1)} %copy-done, s32[1024]{0:T(1024)S(1)} %pad_clamp_fusion.1), kind=kCustom, calls=%fused_computation | custom fusion | bytes 7341824 | tf_op jit(solution)/shard_map/gather | solution.py:36
  23.4 4.4 %copy.50 = bf16[56,4,8,1024]{3,2,0,1:T(8,128)(2,1)} copy(bf16[56,4,8,1024]{3,2,1,0:T(8,128)(2,1)} %bitcast.44) | data formatting | bytes 7340032 | tf_op jit(solution)/shard_map/all_to_all | solution.py:37
  27.8 0.0 copy-start.5
  27.8 4.9 %all-to-all-start = ((bf16[448,4,1024]{2,0,1:T(8,128)(2,1)}), bf16[448,4,1024]{2,0,1:T(8,128)(2,1)}, u32[]{:S(2)}, u32[]{:S(2)}) async-start(bf16[448,4,1024]{2,0,1:T(8,128)(2,1)} %bitcast.45), calls=%async_computation | async-start | bytes 7340032 | tf_op jit(solution)/shard_map/all_to_all | solution.py:37
  32.7 0.0 all-reduce.2.cloned.1.call-start
  32.8 0.0 copy-done.5
  32.8 39.9 %all-to-all-done = bf16[448,4,1024]{2,0,1:T(8,128)(2,1)} async-done(((bf16[448,4,1024]{2,0,1:T(8,128)(2,1)}), bf16[448,4,1024]{2,0,1:T(8,128)(2,1)}, u32[]{:S(2)}, u32[]{:S(2)}) %all-to-all-start) | async-done | bytes 3670048 | tf_op jit(solution)/shard_map/all_to_all | solution.py:37
  72.7 8.1 %gather_fusion.1 = bf16[896,1024]{1,0:T(8,128)(2,1)} fusion(bf16[1792,1024]{1,0:T(8,128)(2,1)} %bitcast.2, s32[1024]{0:T(1024)S(1)} %pad_clamp_fusion), kind=kCustom, calls=%fused_computation.1 | custom fusion | bytes 3673600 | tf_op jit(solution)/shard_map/gather | solution.py:38
  80.8 0.0 copy-start.3
  80.8 3.9 %reshape.197 = bf16[128,7,1024]{2,1,0:T(8,128)(2,1)} reshape(bf16[896,1024]{1,0:T(8,128)(2,1)} %gather_fusion.1) | data formatting | bytes 3670016 | tf_op jit(solution)/shard_map/reshape | solution.py:39
  84.7 0.0 all-gather.2.cloned.1.call-done
  84.7 0.0 copy-done.3
  84.7 3.2 fusion.18
  87.9 0.0 all-reduce.2.cloned.1.call-update
  87.9 0.0 reduce-scatter.3.cloned.1.call-start
  88.0 0.0 copy-start.4
  88.0 2.9 fusion
  90.9 0.1 copy.39
  90.9 6.8 %psum.15 = f32[128,7]{0,1:T(8,128)S(1)} all-reduce(f32[128,7]{0,1:T(8,128)S(1)} %bitcast.47), channel_id=1, replica_groups=mesh['blk'=8,'corpus'=4] {'corpus'}, use_global_device_ids=true, to_apply=%region_6.7 | all-reduce | flops 896 | bytes 7168 | tf_op jit(solution)/shard_map/psum | solution.py:44
  97.8 25.2 %all-reduce.2.cloned.1.call-done = f32[128,1024]{1,0:T(8,128)} async-done(((f32[128,1024]{1,0:T(8,128)}), f32[128,1024]{1,0:T(8,128)}) %all-reduce.2.cloned.1.call-update) | async-done | bytes 524304 | tf_op jit(solution)/shard_map/psum | solution.py:44
  123.0 1.2 multiply_reduce_fusion
  124.2 0.0 copy-done.4
  124.2 1.4 select_reduce_fusion
  125.6 3.9 %fusion.16 = f32[1024,1024]{1,0:T(8,128)} fusion(bf16[128,1024]{1,0:T(8,128)(2,1)S(1)} %copy-done.3, f32[128,1024]{1,0:T(8,128)} %all-reduce.2.cloned.1.call-done, f32[128]{0:T(128)S(1)} %get-tuple-element.9, f32[128]{0:T(128)S(1)} %broadcast_multiply_fusion.1, s32[128]{0:T(128)S(1)} %copy-done.4), kind=kOutput, calls=%fused_computation.57 | convolution fusion | flops 269352960 | bytes 4982272 | tf_op jit(solution)/shard_map/dot_general | solution.py:66
  129.4 0.0 reduce-scatter.3.cloned.1.call-update
  129.5 0.0 reduce-scatter.5.cloned.1.call-start
  129.5 0.1 copy.35
  129.6 0.2 add.143
  129.9 0.1 copy.36
  130.0 0.2 reshape.225
  130.3 44.6 %scatter_fusion = f32[1024,128]{1,0:T(8,128)S(1)} fusion(f32[1024,128]{1,0:T(8,128)S(1)} %broadcast_in_dim.32, s32[896]{0:T(1024)S(1)} %fusion.11, f32[896]{0:T(1024)S(1)} %reshape.225), kind=kCustom, calls=%fused_computation.3 | custom fusion | flops 896 | bytes 17920 | tf_op jit(solution)/shard_map/scatter-add | solution.py:79
  174.8 0.7 fusion.3
  175.5 0.7 convolution_add_fusion
  176.2 51.0 %all_to_all.38 = f32[4,256,1024]{2,1,0:T(8,128)S(1)} all-to-all(f32[4,256,1024]{2,1,0:T(8,128)S(1)} %bitcast.42), channel_id=1, replica_groups=mesh['blk'=8,'corpus'=4] {'corpus'}, dimensions={0} | all-to-all | bytes 8388608 | tf_op jit(solution)/shard_map/all_to_all | solution.py:82
  227.2 2.3 copy.43
  229.5 0.0 reduce-scatter.5.cloned.1.call-update
  229.5 0.0 copy-start.2
  229.5 0.1 copy.40
  229.7 0.6 dynamic_slice.3
  230.2 2.3 fusion.19
  232.6 0.0 copy-done.2
  232.6 0.0 copy-done.1
  232.6 1.4 convolution_add_fusion.1
  234.0 85.4 %reduce-scatter.5.cloned.1.call-done = f32[256,512]{1,0:T(8,128)} async-done(((f32[256,4096]{1,0:T(8,128)}), f32[256,512]{1,0:T(8,128)}) %reduce-scatter.5.cloned.1.call-update) | async-done | bytes 524304 | tf_op jit(solution)/shard_map/reduce_scatter | solution.py:83
  (17 shorter events, 0.2 us)
Async XLA Ops:
  7.2 12.1 %copy-start = (bf16[256,4096]{1,0:T(8,128)(2,1)S(1)}, bf16[256,4096]{1,0:T(8,128)(2,1)}, u32[]{:S(2)}) copy-start(bf16[256,4096]{1,0:T(8,128)(2,1)} %param.9) | copy-start | bytes 6291460
  7.2 77.5 %all-gather.2.cloned.1.call-start = ((), (), s32[]{:S(2)}) async-start(), calls=%async_computation.4 | async-start | bytes 2359296 | tf_op jit(solution)/shard_map/all_gather | solution.py:27
  27.8 4.9 %copy-start.5 = (f32[128]{0:T(128)S(1)}, f32[128]{0:T(128)}, u32[]{:S(2)}) copy-start(f32[128]{0:T(128)} %param.13) | copy-start | bytes 1540
  27.8 44.9 %all-to-all-start = ((bf16[448,4,1024]{2,0,1:T(8,128)(2,1)}), bf16[448,4,1024]{2,0,1:T(8,128)(2,1)}, u32[]{:S(2)}, u32[]{:S(2)}) async-start(bf16[448,4,1024]{2,0,1:T(8,128)(2,1)} %bitcast.45), calls=%async_computation | async-start | bytes 7340032 | tf_op jit(solution)/shard_map/all_to_all | solution.py:37
  32.7 90.3 %all-reduce.2.cloned.1.call-start = ((), (), s32[]{:S(2)}) async-start(), calls=%async_computation.5 | async-start | bytes 1048576 | tf_op jit(solution)/shard_map/psum | solution.py:44
  80.8 3.9 %copy-start.3 = (bf16[128,1024]{1,0:T(8,128)(2,1)S(1)}, bf16[128,1024]{1,0:T(8,128)(2,1)}, u32[]{:S(2)}) copy-start(bf16[128,1024]{1,0:T(8,128)(2,1)} %param.7) | copy-start | bytes 786436
  87.9 146.1 %reduce-scatter.3.cloned.1.call-start = ((), (), s32[]{:S(2)}) async-start(), calls=%async_computation.6 | async-start | bytes 4718592 | tf_op jit(solution)/shard_map/reduce_scatter | solution.py:65
  88.0 36.2 %copy-start.4 = (s32[128]{0:T(128)S(1)}, s32[128]{0:T(128)}, u32[]{:S(2)}) copy-start(s32[128]{0:T(128)} %param.12) | copy-start | bytes 1540
  129.5 190.0 %reduce-scatter.5.cloned.1.call-start = ((), (), s32[]{:S(2)}) async-start(), calls=%async_computation.7 | async-start | bytes 4718592 | tf_op jit(solution)/shard_map/reduce_scatter | solution.py:83
  229.5 3.1 copy-start.2
  229.6 2.9 copy-start.1
Sparse Core Ops, SparseCore 0:
  10.1 50.3 all-gather.1
  88.1 34.8 all-reduce.1
  129.6 89.7 reduce-scatter.2
  229.6 89.7 reduce-scatter.4
where the time goes:
time: 328 us; the launch traced here: 326 us
  waiting for transfers between devices  151 us (46%)
  blocking collectives  57.8 us (18%)
  other arithmetic  50.1 us (15%)
  local copies, waits for them, and re-layouts  32.6 us (10%)
  matrix products  15.1 us (5%)
  between operations  14 us (4%)
  starting transfers between devices  5.03 us (2%)
    reduce_scatter x1, waiting for transfers between devices, per_device(): lax.psum_scatter(owned_grad, 'blk', scatter_dimension=1, tiled=True)  85.4 us
    all_to_all x1, blocking collectives, per_device(): lax.all_to_all(dense_grad, 'corpus', split_axis=0, concat_axis=1, tiled=T...  51 us
    scatter-add x1, other arithmetic, per_device(): mixing = jnp.zeros((table_rows, q_rows), jnp.float32).at[flat_ids, query_...  44.6 us
    all_to_all x1, waiting for transfers between devices, per_device(): lax.all_to_all(outgoing, 'corpus', split_axis=1, concat_axis=0, tiled=True)  39.9 us
    psum x1, waiting for transfers between devices, per_device(): logits, hard_logits = lax.psum((logits, hard_logits), 'corpus')  25.2 us
    gather x1, local copies, waits for them, and re-layouts, per_device(): picked = arrived[slot_index]  8.05 us
    psum x1, blocking collectives, per_device(): logits, hard_logits = lax.psum((logits, hard_logits), 'corpus')  6.83 us
  transfers between devices with their start and end apart: 5, of which 3 were waited for; matrix products, arithmetic and copies ran while one was open for 27% of the time, Pallas kernels for 0%

commit v1 on v0

v1 whole, which is shorter than its diff:
```python
import jax
import jax.numpy as jnp
from jax import lax
from jax.sharding import PartitionSpec as P


def hi_lo(mixing):
    upper = mixing.astype(jnp.bfloat16)
    lower = (mixing - upper.astype(jnp.float32)).astype(jnp.bfloat16)
    return upper, lower


def per_device(queries, passages, table, neg_owner, neg_row, positive, loss_weight):
    q_rows, col_width = queries.shape
    owner_count = lax.axis_size("corpus")
    blk_count = lax.axis_size("blk")
    factor = (col_width * owner_count) ** (-0.5)
    rows_shard = table.shape[0]
    table_rows = owner_count * rows_shard
    owner_index = lax.axis_index("corpus")
    blk_index = lax.axis_index("blk")

    table_cols = lax.all_to_all(table, "corpus", split_axis=1, concat_axis=0, tiled=True)
    all_passages = lax.all_gather(passages, "blk", axis=0, tiled=True)
    all_queries = lax.all_gather(queries, "blk", axis=0, tiled=True)
    ids = neg_owner * rows_shard + neg_row
    all_ids = lax.all_gather(ids, "blk", axis=0, tiled=True)
    all_rows = all_passages.shape[0]

    logits = lax.dot_general(
        queries, all_passages, (((1,), (1,)), ((), ())), preferred_element_type=jnp.float32
    )
    table_scores = lax.dot_general(
        queries, table_cols, (((1,), (1,)), ((), ())), preferred_element_type=jnp.float32
    )
    row_iota = jnp.arange(table_rows, dtype=jnp.int32)
    picks = ids[:, :, None] == row_iota[None, None, :]
    hard_logits = jnp.sum(jnp.where(picks, table_scores[:, None, :], 0.0), axis=2)
    logits, hard_logits = lax.psum((logits, hard_logits), "corpus")
    logits = logits * factor
    hard_logits = hard_logits * factor
    row_top = jnp.maximum(jnp.max(logits, axis=1), jnp.max(hard_logits, axis=1))
    log_total = row_top + jnp.log(
        jnp.sum(jnp.exp(logits - row_top[:, None]), axis=1)
        + jnp.sum(jnp.exp(hard_logits - row_top[:, None]), axis=1)
    )
    one_hot = positive[:, None] == jnp.arange(all_rows, dtype=jnp.int32)[None, :]
    losses = log_total - jnp.sum(jnp.where(one_hot, logits, 0.0), axis=1)
    share = q_rows // owner_count
    loss_share = lax.dynamic_slice_in_dim(losses, owner_index * share, share)
    weighting = (loss_weight * factor)[:, None]
    soft_grad = (
        weighting * (jnp.exp(logits - log_total[:, None]) - one_hot.astype(jnp.float32))
    ).astype(jnp.bfloat16)
    hard_grad = (weighting * jnp.exp(hard_logits - log_total[:, None])).astype(jnp.bfloat16)

    mixing = jnp.sum(jnp.where(picks, hard_grad.astype(jnp.float32)[:, :, None], 0.0), axis=1)
    mix_hi, mix_lo = hi_lo(mixing)
    left = jnp.concatenate([soft_grad, mix_hi, mix_lo], axis=1)
    right = jnp.concatenate([all_passages, table_cols, table_cols], axis=0)
    query_grad = jnp.dot(left, right, preferred_element_type=jnp.float32)

    soft_cols = lax.all_to_all(soft_grad, "blk", split_axis=1, concat_axis=0, tiled=True)
    passage_grad = lax.dot_general(
        soft_cols, all_queries, (((0,), (0,)), ((), ())), preferred_element_type=jnp.float32
    )

    all_hard = lax.all_gather(hard_grad, "blk", axis=0, tiled=True)
    per_col = blk_count // owner_count
    piece_width = col_width // per_col
    shard = blk_index // per_col
    part = blk_index % per_col
    shard_iota = shard * rows_shard + jnp.arange(rows_shard, dtype=jnp.int32)
    shard_picks = all_ids[:, :, None] == shard_iota[None, None, :]
    shard_mix = jnp.sum(
        jnp.where(shard_picks, all_hard.astype(jnp.float32)[:, :, None], 0.0), axis=1
    )
    shard_hi, shard_lo = hi_lo(shard_mix)
    query_part = lax.dynamic_slice_in_dim(all_queries, part * piece_width, piece_width, axis=1)
    dims = (((0,), (0,)), ((), ()))
    piece = lax.dot_general(
        shard_hi, query_part, dims, preferred_element_type=jnp.float32
    ) + lax.dot_general(shard_lo, query_part, dims, preferred_element_type=jnp.float32)
    perm = []
    for b in range(blk_count):
        for c in range(owner_count):
            dest_b = c * per_col + b % per_col
            dest_c = b // per_col
            perm.append((b * owner_count + c, dest_b * owner_count + dest_c))
    table_grad = lax.ppermute(piece, ("blk", "corpus"), perm)
    return (loss_share, query_grad, passage_grad, table_grad)


def solution(mesh):
    placed = (
        P("blk", "corpus"),
        P("blk", "corpus"),
        P("corpus", None),
        P("blk", None),
        P("blk", None),
        P("blk"),
        P("blk"),
    )
    return jax.shard_map(
        per_device,
        mesh=mesh,
        in_specs=placed,
        out_specs=(
            P(("blk", "corpus")),
            P("blk", "corpus"),
            P("blk", "corpus"),
            P("corpus", "blk"),
        ),
        check_vma=False,
    )
```

time: 328 us -> 191 us (0.58)
  waiting for transfers between devices: 151 us -> 67.3 us
  other arithmetic: 50.1 us -> 9.43 us
  local copies, waits for them, and re-layouts: 32.6 us -> 7.28 us
  blocking collectives: 57.8 us -> 69.8 us
  starting transfers between devices: 5.03 us -> 11 us
  matrix products: 15.1 us -> 11.8 us
    reduce_scatter x2 -> x0, waiting for transfers between devices: 85.4 us -> none  [the longest x1 85.4 us: per_device(): lax.psum_scatter(owned_grad, 'blk', scatter_dimension=1, tiled=True)]
    all_gather x0 -> x2, blocking collectives: none -> 63.8 us  [the longest x1 33.2 us: per_device(): all_hard = lax.all_gather(hard_grad, 'blk', axis=0, tiled=True)]
    all_to_all x1 -> x0, blocking collectives: 51 us -> none  [per_device(): lax.all_to_all(dense_grad, 'corpus', split_axis=0, concat_axis=1, tiled=T...]
    scatter-add x1 -> x0, other arithmetic: 44.6 us -> none  [per_device(): mixing = jnp.zeros((table_rows, q_rows), jnp.float32).at[flat_ids, query_...]
    all_gather x1, waiting for transfers between devices: 0.01 us -> 42.9 us  [per_device(): all_passages = lax.all_gather(passages, 'blk', axis=0, tiled=True)]
    all_to_all x1 -> x2, waiting for transfers between devices: 39.9 us -> 0.01 us  [the longest x1 0.01 us: per_device(): lax.all_to_all(soft_grad, 'blk', split_axis=1, concat_axis=0, tiled=True)]
    psum x1, waiting for transfers between devices: 25.2 us -> 0.01 us  [per_device(): logits, hard_logits = lax.psum((logits, hard_logits), 'corpus')]
    ppermute x0 -> x1, waiting for transfers between devices: none -> 19 us  [per_device(): table_grad = lax.ppermute(piece, ('blk', 'corpus'), perm)]
  transfers between devices with their start and end apart: 5 -> 6, of which waited for: 3 -> 3; matrix products, arithmetic and copies ran while one was open for 27% -> 14% of each run, Pallas kernels for 0% -> 0%
where the time goes in v1:
time: 191 us
  blocking collectives  69.8 us (37%)
  waiting for transfers between devices  67.3 us (35%)
  between operations  14 us (7%)
  matrix products  11.8 us (6%)
  starting transfers between devices  11 us (6%)
  other arithmetic  9.43 us (5%)
  local copies, waits for them, and re-layouts  7.28 us (4%)
    all_gather x1, waiting for transfers between devices, per_device(): all_passages = lax.all_gather(passages, 'blk', axis=0, tiled=True)  42.9 us
    all_gather x1, blocking collectives, per_device(): all_hard = lax.all_gather(hard_grad, 'blk', axis=0, tiled=True)  33.2 us
    all_gather x1, blocking collectives, per_device(): all_ids = lax.all_gather(ids, 'blk', axis=0, tiled=True)  30.6 us
    ppermute x1, waiting for transfers between devices, per_device(): table_grad = lax.ppermute(piece, ('blk', 'corpus'), perm)  19 us
    psum x1, blocking collectives, per_device(): logits, hard_logits = lax.psum((logits, hard_logits), 'corpus')  5.93 us
    unnamed x24, local copies, waits for them, and re-layouts  4.18 us
    all_gather x1, waiting for transfers between devices, per_device(): all_queries = lax.all_gather(queries, 'blk', axis=0, tiled=True)  3.95 us
  transfers between devices with their start and end apart: 6, of which 3 were waited for; matrix products, arithmetic and copies ran while one was open for 14% of the time, Pallas kernels for 0%

profile of v1, /device:TPU:2, one launch (start us, length us, event | category | flops | bytes accessed | tf_op | source)
XLA Modules:
  0.0 190.5 jit_solution(2006193391956256831)
XLA Ops:
  7.2 0.0 all-gather.3.cloned.1.call-start
  7.2 0.7 all-gather.3.cloned.1.call-update
  7.9 3.3 %copy.26 = bf16[256,4096]{0,1:T(8,128)(2,1)S(1)} copy(bf16[256,4096]{1,0:T(8,128)(2,1)} %param.9) | data formatting | bytes 4194304 | tf_op args[2]
  11.2 2.5 %copy.27 = bf16[256,4,1024]{2,0,1:T(8,128)(2,1)} copy(bf16[256,4,1024]{0,2,1:T(8,128)(2,1)S(1)} %bitcast.20) | data formatting | bytes 4194304 | tf_op jit(solution)/shard_map/all_to_all | solution.py:23
  13.7 0.0 copy-start.2
  13.7 3.7 %all-to-all-start = ((bf16[256,4,1024]{2,0,1:T(8,128)(2,1)}), bf16[256,4,1024]{2,0,1:T(8,128)(2,1)S(1)}, u32[]{:S(2)}, u32[]{:S(2)}) async-start(bf16[256,4,1024]{2,0,1:T(8,128)(2,1)} %copy.27), calls=%async_computation | async-start | bytes 4194304 | tf_op jit(solution)/shard_map/all_to_all | solution.py:23
  17.4 0.0 copy-start.8
  17.4 0.0 copy-start.9
  17.5 0.0 copy-start.10
  17.5 0.0 copy-start.3
  17.5 0.0 all-reduce.2.cloned.1.call-start
  17.5 42.9 %all-gather.3.cloned.1.call-done = bf16[1024,1024]{1,0:T(8,128)(2,1)} async-done(((bf16[128,1024]{1,0:T(8,128)(2,1)}), bf16[1024,1024]{1,0:T(8,128)(2,1)}) %all-gather.3.cloned.1.call-update) | async-done | bytes 2097168 | tf_op jit(solution)/shard_map/all_gather | solution.py:24
  60.5 0.0 copy-done.2
  60.5 3.2 %fusion.21 = f32[128,1024]{1,0:T(8,128)} fusion(bf16[128,1024]{1,0:T(8,128)(2,1)S(1)} %copy-done.2, bf16[1024,1024]{1,0:T(8,128)(2,1)} %all-gather.3.cloned.1.call-done), kind=kOutput, calls=%fused_computation.41 | convolution fusion | flops 268435456 | bytes 2883584 | tf_op jit(solution)/shard_map/dot_general | solution.py:30
  63.7 0.0 all-reduce.2.cloned.1.call-update
  63.7 0.0 all-gather.5.cloned.1.call-start
  63.7 0.7 all-gather.5.cloned.1.call-update
  64.4 0.0 copy-start.7
  64.5 0.0 copy-done.8
  64.5 0.0 copy-done.9
  64.5 30.6 %all_gather.14 = s32[1024,7]{0,1:T(8,128)S(1)} all-gather(s32[128,7]{0,1:T(8,128)S(1)} %multiply_add_fusion), channel_id=1, replica_groups=mesh['blk'=8,'corpus'=4] {'blk'}, dimensions={0}, use_global_device_ids=true | all-gather | bytes 32256 | tf_op jit(solution)/shard_map/all_gather | solution.py:27
  95.1 0.0 copy-done.10
  95.1 0.0 all-to-all-done
  95.1 0.0 copy-done.3
  95.1 0.8 fusion.22
  96.0 0.6 select_reduce_fusion.2
  96.6 5.9 %psum.15 = f32[128,7]{0,1:T(8,128)S(1)} all-reduce(f32[128,7]{0,1:T(8,128)S(1)} %select_reduce_fusion.2), channel_id=1, replica_groups=mesh['blk'=8,'corpus'=4] {'corpus'}, use_global_device_ids=true, to_apply=%region_3.4 | all-reduce | flops 896 | bytes 7168 | tf_op jit(solution)/shard_map/psum | solution.py:39
  102.5 0.0 all-reduce.2.cloned.1.call-done
  102.5 1.2 multiply_reduce_fusion
  103.7 0.0 copy-done.7
  103.7 1.4 select_reduce_fusion.3
  105.1 2.1 %copy_bitcast_fusion = bf16[128,8,128]{2,0,1:T(8,128)(2,1)} fusion(s32[128]{0:T(128)S(1)} %copy-done.7, f32[128]{0:T(128)S(1)} %get-tuple-element.11, f32[128,1024]{1,0:T(8,128)} %all-reduce.2.cloned.1.call-done, f32[128]{0:T(128)S(1)} %broadcast_multiply_fusion), kind=kLoop, calls=%fused_computation.26 | loop fusion | flops 917504 | bytes 787968 | tf_op jit(solution)/shard_map/all_to_all | solution.py:63
  107.2 3.4 %all-to-all-start.1 = ((bf16[128,8,128]{2,0,1:T(8,128)(2,1)}), bf16[128,8,128]{2,0,1:T(8,128)(2,1)S(1)}, u32[]{:S(2)}, u32[]{:S(2)}) async-start(bf16[128,8,128]{2,0,1:T(8,128)(2,1)} %copy_bitcast_fusion), calls=%async_computation.1 | async-start | bytes 524288 | tf_op jit(solution)/shard_map/all_to_all | solution.py:63
  110.6 33.2 %all_gather.15 = bf16[1024,7]{0,1:T(8,128)(2,1)S(1)} all-gather(bf16[128,7]{0,1:T(8,128)(2,1)S(1)} %get-tuple-element.9), channel_id=1, replica_groups=mesh['blk'=8,'corpus'=4] {'blk'}, dimensions={0}, use_global_device_ids=true | all-gather | bytes 16128 | tf_op jit(solution)/shard_map/all_gather | solution.py:68
  143.8 0.5 select_reduce_fusion.1
  144.3 0.9 subtract_convert_fusion.2
  145.2 2.5 %select_reduce_fusion = f32[1024,256]{1,0:T(8,128)S(1)} fusion(f32[1024,7]{0,1:T(8,128)S(1)} %convert_element_type.40, s32[256]{0:T(256)S(1)} %iota_add_fusion, s32[1024,7]{0,1:T(8,128)S(1)} %all_gather.14), kind=kLoop, calls=%fused_computation | loop fusion | flops 5242880 | bytes 1106944 | tf_op jit(solution)/shard_map/reduce_sum | solution.py:75
  147.7 3.9 %all-gather.5.cloned.1.call-done = bf16[1024,1024]{1,0:T(8,128)(2,1)} async-done(((bf16[128,1024]{1,0:T(8,128)(2,1)}), bf16[1024,1024]{1,0:T(8,128)(2,1)}) %all-gather.5.cloned.1.call-update) | async-done | bytes 2097168 | tf_op jit(solution)/shard_map/all_gather | solution.py:25
  151.7 0.0 copy-start
  151.7 1.8 fusion.7
  153.5 0.1 copy-done
  153.6 0.0 copy-start.1
  153.6 0.0 copy-start.4
  153.6 0.0 copy-start.5
  153.6 0.0 copy-start.6
  153.6 1.3 convolution_add_fusion
  154.9 3.7 %collective-permute-start = (f32[256,512]{1,0:T(8,128)}, f32[256,512]{1,0:T(8,128)S(1)}, u32[]{:S(2)}, u32[]{:S(2)}) collective-permute-start(f32[256,512]{1,0:T(8,128)} %convolution_add_fusion), channel_id=1, source_target_pairs={{0,0},{1,8},{2,16},{3,24},{4,4},{5,12},{6,20},{7,28},{8,1},{9,9},{... | collective-permute-start | bytes 1572872 | tf_op jit(solution)/shard_map/ppermute | solution.py:90
  158.6 0.0 copy-done.1
  158.7 0.3 multiply_convert_fusion
  158.9 0.0 copy-done.4
  159.0 0.0 copy-done.5
  159.0 0.0 copy-done.6
  159.0 1.8 fusion
  160.8 0.6 dynamic_slice.6
  161.4 0.0 all-to-all-done.1
  161.4 2.9 %fusion.23 = f32[128,1024]{1,0:T(8,128)} fusion(bf16[1024,128]{1,0:T(8,128)(2,1)S(1)} %bitcast.21, bf16[1024,1024]{1,0:T(8,128)(2,1)} %all-gather.5.cloned.1.call-done), kind=kOutput, calls=%fused_computation.43 | convolution fusion | flops 268435456 | bytes 2883584 | tf_op jit(solution)/shard_map/dot_general | solution.py:64
  164.2 19.0 %collective-permute-done = f32[256,512]{1,0:T(8,128)S(1)} collective-permute-done((f32[256,512]{1,0:T(8,128)}, f32[256,512]{1,0:T(8,128)S(1)}, u32[]{:S(2)}, u32[]{:S(2)}) %collective-permute-start) | collective-permute-done | bytes 524320 | tf_op jit(solution)/shard_map/ppermute | solution.py:90
  183.2 0.8 copy.33
  (9 shorter events, 0.1 us)
Async XLA Ops:
  7.2 53.3 %all-gather.3.cloned.1.call-start = ((), (), s32[]{:S(2)}) async-start(), calls=%async_computation.2 | async-start | bytes 2359296 | tf_op jit(solution)/shard_map/all_gather | solution.py:24
  13.7 46.8 %copy-start.2 = (bf16[128,1024]{1,0:T(8,128)(2,1)S(1)}, bf16[128,1024]{1,0:T(8,128)(2,1)}, u32[]{:S(2)}) copy-start(bf16[128,1024]{1,0:T(8,128)(2,1)} %param.7) | copy-start | bytes 786436
  13.7 81.4 %all-to-all-start = ((bf16[256,4,1024]{2,0,1:T(8,128)(2,1)}), bf16[256,4,1024]{2,0,1:T(8,128)(2,1)S(1)}, u32[]{:S(2)}, u32[]{:S(2)}) async-start(bf16[256,4,1024]{2,0,1:T(8,128)(2,1)} %copy.27), calls=%async_computation | async-start | bytes 4194304 | tf_op jit(solution)/shard_map/all_to_all | solution.py:23
  17.4 47.0 %copy-start.8 = (s32[128,7]{0,1:T(8,128)S(1)}, s32[128,7]{0,1:T(8,128)}, u32[]{:S(2)}) copy-start(s32[128,7]{0,1:T(8,128)} %param.11) | copy-start | bytes 10756
  17.4 47.0 %copy-start.9 = (s32[128,7]{0,1:T(8,128)S(1)}, s32[128,7]{0,1:T(8,128)}, u32[]{:S(2)}) copy-start(s32[128,7]{0,1:T(8,128)} %param.10) | copy-start | bytes 10756
  17.5 77.7 %copy-start.10 = (f32[128]{0:T(128)S(1)}, f32[128]{0:T(128)}, u32[]{:S(2)}) copy-start(f32[128]{0:T(128)} %param.13) | copy-start | bytes 1540
  17.5 77.7 %copy-start.3 = (bf16[128,1024]{1,0:T(8,128)(2,1)S(1)}, bf16[128,1024]{1,0:T(8,128)(2,1)}, u32[]{:S(2)}) copy-start(bf16[128,1024]{1,0:T(8,128)(2,1)} %param.7) | copy-start | bytes 786436
  17.5 85.1 %all-reduce.2.cloned.1.call-start = ((), (), s32[]{:S(2)}) async-start(), calls=%async_computation.3 | async-start | bytes 1048576 | tf_op jit(solution)/shard_map/psum | solution.py:39
  63.7 88.0 %all-gather.5.cloned.1.call-start = ((), (), s32[]{:S(2)}) async-start(), calls=%async_computation.4 | async-start | bytes 2359296 | tf_op jit(solution)/shard_map/all_gather | solution.py:25
  64.4 39.3 %copy-start.7 = (s32[128]{0:T(128)S(1)}, s32[128]{0:T(128)}, u32[]{:S(2)}) copy-start(s32[128]{0:T(128)} %param.12) | copy-start | bytes 1540
  107.2 54.2 %all-to-all-start.1 = ((bf16[128,8,128]{2,0,1:T(8,128)(2,1)}), bf16[128,8,128]{2,0,1:T(8,128)(2,1)S(1)}, u32[]{:S(2)}, u32[]{:S(2)}) async-start(bf16[128,8,128]{2,0,1:T(8,128)(2,1)} %copy_bitcast_fusion), calls=%async_computation.1 | async-start | bytes 524288 | tf_op jit(solution)/shard_map/all_to_all | solution.py:63
  151.7 1.9 %copy-start = (bf16[1024,1024]{1,0:T(8,128)(2,1)S(1)}, bf16[1024,1024]{1,0:T(8,128)(2,1)}, u32[]{:S(2)}) copy-start(bf16[1024,1024]{1,0:T(8,128)(2,1)} %all-gather.5.cloned.1.call-done) | copy-start | bytes 6291460
  153.6 5.0 %copy-start.1 = (f32[128,1024]{1,0:T(8,128)S(1)}, f32[128,1024]{1,0:T(8,128)}, u32[]{:S(2)}) copy-start(f32[128,1024]{1,0:T(8,128)} %all-reduce.2.cloned.1.call-done) | copy-start | bytes 1572868
  153.6 5.3 %copy-start.4 = (bf16[1024,1024]{1,0:T(8,128)(2,1)S(1)}, bf16[1024,1024]{1,0:T(8,128)(2,1)}, u32[]{:S(2)}) copy-start(bf16[1024,1024]{1,0:T(8,128)(2,1)} %all-gather.3.cloned.1.call-done) | copy-start | bytes 6291460
  153.6 5.3 %copy-start.5 = (bf16[128,1024]{1,0:T(8,128)(2,1)S(1)}, bf16[128,1024]{1,0:T(8,128)(2,1)}, u32[]{:S(2)}) copy-start(bf16[128,1024]{1,0:T(8,128)(2,1)} %get-tuple-element.6) | copy-start | bytes 786436
  153.6 5.4 %copy-start.6 = (bf16[128,1024]{1,0:T(8,128)(2,1)S(1)}, bf16[128,1024]{1,0:T(8,128)(2,1)}, u32[]{:S(2)}) copy-start(bf16[128,1024]{1,0:T(8,128)(2,1)} %get-tuple-element.7) | copy-start | bytes 786436
  154.9 28.3 %collective-permute-start = (f32[256,512]{1,0:T(8,128)}, f32[256,512]{1,0:T(8,128)S(1)}, u32[]{:S(2)}, u32[]{:S(2)}) collective-permute-start(f32[256,512]{1,0:T(8,128)} %convolution_add_fusion), channel_id=1, source_target_pairs={{0,0},{1,8},{2,16},{3,24},{4,4},{5,12},{6,20},{7,28},{8,1},{9,9},{... | collective-permute-start | bytes 1572872 | tf_op jit(solution)/shard_map/ppermute | solution.py:90
Sparse Core Ops, SparseCore 0:
  10.1 50.3 all-gather.2
  63.8 30.5 all-reduce.1
  96.6 55.0 all-gather.4

commit v2 on v1

--- a/solution.py
+++ b/solution.py
@@ -10,7 +10,7 @@
     return upper, lower
 
 
-def per_device(queries, passages, table, neg_owner, neg_row, positive, loss_weight):
+def per_device_body(queries, passages, table, neg_owner, neg_row, positive, loss_weight):
     q_rows, col_width = queries.shape
     owner_count = lax.axis_size("corpus")
     blk_count = lax.axis_size("blk")
@@ -20,11 +20,28 @@
     owner_index = lax.axis_index("corpus")
     blk_index = lax.axis_index("blk")
 
-    table_cols = lax.all_to_all(table, "corpus", split_axis=1, concat_axis=0, tiled=True)
+    slice_of = lambda k: lax.dynamic_slice_in_dim(
+        table, ((owner_index + k) % owner_count) * col_width, col_width, axis=1
+    )
+    table_cols = jnp.zeros((table_rows, col_width), table.dtype)
+    table_cols = lax.dynamic_update_slice_in_dim(
+        table_cols, slice_of(0), owner_index * rows_shard, axis=0
+    )
+    for k in range(1, owner_count):
+        shift = [(j, (j + k) % owner_count) for j in range(owner_count)]
+        got = lax.ppermute(slice_of(k), "corpus", shift)
+        source = (owner_index - k) % owner_count
+        table_cols = lax.dynamic_update_slice_in_dim(table_cols, got, source * rows_shard, axis=0)
     all_passages = lax.all_gather(passages, "blk", axis=0, tiled=True)
-    all_queries = lax.all_gather(queries, "blk", axis=0, tiled=True)
+    all_passages, later = lax.optimization_barrier((all_passages, queries))
+    all_queries = jnp.zeros((blk_count * q_rows, col_width), queries.dtype)
+    all_queries = lax.dynamic_update_slice_in_dim(all_queries, queries, blk_index * q_rows, axis=0)
+    for k in range(1, blk_count):
+        shift = [(j, (j + k) % blk_count) for j in range(blk_count)]
+        got = lax.ppermute(later, "blk", shift)
+        source = (blk_index - k) % blk_count
+        all_queries = lax.dynamic_update_slice_in_dim(all_queries, got, source * q_rows, axis=0)
     ids = neg_owner * rows_shard + neg_row
-    all_ids = lax.all_gather(ids, "blk", axis=0, tiled=True)
     all_rows = all_passages.shape[0]
 
     logits = lax.dot_general(
@@ -36,23 +53,46 @@
     row_iota = jnp.arange(table_rows, dtype=jnp.int32)
     picks = ids[:, :, None] == row_iota[None, None, :]
     hard_logits = jnp.sum(jnp.where(picks, table_scores[:, None, :], 0.0), axis=2)
-    logits, hard_logits = lax.psum((logits, hard_logits), "corpus")
-    logits = logits * factor
-    hard_logits = hard_logits * factor
+    negs = ids.shape[1]
+    pad = jnp.zeros((q_rows, 128 - negs), jnp.float32)
+    partial = jnp.concatenate([logits, hard_logits, pad], axis=1)
+    share = q_rows // owner_count
+    chunk_of = lambda k: lax.dynamic_slice_in_dim(
+        partial, ((owner_index + k) % owner_count) * share, share, axis=0
+    )
+    summed = chunk_of(0)
+    for k in range(1, owner_count):
+        shift = [(j, (j + k) % owner_count) for j in range(owner_count)]
+        got = lax.ppermute(chunk_of(k), "corpus", shift)
+        summed = summed + got
+    logits = summed[:, :all_rows] * factor
+    hard_logits = summed[:, all_rows:all_rows + negs] * factor
+    my_positive = lax.dynamic_slice_in_dim(positive, owner_index * share, share)
+    my_weight = lax.dynamic_slice_in_dim(loss_weight, owner_index * share, share)
     row_top = jnp.maximum(jnp.max(logits, axis=1), jnp.max(hard_logits, axis=1))
     log_total = row_top + jnp.log(
         jnp.sum(jnp.exp(logits - row_top[:, None]), axis=1)
         + jnp.sum(jnp.exp(hard_logits - row_top[:, None]), axis=1)
     )
-    one_hot = positive[:, None] == jnp.arange(all_rows, dtype=jnp.int32)[None, :]
-    losses = log_total - jnp.sum(jnp.where(one_hot, logits, 0.0), axis=1)
-    share = q_rows // owner_count
-    loss_share = lax.dynamic_slice_in_dim(losses, owner_index * share, share)
-    weighting = (loss_weight * factor)[:, None]
-    soft_grad = (
+    one_hot = my_positive[:, None] == jnp.arange(all_rows, dtype=jnp.int32)[None, :]
+    loss_share = log_total - jnp.sum(jnp.where(one_hot, logits, 0.0), axis=1)
+    weighting = (my_weight * factor)[:, None]
+    soft_part = (
         weighting * (jnp.exp(logits - log_total[:, None]) - one_hot.astype(jnp.float32))
     ).astype(jnp.bfloat16)
-    hard_grad = (weighting * jnp.exp(hard_logits - log_total[:, None])).astype(jnp.bfloat16)
+    hard_part = (weighting * jnp.exp(hard_logits - log_total[:, None])).astype(jnp.bfloat16)
+    grads_part = jnp.concatenate(
+        [soft_part, hard_part, jnp.zeros((share, 128 - negs), jnp.bfloat16)], axis=1
+    )
+    grads = jnp.zeros((q_rows, grads_part.shape[1]), jnp.bfloat16)
+    grads = lax.dynamic_update_slice_in_dim(grads, grads_part, owner_index * share, axis=0)
+    for k in range(1, owner_count):
+        shift = [(j, (j + k) % owner_count) for j in range(owner_count)]
+        got = lax.ppermute(grads_part, "corpus", shift)
+        source = (owner_index - k) % owner_count
+        grads = lax.dynamic_update_slice_in_dim(grads, got, source * share, axis=0)
+    soft_grad = grads[:, :all_rows]
+    hard_grad = grads[:, all_rows:all_rows + negs]
 
     mixing = jnp.sum(jnp.where(picks, hard_grad.astype(jnp.float32)[:, :, None], 0.0), axis=1)
     mix_hi, mix_lo = hi_lo(mixing)
@@ -60,12 +100,34 @@
     right = jnp.concatenate([all_passages, table_cols, table_cols], axis=0)
     query_grad = jnp.dot(left, right, preferred_element_type=jnp.float32)
 
-    soft_cols = lax.all_to_all(soft_grad, "blk", split_axis=1, concat_axis=0, tiled=True)
+    extra = jnp.concatenate(
+        [
+            hard_grad,
+            neg_owner.astype(jnp.bfloat16),
+            neg_row.astype(jnp.bfloat16),
+            jnp.zeros((q_rows, 32 - 3 * negs), jnp.bfloat16),
+        ],
+        axis=1,
+    )
+    cols_per = all_rows // blk_count
+    packed = jnp.concatenate(
+        [
+            soft_grad.reshape(q_rows, blk_count, cols_per),
+            jnp.broadcast_to(extra[:, None, :], (q_rows, blk_count, 32)),
+        ],
+        axis=2,
+    ).reshape(q_rows, blk_count * (cols_per + 32))
+    moved = lax.all_to_all(packed, "blk", split_axis=1, concat_axis=0, tiled=True)
+    soft_cols = moved[:, :cols_per]
+    all_hard = moved[:, cols_per:cols_per + negs]
+    all_ids = (
+        moved[:, cols_per + negs:cols_per + 2 * negs].astype(jnp.int32) * rows_shard
+        + moved[:, cols_per + 2 * negs:cols_per + 3 * negs].astype(jnp.int32)
+    )
     passage_grad = lax.dot_general(
         soft_cols, all_queries, (((0,), (0,)), ((), ())), preferred_element_type=jnp.float32
     )
 
-    all_hard = lax.all_gather(hard_grad, "blk", axis=0, tiled=True)
     per_col = blk_count // owner_count
     piece_width = col_width // per_col
     shard = blk_index // per_col
@@ -102,7 +164,7 @@
         P("blk"),
     )
     return jax.shard_map(
-        per_device,
+        per_device_body,
         mesh=mesh,
         in_specs=placed,
         out_specs=(

time: 191 us -> 172 us (0.901)
  blocking collectives: 69.8 us -> 0 us
  starting transfers between devices: 11 us -> 32.5 us
  local copies, waits for them, and re-layouts: 7.28 us -> 25.4 us
  waiting for transfers between devices: 67.3 us -> 84 us
  matrix products: 11.8 us -> 7.15 us
  other arithmetic: 9.43 us -> 6.52 us
    all_gather x2 -> x0, blocking collectives: 63.8 us -> none  [the longest x1 33.2 us: per_device(): all_hard = lax.all_gather(hard_grad, 'blk', axis=0, tiled=True)]
    ppermute x1 -> x17, waiting for transfers between devices: 19 us -> 58.4 us  [the longest x1 20.1 us: per_device_body(): table_grad = lax.ppermute(piece, ('blk', 'corpus'), perm)]
    ppermute x1 -> x17, starting transfers between devices: 3.74 us -> 28 us  [the longest x7 12.4 us: per_device_body(): got = lax.ppermute(later, 'blk', shift)]
    all_gather x2 -> x1, waiting for transfers between devices: 46.9 us -> 24.9 us  [per_device_body(): all_passages = lax.all_gather(passages, 'blk', axis=0, tiled=True)]
    dynamic_update_slice x0 -> x15, local copies, waits for them, and re-layouts: none -> 16.8 us  [the longest x3 7.69 us: per_device_body(): grads = lax.dynamic_update_slice_in_dim(grads, got, source * share, axis=0)]
    psum x1 -> x0, blocking collectives: 5.93 us -> none  [per_device(): logits, hard_logits = lax.psum((logits, hard_logits), 'corpus')]
    dot_general x6, matrix products: 11.8 us -> 7.15 us  [the longest x1 2.41 us: per_device_body(): lax.dot_general(queries, all_passages, (((1,), (1,)), ((), ())), preferre...]
    all_to_all x2 -> x1, starting transfers between devices: 7.14 us -> 4.52 us  [per_device_body(): lax.all_to_all(packed, 'blk', split_axis=1, concat_axis=0, tiled=True)]
  transfers between devices with their start and end apart: 6 -> 19, of which waited for: 3 -> 8; matrix products, arithmetic and copies ran while one was open for 14% -> 16% of each run, Pallas kernels for 0% -> 0%
where the time goes in v2:
time: 172 us; the launch traced here: 170 us
  waiting for transfers between devices  84 us (49%)
  starting transfers between devices  32.5 us (19%)
  local copies, waits for them, and re-layouts  25.4 us (15%)
  between operations  14.6 us (8%)
  matrix products  7.15 us (4%)
  other arithmetic  6.52 us (4%)
    all_gather x1, waiting for transfers between devices, per_device_body(): all_passages = lax.all_gather(passages, 'blk', axis=0, tiled=True)  24.9 us
    ppermute x1, waiting for transfers between devices, per_device_body(): table_grad = lax.ppermute(piece, ('blk', 'corpus'), perm)  20.1 us
    ppermute x3, waiting for transfers between devices, per_device_body(): got = lax.ppermute(slice_of(k), 'corpus', shift)  20.1 us
    ppermute x7, starting transfers between devices, per_device_body(): got = lax.ppermute(later, 'blk', shift)  12.4 us
    ppermute x7, waiting for transfers between devices, per_device_body(): got = lax.ppermute(later, 'blk', shift)  11.9 us
    ppermute x1, starting transfers between devices, per_device_body(): table_grad = lax.ppermute(piece, ('blk', 'corpus'), perm)  10 us
    dynamic_update_slice x3, local copies, waits for them, and re-layouts, per_device_body(): grads = lax.dynamic_update_slice_in_dim(grads, got, source * share, axis=0)  7.69 us
    ppermute x3, waiting for transfers between devices, per_device_body(): got = lax.ppermute(chunk_of(k), 'corpus', shift)  6.21 us
  transfers between devices with their start and end apart: 19, of which 8 were waited for; matrix products, arithmetic and copies ran while one was open for 16% of the time, Pallas kernels for 0%

profile of v2, /device:TPU:2, one launch (start us, length us, event | category | flops | bytes accessed | tf_op | source)
XLA Modules:
  0.0 170.2 jit_solution(16955753170632354659)
XLA Ops:
  7.2 0.7 all-gather.2.cloned.1.call-update
  8.0 0.3 broadcast.31.clone
  8.2 1.3 copy-done.3
  9.6 1.2 constant_dynamic-slice_fusion.3
  10.8 1.7 %collective-permute-start.2 = (bf16[256,1024]{1,0:T(8,128)(2,1)}, bf16[256,1024]{1,0:T(8,128)(2,1)S(1)}, u32[]{:S(2)}, u32[]{:S(2)}) collective-permute-start(bf16[256,1024]{1,0:T(8,128)(2,1)} %get-tuple-element.14), channel_id=1, source_target_pairs={{0,3},{1,0},{2,1},{3,2},{4,7},{5,4},{6,5},{7,6},{8,11},{9,8},{10,9... | collective-permute-start | bytes 1572872 | tf_op jit(solution)/shard_map/ppermute | solution.py:32
  12.5 12.2 %collective-permute-done = bf16[256,1024]{1,0:T(8,128)(2,1)} collective-permute-done((bf16[256,1024]{1,0:T(8,128)(2,1)}, bf16[256,1024]{1,0:T(8,128)(2,1)}, u32[]{:S(2)}, u32[]{:S(2)}) %collective-permute-start) | collective-permute-done | bytes 524320 | tf_op jit(solution)/shard_map/ppermute | solution.py:32
  24.7 1.1 constant_dynamic-update-slice_fusion.10
  25.9 7.9 %collective-permute-done.2 = bf16[256,1024]{1,0:T(8,128)(2,1)S(1)} collective-permute-done((bf16[256,1024]{1,0:T(8,128)(2,1)}, bf16[256,1024]{1,0:T(8,128)(2,1)S(1)}, u32[]{:S(2)}, u32[]{:S(2)}) %collective-permute-start.2) | collective-permute-done | bytes 524320 | tf_op jit(solution)/shard_map/ppermute | solution.py:32
  33.8 0.7 convolution_bitcast_fusion
  34.5 0.2 copy.69
  34.8 0.6 select_reduce_fusion.2
  35.4 0.1 copy.70
  35.5 24.9 %all-gather.2.cloned.1.call-done = bf16[1024,1024]{1,0:T(8,128)(2,1)} async-done(((bf16[128,1024]{1,0:T(8,128)(2,1)}), bf16[1024,1024]{1,0:T(8,128)(2,1)}) %all-gather.2.cloned.1.call-update) | async-done | bytes 2097168 | tf_op jit(solution)/shard_map/all_gather | solution.py:35
  60.4 2.4 %convolution_bitcast_fusion.1 = f32[128,1024]{1,0:T(8,128)S(1)} fusion(bf16[1024,1024]{1,0:T(8,128)(2,1)} %all-gather.2.cloned.1.call-done, bf16[128,1024]{1,0:T(8,128)(2,1)S(1)} %copy-done.2), kind=kOutput, calls=%fused_computation.12 | convolution fusion | flops 268435456 | bytes 2883584 | tf_op jit(solution)/shard_map/dot_general | solution.py:47
  62.9 0.7 constant_dynamic-slice_fusion.2
  63.7 0.6 collective-permute-start.4
  64.3 0.2 collective-permute-start.3
  64.5 0.6 dynamic-slice_multiply_fusion
  65.2 0.6 pad.5.clone
  65.8 0.3 broadcast.31.clone.1
  66.1 1.9 %collective-permute-done.5 = f32[32,1152]{1,0:T(8,128)S(1)} collective-permute-done((f32[32,1152]{1,0:T(8,128)}, f32[32,1152]{1,0:T(8,128)S(1)}, u32[]{:S(2)}, u32[]{:S(2)}) %collective-permute-start.5) | collective-permute-done | bytes 147488 | tf_op jit(solution)/shard_map/ppermute | solution.py:66
  68.1 3.3 %collective-permute-done.4 = f32[32,1152]{1,0:T(8,128)S(1)} collective-permute-done((f32[32,1152]{1,0:T(8,128)}, f32[32,1152]{1,0:T(8,128)S(1)}, u32[]{:S(2)}, u32[]{:S(2)}) %collective-permute-start.4) | collective-permute-done | bytes 147488 | tf_op jit(solution)/shard_map/ppermute | solution.py:66
  71.4 1.0 collective-permute-done.3
  72.4 0.1 fusion.18
  72.5 0.1 fusion.19
  72.6 0.2 exponential_reduce_fusion.1
  72.8 0.2 select_reduce_fusion.3
  73.0 0.5 fusion.23
  73.9 1.5 collective-permute-start.7
  75.4 1.4 collective-permute-start.8
  76.8 0.6 collective-permute-start.9
  77.4 1.6 collective-permute-start.10
  79.0 0.2 copy.71
  79.3 3.0 %dynamic_update_slice.52 = bf16[128,1152]{0,1:T(8,128)(2,1)S(1)} dynamic-update-slice(bf16[128,1152]{0,1:T(8,128)(2,1)S(1)} %broadcast_in_dim.74, bf16[32,1152]{0,1:T(8,128)(2,1)S(1)} %copy.71, s32[]{:T(128)S(6)} %select_n.194, s32[]{:T(128)} %constant.140.clone.1) | dynamic-update-slice | bytes 147460 | tf_op jit(solution)/shard_map/dynamic_update_slice | solution.py:88
  82.2 1.8 %collective-permute-start.11 = (bf16[128,1024]{1,0:T(8,128)(2,1)S(1)}, bf16[128,1024]{1,0:T(8,128)(2,1)}, u32[]{:S(2)}, u32[]{:S(2)}) collective-permute-start(bf16[128,1024]{1,0:T(8,128)(2,1)S(1)} %copy-done.2), channel_id=1, source_target_pairs={{0,12},{4,16},{8,20},{12,24},{16,28},{20,0},{24,4},{28,8},{1,13},{... | collective-permute-start | bytes 786440 | tf_op jit(solution)/shard_map/ppermute | solution.py:41
  84.1 0.2 copy.72
  84.3 3.0 %dynamic_update_slice.53 = bf16[128,1152]{0,1:T(8,128)(2,1)S(1)} dynamic-update-slice(bf16[128,1152]{0,1:T(8,128)(2,1)S(1)} %dynamic_update_slice.52, bf16[32,1152]{0,1:T(8,128)(2,1)S(1)} %copy.72, s32[]{:T(128)S(6)} %select_n.196, s32[]{:T(128)} %constant.140.clone.1) | dynamic-update-slice | bytes 147460 | tf_op jit(solution)/shard_map/dynamic_update_slice | solution.py:93
  87.3 3.0 %collective-permute-start.12 = (bf16[128,1024]{1,0:T(8,128)(2,1)S(1)}, bf16[128,1024]{1,0:T(8,128)(2,1)}, u32[]{:S(2)}, u32[]{:S(2)}) collective-permute-start(bf16[128,1024]{1,0:T(8,128)(2,1)S(1)} %copy-done.2), channel_id=1, source_target_pairs={{0,16},{4,20},{8,24},{12,28},{16,0},{20,4},{24,8},{28,12},{1,17},{... | collective-permute-start | bytes 786440 | tf_op jit(solution)/shard_map/ppermute | solution.py:41
  90.3 0.2 copy.73
  90.6 1.7 %dynamic_update_slice.54 = bf16[128,1152]{0,1:T(8,128)(2,1)S(1)} dynamic-update-slice(bf16[128,1152]{0,1:T(8,128)(2,1)S(1)} %dynamic_update_slice.53, bf16[32,1152]{0,1:T(8,128)(2,1)S(1)} %copy.73, s32[]{:T(128)S(6)} %select_n.197, s32[]{:T(128)} %constant.140.clone.1) | dynamic-update-slice | bytes 147460 | tf_op jit(solution)/shard_map/dynamic_update_slice | solution.py:93
  92.4 0.2 copy.74
  92.6 3.0 %dynamic_update_slice.55 = bf16[128,1152]{0,1:T(8,128)(2,1)S(1)} dynamic-update-slice(bf16[128,1152]{0,1:T(8,128)(2,1)S(1)} %dynamic_update_slice.54, bf16[32,1152]{0,1:T(8,128)(2,1)S(1)} %copy.74, s32[]{:T(128)S(6)} %select_n.198, s32[]{:T(128)} %constant.140.clone.1) | dynamic-update-slice | bytes 147460 | tf_op jit(solution)/shard_map/dynamic_update_slice | solution.py:93
  95.6 0.7 copy-done.5
  96.3 0.5 select_reduce_fusion.1
  96.8 0.2 copy.75
  97.2 1.0 slice.34
  98.2 0.7 pad_maximum_fusion
  98.9 4.5 %all-to-all-start = ((bf16[128,8,160]{0,2,1:T(8,128)(2,1)}), bf16[128,8,160]{0,2,1:T(8,128)(2,1)S(1)}, u32[]{:S(2)}, u32[]{:S(2)}) async-start(bf16[128,8,160]{0,2,1:T(8,128)(2,1)} %pad_maximum_fusion), calls=%async_computation | async-start | bytes 655360 | tf_op jit(solution)/shard_map/all_to_all | solution.py:120
  103.4 3.8 %collective-permute-start.14 = (bf16[128,1024]{1,0:T(8,128)(2,1)S(1)}, bf16[128,1024]{1,0:T(8,128)(2,1)S(1)}, u32[]{:S(2)}, u32[]{:S(2)}) collective-permute-start(bf16[128,1024]{1,0:T(8,128)(2,1)S(1)} %copy-done.2), channel_id=1, source_target_pairs={{0,24},{4,28},{8,0},{12,4},{16,8},{20,12},{24,16},{28,20},{1,25},{... | collective-permute-start | bytes 786440 | tf_op jit(solution)/shard_map/ppermute | solution.py:41
  107.2 1.0 constant_dynamic-update-slice_fusion.6
  108.2 1.5 collective-permute-start.15
  109.7 1.0 constant_dynamic-update-slice_fusion.5
  110.7 1.0 constant_dynamic-update-slice_fusion.4
  111.7 1.0 constant_dynamic-update-slice_fusion.3
  112.7 1.0 constant_dynamic-update-slice_fusion.2
  113.7 11.9 %collective-permute-done.14 = bf16[128,1024]{1,0:T(8,128)(2,1)S(1)} collective-permute-done((bf16[128,1024]{1,0:T(8,128)(2,1)S(1)}, bf16[128,1024]{1,0:T(8,128)(2,1)S(1)}, u32[]{:S(2)}, u32[]{:S(2)}) %collective-permute-start.14) | collective-permute-done | bytes 262176 | tf_op jit(solution)/shard_map/ppermute | solution.py:41
  125.7 2.5 %select_reduce_fusion = f32[1024,256]{1,0:T(8,128)S(1)} fusion(f32[1024,7]{0,1:T(8,128)S(1)} %slice_convert_fusion, s32[256]{0:T(256)S(1)} %iota_add_fusion, s32[1024,7]{0,1:T(8,128)S(1)} %convert_add_fusion), kind=kLoop, calls=%fused_computation | loop fusion | flops 5242880 | bytes 1106944 | tf_op jit(solution)/shard_map/reduce_sum | solution.py:137
  128.3 0.5 fusion.6
  128.8 0.5 convolution_add_fusion
  129.3 10.0 %collective-permute-start.16 = (f32[256,512]{1,0:T(8,128)S(1)}, f32[256,512]{1,0:T(8,128)S(1)}, u32[]{:S(2)}, u32[]{:S(2)}) collective-permute-start(f32[256,512]{1,0:T(8,128)S(1)} %convolution_add_fusion), channel_id=1, source_target_pairs={{0,0},{1,8},{2,16},{3,24},{4,4},{5,12},{6,20},{7,28},{8,1},{9,9},{... | collective-permute-start | bytes 1572872 | tf_op jit(solution)/shard_map/ppermute | solution.py:152
  139.3 1.8 %fusion = f32[128,1024]{1,0:T(8,128)} fusion(bf16[1024,1024]{1,0:T(8,128)(2,1)S(1)} %copy-done.1, bf16[1024,1024]{1,0:T(8,128)(2,1)S(1)} %copy-done.4, bf16[128,1024]{0,1:T(8,128)(2,1)S(1)} %get-tuple-element.10, bf16[128,1024]{0,1:T(8,128)(2,1)S(1)} %get-tuple-element.11, bf16[128,1024]{0,1:T(8,128)(2,1)S(1)} %slice.34), kind=kOutput, calls=%fused_computation.1 | convolution fusion | flops 826540032 | bytes 5505024 | tf_op jit(solution)/shard_map/dot_general | solution.py:101
  141.2 1.3 fusion.14
  142.4 20.1 %collective-permute-done.16 = f32[256,512]{1,0:T(8,128)S(1)} collective-permute-done((f32[256,512]{1,0:T(8,128)S(1)}, f32[256,512]{1,0:T(8,128)S(1)}, u32[]{:S(2)}, u32[]{:S(2)}) %collective-permute-start.16) | collective-permute-done | bytes 524320 | tf_op jit(solution)/shard_map/ppermute | solution.py:152
  162.6 0.8 copy.98
  (64 shorter events, 1.2 us)
Async XLA Ops:
  7.2 53.2 %all-gather.2.cloned.1.call-start = ((), (), s32[]{:S(2)}) async-start(), calls=%async_computation.1 | async-start | bytes 2359296 | tf_op jit(solution)/shard_map/all_gather | solution.py:35
  8.0 1.6 copy-start.3
  9.6 2.9 %copy-start.6 = (s32[128,7]{0,1:T(8,128)S(1)}, s32[128,7]{0,1:T(8,128)}, u32[]{:S(2)}) copy-start(s32[128,7]{0,1:T(8,128)} %param.10) | copy-start | bytes 10756
  9.6 2.9 %copy-start.7 = (s32[128,7]{0,1:T(8,128)S(1)}, s32[128,7]{0,1:T(8,128)}, u32[]{:S(2)}) copy-start(s32[128,7]{0,1:T(8,128)} %param.11) | copy-start | bytes 10756
  10.7 23.1 %copy-start.2 = (bf16[128,1024]{1,0:T(8,128)(2,1)S(1)}, bf16[128,1024]{1,0:T(8,128)(2,1)}, u32[]{:S(2)}) copy-start(bf16[128,1024]{1,0:T(8,128)(2,1)} %param.7) | copy-start | bytes 786436
  10.7 14.0 %collective-permute-start = (bf16[256,1024]{1,0:T(8,128)(2,1)}, bf16[256,1024]{1,0:T(8,128)(2,1)}, u32[]{:S(2)}, u32[]{:S(2)}) collective-permute-start(bf16[256,1024]{1,0:T(8,128)(2,1)} %get-tuple-element.15), channel_id=1, source_target_pairs={{0,1},{1,2},{2,3},{3,0},{4,5},{5,6},{6,7},{7,4},{8,9},{9,10},{10,1... | collective-permute-start | bytes 1572872 | tf_op jit(solution)/shard_map/ppermute | solution.py:32
  10.8 15.0 %collective-permute-start.1 = (bf16[256,1024]{1,0:T(8,128)(2,1)}, bf16[256,1024]{1,0:T(8,128)(2,1)S(1)}, u32[]{:S(2)}, u32[]{:S(2)}) collective-permute-start(bf16[256,1024]{1,0:T(8,128)(2,1)} %get-tuple-element.17), channel_id=1, source_target_pairs={{0,2},{1,3},{2,0},{3,1},{4,6},{5,7},{6,4},{7,5},{8,10},{9,11},{10,... | collective-permute-start | bytes 1572872 | tf_op jit(solution)/shard_map/ppermute | solution.py:32
  10.8 23.0 %collective-permute-start.2 = (bf16[256,1024]{1,0:T(8,128)(2,1)}, bf16[256,1024]{1,0:T(8,128)(2,1)S(1)}, u32[]{:S(2)}, u32[]{:S(2)}) collective-permute-start(bf16[256,1024]{1,0:T(8,128)(2,1)} %get-tuple-element.14), channel_id=1, source_target_pairs={{0,3},{1,0},{2,1},{3,2},{4,7},{5,4},{6,5},{7,6},{8,11},{9,8},{10,9... | collective-permute-start | bytes 1572872 | tf_op jit(solution)/shard_map/ppermute | solution.py:32
  33.8 1.5 copy-start
  35.5 29.1 %copy-start.10 = (f32[128]{0:T(128)S(1)}, f32[128]{0:T(128)}, u32[]{:S(2)}) copy-start(f32[128]{0:T(128)} %param.13) | copy-start | bytes 1540
  35.5 29.6 %copy-start.11 = (s32[128]{0:T(128)S(1)}, s32[128]{0:T(128)}, u32[]{:S(2)}) copy-start(s32[128]{0:T(128)} %param.12) | copy-start | bytes 1540
  63.7 4.4 %collective-permute-start.5 = (f32[32,1152]{1,0:T(8,128)}, f32[32,1152]{1,0:T(8,128)S(1)}, u32[]{:S(2)}, u32[]{:S(2)}) collective-permute-start(f32[32,1152]{1,0:T(8,128)} %get-tuple-element.19), channel_id=1, source_target_pairs={{0,3},{1,0},{2,1},{3,2},{4,7},{5,4},{6,5},{7,6},{8,11},{9,8},{10,9... | collective-permute-start | bytes 442376 | tf_op jit(solution)/shard_map/ppermute | solution.py:66
  63.7 7.7 %collective-permute-start.4 = (f32[32,1152]{1,0:T(8,128)}, f32[32,1152]{1,0:T(8,128)S(1)}, u32[]{:S(2)}, u32[]{:S(2)}) collective-permute-start(f32[32,1152]{1,0:T(8,128)} %get-tuple-element.20), channel_id=1, source_target_pairs={{0,2},{1,3},{2,0},{3,1},{4,6},{5,7},{6,4},{7,5},{8,10},{9,11},{10,... | collective-permute-start | bytes 442376 | tf_op jit(solution)/shard_map/ppermute | solution.py:66
  64.3 8.1 %collective-permute-start.3 = (f32[32,1152]{1,0:T(8,128)S(1)}, f32[32,1152]{1,0:T(8,128)S(1)}, u32[]{:S(2)}, u32[]{:S(2)}) collective-permute-start(f32[32,1152]{1,0:T(8,128)S(1)} %get-tuple-element.18), channel_id=1, source_target_pairs={{0,1},{1,2},{2,3},{3,0},{4,5},{5,6},{6,7},{7,4},{8,9},{9,10},{10,1... | collective-permute-start | bytes 442376 | tf_op jit(solution)/shard_map/ppermute | solution.py:66
  65.8 7.7 %copy-start.8 = (f32[32]{0:T(128)S(1)}, f32[32]{0:T(128)}, u32[]{:S(2)}) copy-start(f32[32]{0:T(128)} %dynamic-slice_multiply_fusion) | copy-start | bytes 388
  73.9 8.4 %collective-permute-start.6 = (bf16[32,1152]{1,0:T(8,128)(2,1)S(1)}, bf16[32,1152]{1,0:T(8,128)(2,1)S(1)}, u32[]{:S(2)}, u32[]{:S(2)}) collective-permute-start(bf16[32,1152]{1,0:T(8,128)(2,1)S(1)} %concatenate.19), channel_id=1, source_target_pairs={{0,1},{1,2},{2,3},{3,0},{4,5},{5,6},{6,7},{7,4},{8,9},{9,10},{10,1... | collective-permute-start | bytes 221192 | tf_op jit(solution)/shard_map/ppermute | solution.py:91
  73.9 13.4 %collective-permute-start.7 = (bf16[32,1152]{1,0:T(8,128)(2,1)S(1)}, bf16[32,1152]{1,0:T(8,128)(2,1)S(1)}, u32[]{:S(2)}, u32[]{:S(2)}) collective-permute-start(bf16[32,1152]{1,0:T(8,128)(2,1)S(1)} %concatenate.19), channel_id=1, source_target_pairs={{0,2},{1,3},{2,0},{3,1},{4,6},{5,7},{6,4},{7,5},{8,10},{9,11},{10,... | collective-permute-start | bytes 221192 | tf_op jit(solution)/shard_map/ppermute | solution.py:91
  75.4 16.9 %collective-permute-start.8 = (bf16[32,1152]{1,0:T(8,128)(2,1)S(1)}, bf16[32,1152]{1,0:T(8,128)(2,1)S(1)}, u32[]{:S(2)}, u32[]{:S(2)}) collective-permute-start(bf16[32,1152]{1,0:T(8,128)(2,1)S(1)} %concatenate.19), channel_id=1, source_target_pairs={{0,3},{1,0},{2,1},{3,2},{4,7},{5,4},{6,5},{7,6},{8,11},{9,8},{10,9... | collective-permute-start | bytes 221192 | tf_op jit(solution)/shard_map/ppermute | solution.py:91
  76.8 26.6 %collective-permute-start.9 = (bf16[128,1024]{1,0:T(8,128)(2,1)S(1)}, bf16[128,1024]{1,0:T(8,128)(2,1)}, u32[]{:S(2)}, u32[]{:S(2)}) collective-permute-start(bf16[128,1024]{1,0:T(8,128)(2,1)S(1)} %copy-done.2), channel_id=1, source_target_pairs={{0,4},{4,8},{8,12},{12,16},{16,20},{20,24},{24,28},{28,0},{1,5},{5... | collective-permute-start | bytes 786440 | tf_op jit(solution)/shard_map/ppermute | solution.py:41
  77.4 30.8 %collective-permute-start.10 = (bf16[128,1024]{1,0:T(8,128)(2,1)S(1)}, bf16[128,1024]{1,0:T(8,128)(2,1)}, u32[]{:S(2)}, u32[]{:S(2)}) collective-permute-start(bf16[128,1024]{1,0:T(8,128)(2,1)S(1)} %copy-done.2), channel_id=1, source_target_pairs={{0,8},{4,12},{8,16},{12,20},{16,24},{20,28},{24,0},{28,4},{1,9},{5... | collective-permute-start | bytes 786440 | tf_op jit(solution)/shard_map/ppermute | solution.py:41
  82.2 28.5 %collective-permute-start.11 = (bf16[128,1024]{1,0:T(8,128)(2,1)S(1)}, bf16[128,1024]{1,0:T(8,128)(2,1)}, u32[]{:S(2)}, u32[]{:S(2)}) collective-permute-start(bf16[128,1024]{1,0:T(8,128)(2,1)S(1)} %copy-done.2), channel_id=1, source_target_pairs={{0,12},{4,16},{8,20},{12,24},{16,28},{20,0},{24,4},{28,8},{1,13},{... | collective-permute-start | bytes 786440 | tf_op jit(solution)/shard_map/ppermute | solution.py:41
  87.3 24.4 %collective-permute-start.12 = (bf16[128,1024]{1,0:T(8,128)(2,1)S(1)}, bf16[128,1024]{1,0:T(8,128)(2,1)}, u32[]{:S(2)}, u32[]{:S(2)}) collective-permute-start(bf16[128,1024]{1,0:T(8,128)(2,1)S(1)} %copy-done.2), channel_id=1, source_target_pairs={{0,16},{4,20},{8,24},{12,28},{16,0},{20,4},{24,8},{28,12},{1,17},{... | collective-permute-start | bytes 786440 | tf_op jit(solution)/shard_map/ppermute | solution.py:41
  90.6 6.5 %copy-start.9 = (bf16[32]{0:T(256)(128)(2,1)S(1)}, bf16[32]{0:T(256)(128)(2,1)}, u32[]{:S(2)}) copy-start(bf16[32]{0:T(256)(128)(2,1)} %pad.5.clone) | copy-start | bytes 196
  92.3 20.4 %collective-permute-start.13 = (bf16[128,1024]{1,0:T(8,128)(2,1)S(1)}, bf16[128,1024]{1,0:T(8,128)(2,1)}, u32[]{:S(2)}, u32[]{:S(2)}) collective-permute-start(bf16[128,1024]{1,0:T(8,128)(2,1)S(1)} %copy-done.2), channel_id=1, source_target_pairs={{0,20},{4,24},{8,28},{12,0},{16,4},{20,8},{24,12},{28,16},{1,21},{... | collective-permute-start | bytes 786440 | tf_op jit(solution)/shard_map/ppermute | solution.py:41
  95.6 0.7 copy-start.5
  98.9 26.8 %all-to-all-start = ((bf16[128,8,160]{0,2,1:T(8,128)(2,1)}), bf16[128,8,160]{0,2,1:T(8,128)(2,1)S(1)}, u32[]{:S(2)}, u32[]{:S(2)}) async-start(bf16[128,8,160]{0,2,1:T(8,128)(2,1)} %pad_maximum_fusion), calls=%async_computation | async-start | bytes 655360 | tf_op jit(solution)/shard_map/all_to_all | solution.py:120
  103.4 22.2 %collective-permute-start.14 = (bf16[128,1024]{1,0:T(8,128)(2,1)S(1)}, bf16[128,1024]{1,0:T(8,128)(2,1)S(1)}, u32[]{:S(2)}, u32[]{:S(2)}) collective-permute-start(bf16[128,1024]{1,0:T(8,128)(2,1)S(1)} %copy-done.2), channel_id=1, source_target_pairs={{0,24},{4,28},{8,0},{12,4},{16,8},{20,12},{24,16},{28,20},{1,25},{... | collective-permute-start | bytes 786440 | tf_op jit(solution)/shard_map/ppermute | solution.py:41
  108.2 17.4 %collective-permute-start.15 = (bf16[128,1024]{1,0:T(8,128)(2,1)S(1)}, bf16[128,1024]{1,0:T(8,128)(2,1)S(1)}, u32[]{:S(2)}, u32[]{:S(2)}) collective-permute-start(bf16[128,1024]{1,0:T(8,128)(2,1)S(1)} %copy-done.2), channel_id=1, source_target_pairs={{0,28},{4,0},{8,4},{12,8},{16,12},{20,16},{24,20},{28,24},{1,29},{... | collective-permute-start | bytes 786440 | tf_op jit(solution)/shard_map/ppermute | solution.py:41
  128.3 11.0 %copy-start.4 = (bf16[1024,1024]{1,0:T(8,128)(2,1)S(1)}, bf16[1024,1024]{1,0:T(8,128)(2,1)}, u32[]{:S(2)}) copy-start(bf16[1024,1024]{1,0:T(8,128)(2,1)} %all-gather.2.cloned.1.call-done) | copy-start | bytes 6291460
  128.8 10.6 %copy-start.1 = (bf16[1024,1024]{1,0:T(8,128)(2,1)S(1)}, bf16[1024,1024]{1,0:T(8,128)(2,1)}, u32[]{:S(2)}) copy-start(bf16[1024,1024]{1,0:T(8,128)(2,1)} %copy-done) | copy-start | bytes 6291460
  129.3 33.3 %collective-permute-start.16 = (f32[256,512]{1,0:T(8,128)S(1)}, f32[256,512]{1,0:T(8,128)S(1)}, u32[]{:S(2)}, u32[]{:S(2)}) collective-permute-start(f32[256,512]{1,0:T(8,128)S(1)} %convolution_add_fusion), channel_id=1, source_target_pairs={{0,0},{1,8},{2,16},{3,24},{4,4},{5,12},{6,20},{7,28},{8,1},{9,9},{... | collective-permute-start | bytes 1572872 | tf_op jit(solution)/shard_map/ppermute | solution.py:152
Sparse Core Ops, SparseCore 0:
  10.1 50.2 all-gather.1

commit v3 on v2

--- a/solution.py
+++ b/solution.py
@@ -8,6 +8,18 @@
     upper = mixing.astype(jnp.bfloat16)
     lower = (mixing - upper.astype(jnp.float32)).astype(jnp.bfloat16)
     return upper, lower
+
+
+def gather_blocks(own, received, index, count):
+    candidates = [own] + list(received)
+    blocks = []
+    for place in range(count):
+        shift = (index - place) % count
+        block = candidates[0]
+        for k in range(1, count):
+            block = jnp.where(shift == k, candidates[k], block)
+        blocks.append(block)
+    return jnp.concatenate(blocks, axis=0)
 
 
 def per_device_body(queries, passages, table, neg_owner, neg_row, positive, loss_weight):
@@ -23,24 +35,13 @@
     slice_of = lambda k: lax.dynamic_slice_in_dim(
         table, ((owner_index + k) % owner_count) * col_width, col_width, axis=1
     )
-    table_cols = jnp.zeros((table_rows, col_width), table.dtype)
-    table_cols = lax.dynamic_update_slice_in_dim(
-        table_cols, slice_of(0), owner_index * rows_shard, axis=0
-    )
+    received = []
     for k in range(1, owner_count):
         shift = [(j, (j + k) % owner_count) for j in range(owner_count)]
-        got = lax.ppermute(slice_of(k), "corpus", shift)
-        source = (owner_index - k) % owner_count
-        table_cols = lax.dynamic_update_slice_in_dim(table_cols, got, source * rows_shard, axis=0)
+        received.append(lax.ppermute(slice_of(k), "corpus", shift))
+    table_cols = gather_blocks(slice_of(0), received, owner_index, owner_count)
     all_passages = lax.all_gather(passages, "blk", axis=0, tiled=True)
-    all_passages, later = lax.optimization_barrier((all_passages, queries))
-    all_queries = jnp.zeros((blk_count * q_rows, col_width), queries.dtype)
-    all_queries = lax.dynamic_update_slice_in_dim(all_queries, queries, blk_index * q_rows, axis=0)
-    for k in range(1, blk_count):
-        shift = [(j, (j + k) % blk_count) for j in range(blk_count)]
-        got = lax.ppermute(later, "blk", shift)
-        source = (blk_index - k) % blk_count
-        all_queries = lax.dynamic_update_slice_in_dim(all_queries, got, source * q_rows, axis=0)
+    all_queries = lax.all_gather(queries, "blk", axis=0, tiled=True)
     ids = neg_owner * rows_shard + neg_row
     all_rows = all_passages.shape[0]
 
@@ -63,8 +64,7 @@
     summed = chunk_of(0)
     for k in range(1, owner_count):
         shift = [(j, (j + k) % owner_count) for j in range(owner_count)]
-        got = lax.ppermute(chunk_of(k), "corpus", shift)
-        summed = summed + got
+        summed = summed + lax.ppermute(chunk_of(k), "corpus", shift)
     logits = summed[:, :all_rows] * factor
     hard_logits = summed[:, all_rows:all_rows + negs] * factor
     my_positive = lax.dynamic_slice_in_dim(positive, owner_index * share, share)
@@ -84,13 +84,11 @@
     grads_part = jnp.concatenate(
         [soft_part, hard_part, jnp.zeros((share, 128 - negs), jnp.bfloat16)], axis=1
     )
-    grads = jnp.zeros((q_rows, grads_part.shape[1]), jnp.bfloat16)
-    grads = lax.dynamic_update_slice_in_dim(grads, grads_part, owner_index * share, axis=0)
+    received = []
     for k in range(1, owner_count):
         shift = [(j, (j + k) % owner_count) for j in range(owner_count)]
-        got = lax.ppermute(grads_part, "corpus", shift)
-        source = (owner_index - k) % owner_count
-        grads = lax.dynamic_update_slice_in_dim(grads, got, source * share, axis=0)
+        received.append(lax.ppermute(grads_part, "corpus", shift))
+    grads = gather_blocks(grads_part, received, owner_index, owner_count)
     soft_grad = grads[:, :all_rows]
     hard_grad = grads[:, all_rows:all_rows + negs]
 

time: 172 us -> 159 us (0.924)
  starting transfers between devices: 32.5 us -> 9.73 us
  waiting for transfers between devices: 84 us -> 92.9 us
  local copies, waits for them, and re-layouts: 25.4 us -> 16.9 us
  other arithmetic: 6.52 us -> 12.8 us
  matrix products: 7.15 us -> 11.5 us
    ppermute x16 -> x9, waiting for transfers between devices: 38.3 us -> 15 us  [the longest x3 12 us: per_device_body(): received.append(lax.ppermute(grads_part, 'corpus', shift))]
    all_gather x1, waiting for transfers between devices: 24.9 us -> 47.1 us  [per_device_body(): all_passages = lax.all_gather(passages, 'blk', axis=0, tiled=True)]
    dynamic_update_slice x15 -> x0, local copies, waits for them, and re-layouts: 16.8 us -> none  [the longest x3 7.69 us: per_device_body(): grads = lax.dynamic_update_slice_in_dim(grads, got, source * share, axis=0)]
    ppermute x16 -> x9, starting transfers between devices: 17.9 us -> 4.17 us  [the longest x3 1.74 us: per_device_body(): received.append(lax.ppermute(grads_part, 'corpus', shift))]
    all_to_all x1, waiting for transfers between devices: 0.01 us -> 10.7 us  [per_device_body(): lax.all_to_all(packed, 'blk', split_axis=1, concat_axis=0, tiled=True)]
    ppermute x1, starting transfers between devices: 10 us -> 2.05 us  [per_device_body(): table_grad = lax.ppermute(piece, ('blk', 'corpus'), perm)]
    unnamed x25 -> x19, local copies, waits for them, and re-layouts: 2.86 us -> 9.71 us
    unnamed x0 -> x4, other arithmetic: none -> 4.78 us
  transfers between devices with their start and end apart: 19 -> 13, of which waited for: 8 -> 8; matrix products, arithmetic and copies ran while one was open for 16% -> 23% of each run, Pallas kernels for 0% -> 0%
where the time goes in v3:
time: 159 us; the launch traced here: 158 us
  waiting for transfers between devices  92.9 us (58%)
  local copies, waits for them, and re-layouts  16.9 us (11%)
  between operations  14.4 us (9%)
  other arithmetic  12.8 us (8%)
  matrix products  11.5 us (7%)
  starting transfers between devices  9.73 us (6%)
    all_gather x1, waiting for transfers between devices, per_device_body(): all_passages = lax.all_gather(passages, 'blk', axis=0, tiled=True)  47.1 us
    ppermute x1, waiting for transfers between devices, per_device_body(): table_grad = lax.ppermute(piece, ('blk', 'corpus'), perm)  19.3 us
    ppermute x3, waiting for transfers between devices, per_device_body(): received.append(lax.ppermute(grads_part, 'corpus', shift))  12 us
    all_to_all x1, waiting for transfers between devices, per_device_body(): lax.all_to_all(packed, 'blk', split_axis=1, concat_axis=0, tiled=True)  10.7 us
    unnamed x19, local copies, waits for them, and re-layouts  9.71 us
    unnamed x4, other arithmetic  4.78 us
    dot_general x1, matrix products, per_device_body(): query_grad = jnp.dot(left, right, preferred_element_type=jnp.float32)  4.6 us
    all_to_all x1, starting transfers between devices, per_device_body(): lax.all_to_all(packed, 'blk', split_axis=1, concat_axis=0, tiled=True)  3.43 us
  transfers between devices with their start and end apart: 13, of which 8 were waited for; matrix products, arithmetic and copies ran while one was open for 23% of the time, Pallas kernels for 0%

profile of v3, /device:TPU:2, one launch (start us, length us, event | category | flops | bytes accessed | tf_op | source)
XLA Modules:
  0.0 158.1 jit_solution(3705401304334481386)
XLA Ops:
  7.2 0.7 all-gather.3.cloned.1.call-update
  8.0 1.5 constant_dynamic-slice_fusion.3
  9.5 0.1 collective-permute-start
  9.6 1.5 collective-permute-start.1
  11.0 0.7 dynamic-slice_multiply_fusion
  11.8 0.7 dynamic_slice.41
  12.5 0.1 pad.5.clone
  12.6 0.8 fusion.32
  13.3 47.1 %all-gather.3.cloned.1.call-done = bf16[1024,1024]{1,0:T(8,128)(2,1)} async-done(((bf16[128,1024]{1,0:T(8,128)(2,1)}), bf16[1024,1024]{1,0:T(8,128)(2,1)}) %all-gather.3.cloned.1.call-update) | async-done | bytes 2097168 | tf_op jit(solution)/shard_map/all_gather | solution.py:43
  60.4 3.2 %constant_dynamic-update-slice_fusion.8 = bf16[3072,1024]{1,0:T(8,128)(2,1)} fusion(bf16[1024,1024]{1,0:T(8,128)(2,1)} %all-gather.3.cloned.1.call-done), kind=kLoop, calls=%fused_computation.56 | loop fusion | bytes 4194304
  63.7 1.2 constant_dynamic-update-slice_fusion.7
  64.9 1.2 constant_dynamic-update-slice_fusion.6
  66.1 1.2 constant_dynamic-update-slice_fusion.5
  67.3 1.2 constant_dynamic-update-slice_fusion.4
  68.5 1.5 fusion.8
  70.0 1.2 copy.59
  71.3 0.6 select_reduce_fusion.2
  71.9 0.7 fusion.33
  72.6 0.4 concatenate.26
  73.0 0.5 constant_dynamic-slice_fusion.2
  73.5 0.2 copy.65
  73.8 0.2 copy.63
  74.0 0.6 collective-permute-start.4
  74.6 0.2 copy.61
  74.8 0.3 collective-permute-start.3
  75.0 1.9 %constant_dynamic-update-slice_fusion.3 = bf16[3072,1024]{1,0:T(8,128)(2,1)} fusion(bf16[3072,1024]{1,0:T(8,128)(2,1)} %get-tuple-element.10, bf16[256,1024]{1,0:T(8,128)(2,1)} %copy-done.4), kind=kLoop, calls=%fused_computation.51 | loop fusion | bytes 1048576
  76.9 1.9 %constant_dynamic-update-slice_fusion.2 = bf16[3072,1024]{1,0:T(8,128)(2,1)} fusion(bf16[3072,1024]{1,0:T(8,128)(2,1)} %constant_dynamic-update-slice_fusion.3, bf16[256,1024]{1,0:T(8,128)(2,1)} %copy-done.5), kind=kLoop, calls=%fused_computation.50 | loop fusion | bytes 1048576
  78.8 0.2 copy.66
  79.0 1.9 %collective-permute-done.4 = f32[32,1152]{1,0:T(8,128)S(1)} collective-permute-done((f32[32,1152]{1,0:T(8,128)S(1)}, f32[32,1152]{1,0:T(8,128)S(1)}, u32[]{:S(2)}, u32[]{:S(2)}) %collective-permute-start.4) | collective-permute-done | bytes 147488 | tf_op jit(solution)/shard_map/ppermute | solution.py:67
  80.9 0.2 copy.64
  81.2 1.0 collective-permute-done.3
  82.2 0.2 copy.62
  82.4 0.2 add_add_fusion
  82.7 0.2 fusion.20
  82.8 0.2 select_reduce_fusion.3
  83.1 0.5 fusion.31
  83.6 0.2 multiply_convert_fusion
  83.8 0.4 concatenate.27
  84.2 0.1 collective-permute-start.6
  84.3 1.5 collective-permute-start.7
  85.8 0.2 collective-permute-start.8
  86.0 1.9 %constant_dynamic-update-slice_fusion.1 = bf16[3072,1024]{1,0:T(8,128)(2,1)} fusion(bf16[3072,1024]{1,0:T(8,128)(2,1)} %constant_dynamic-update-slice_fusion.2, bf16[256,1024]{1,0:T(8,128)(2,1)} %copy-done.3), kind=kLoop, calls=%fused_computation.49 | loop fusion | bytes 1048576
  87.9 2.8 %collective-permute-done.6 = bf16[32,1152]{0,1:T(8,128)(2,1)S(1)} collective-permute-done((bf16[32,1152]{0,1:T(8,128)(2,1)S(1)}, bf16[32,1152]{0,1:T(8,128)(2,1)S(1)}, u32[]{:S(2)}, u32[]{:S(2)}) %collective-permute-start.6) | collective-permute-done | bytes 73760 | tf_op jit(solution)/shard_map/ppermute | solution.py:90
  90.7 9.1 %collective-permute-done.7 = bf16[32,1152]{0,1:T(8,128)(2,1)S(1)} collective-permute-done((bf16[32,1152]{0,1:T(8,128)(2,1)S(1)}, bf16[32,1152]{0,1:T(8,128)(2,1)S(1)}, u32[]{:S(2)}, u32[]{:S(2)}) %collective-permute-start.7) | collective-permute-done | bytes 73760 | tf_op jit(solution)/shard_map/ppermute | solution.py:90
  99.8 0.1 collective-permute-done.8
  99.9 0.1 select_select_fusion.7
  100.1 0.4 pad_maximum_fusion.1
  100.5 0.1 fusion.30
  100.6 0.1 maximum_maximum_fusion
  100.7 0.7 pad_maximum_fusion
  101.4 3.4 %all-to-all-start = ((bf16[128,8,160]{0,2,1:T(8,128)(2,1)}), bf16[128,8,160]{0,2,1:T(8,128)(2,1)S(1)}, u32[]{:S(2)}, u32[]{:S(2)}) async-start(bf16[128,8,160]{0,2,1:T(8,128)(2,1)} %pad_maximum_fusion), calls=%async_computation | async-start | bytes 655360 | tf_op jit(solution)/shard_map/all_to_all | solution.py:118
  104.9 0.8 constant_dynamic-update-slice_fusion
  105.7 0.5 select_reduce_fusion.1
  106.2 0.2 copy.67
  106.4 0.1 subtract_convert_fusion.2
  106.5 10.7 %all-to-all-done = bf16[128,8,160]{0,2,1:T(8,128)(2,1)S(1)} async-done(((bf16[128,8,160]{0,2,1:T(8,128)(2,1)}), bf16[128,8,160]{0,2,1:T(8,128)(2,1)S(1)}, u32[]{:S(2)}, u32[]{:S(2)}) %all-to-all-start) | async-done | bytes 327712 | tf_op jit(solution)/shard_map/all_to_all | solution.py:118
  117.3 2.5 %select_reduce_fusion = f32[1024,256]{1,0:T(8,128)S(1)} fusion(f32[1024,7]{0,1:T(8,128)S(1)} %slice_convert_fusion, s32[256]{0:T(256)S(1)} %iota_add_fusion, s32[1024,7]{0,1:T(8,128)S(1)} %convert_add_fusion), kind=kLoop, calls=%fused_computation | loop fusion | flops 5242880 | bytes 1106944 | tf_op jit(solution)/shard_map/reduce_sum | solution.py:135
  119.8 1.7 %fusion.12 = f32[256,512]{1,0:T(8,128)S(1)} fusion(bf16[1024,1024]{1,0:T(8,128)(2,1)} %all-gather.5.cloned.1.call-done, s32[]{:T(128)S(6)} %select_n.322, f32[1024,256]{1,0:T(8,128)S(1)} %select_reduce_fusion), kind=kOutput, calls=%fused_computation.16 | convolution fusion | flops 268697600 | bytes 2621444 | tf_op jit(solution)/shard_map/dot_general | solution.py:141
  121.6 1.7 %convolution_add_fusion = f32[256,512]{1,0:T(8,128)S(1)} fusion(f32[256,512]{1,0:T(8,128)S(1)} %fusion.12, bf16[1024,1024]{1,0:T(8,128)(2,1)} %all-gather.5.cloned.1.call-done, s32[]{:T(128)S(6)} %select_n.322, f32[1024,256]{1,0:T(8,128)S(1)} %select_reduce_fusion), kind=kOutput, calls=%fused_computation.12 | convolution fusion | flops 269615104 | bytes 3145732 | tf_op jit(solution)/shard_map/dot_general | solution.py:143
  123.3 2.1 %collective-permute-start.9 = (f32[256,512]{1,0:T(8,128)S(1)}, f32[256,512]{1,0:T(8,128)S(1)}, u32[]{:S(2)}, u32[]{:S(2)}) collective-permute-start(f32[256,512]{1,0:T(8,128)S(1)} %convolution_add_fusion), channel_id=1, source_target_pairs={{0,0},{1,8},{2,16},{3,24},{4,4},{5,12},{6,20},{7,28},{8,1},{9,9},{... | collective-permute-start | bytes 1572872 | tf_op jit(solution)/shard_map/ppermute | solution.py:150
  125.3 4.6 %fusion.14 = f32[128,1024]{1,0:T(8,128)} fusion(bf16[3072,1024]{1,0:T(8,128)(2,1)} %constant_dynamic-update-slice_fusion, bf16[128,1024]{0,1:T(8,128)(2,1)S(1)} %get-tuple-element.6, bf16[128,1024]{0,1:T(8,128)(2,1)S(1)} %get-tuple-element.7, bf16[128,1024]{0,1:T(8,128)(2,1)S(1)} %slice.34), kind=kOutput, calls=%fused_computation.18 | convolution fusion | flops 807665664 | bytes 7602176 | tf_op jit(solution)/shard_map/dot_general | solution.py:99
  129.9 1.2 fusion.21
  131.2 19.3 %collective-permute-done.9 = f32[256,512]{1,0:T(8,128)S(1)} collective-permute-done((f32[256,512]{1,0:T(8,128)S(1)}, f32[256,512]{1,0:T(8,128)S(1)}, u32[]{:S(2)}, u32[]{:S(2)}) %collective-permute-start.9) | collective-permute-done | bytes 524320 | tf_op jit(solution)/shard_map/ppermute | solution.py:150
  150.5 0.8 copy.82
  (37 shorter events, 0.4 us)
Async XLA Ops:
  7.2 53.3 %all-gather.3.cloned.1.call-start = ((), (), s32[]{:S(2)}) async-start(), calls=%async_computation.1 | async-start | bytes 2359296 | tf_op jit(solution)/shard_map/all_gather | solution.py:43
  7.9 111.9 %all-gather.5.cloned.1.call-start = ((), (), s32[]{:S(2)}) async-start(), calls=%async_computation.2 | async-start | bytes 2359296 | tf_op jit(solution)/shard_map/all_gather | solution.py:44
  9.5 54.2 %collective-permute-start = (bf16[256,1024]{1,0:T(8,128)(2,1)S(1)}, bf16[256,1024]{1,0:T(8,128)(2,1)S(1)}, u32[]{:S(2)}, u32[]{:S(2)}) collective-permute-start(bf16[256,1024]{1,0:T(8,128)(2,1)S(1)} %get-tuple-element.22), channel_id=1, source_target_pairs={{0,3},{1,0},{2,1},{3,2},{4,7},{5,4},{6,5},{7,6},{8,11},{9,8},{10,9... | collective-permute-start | bytes 1572872 | tf_op jit(solution)/shard_map/ppermute | solution.py:41
  9.6 54.1 %collective-permute-start.1 = (bf16[256,1024]{1,0:T(8,128)(2,1)S(1)}, bf16[256,1024]{1,0:T(8,128)(2,1)S(1)}, u32[]{:S(2)}, u32[]{:S(2)}) collective-permute-start(bf16[256,1024]{1,0:T(8,128)(2,1)S(1)} %get-tuple-element.21), channel_id=1, source_target_pairs={{0,2},{1,3},{2,0},{3,1},{4,6},{5,7},{6,4},{7,5},{8,10},{9,11},{10,... | collective-permute-start | bytes 1572872 | tf_op jit(solution)/shard_map/ppermute | solution.py:41
  11.0 52.7 %collective-permute-start.2 = (bf16[256,1024]{1,0:T(8,128)(2,1)S(1)}, bf16[256,1024]{1,0:T(8,128)(2,1)S(1)}, u32[]{:S(2)}, u32[]{:S(2)}) collective-permute-start(bf16[256,1024]{1,0:T(8,128)(2,1)S(1)} %get-tuple-element.20), channel_id=1, source_target_pairs={{0,1},{1,2},{2,3},{3,0},{4,5},{5,6},{6,7},{7,4},{8,9},{9,10},{10,1... | collective-permute-start | bytes 1572872 | tf_op jit(solution)/shard_map/ppermute | solution.py:41
  60.4 3.3 %copy-start.2 = (bf16[256,4096]{1,0:T(8,128)(2,1)S(1)}, bf16[256,4096]{1,0:T(8,128)(2,1)}, u32[]{:S(2)}) copy-start(bf16[256,4096]{1,0:T(8,128)(2,1)} %param.9) | copy-start | bytes 6291460
  64.9 3.6 %copy-start.4 = (bf16[256,1024]{1,0:T(8,128)(2,1)}, bf16[256,1024]{1,0:T(8,128)(2,1)S(1)}, u32[]{:S(2)}) copy-start(bf16[256,1024]{1,0:T(8,128)(2,1)S(1)} %get-tuple-element.17) | copy-start | bytes 1572868
  64.9 3.6 %copy-start.6 = (bf16[128,1024]{1,0:T(8,128)(2,1)S(1)}, bf16[128,1024]{1,0:T(8,128)(2,1)}, u32[]{:S(2)}) copy-start(bf16[128,1024]{1,0:T(8,128)(2,1)} %param.7) | copy-start | bytes 786436
  66.1 2.4 %copy-start.5 = (bf16[256,1024]{1,0:T(8,128)(2,1)}, bf16[256,1024]{1,0:T(8,128)(2,1)S(1)}, u32[]{:S(2)}) copy-start(bf16[256,1024]{1,0:T(8,128)(2,1)S(1)} %get-tuple-element.15) | copy-start | bytes 1572868
  67.3 1.2 copy-start.3
  68.5 3.4 %copy-start.1 = (bf16[1024,1024]{1,0:T(8,128)(2,1)S(1)}, bf16[1024,1024]{1,0:T(8,128)(2,1)}, u32[]{:S(2)}) copy-start(bf16[1024,1024]{1,0:T(8,128)(2,1)} %all-gather.3.cloned.1.call-done) | copy-start | bytes 6291460
  73.7 5.1 %collective-permute-start.5 = (f32[32,1152]{1,0:T(8,128)S(1)}, f32[32,1152]{1,0:T(8,128)S(1)}, u32[]{:S(2)}, u32[]{:S(2)}) collective-permute-start(f32[32,1152]{1,0:T(8,128)S(1)} %copy.65), channel_id=1, source_target_pairs={{0,3},{1,0},{2,1},{3,2},{4,7},{5,4},{6,5},{7,6},{8,11},{9,8},{10,9... | collective-permute-start | bytes 442376 | tf_op jit(solution)/shard_map/ppermute | solution.py:67
  74.0 7.0 %collective-permute-start.4 = (f32[32,1152]{1,0:T(8,128)S(1)}, f32[32,1152]{1,0:T(8,128)S(1)}, u32[]{:S(2)}, u32[]{:S(2)}) collective-permute-start(f32[32,1152]{1,0:T(8,128)S(1)} %copy.63), channel_id=1, source_target_pairs={{0,2},{1,3},{2,0},{3,1},{4,6},{5,7},{6,4},{7,5},{8,10},{9,11},{10,... | collective-permute-start | bytes 442376 | tf_op jit(solution)/shard_map/ppermute | solution.py:67
  74.8 7.4 %collective-permute-start.3 = (f32[32,1152]{1,0:T(8,128)S(1)}, f32[32,1152]{1,0:T(8,128)S(1)}, u32[]{:S(2)}, u32[]{:S(2)}) collective-permute-start(f32[32,1152]{1,0:T(8,128)S(1)} %copy.61), channel_id=1, source_target_pairs={{0,1},{1,2},{2,3},{3,0},{4,5},{5,6},{6,7},{7,4},{8,9},{9,10},{10,1... | collective-permute-start | bytes 442376 | tf_op jit(solution)/shard_map/ppermute | solution.py:67
  84.2 6.5 %collective-permute-start.6 = (bf16[32,1152]{0,1:T(8,128)(2,1)S(1)}, bf16[32,1152]{0,1:T(8,128)(2,1)S(1)}, u32[]{:S(2)}, u32[]{:S(2)}) collective-permute-start(bf16[32,1152]{0,1:T(8,128)(2,1)S(1)} %concatenate.27), channel_id=1, source_target_pairs={{0,3},{1,0},{2,1},{3,2},{4,7},{5,4},{6,5},{7,6},{8,11},{9,8},{10,9... | collective-permute-start | bytes 221192 | tf_op jit(solution)/shard_map/ppermute | solution.py:90
  84.3 15.5 %collective-permute-start.7 = (bf16[32,1152]{0,1:T(8,128)(2,1)S(1)}, bf16[32,1152]{0,1:T(8,128)(2,1)S(1)}, u32[]{:S(2)}, u32[]{:S(2)}) collective-permute-start(bf16[32,1152]{0,1:T(8,128)(2,1)S(1)} %concatenate.27), channel_id=1, source_target_pairs={{0,2},{1,3},{2,0},{3,1},{4,6},{5,7},{6,4},{7,5},{8,10},{9,11},{10,... | collective-permute-start | bytes 221192 | tf_op jit(solution)/shard_map/ppermute | solution.py:90
  85.8 14.1 %collective-permute-start.8 = (bf16[32,1152]{0,1:T(8,128)(2,1)S(1)}, bf16[32,1152]{0,1:T(8,128)(2,1)S(1)}, u32[]{:S(2)}, u32[]{:S(2)}) collective-permute-start(bf16[32,1152]{0,1:T(8,128)(2,1)S(1)} %concatenate.27), channel_id=1, source_target_pairs={{0,1},{1,2},{2,3},{3,0},{4,5},{5,6},{6,7},{7,4},{8,9},{9,10},{10,1... | collective-permute-start | bytes 221192 | tf_op jit(solution)/shard_map/ppermute | solution.py:90
  101.4 15.8 %all-to-all-start = ((bf16[128,8,160]{0,2,1:T(8,128)(2,1)}), bf16[128,8,160]{0,2,1:T(8,128)(2,1)S(1)}, u32[]{:S(2)}, u32[]{:S(2)}) async-start(bf16[128,8,160]{0,2,1:T(8,128)(2,1)} %pad_maximum_fusion), calls=%async_computation | async-start | bytes 655360 | tf_op jit(solution)/shard_map/all_to_all | solution.py:118
  123.3 6.7 %copy-start = (bf16[1024,1024]{1,0:T(8,128)(2,1)S(1)}, bf16[1024,1024]{1,0:T(8,128)(2,1)}, u32[]{:S(2)}) copy-start(bf16[1024,1024]{1,0:T(8,128)(2,1)} %all-gather.5.cloned.1.call-done) | copy-start | bytes 6291460
  123.3 27.2 %collective-permute-start.9 = (f32[256,512]{1,0:T(8,128)S(1)}, f32[256,512]{1,0:T(8,128)S(1)}, u32[]{:S(2)}, u32[]{:S(2)}) collective-permute-start(f32[256,512]{1,0:T(8,128)S(1)} %convolution_add_fusion), channel_id=1, source_target_pairs={{0,0},{1,8},{2,16},{3,24},{4,4},{5,12},{6,20},{7,28},{8,1},{9,9},{... | collective-permute-start | bytes 1572872 | tf_op jit(solution)/shard_map/ppermute | solution.py:150
Sparse Core Ops, SparseCore 0:
  10.1 50.2 all-gather.2
  62.6 49.8 all-gather.4

commit v4 on v3

--- a/solution.py
+++ b/solution.py
@@ -94,9 +94,11 @@
 
     mixing = jnp.sum(jnp.where(picks, hard_grad.astype(jnp.float32)[:, :, None], 0.0), axis=1)
     mix_hi, mix_lo = hi_lo(mixing)
-    left = jnp.concatenate([soft_grad, mix_hi, mix_lo], axis=1)
-    right = jnp.concatenate([all_passages, table_cols, table_cols], axis=0)
-    query_grad = jnp.dot(left, right, preferred_element_type=jnp.float32)
+    query_grad = (
+        jnp.dot(soft_grad, all_passages, preferred_element_type=jnp.float32)
+        + jnp.dot(mix_hi, table_cols, preferred_element_type=jnp.float32)
+        + jnp.dot(mix_lo, table_cols, preferred_element_type=jnp.float32)
+    )
 
     extra = jnp.concatenate(
         [

time: 159 us -> 157 us (0.987)
  waiting for transfers between devices: 92.9 us -> 106 us
  local copies, waits for them, and re-layouts: 16.9 us -> 7.86 us
  other arithmetic: 12.8 us -> 8.35 us
  matrix products: 11.5 us -> 9.59 us
    all_gather x1, waiting for transfers between devices: 47.1 us -> 20.9 us  [per_device_body(): all_passages = lax.all_gather(passages, 'blk', axis=0, tiled=True)]
    ppermute x3, waiting for transfers between devices: 0.01 us -> 24.1 us  [per_device_body(): received.append(lax.ppermute(slice_of(k), 'corpus', shift))]
    unnamed x19 -> x35, local copies, waits for them, and re-layouts: 9.71 us -> 3.35 us
    all_to_all x1, waiting for transfers between devices: 10.7 us -> 15.6 us  [per_device_body(): lax.all_to_all(packed, 'blk', split_axis=1, concat_axis=0, tiled=True)]
    unnamed x4 -> x0, other arithmetic: 4.78 us -> none
    ppermute x3, waiting for transfers between devices: 2.94 us -> 6.37 us  [per_device_body(): summed = summed + lax.ppermute(chunk_of(k), 'corpus', shift)]
    ppermute x1, waiting for transfers between devices: 19.3 us -> 22.5 us  [per_device_body(): table_grad = lax.ppermute(piece, ('blk', 'corpus'), perm)]
    all_gather x1, waiting for transfers between devices: 0.02 us -> 2.14 us  [per_device_body(): all_queries = lax.all_gather(queries, 'blk', axis=0, tiled=True)]
  transfers between devices with their start and end apart: 13 -> 13, of which waited for: 8 -> 13; matrix products, arithmetic and copies ran while one was open for 23% -> 11% of each run, Pallas kernels for 0% -> 0%
where the time goes in v4:
time: 157 us
  waiting for transfers between devices  106 us (68%)
  between operations  14.5 us (9%)
  starting transfers between devices  9.96 us (6%)
  matrix products  9.59 us (6%)
  other arithmetic  8.35 us (5%)
  local copies, waits for them, and re-layouts  7.86 us (5%)
    ppermute x3, waiting for transfers between devices, per_device_body(): received.append(lax.ppermute(slice_of(k), 'corpus', shift))  24.1 us
    ppermute x1, waiting for transfers between devices, per_device_body(): table_grad = lax.ppermute(piece, ('blk', 'corpus'), perm)  22.5 us
    all_gather x1, waiting for transfers between devices, per_device_body(): all_passages = lax.all_gather(passages, 'blk', axis=0, tiled=True)  20.9 us
    all_to_all x1, waiting for transfers between devices, per_device_body(): lax.all_to_all(packed, 'blk', split_axis=1, concat_axis=0, tiled=True)  15.6 us
    ppermute x3, waiting for transfers between devices, per_device_body(): received.append(lax.ppermute(grads_part, 'corpus', shift))  13.9 us
    ppermute x3, waiting for transfers between devices, per_device_body(): summed = summed + lax.ppermute(chunk_of(k), 'corpus', shift)  6.37 us
    all_to_all x1, starting transfers between devices, per_device_body(): lax.all_to_all(packed, 'blk', split_axis=1, concat_axis=0, tiled=True)  3.43 us
    unnamed x35, local copies, waits for them, and re-layouts  3.35 us
  transfers between devices with their start and end apart: 13, of which 13 were waited for; matrix products, arithmetic and copies ran while one was open for 11% of the time, Pallas kernels for 0%

profile of v4, /device:TPU:2, one launch (start us, length us, event | category | flops | bytes accessed | tf_op | source)
XLA Modules:
  0.0 156.5 jit_solution(2236080381403064860)
XLA Ops:
  7.2 0.7 all-gather.3.cloned.1.call-update
  8.0 1.5 constant_dynamic-slice_fusion.3
  9.6 1.5 collective-permute-start.1
  11.1 10.8 %collective-permute-done = bf16[256,1024]{1,0:T(8,128)(2,1)S(1)} collective-permute-done((bf16[256,1024]{1,0:T(8,128)(2,1)S(1)}, bf16[256,1024]{1,0:T(8,128)(2,1)S(1)}, u32[]{:S(2)}, u32[]{:S(2)}) %collective-permute-start) | collective-permute-done | bytes 524320 | tf_op jit(solution)/shard_map/ppermute | solution.py:41
  21.9 13.0 %collective-permute-done.1 = bf16[256,1024]{1,0:T(8,128)(2,1)S(1)} collective-permute-done((bf16[256,1024]{1,0:T(8,128)(2,1)S(1)}, bf16[256,1024]{1,0:T(8,128)(2,1)S(1)}, u32[]{:S(2)}, u32[]{:S(2)}) %collective-permute-start.1) | collective-permute-done | bytes 524320 | tf_op jit(solution)/shard_map/ppermute | solution.py:41
  34.9 0.2 collective-permute-done.2
  35.1 1.8 %select_select_fusion.3 = (bf16[256,1024]{1,0:T(8,128)(2,1)S(1)}, bf16[256,1024]{1,0:T(8,128)(2,1)S(1)}, bf16[256,1024]{1,0:T(8,128)(2,1)S(1)}, bf16[256,1024]{1,0:T(8,128)(2,1)S(1)}) fusion(bf16[256,1024]{1,0:T(8,128)(2,1)S(1)} %collective-permute-done, bf16[256,1024]{1,0:T(8,128)(2,1)S(1)} %collective-permute-done.1, ...), kind=kLoop, calls=%fused_computation.23 | loop fusion | flops 3145728 | bytes 4194320 | tf_op jit(solution)/shard_map/jit(_where)/select_n | solution.py:20
  37.0 0.8 copy-done.3
  37.8 0.2 copy-done.5
  37.9 0.2 copy-done.7
  38.1 0.7 convolution_bitcast_fusion
  38.8 0.2 copy.55
  39.0 0.6 select_reduce_fusion.2
  39.6 20.9 %all-gather.3.cloned.1.call-done = bf16[1024,1024]{1,0:T(8,128)(2,1)} async-done(((bf16[128,1024]{1,0:T(8,128)(2,1)}), bf16[1024,1024]{1,0:T(8,128)(2,1)}) %all-gather.3.cloned.1.call-update) | async-done | bytes 2097168 | tf_op jit(solution)/shard_map/all_gather | solution.py:43
  60.5 2.3 %fusion.18 = f32[128,1024]{0,1:T(8,128)S(1)} fusion(bf16[128,1024]{1,0:T(8,128)(2,1)S(1)} %copy-done.2, bf16[1024,1024]{1,0:T(8,128)(2,1)} %all-gather.3.cloned.1.call-done), kind=kOutput, calls=%fused_computation.63 | convolution fusion | flops 268435456 | bytes 2883584 | tf_op jit(solution)/shard_map/dot_general | solution.py:48
  62.8 0.4 concatenate.19
  63.2 0.5 constant_dynamic-slice_fusion.2
  63.7 0.2 copy.61
  64.0 0.2 copy.59
  64.2 0.6 collective-permute-start.4
  64.8 0.2 copy.57
  65.0 0.3 collective-permute-start.3
  65.3 0.1 dynamic_slice.41
  65.4 0.1 pad.5.clone
  65.5 0.1 dynamic-slice_multiply_fusion
  65.6 2.3 %collective-permute-done.5 = f32[32,1152]{1,0:T(8,128)S(1)} collective-permute-done((f32[32,1152]{1,0:T(8,128)S(1)}, f32[32,1152]{1,0:T(8,128)S(1)}, u32[]{:S(2)}, u32[]{:S(2)}) %collective-permute-start.5) | collective-permute-done | bytes 147488 | tf_op jit(solution)/shard_map/ppermute | solution.py:67
  67.9 0.2 copy.62
  68.1 3.1 %collective-permute-done.4 = f32[32,1152]{1,0:T(8,128)S(1)} collective-permute-done((f32[32,1152]{1,0:T(8,128)S(1)}, f32[32,1152]{1,0:T(8,128)S(1)}, u32[]{:S(2)}, u32[]{:S(2)}) %collective-permute-start.4) | collective-permute-done | bytes 147488 | tf_op jit(solution)/shard_map/ppermute | solution.py:67
  71.2 0.2 copy.60
  71.4 1.0 collective-permute-done.3
  72.4 0.2 copy.58
  72.6 0.2 add_add_fusion
  72.9 0.2 fusion.3
  73.1 0.2 select_reduce_fusion.3
  73.3 0.5 fusion.16
  73.8 0.2 multiply_convert_fusion
  74.0 0.4 concatenate.20
  74.5 1.5 collective-permute-start.7
  76.0 0.2 collective-permute-start.8
  76.2 4.7 %collective-permute-done.6 = bf16[32,1152]{0,1:T(8,128)(2,1)S(1)} collective-permute-done((bf16[32,1152]{0,1:T(8,128)(2,1)S(1)}, bf16[32,1152]{0,1:T(8,128)(2,1)S(1)}, u32[]{:S(2)}, u32[]{:S(2)}) %collective-permute-start.6) | collective-permute-done | bytes 73760 | tf_op jit(solution)/shard_map/ppermute | solution.py:90
  80.9 9.1 %collective-permute-done.7 = bf16[32,1152]{0,1:T(8,128)(2,1)S(1)} collective-permute-done((bf16[32,1152]{0,1:T(8,128)(2,1)S(1)}, bf16[32,1152]{0,1:T(8,128)(2,1)S(1)}, u32[]{:S(2)}, u32[]{:S(2)}) %collective-permute-start.7) | collective-permute-done | bytes 73760 | tf_op jit(solution)/shard_map/ppermute | solution.py:90
  90.0 0.1 collective-permute-done.8
  90.1 0.1 select_select_fusion.7
  90.3 0.4 pad_maximum_fusion.2
  90.7 0.1 fusion.15
  90.8 0.1 maximum_maximum_fusion
  90.9 0.8 pad_maximum_fusion.1
  91.7 3.4 %all-to-all-start = ((bf16[128,8,160]{0,2,1:T(8,128)(2,1)}), bf16[128,8,160]{0,2,1:T(8,128)(2,1)S(1)}, u32[]{:S(2)}, u32[]{:S(2)}) async-start(bf16[128,8,160]{0,2,1:T(8,128)(2,1)} %pad_maximum_fusion.1), calls=%async_computation | async-start | bytes 655360 | tf_op jit(solution)/shard_map/all_to_all | solution.py:120
  95.1 0.5 select_reduce_fusion.1
  95.7 0.5 fusion.9
  96.1 0.3 copy-done.10
  96.4 1.0 copy-done
  97.4 1.3 convolution_add_fusion.2
  98.7 15.6 %all-to-all-done = bf16[128,8,160]{0,2,1:T(8,128)(2,1)S(1)} async-done(((bf16[128,8,160]{0,2,1:T(8,128)(2,1)}), bf16[128,8,160]{0,2,1:T(8,128)(2,1)S(1)}, u32[]{:S(2)}, u32[]{:S(2)}) %all-to-all-start) | async-done | bytes 327712 | tf_op jit(solution)/shard_map/all_to_all | solution.py:120
  114.4 2.5 %select_reduce_fusion = f32[1024,256]{1,0:T(8,128)S(1)} fusion(f32[1024,7]{0,1:T(8,128)S(1)} %slice_convert_fusion, s32[256]{0:T(256)S(1)} %iota_add_fusion, s32[1024,7]{0,1:T(8,128)S(1)} %convert_add_fusion), kind=kLoop, calls=%fused_computation | loop fusion | flops 5242880 | bytes 1106944 | tf_op jit(solution)/shard_map/reduce_sum | solution.py:137
  116.9 2.1 %all-gather.5.cloned.1.call-done = bf16[1024,1024]{1,0:T(8,128)(2,1)} async-done(((bf16[128,1024]{1,0:T(8,128)(2,1)}), bf16[1024,1024]{1,0:T(8,128)(2,1)}) %all-gather.5.cloned.1.call-update) | async-done | bytes 2097168 | tf_op jit(solution)/shard_map/all_gather | solution.py:44
  119.1 1.8 %fusion.1 = f32[256,512]{1,0:T(8,128)S(1)} fusion(bf16[1024,1024]{1,0:T(8,128)(2,1)} %all-gather.5.cloned.1.call-done, s32[]{:T(128)S(6)} %select_n.322, f32[1024,256]{1,0:T(8,128)S(1)} %select_reduce_fusion), kind=kOutput, calls=%fused_computation.11 | convolution fusion | flops 268697600 | bytes 2621444 | tf_op jit(solution)/shard_map/dot_general | solution.py:143
  120.9 0.1 copy-done.1
  121.0 0.5 convolution_add_fusion
  121.5 2.3 %collective-permute-start.9 = (f32[256,512]{1,0:T(8,128)S(1)}, f32[256,512]{1,0:T(8,128)S(1)}, u32[]{:S(2)}, u32[]{:S(2)}) collective-permute-start(f32[256,512]{1,0:T(8,128)S(1)} %convolution_add_fusion), channel_id=1, source_target_pairs={{0,0},{1,8},{2,16},{3,24},{4,4},{5,12},{6,20},{7,28},{8,1},{9,9},{... | collective-permute-start | bytes 1572872 | tf_op jit(solution)/shard_map/ppermute | solution.py:152
  123.8 1.3 convolution_add_fusion.1
  125.1 1.2 fusion.4
  126.3 22.5 %collective-permute-done.9 = f32[256,512]{1,0:T(8,128)S(1)} collective-permute-done((f32[256,512]{1,0:T(8,128)S(1)}, f32[256,512]{1,0:T(8,128)S(1)}, u32[]{:S(2)}, u32[]{:S(2)}) %collective-permute-start.9) | collective-permute-done | bytes 524320 | tf_op jit(solution)/shard_map/ppermute | solution.py:152
  148.9 0.8 copy.68
  (49 shorter events, 0.5 us)
Async XLA Ops:
  7.2 3.9 %copy-start.13 = (s32[128,7]{0,1:T(8,128)S(1)}, s32[128,7]{0,1:T(8,128)}, u32[]{:S(2)}) copy-start(s32[128,7]{0,1:T(8,128)} %param.10) | copy-start | bytes 10756
  7.2 3.9 %copy-start.14 = (s32[128,7]{0,1:T(8,128)S(1)}, s32[128,7]{0,1:T(8,128)}, u32[]{:S(2)}) copy-start(s32[128,7]{0,1:T(8,128)} %param.11) | copy-start | bytes 10756
  7.2 53.3 %all-gather.3.cloned.1.call-start = ((), (), s32[]{:S(2)}) async-start(), calls=%async_computation.1 | async-start | bytes 2359296 | tf_op jit(solution)/shard_map/all_gather | solution.py:43
  7.9 111.1 %all-gather.5.cloned.1.call-start = ((), (), s32[]{:S(2)}) async-start(), calls=%async_computation.2 | async-start | bytes 2359296 | tf_op jit(solution)/shard_map/all_gather | solution.py:44
  9.5 12.4 %collective-permute-start = (bf16[256,1024]{1,0:T(8,128)(2,1)S(1)}, bf16[256,1024]{1,0:T(8,128)(2,1)S(1)}, u32[]{:S(2)}, u32[]{:S(2)}) collective-permute-start(bf16[256,1024]{1,0:T(8,128)(2,1)S(1)} %get-tuple-element.16), channel_id=1, source_target_pairs={{0,3},{1,0},{2,1},{3,2},{4,7},{5,4},{6,5},{7,6},{8,11},{9,8},{10,9... | collective-permute-start | bytes 1572872 | tf_op jit(solution)/shard_map/ppermute | solution.py:41
  9.6 25.4 %collective-permute-start.1 = (bf16[256,1024]{1,0:T(8,128)(2,1)S(1)}, bf16[256,1024]{1,0:T(8,128)(2,1)S(1)}, u32[]{:S(2)}, u32[]{:S(2)}) collective-permute-start(bf16[256,1024]{1,0:T(8,128)(2,1)S(1)} %get-tuple-element.15), channel_id=1, source_target_pairs={{0,2},{1,3},{2,0},{3,1},{4,6},{5,7},{6,4},{7,5},{8,10},{9,11},{10,... | collective-permute-start | bytes 1572872 | tf_op jit(solution)/shard_map/ppermute | solution.py:41
  11.0 24.1 %collective-permute-start.2 = (bf16[256,1024]{1,0:T(8,128)(2,1)S(1)}, bf16[256,1024]{1,0:T(8,128)(2,1)}, u32[]{:S(2)}, u32[]{:S(2)}) collective-permute-start(bf16[256,1024]{1,0:T(8,128)(2,1)S(1)} %get-tuple-element.14), channel_id=1, source_target_pairs={{0,1},{1,2},{2,3},{3,0},{4,5},{5,6},{6,7},{7,4},{8,9},{9,10},{10,1... | collective-permute-start | bytes 1572872 | tf_op jit(solution)/shard_map/ppermute | solution.py:41
  11.0 27.0 %copy-start.2 = (bf16[128,1024]{1,0:T(8,128)(2,1)S(1)}, bf16[128,1024]{1,0:T(8,128)(2,1)}, u32[]{:S(2)}) copy-start(bf16[128,1024]{1,0:T(8,128)(2,1)} %param.7) | copy-start | bytes 786436
  37.0 0.8 copy-start.3
  37.0 1.0 copy-start.5
  37.0 1.1 copy-start.7
  63.7 1.6 %copy-start.15 = (s32[128]{0:T(128)S(1)}, s32[128]{0:T(128)}, u32[]{:S(2)}) copy-start(s32[128]{0:T(128)} %param.12) | copy-start | bytes 1540
  63.7 1.8 %copy-start.16 = (f32[128]{0:T(128)S(1)}, f32[128]{0:T(128)}, u32[]{:S(2)}) copy-start(f32[128]{0:T(128)} %param.13) | copy-start | bytes 1540
  63.9 3.9 %collective-permute-start.5 = (f32[32,1152]{1,0:T(8,128)S(1)}, f32[32,1152]{1,0:T(8,128)S(1)}, u32[]{:S(2)}, u32[]{:S(2)}) collective-permute-start(f32[32,1152]{1,0:T(8,128)S(1)} %copy.61), channel_id=1, source_target_pairs={{0,3},{1,0},{2,1},{3,2},{4,7},{5,4},{6,5},{7,6},{8,11},{9,8},{10,9... | collective-permute-start | bytes 442376 | tf_op jit(solution)/shard_map/ppermute | solution.py:67
  64.2 7.0 %collective-permute-start.4 = (f32[32,1152]{1,0:T(8,128)S(1)}, f32[32,1152]{1,0:T(8,128)S(1)}, u32[]{:S(2)}, u32[]{:S(2)}) collective-permute-start(f32[32,1152]{1,0:T(8,128)S(1)} %copy.59), channel_id=1, source_target_pairs={{0,2},{1,3},{2,0},{3,1},{4,6},{5,7},{6,4},{7,5},{8,10},{9,11},{10,... | collective-permute-start | bytes 442376 | tf_op jit(solution)/shard_map/ppermute | solution.py:67
  65.0 7.4 %collective-permute-start.3 = (f32[32,1152]{1,0:T(8,128)S(1)}, f32[32,1152]{1,0:T(8,128)S(1)}, u32[]{:S(2)}, u32[]{:S(2)}) collective-permute-start(f32[32,1152]{1,0:T(8,128)S(1)} %copy.57), channel_id=1, source_target_pairs={{0,1},{1,2},{2,3},{3,0},{4,5},{5,6},{6,7},{7,4},{8,9},{9,10},{10,1... | collective-permute-start | bytes 442376 | tf_op jit(solution)/shard_map/ppermute | solution.py:67
  74.4 6.5 %collective-permute-start.6 = (bf16[32,1152]{0,1:T(8,128)(2,1)S(1)}, bf16[32,1152]{0,1:T(8,128)(2,1)S(1)}, u32[]{:S(2)}, u32[]{:S(2)}) collective-permute-start(bf16[32,1152]{0,1:T(8,128)(2,1)S(1)} %concatenate.20), channel_id=1, source_target_pairs={{0,3},{1,0},{2,1},{3,2},{4,7},{5,4},{6,5},{7,6},{8,11},{9,8},{10,9... | collective-permute-start | bytes 221192 | tf_op jit(solution)/shard_map/ppermute | solution.py:90
  74.5 15.5 %collective-permute-start.7 = (bf16[32,1152]{0,1:T(8,128)(2,1)S(1)}, bf16[32,1152]{0,1:T(8,128)(2,1)S(1)}, u32[]{:S(2)}, u32[]{:S(2)}) collective-permute-start(bf16[32,1152]{0,1:T(8,128)(2,1)S(1)} %concatenate.20), channel_id=1, source_target_pairs={{0,2},{1,3},{2,0},{3,1},{4,6},{5,7},{6,4},{7,5},{8,10},{9,11},{10,... | collective-permute-start | bytes 221192 | tf_op jit(solution)/shard_map/ppermute | solution.py:90
  76.0 14.1 %collective-permute-start.8 = (bf16[32,1152]{0,1:T(8,128)(2,1)S(1)}, bf16[32,1152]{0,1:T(8,128)(2,1)S(1)}, u32[]{:S(2)}, u32[]{:S(2)}) collective-permute-start(bf16[32,1152]{0,1:T(8,128)(2,1)S(1)} %concatenate.20), channel_id=1, source_target_pairs={{0,1},{1,2},{2,3},{3,0},{4,5},{5,6},{6,7},{7,4},{8,9},{9,10},{10,1... | collective-permute-start | bytes 221192 | tf_op jit(solution)/shard_map/ppermute | solution.py:90
  90.7 4.9 %copy-start.4 = (bf16[256,1024]{1,0:T(8,128)(2,1)S(1)}, bf16[256,1024]{1,0:T(8,128)(2,1)}, u32[]{:S(2)}) copy-start(bf16[256,1024]{1,0:T(8,128)(2,1)} %copy-done.3) | copy-start | bytes 1572868
  90.7 4.9 %copy-start.6 = (bf16[256,1024]{1,0:T(8,128)(2,1)S(1)}, bf16[256,1024]{1,0:T(8,128)(2,1)}, u32[]{:S(2)}) copy-start(bf16[256,1024]{1,0:T(8,128)(2,1)} %copy-done.5) | copy-start | bytes 1572868
  90.7 4.9 %copy-start.8 = (bf16[256,1024]{1,0:T(8,128)(2,1)S(1)}, bf16[256,1024]{1,0:T(8,128)(2,1)}, u32[]{:S(2)}) copy-start(bf16[256,1024]{1,0:T(8,128)(2,1)} %copy-done.7) | copy-start | bytes 1572868
  91.7 22.6 %all-to-all-start = ((bf16[128,8,160]{0,2,1:T(8,128)(2,1)}), bf16[128,8,160]{0,2,1:T(8,128)(2,1)S(1)}, u32[]{:S(2)}, u32[]{:S(2)}) async-start(bf16[128,8,160]{0,2,1:T(8,128)(2,1)} %pad_maximum_fusion.1), calls=%async_computation | async-start | bytes 655360 | tf_op jit(solution)/shard_map/all_to_all | solution.py:120
  95.6 0.8 copy-start.10
  95.6 1.8 %copy-start = (bf16[1024,1024]{1,0:T(8,128)(2,1)S(1)}, bf16[1024,1024]{1,0:T(8,128)(2,1)}, u32[]{:S(2)}) copy-start(bf16[1024,1024]{1,0:T(8,128)(2,1)} %all-gather.3.cloned.1.call-done) | copy-start | bytes 6291460
  119.1 1.9 %copy-start.1 = (bf16[1024,1024]{1,0:T(8,128)(2,1)S(1)}, bf16[1024,1024]{1,0:T(8,128)(2,1)}, u32[]{:S(2)}) copy-start(bf16[1024,1024]{1,0:T(8,128)(2,1)} %all-gather.5.cloned.1.call-done) | copy-start | bytes 6291460
  121.0 2.8 %copy-start.9 = (bf16[256,1024]{1,0:T(8,128)(2,1)S(1)}, bf16[256,1024]{1,0:T(8,128)(2,1)}, u32[]{:S(2)}) copy-start(bf16[256,1024]{1,0:T(8,128)(2,1)} %copy-done.7) | copy-start | bytes 1572868
  121.0 2.8 %copy-start.11 = (f32[128,1024]{1,0:T(8,128)S(1)}, f32[128,1024]{1,0:T(8,128)}, u32[]{:S(2)}) copy-start(f32[128,1024]{1,0:T(8,128)} %copy-done.10) | copy-start | bytes 1572868
  121.0 2.8 %copy-start.12 = (f32[128,1024]{1,0:T(8,128)S(1)}, f32[128,1024]{1,0:T(8,128)}, u32[]{:S(2)}) copy-start(f32[128,1024]{1,0:T(8,128)} %convolution_add_fusion.2) | copy-start | bytes 1572868
  121.5 27.4 %collective-permute-start.9 = (f32[256,512]{1,0:T(8,128)S(1)}, f32[256,512]{1,0:T(8,128)S(1)}, u32[]{:S(2)}, u32[]{:S(2)}) collective-permute-start(f32[256,512]{1,0:T(8,128)S(1)} %convolution_add_fusion), channel_id=1, source_target_pairs={{0,0},{1,8},{2,16},{3,24},{4,4},{5,12},{6,20},{7,28},{8,1},{9,9},{... | collective-permute-start | bytes 1572872 | tf_op jit(solution)/shard_map/ppermute | solution.py:152
Sparse Core Ops, SparseCore 0:
  10.1 50.2 all-gather.2
  65.4 53.6 all-gather.4

commit v5 on v4

--- a/solution.py
+++ b/solution.py
@@ -129,27 +129,35 @@
     )
 
     per_col = blk_count // owner_count
+    half = blk_count // 2
     piece_width = col_width // per_col
-    shard = blk_index // per_col
-    part = blk_index % per_col
-    shard_iota = shard * rows_shard + jnp.arange(rows_shard, dtype=jnp.int32)
-    shard_picks = all_ids[:, :, None] == shard_iota[None, None, :]
-    shard_mix = jnp.sum(
-        jnp.where(shard_picks, all_hard.astype(jnp.float32)[:, :, None], 0.0), axis=1
+    first = 2 * (blk_index % half)
+    part = first // owner_count
+    shard = first % owner_count
+    pair_iota = shard * rows_shard + jnp.arange(2 * rows_shard, dtype=jnp.int32)
+    pair_picks = all_ids[:, :, None] == pair_iota[None, None, :]
+    pair_mix = jnp.sum(
+        jnp.where(pair_picks, all_hard.astype(jnp.float32)[:, :, None], 0.0), axis=1
     )
-    shard_hi, shard_lo = hi_lo(shard_mix)
+    pair_hi, pair_lo = hi_lo(pair_mix)
     query_part = lax.dynamic_slice_in_dim(all_queries, part * piece_width, piece_width, axis=1)
     dims = (((0,), (0,)), ((), ()))
-    piece = lax.dot_general(
-        shard_hi, query_part, dims, preferred_element_type=jnp.float32
-    ) + lax.dot_general(shard_lo, query_part, dims, preferred_element_type=jnp.float32)
-    perm = []
-    for b in range(blk_count):
-        for c in range(owner_count):
-            dest_b = c * per_col + b % per_col
-            dest_c = b // per_col
-            perm.append((b * owner_count + c, dest_b * owner_count + dest_c))
-    table_grad = lax.ppermute(piece, ("blk", "corpus"), perm)
+    pieces = lax.dot_general(
+        pair_hi, query_part, dims, preferred_element_type=jnp.float32
+    ) + lax.dot_general(pair_lo, query_part, dims, preferred_element_type=jnp.float32)
+    perms = ([], [])
+    for c in range(owner_count):
+        side = (c * per_col) // half
+        for r in range(half):
+            b = side * half + r
+            for j in range(2):
+                q = 2 * r + j
+                dest_b = c * per_col + q // owner_count
+                dest_c = q % owner_count
+                perms[j].append((b * owner_count + c, dest_b * owner_count + dest_c))
+    table_grad = lax.ppermute(
+        pieces[:rows_shard], ("blk", "corpus"), perms[0]
+    ) + lax.ppermute(pieces[rows_shard:], ("blk", "corpus"), perms[1])
     return (loss_share, query_grad, passage_grad, table_grad)
 
 

time: 157 us -> 159 us (1.013)
  the two profiles are of different devices: /device:TPU:2 before, /device:TPU:3 now
where the time goes in v5:
time: 159 us
  waiting for transfers between devices  102 us (64%)
  starting transfers between devices  15.6 us (10%)
  between operations  14.6 us (9%)
  matrix products  10.2 us (6%)
  other arithmetic  9.29 us (6%)
  local copies, waits for them, and re-layouts  7.09 us (4%)
    ppermute x1, waiting for transfers between devices, per_device_body(): lax.ppermute(pieces[rows_shard:], ('blk', 'corpus'), perms[1])  24.4 us
    ppermute x3, waiting for transfers between devices, per_device_body(): received.append(lax.ppermute(slice_of(k), 'corpus', shift))  21.1 us
    all_gather x1, waiting for transfers between devices, per_device_body(): all_passages = lax.all_gather(passages, 'blk', axis=0, tiled=True)  21.1 us
    all_to_all x1, waiting for transfers between devices, per_device_body(): lax.all_to_all(packed, 'blk', split_axis=1, concat_axis=0, tiled=True)  15.2 us
    ppermute x3, waiting for transfers between devices, per_device_body(): received.append(lax.ppermute(grads_part, 'corpus', shift))  11.6 us
    ppermute x3, starting transfers between devices, per_device_body(): summed = summed + lax.ppermute(chunk_of(k), 'corpus', shift)  4.37 us
    ppermute x3, waiting for transfers between devices, per_device_body(): summed = summed + lax.ppermute(chunk_of(k), 'corpus', shift)  4.09 us
    all_gather x1, waiting for transfers between devices, per_device_body(): all_queries = lax.all_gather(queries, 'blk', axis=0, tiled=True)  3.89 us
  transfers between devices with their start and end apart: 14, of which 13 were waited for; matrix products, arithmetic and copies ran while one was open for 11% of the time, Pallas kernels for 0%

profile of v5, /device:TPU:3, one launch (start us, length us, event | category | flops | bytes accessed | tf_op | source)
XLA Modules:
  0.0 158.8 jit_solution(14830975242924636394)
XLA Ops:
  7.2 0.7 all-gather.3.cloned.1.call-update
  8.0 1.5 constant_dynamic-slice_fusion.3
  9.5 0.7 collective-permute-start
  10.2 1.7 %collective-permute-start.2 = (bf16[256,1024]{1,0:T(8,128)(2,1)S(1)}, bf16[256,1024]{1,0:T(8,128)(2,1)}, u32[]{:S(2)}, u32[]{:S(2)}) collective-permute-start(bf16[256,1024]{1,0:T(8,128)(2,1)S(1)} %get-tuple-element.14), channel_id=1, source_target_pairs={{0,1},{1,2},{2,3},{3,0},{4,5},{5,6},{6,7},{7,4},{8,9},{9,10},{10,1... | collective-permute-start | bytes 1572872 | tf_op jit(solution)/shard_map/ppermute | solution.py:41
  12.0 12.1 %collective-permute-done = bf16[256,1024]{1,0:T(8,128)(2,1)S(1)} collective-permute-done((bf16[256,1024]{1,0:T(8,128)(2,1)S(1)}, bf16[256,1024]{1,0:T(8,128)(2,1)S(1)}, u32[]{:S(2)}, u32[]{:S(2)}) %collective-permute-start) | collective-permute-done | bytes 524320 | tf_op jit(solution)/shard_map/ppermute | solution.py:41
  24.1 0.2 collective-permute-done.1
  24.3 8.7 %collective-permute-done.2 = bf16[256,1024]{1,0:T(8,128)(2,1)} collective-permute-done((bf16[256,1024]{1,0:T(8,128)(2,1)S(1)}, bf16[256,1024]{1,0:T(8,128)(2,1)}, u32[]{:S(2)}, u32[]{:S(2)}) %collective-permute-start.2) | collective-permute-done | bytes 524320 | tf_op jit(solution)/shard_map/ppermute | solution.py:41
  33.0 1.8 %select_select_fusion.3 = (bf16[256,1024]{1,0:T(8,128)(2,1)S(1)}, bf16[256,1024]{1,0:T(8,128)(2,1)S(1)}, bf16[256,1024]{1,0:T(8,128)(2,1)S(1)}, bf16[256,1024]{1,0:T(8,128)(2,1)S(1)}) fusion(bf16[256,1024]{1,0:T(8,128)(2,1)S(1)} %collective-permute-done, bf16[256,1024]{1,0:T(8,128)(2,1)S(1)} %collective-permute-done.1, ...), kind=kLoop, calls=%fused_computation.25 | loop fusion | flops 3145728 | bytes 4194320 | tf_op jit(solution)/shard_map/jit(_where)/select_n | solution.py:20
  34.9 0.8 copy-done.3
  35.6 0.2 copy-done.6
  35.8 0.2 copy-done.9
  36.0 0.7 convolution_bitcast_fusion
  36.7 0.2 copy.55
  36.9 0.6 select_reduce_fusion.2
  37.5 21.1 %all-gather.3.cloned.1.call-done = bf16[1024,1024]{1,0:T(8,128)(2,1)} async-done(((bf16[128,1024]{1,0:T(8,128)(2,1)}), bf16[1024,1024]{1,0:T(8,128)(2,1)}) %all-gather.3.cloned.1.call-update) | async-done | bytes 2097168 | tf_op jit(solution)/shard_map/all_gather | solution.py:43
  58.5 2.3 %fusion.19 = f32[128,1024]{0,1:T(8,128)S(1)} fusion(bf16[128,1024]{1,0:T(8,128)(2,1)S(1)} %copy-done.2, bf16[1024,1024]{1,0:T(8,128)(2,1)} %all-gather.3.cloned.1.call-done), kind=kOutput, calls=%fused_computation.64 | convolution fusion | flops 268435456 | bytes 2883584 | tf_op jit(solution)/shard_map/dot_general | solution.py:48
  60.9 0.4 concatenate.19
  61.3 0.5 constant_dynamic-slice_fusion.2
  61.8 0.2 copy.61
  62.0 2.6 %collective-permute-start.5 = (f32[32,1152]{1,0:T(8,128)S(1)}, f32[32,1152]{1,0:T(8,128)S(1)}, u32[]{:S(2)}, u32[]{:S(2)}) collective-permute-start(f32[32,1152]{1,0:T(8,128)S(1)} %copy.61), channel_id=1, source_target_pairs={{0,3},{1,0},{2,1},{3,2},{4,7},{5,4},{6,5},{7,6},{8,11},{9,8},{10,9... | collective-permute-start | bytes 442376 | tf_op jit(solution)/shard_map/ppermute | solution.py:67
  64.7 0.2 copy.59
  64.8 0.3 collective-permute-start.4
  65.2 0.2 copy.57
  65.4 1.4 collective-permute-start.3
  66.9 0.1 dynamic_slice.41
  67.1 0.9 collective-permute-done.5
  68.0 0.2 copy.62
  68.2 2.5 %collective-permute-done.4 = f32[32,1152]{1,0:T(8,128)S(1)} collective-permute-done((f32[32,1152]{1,0:T(8,128)S(1)}, f32[32,1152]{1,0:T(8,128)S(1)}, u32[]{:S(2)}, u32[]{:S(2)}) %collective-permute-start.4) | collective-permute-done | bytes 147488 | tf_op jit(solution)/shard_map/ppermute | solution.py:67
  70.8 0.2 copy.60
  71.0 0.7 collective-permute-done.3
  71.7 0.2 copy.58
  71.9 0.2 add_add_fusion
  72.1 0.2 fusion.5
  72.3 0.2 select_reduce_fusion.3
  72.5 0.5 fusion.16
  73.1 0.2 multiply_convert_fusion
  73.3 0.4 concatenate.20
  73.7 1.5 collective-permute-start.6
  75.2 1.2 collective-permute-start.7
  76.3 0.5 collective-permute-start.8
  76.9 7.2 %collective-permute-done.6 = bf16[32,1152]{0,1:T(8,128)(2,1)S(1)} collective-permute-done((bf16[32,1152]{0,1:T(8,128)(2,1)S(1)}, bf16[32,1152]{0,1:T(8,128)(2,1)S(1)}, u32[]{:S(2)}, u32[]{:S(2)}) %collective-permute-start.6) | collective-permute-done | bytes 73760 | tf_op jit(solution)/shard_map/ppermute | solution.py:90
  84.1 0.2 collective-permute-done.7
  84.3 4.2 %collective-permute-done.8 = bf16[32,1152]{0,1:T(8,128)(2,1)S(1)} collective-permute-done((bf16[32,1152]{0,1:T(8,128)(2,1)S(1)}, bf16[32,1152]{0,1:T(8,128)(2,1)S(1)}, u32[]{:S(2)}, u32[]{:S(2)}) %collective-permute-start.8) | collective-permute-done | bytes 73760 | tf_op jit(solution)/shard_map/ppermute | solution.py:90
  88.5 0.1 select_select_fusion.7
  88.6 0.4 pad_maximum_fusion.2
  89.1 0.1 fusion.15
  89.3 0.7 pad_maximum_fusion.1
  90.0 3.4 %all-to-all-start = ((bf16[128,8,160]{0,2,1:T(8,128)(2,1)}), bf16[128,8,160]{0,2,1:T(8,128)(2,1)S(1)}, u32[]{:S(2)}, u32[]{:S(2)}) async-start(bf16[128,8,160]{0,2,1:T(8,128)(2,1)} %pad_maximum_fusion.1), calls=%async_computation | async-start | bytes 655360 | tf_op jit(solution)/shard_map/all_to_all | solution.py:120
  93.5 0.5 select_reduce_fusion.1
  94.0 0.5 fusion.9
  94.5 0.3 copy-done.12
  94.8 1.0 copy-done
  95.8 1.3 convolution_add_fusion.2
  97.1 15.2 %all-to-all-done = bf16[128,8,160]{0,2,1:T(8,128)(2,1)S(1)} async-done(((bf16[128,8,160]{0,2,1:T(8,128)(2,1)}), bf16[128,8,160]{0,2,1:T(8,128)(2,1)S(1)}, u32[]{:S(2)}, u32[]{:S(2)}) %all-to-all-start) | async-done | bytes 327712 | tf_op jit(solution)/shard_map/all_to_all | solution.py:120
  112.4 2.6 %select_reduce_fusion = f32[1024,512]{1,0:T(8,128)S(1)} fusion(f32[1024,7]{0,1:T(8,128)S(1)} %slice_convert_fusion, s32[512]{0:T(512)S(1)} %iota_add_fusion, s32[1024,7]{0,1:T(8,128)S(1)} %convert_add_fusion), kind=kLoop, calls=%fused_computation | loop fusion | flops 10485760 | bytes 2156544 | tf_op jit(solution)/shard_map/reduce_sum | solution.py:139
  115.0 3.9 %all-gather.5.cloned.1.call-done = bf16[1024,1024]{1,0:T(8,128)(2,1)} async-done(((bf16[128,1024]{1,0:T(8,128)(2,1)}), bf16[1024,1024]{1,0:T(8,128)(2,1)}) %all-gather.5.cloned.1.call-update) | async-done | bytes 2097168 | tf_op jit(solution)/shard_map/all_gather | solution.py:44
  118.9 2.1 %fusion.1 = f32[512,512]{1,0:T(8,128)S(1)} fusion(bf16[1024,1024]{1,0:T(8,128)(2,1)} %all-gather.5.cloned.1.call-done, s32[]{:T(128)S(6)} %select_n.327, f32[1024,512]{1,0:T(8,128)S(1)} %select_reduce_fusion), kind=kOutput, calls=%fused_computation.11 | convolution fusion | flops 537395200 | bytes 4194308 | tf_op jit(solution)/shard_map/dot_general | solution.py:145
  121.0 0.8 convolution_add_fusion
  122.0 0.8 collective-permute-start.9
  122.8 1.3 collective-permute-start.10
  124.2 1.2 convolution_add_fusion.1
  125.4 1.2 fusion.6
  126.7 24.4 %collective-permute-done.10 = f32[256,512]{1,0:T(8,128)S(1)} collective-permute-done((f32[256,512]{1,0:T(8,128)S(1)}, f32[256,512]{1,0:T(8,128)S(1)}, u32[]{:S(2)}, u32[]{:S(2)}) %collective-permute-start.10) | collective-permute-done | bytes 524320 | tf_op jit(solution)/shard_map/ppermute | solution.py:160
  151.1 0.9 add.169
  (56 shorter events, 0.7 us)
Async XLA Ops:
  7.2 4.8 %copy-start.15 = (s32[128,7]{0,1:T(8,128)S(1)}, s32[128,7]{0,1:T(8,128)}, u32[]{:S(2)}) copy-start(s32[128,7]{0,1:T(8,128)} %param.10) | copy-start | bytes 10756
  7.2 4.8 %copy-start.16 = (s32[128,7]{0,1:T(8,128)S(1)}, s32[128,7]{0,1:T(8,128)}, u32[]{:S(2)}) copy-start(s32[128,7]{0,1:T(8,128)} %param.11) | copy-start | bytes 10756
  7.2 51.4 %all-gather.3.cloned.1.call-start = ((), (), s32[]{:S(2)}) async-start(), calls=%async_computation.1 | async-start | bytes 2359296 | tf_op jit(solution)/shard_map/all_gather | solution.py:43
  7.9 111.0 %all-gather.5.cloned.1.call-start = ((), (), s32[]{:S(2)}) async-start(), calls=%async_computation.2 | async-start | bytes 2359296 | tf_op jit(solution)/shard_map/all_gather | solution.py:44
  9.5 14.6 %collective-permute-start = (bf16[256,1024]{1,0:T(8,128)(2,1)S(1)}, bf16[256,1024]{1,0:T(8,128)(2,1)S(1)}, u32[]{:S(2)}, u32[]{:S(2)}) collective-permute-start(bf16[256,1024]{1,0:T(8,128)(2,1)S(1)} %get-tuple-element.16), channel_id=1, source_target_pairs={{0,3},{1,0},{2,1},{3,2},{4,7},{5,4},{6,5},{7,6},{8,11},{9,8},{10,9... | collective-permute-start | bytes 1572872 | tf_op jit(solution)/shard_map/ppermute | solution.py:41
  10.2 14.0 %collective-permute-start.1 = (bf16[256,1024]{1,0:T(8,128)(2,1)S(1)}, bf16[256,1024]{1,0:T(8,128)(2,1)S(1)}, u32[]{:S(2)}, u32[]{:S(2)}) collective-permute-start(bf16[256,1024]{1,0:T(8,128)(2,1)S(1)} %get-tuple-element.15), channel_id=1, source_target_pairs={{0,2},{1,3},{2,0},{3,1},{4,6},{5,7},{6,4},{7,5},{8,10},{9,11},{10,... | collective-permute-start | bytes 1572872 | tf_op jit(solution)/shard_map/ppermute | solution.py:41
  10.2 22.8 %collective-permute-start.2 = (bf16[256,1024]{1,0:T(8,128)(2,1)S(1)}, bf16[256,1024]{1,0:T(8,128)(2,1)}, u32[]{:S(2)}, u32[]{:S(2)}) collective-permute-start(bf16[256,1024]{1,0:T(8,128)(2,1)S(1)} %get-tuple-element.14), channel_id=1, source_target_pairs={{0,1},{1,2},{2,3},{3,0},{4,5},{5,6},{6,7},{7,4},{8,9},{9,10},{10,1... | collective-permute-start | bytes 1572872 | tf_op jit(solution)/shard_map/ppermute | solution.py:41
  12.0 24.0 %copy-start.2 = (bf16[128,1024]{1,0:T(8,128)(2,1)S(1)}, bf16[128,1024]{1,0:T(8,128)(2,1)}, u32[]{:S(2)}) copy-start(bf16[128,1024]{1,0:T(8,128)(2,1)} %param.7) | copy-start | bytes 786436
  34.8 0.8 copy-start.3
  34.9 1.0 copy-start.6
  34.9 1.1 copy-start.9
  61.8 5.1 %copy-start.17 = (s32[128]{0:T(128)S(1)}, s32[128]{0:T(128)}, u32[]{:S(2)}) copy-start(s32[128]{0:T(128)} %param.12) | copy-start | bytes 1540
  61.8 5.2 %copy-start.18 = (f32[128]{0:T(128)S(1)}, f32[128]{0:T(128)}, u32[]{:S(2)}) copy-start(f32[128]{0:T(128)} %param.13) | copy-start | bytes 1540
  62.0 6.0 %collective-permute-start.5 = (f32[32,1152]{1,0:T(8,128)S(1)}, f32[32,1152]{1,0:T(8,128)S(1)}, u32[]{:S(2)}, u32[]{:S(2)}) collective-permute-start(f32[32,1152]{1,0:T(8,128)S(1)} %copy.61), channel_id=1, source_target_pairs={{0,3},{1,0},{2,1},{3,2},{4,7},{5,4},{6,5},{7,6},{8,11},{9,8},{10,9... | collective-permute-start | bytes 442376 | tf_op jit(solution)/shard_map/ppermute | solution.py:67
  64.8 5.9 %collective-permute-start.4 = (f32[32,1152]{1,0:T(8,128)S(1)}, f32[32,1152]{1,0:T(8,128)S(1)}, u32[]{:S(2)}, u32[]{:S(2)}) collective-permute-start(f32[32,1152]{1,0:T(8,128)S(1)} %copy.59), channel_id=1, source_target_pairs={{0,2},{1,3},{2,0},{3,1},{4,6},{5,7},{6,4},{7,5},{8,10},{9,11},{10,... | collective-permute-start | bytes 442376 | tf_op jit(solution)/shard_map/ppermute | solution.py:67
  65.4 6.3 %collective-permute-start.3 = (f32[32,1152]{1,0:T(8,128)S(1)}, f32[32,1152]{1,0:T(8,128)S(1)}, u32[]{:S(2)}, u32[]{:S(2)}) collective-permute-start(f32[32,1152]{1,0:T(8,128)S(1)} %copy.57), channel_id=1, source_target_pairs={{0,1},{1,2},{2,3},{3,0},{4,5},{5,6},{6,7},{7,4},{8,9},{9,10},{10,1... | collective-permute-start | bytes 442376 | tf_op jit(solution)/shard_map/ppermute | solution.py:67
  73.7 10.4 %collective-permute-start.6 = (bf16[32,1152]{0,1:T(8,128)(2,1)S(1)}, bf16[32,1152]{0,1:T(8,128)(2,1)S(1)}, u32[]{:S(2)}, u32[]{:S(2)}) collective-permute-start(bf16[32,1152]{0,1:T(8,128)(2,1)S(1)} %concatenate.20), channel_id=1, source_target_pairs={{0,3},{1,0},{2,1},{3,2},{4,7},{5,4},{6,5},{7,6},{8,11},{9,8},{10,9... | collective-permute-start | bytes 221192 | tf_op jit(solution)/shard_map/ppermute | solution.py:90
  75.2 9.1 %collective-permute-start.7 = (bf16[32,1152]{0,1:T(8,128)(2,1)S(1)}, bf16[32,1152]{0,1:T(8,128)(2,1)S(1)}, u32[]{:S(2)}, u32[]{:S(2)}) collective-permute-start(bf16[32,1152]{0,1:T(8,128)(2,1)S(1)} %concatenate.20), channel_id=1, source_target_pairs={{0,2},{1,3},{2,0},{3,1},{4,6},{5,7},{6,4},{7,5},{8,10},{9,11},{10,... | collective-permute-start | bytes 221192 | tf_op jit(solution)/shard_map/ppermute | solution.py:90
  76.3 12.2 %collective-permute-start.8 = (bf16[32,1152]{0,1:T(8,128)(2,1)S(1)}, bf16[32,1152]{0,1:T(8,128)(2,1)S(1)}, u32[]{:S(2)}, u32[]{:S(2)}) collective-permute-start(bf16[32,1152]{0,1:T(8,128)(2,1)S(1)} %concatenate.20), channel_id=1, source_target_pairs={{0,1},{1,2},{2,3},{3,0},{4,5},{5,6},{6,7},{7,4},{8,9},{9,10},{10,1... | collective-permute-start | bytes 221192 | tf_op jit(solution)/shard_map/ppermute | solution.py:90
  89.0 4.9 %copy-start.4 = (bf16[256,1024]{1,0:T(8,128)(2,1)S(1)}, bf16[256,1024]{1,0:T(8,128)(2,1)}, u32[]{:S(2)}) copy-start(bf16[256,1024]{1,0:T(8,128)(2,1)} %copy-done.3) | copy-start | bytes 1572868
  89.1 4.9 %copy-start.7 = (bf16[256,1024]{1,0:T(8,128)(2,1)S(1)}, bf16[256,1024]{1,0:T(8,128)(2,1)}, u32[]{:S(2)}) copy-start(bf16[256,1024]{1,0:T(8,128)(2,1)} %copy-done.6) | copy-start | bytes 1572868
  89.1 4.9 %copy-start.10 = (bf16[256,1024]{1,0:T(8,128)(2,1)S(1)}, bf16[256,1024]{1,0:T(8,128)(2,1)}, u32[]{:S(2)}) copy-start(bf16[256,1024]{1,0:T(8,128)(2,1)} %copy-done.9) | copy-start | bytes 1572868
  90.0 22.3 %all-to-all-start = ((bf16[128,8,160]{0,2,1:T(8,128)(2,1)}), bf16[128,8,160]{0,2,1:T(8,128)(2,1)S(1)}, u32[]{:S(2)}, u32[]{:S(2)}) async-start(bf16[128,8,160]{0,2,1:T(8,128)(2,1)} %pad_maximum_fusion.1), calls=%async_computation | async-start | bytes 655360 | tf_op jit(solution)/shard_map/all_to_all | solution.py:120
  94.0 0.8 copy-start.12
  94.0 1.8 %copy-start = (bf16[1024,1024]{1,0:T(8,128)(2,1)S(1)}, bf16[1024,1024]{1,0:T(8,128)(2,1)}, u32[]{:S(2)}) copy-start(bf16[1024,1024]{1,0:T(8,128)(2,1)} %all-gather.3.cloned.1.call-done) | copy-start | bytes 6291460
  118.9 2.1 %copy-start.1 = (bf16[1024,1024]{1,0:T(8,128)(2,1)S(1)}, bf16[1024,1024]{1,0:T(8,128)(2,1)}, u32[]{:S(2)}) copy-start(bf16[1024,1024]{1,0:T(8,128)(2,1)} %all-gather.5.cloned.1.call-done) | copy-start | bytes 6291460
  121.0 3.1 %copy-start.14 = (f32[128,1024]{1,0:T(8,128)S(1)}, f32[128,1024]{1,0:T(8,128)}, u32[]{:S(2)}) copy-start(f32[128,1024]{1,0:T(8,128)} %convolution_add_fusion.2) | copy-start | bytes 1572868
  121.9 2.3 %copy-start.5 = (bf16[256,1024]{1,0:T(8,128)(2,1)S(1)}, bf16[256,1024]{1,0:T(8,128)(2,1)}, u32[]{:S(2)}) copy-start(bf16[256,1024]{1,0:T(8,128)(2,1)} %copy-done.3) | copy-start | bytes 1572868
  121.9 2.3 %copy-start.8 = (bf16[256,1024]{1,0:T(8,128)(2,1)S(1)}, bf16[256,1024]{1,0:T(8,128)(2,1)}, u32[]{:S(2)}) copy-start(bf16[256,1024]{1,0:T(8,128)(2,1)} %copy-done.6) | copy-start | bytes 1572868
  121.9 2.3 %copy-start.11 = (bf16[256,1024]{1,0:T(8,128)(2,1)S(1)}, bf16[256,1024]{1,0:T(8,128)(2,1)}, u32[]{:S(2)}) copy-start(bf16[256,1024]{1,0:T(8,128)(2,1)} %copy-done.9) | copy-start | bytes 1572868
  121.9 2.3 %copy-start.13 = (f32[128,1024]{1,0:T(8,128)S(1)}, f32[128,1024]{1,0:T(8,128)}, u32[]{:S(2)}) copy-start(f32[128,1024]{1,0:T(8,128)} %copy-done.12) | copy-start | bytes 1572868
  122.0 4.7 %collective-permute-start.9 = (f32[256,512]{1,0:T(8,128)S(1)}, f32[256,512]{1,0:T(8,128)S(1)}, u32[]{:S(2)}, u32[]{:S(2)}) collective-permute-start(f32[256,512]{1,0:T(8,128)S(1)} %get-tuple-element.22), channel_id=1, source_target_pairs={{0,0},{4,2},{8,4},{12,6},{1,8},{5,10},{9,12},{13,14},{18,16},{22,1... | collective-permute-start | bytes 1572872 | tf_op jit(solution)/shard_map/ppermute | solution.py:158
  122.8 28.3 %collective-permute-start.10 = (f32[256,512]{1,0:T(8,128)S(1)}, f32[256,512]{1,0:T(8,128)S(1)}, u32[]{:S(2)}, u32[]{:S(2)}) collective-permute-start(f32[256,512]{1,0:T(8,128)S(1)} %get-tuple-element.21), channel_id=1, source_target_pairs={{0,1},{4,3},{8,5},{12,7},{1,9},{5,11},{9,13},{13,15},{18,17},{22,1... | collective-permute-start | bytes 1572872 | tf_op jit(solution)/shard_map/ppermute | solution.py:160
Sparse Core Ops, SparseCore 0:
  10.1 48.3 all-gather.2
  66.9 51.9 all-gather.4

commit v6 on v4

--- a/solution.py
+++ b/solution.py
@@ -130,26 +130,27 @@
 
     per_col = blk_count // owner_count
     piece_width = col_width // per_col
-    shard = blk_index // per_col
     part = blk_index % per_col
-    shard_iota = shard * rows_shard + jnp.arange(rows_shard, dtype=jnp.int32)
-    shard_picks = all_ids[:, :, None] == shard_iota[None, None, :]
-    shard_mix = jnp.sum(
-        jnp.where(shard_picks, all_hard.astype(jnp.float32)[:, :, None], 0.0), axis=1
-    )
-    shard_hi, shard_lo = hi_lo(shard_mix)
+    holder = blk_index // per_col
+    all_picks = all_ids[:, :, None] == row_iota[None, None, :]
+    all_mix = jnp.sum(jnp.where(all_picks, all_hard.astype(jnp.float32)[:, :, None], 0.0), axis=1)
+    all_hi, all_lo = hi_lo(all_mix)
     query_part = lax.dynamic_slice_in_dim(all_queries, part * piece_width, piece_width, axis=1)
     dims = (((0,), (0,)), ((), ()))
-    piece = lax.dot_general(
-        shard_hi, query_part, dims, preferred_element_type=jnp.float32
-    ) + lax.dot_general(shard_lo, query_part, dims, preferred_element_type=jnp.float32)
-    perm = []
-    for b in range(blk_count):
-        for c in range(owner_count):
-            dest_b = c * per_col + b % per_col
-            dest_c = b // per_col
-            perm.append((b * owner_count + c, dest_b * owner_count + dest_c))
-    table_grad = lax.ppermute(piece, ("blk", "corpus"), perm)
+    pieces = lax.dot_general(
+        all_hi, query_part, dims, preferred_element_type=jnp.float32
+    ) + lax.dot_general(all_lo, query_part, dims, preferred_element_type=jnp.float32)
+    own = lax.dynamic_slice_in_dim(pieces, owner_index * rows_shard, rows_shard, axis=0)
+    table_grad = jnp.where(owner_index == holder, own, 0.0)
+    for k in range(1, owner_count):
+        pairs = [
+            (b * owner_count + b // per_col, b * owner_count + (b // per_col + k) % owner_count)
+            for b in range(blk_count)
+        ]
+        sent = lax.dynamic_slice_in_dim(
+            pieces, ((owner_index + k) % owner_count) * rows_shard, rows_shard, axis=0
+        )
+        table_grad = table_grad + lax.ppermute(sent, ("blk", "corpus"), pairs)
     return (loss_share, query_grad, passage_grad, table_grad)
 
 

time: 157 us -> 157 us (level)
  waiting for transfers between devices: 106 us -> 95.5 us
  other arithmetic: 8.35 us -> 13.1 us
  matrix products: 9.59 us -> 12.4 us
  starting transfers between devices: 9.96 us -> 12.6 us
    all_gather x1, waiting for transfers between devices: 2.14 us -> 14.6 us  [per_device_body(): all_queries = lax.all_gather(queries, 'blk', axis=0, tiled=True)]
    ppermute x1 -> x3, waiting for transfers between devices: 22.5 us -> 10.7 us  [per_device_body(): table_grad = table_grad + lax.ppermute(sent, ('blk', 'corpus'), pairs)]
    all_to_all x1, waiting for transfers between devices: 15.6 us -> 7.24 us  [per_device_body(): lax.all_to_all(packed, 'blk', split_axis=1, concat_axis=0, tiled=True)]
    reduce_sum x1, other arithmetic: 2.54 us -> 6.24 us  [per_device_body(): jnp.sum(jnp.where(all_picks, all_hard.astype(jnp.float32)[:, :, None], 0....]
    ppermute x3, waiting for transfers between devices: 24.1 us -> 20.9 us  [per_device_body(): received.append(lax.ppermute(slice_of(k), 'corpus', shift))]
    all_gather x1, waiting for transfers between devices: 20.9 us -> 23.7 us  [per_device_body(): all_passages = lax.all_gather(passages, 'blk', axis=0, tiled=True)]
    dot_general x2, matrix products: 2.35 us -> 5.2 us  [the longest x1 3.92 us: per_device_body(): lax.dot_general(all_hi, query_part, dims, preferred_element_type=jnp.floa...]
    ppermute x3, waiting for transfers between devices: 13.9 us -> 11.5 us  [per_device_body(): received.append(lax.ppermute(grads_part, 'corpus', shift))]
  transfers between devices with their start and end apart: 13 -> 15, of which waited for: 13 -> 13; matrix products, arithmetic and copies ran while one was open for 11% -> 12% of each run, Pallas kernels for 0% -> 0%
where the time goes in v6:
time: 157 us; the launch traced here: 156 us
  waiting for transfers between devices  95.5 us (61%)
  between operations  14.6 us (9%)
  other arithmetic  13.1 us (8%)
  starting transfers between devices  12.6 us (8%)
  matrix products  12.4 us (8%)
  local copies, waits for them, and re-layouts  7.64 us (5%)
    all_gather x1, waiting for transfers between devices, per_device_body(): all_passages = lax.all_gather(passages, 'blk', axis=0, tiled=True)  23.7 us
    ppermute x3, waiting for transfers between devices, per_device_body(): received.append(lax.ppermute(slice_of(k), 'corpus', shift))  20.9 us
    all_gather x1, waiting for transfers between devices, per_device_body(): all_queries = lax.all_gather(queries, 'blk', axis=0, tiled=True)  14.6 us
    ppermute x3, waiting for transfers between devices, per_device_body(): received.append(lax.ppermute(grads_part, 'corpus', shift))  11.5 us
    ppermute x3, waiting for transfers between devices, per_device_body(): table_grad = table_grad + lax.ppermute(sent, ('blk', 'corpus'), pairs)  10.7 us
    all_to_all x1, waiting for transfers between devices, per_device_body(): lax.all_to_all(packed, 'blk', split_axis=1, concat_axis=0, tiled=True)  7.24 us
    reduce_sum x1, other arithmetic, per_device_body(): jnp.sum(jnp.where(all_picks, all_hard.astype(jnp.float32)[:, :, None], 0....  6.24 us
    ppermute x3, waiting for transfers between devices, per_device_body(): summed = summed + lax.ppermute(chunk_of(k), 'corpus', shift)  6.13 us
  transfers between devices with their start and end apart: 15, of which 13 were waited for; matrix products, arithmetic and copies ran while one was open for 12% of the time, Pallas kernels for 0%

profile of v6, /device:TPU:2, one launch (start us, length us, event | category | flops | bytes accessed | tf_op | source)
XLA Modules:
  0.0 155.8 jit_solution(2610526141732268894)
XLA Ops:
  7.2 0.7 all-gather.3.cloned.1.call-update
  8.0 1.5 constant_dynamic-slice_fusion.6
  9.7 1.7 %collective-permute-start = (bf16[256,1024]{1,0:T(8,128)(2,1)S(1)}, bf16[256,1024]{1,0:T(8,128)(2,1)}, u32[]{:S(2)}, u32[]{:S(2)}) collective-permute-start(bf16[256,1024]{1,0:T(8,128)(2,1)S(1)} %get-tuple-element.19), channel_id=1, source_target_pairs={{0,3},{1,0},{2,1},{3,2},{4,7},{5,4},{6,5},{7,6},{8,11},{9,8},{10,9... | collective-permute-start | bytes 1572872 | tf_op jit(solution)/shard_map/ppermute | solution.py:41
  11.3 11.8 %collective-permute-done.2 = bf16[256,1024]{1,0:T(8,128)(2,1)S(1)} collective-permute-done((bf16[256,1024]{1,0:T(8,128)(2,1)S(1)}, bf16[256,1024]{1,0:T(8,128)(2,1)S(1)}, u32[]{:S(2)}, u32[]{:S(2)}) %collective-permute-start.2) | collective-permute-done | bytes 524320 | tf_op jit(solution)/shard_map/ppermute | solution.py:41
  23.1 1.3 collective-permute-done.1
  24.4 7.8 %collective-permute-done = bf16[256,1024]{1,0:T(8,128)(2,1)} collective-permute-done((bf16[256,1024]{1,0:T(8,128)(2,1)S(1)}, bf16[256,1024]{1,0:T(8,128)(2,1)}, u32[]{:S(2)}, u32[]{:S(2)}) %collective-permute-start) | collective-permute-done | bytes 524320 | tf_op jit(solution)/shard_map/ppermute | solution.py:41
  32.3 1.8 %select_select_fusion.3 = (bf16[256,1024]{1,0:T(8,128)(2,1)S(1)}, bf16[256,1024]{1,0:T(8,128)(2,1)S(1)}, bf16[256,1024]{1,0:T(8,128)(2,1)S(1)}, bf16[256,1024]{1,0:T(8,128)(2,1)S(1)}) fusion(bf16[256,1024]{1,0:T(8,128)(2,1)} %collective-permute-done, bf16[256,1024]{1,0:T(8,128)(2,1)S(1)} %collective-permute-done.1, ...), kind=kLoop, calls=%fused_computation.28 | loop fusion | flops 3145728 | bytes 4194320 | tf_op jit(solution)/shard_map/jit(_where)/select_n | solution.py:20
  34.1 0.8 copy-done.4
  34.9 0.2 copy-done.6
  35.0 0.2 copy-done.8
  35.2 0.7 convolution_bitcast_fusion
  35.9 0.2 copy.55
  36.1 0.6 select_reduce_fusion.2
  36.7 23.7 %all-gather.3.cloned.1.call-done = bf16[1024,1024]{1,0:T(8,128)(2,1)} async-done(((bf16[128,1024]{1,0:T(8,128)(2,1)}), bf16[1024,1024]{1,0:T(8,128)(2,1)}) %all-gather.3.cloned.1.call-update) | async-done | bytes 2097168 | tf_op jit(solution)/shard_map/all_gather | solution.py:43
  60.5 2.3 %fusion.20 = f32[128,1024]{0,1:T(8,128)S(1)} fusion(bf16[128,1024]{1,0:T(8,128)(2,1)S(1)} %copy-done.3, bf16[1024,1024]{1,0:T(8,128)(2,1)} %all-gather.3.cloned.1.call-done), kind=kOutput, calls=%fused_computation.68 | convolution fusion | flops 268435456 | bytes 2883584 | tf_op jit(solution)/shard_map/dot_general | solution.py:48
  62.8 0.4 concatenate.19
  63.2 0.5 constant_dynamic-slice_fusion.5
  63.7 0.2 copy.57
  63.9 0.2 copy.61
  64.2 1.7 %collective-permute-start.5 = (f32[32,1152]{1,0:T(8,128)S(1)}, f32[32,1152]{1,0:T(8,128)S(1)}, u32[]{:S(2)}, u32[]{:S(2)}) collective-permute-start(f32[32,1152]{1,0:T(8,128)S(1)} %copy.61), channel_id=1, source_target_pairs={{0,3},{1,0},{2,1},{3,2},{4,7},{5,4},{6,5},{7,6},{8,11},{9,8},{10,9... | collective-permute-start | bytes 442376 | tf_op jit(solution)/shard_map/ppermute | solution.py:67
  65.9 0.2 copy.59
  66.1 0.6 collective-permute-start.4
  66.9 2.6 %collective-permute-done.3 = f32[32,1152]{1,0:T(8,128)S(1)} collective-permute-done((f32[32,1152]{1,0:T(8,128)S(1)}, f32[32,1152]{1,0:T(8,128)S(1)}, u32[]{:S(2)}, u32[]{:S(2)}) %collective-permute-start.3) | collective-permute-done | bytes 147488 | tf_op jit(solution)/shard_map/ppermute | solution.py:67
  69.5 0.2 copy.58
  69.7 0.3 collective-permute-done.5
  70.0 0.2 copy.62
  70.2 3.3 %collective-permute-done.4 = f32[32,1152]{1,0:T(8,128)S(1)} collective-permute-done((f32[32,1152]{1,0:T(8,128)S(1)}, f32[32,1152]{1,0:T(8,128)S(1)}, u32[]{:S(2)}, u32[]{:S(2)}) %collective-permute-start.4) | collective-permute-done | bytes 147488 | tf_op jit(solution)/shard_map/ppermute | solution.py:67
  73.5 0.2 copy.60
  73.7 0.2 add_add_fusion
  74.0 0.2 fusion.7
  74.2 0.2 select_reduce_fusion.3
  74.4 0.5 fusion.18
  74.9 0.2 multiply_convert_fusion
  75.1 0.4 concatenate.20
  75.6 0.6 collective-permute-start.7
  76.2 1.4 collective-permute-start.6
  77.8 6.5 %collective-permute-done.8 = bf16[32,1152]{0,1:T(8,128)(2,1)S(1)} collective-permute-done((bf16[32,1152]{0,1:T(8,128)(2,1)S(1)}, bf16[32,1152]{0,1:T(8,128)(2,1)S(1)}, u32[]{:S(2)}, u32[]{:S(2)}) %collective-permute-start.8) | collective-permute-done | bytes 73760 | tf_op jit(solution)/shard_map/ppermute | solution.py:90
  84.2 1.3 collective-permute-done.7
  85.5 3.7 %collective-permute-done.6 = bf16[32,1152]{0,1:T(8,128)(2,1)S(1)} collective-permute-done((bf16[32,1152]{0,1:T(8,128)(2,1)S(1)}, bf16[32,1152]{0,1:T(8,128)(2,1)S(1)}, u32[]{:S(2)}, u32[]{:S(2)}) %collective-permute-start.6) | collective-permute-done | bytes 73760 | tf_op jit(solution)/shard_map/ppermute | solution.py:90
  89.3 0.1 select_select_fusion.7
  89.4 0.4 pad_maximum_fusion.2
  89.9 0.1 fusion.17
  90.0 0.1 maximum_maximum_fusion
  90.1 0.8 pad_maximum_fusion.1
  90.8 3.4 %all-to-all-start = ((bf16[128,8,160]{0,2,1:T(8,128)(2,1)}), bf16[128,8,160]{0,2,1:T(8,128)(2,1)S(1)}, u32[]{:S(2)}, u32[]{:S(2)}) async-start(bf16[128,8,160]{0,2,1:T(8,128)(2,1)} %pad_maximum_fusion.1), calls=%async_computation | async-start | bytes 655360 | tf_op jit(solution)/shard_map/all_to_all | solution.py:120
  94.2 0.5 select_reduce_fusion.1
  94.8 0.5 fusion.11
  95.3 0.3 copy-done.10
  95.6 1.0 copy-done.1
  96.6 1.3 convolution_add_fusion.1
  97.8 7.2 %all-to-all-done = bf16[128,8,160]{0,2,1:T(8,128)(2,1)S(1)} async-done(((bf16[128,8,160]{0,2,1:T(8,128)(2,1)}), bf16[128,8,160]{0,2,1:T(8,128)(2,1)S(1)}, u32[]{:S(2)}, u32[]{:S(2)}) %all-to-all-start) | async-done | bytes 327712 | tf_op jit(solution)/shard_map/all_to_all | solution.py:120
  105.2 6.2 %select_reduce_fusion = f32[1024,1024]{1,0:T(8,128)} fusion(f32[1024,7]{0,1:T(8,128)S(1)} %slice_convert_fusion, s32[1024,7]{0,1:T(8,128)S(1)} %convert_add_fusion), kind=kLoop, calls=%fused_computation | loop fusion | flops 20971520 | bytes 4251648 | tf_op jit(solution)/shard_map/reduce_sum | solution.py:136
  111.4 14.6 %all-gather.5.cloned.1.call-done = bf16[1024,1024]{1,0:T(8,128)(2,1)} async-done(((bf16[128,1024]{1,0:T(8,128)(2,1)}), bf16[1024,1024]{1,0:T(8,128)(2,1)}) %all-gather.5.cloned.1.call-update) | async-done | bytes 2097168 | tf_op jit(solution)/shard_map/all_gather | solution.py:44
  126.0 3.9 %fusion.3 = f32[1024,512]{1,0:T(8,128)S(1)} fusion(f32[1024,1024]{1,0:T(8,128)} %select_reduce_fusion, bf16[1024,1024]{1,0:T(8,128)(2,1)} %all-gather.5.cloned.1.call-done, s32[]{:T(128)S(6)} %select_n.349), kind=kOutput, calls=%fused_computation.13 | convolution fusion | flops 1074790400 | bytes 7340036 | tf_op jit(solution)/shard_map/dot_general | solution.py:140
  129.9 0.5 copy-done.2
  130.4 1.3 fusion.1
  131.7 0.1 constant_dynamic-slice_fusion.2
  131.9 0.8 collective-permute-start.9
  132.7 0.7 collective-permute-start.11
  133.4 1.3 collective-permute-start.10
  134.7 1.3 convolution_add_fusion
  136.0 1.2 fusion.8
  137.2 10.7 %collective-permute-done.10 = f32[256,512]{1,0:T(8,128)S(1)} collective-permute-done((f32[256,512]{1,0:T(8,128)S(1)}, f32[256,512]{1,0:T(8,128)S(1)}, u32[]{:S(2)}, u32[]{:S(2)}) %collective-permute-start.10) | collective-permute-done | bytes 524320 | tf_op jit(solution)/shard_map/ppermute | solution.py:153
  147.9 1.0 add_add_fusion.1
  (53 shorter events, 0.8 us)
Async XLA Ops:
  7.2 4.1 %copy-start.14 = (s32[128,7]{0,1:T(8,128)S(1)}, s32[128,7]{0,1:T(8,128)}, u32[]{:S(2)}) copy-start(s32[128,7]{0,1:T(8,128)} %param.11) | copy-start | bytes 10756
  7.2 4.1 %copy-start.13 = (s32[128,7]{0,1:T(8,128)S(1)}, s32[128,7]{0,1:T(8,128)}, u32[]{:S(2)}) copy-start(s32[128,7]{0,1:T(8,128)} %param.10) | copy-start | bytes 10756
  7.2 53.3 %all-gather.3.cloned.1.call-start = ((), (), s32[]{:S(2)}) async-start(), calls=%async_computation.1 | async-start | bytes 2359296 | tf_op jit(solution)/shard_map/all_gather | solution.py:43
  7.9 118.1 %all-gather.5.cloned.1.call-start = ((), (), s32[]{:S(2)}) async-start(), calls=%async_computation.2 | async-start | bytes 2359296 | tf_op jit(solution)/shard_map/all_gather | solution.py:44
  9.5 13.6 %collective-permute-start.2 = (bf16[256,1024]{1,0:T(8,128)(2,1)S(1)}, bf16[256,1024]{1,0:T(8,128)(2,1)S(1)}, u32[]{:S(2)}, u32[]{:S(2)}) collective-permute-start(bf16[256,1024]{1,0:T(8,128)(2,1)S(1)} %get-tuple-element.17), channel_id=1, source_target_pairs={{0,1},{1,2},{2,3},{3,0},{4,5},{5,6},{6,7},{7,4},{8,9},{9,10},{10,1... | collective-permute-start | bytes 1572872 | tf_op jit(solution)/shard_map/ppermute | solution.py:41
  9.6 14.9 %collective-permute-start.1 = (bf16[256,1024]{1,0:T(8,128)(2,1)S(1)}, bf16[256,1024]{1,0:T(8,128)(2,1)S(1)}, u32[]{:S(2)}, u32[]{:S(2)}) collective-permute-start(bf16[256,1024]{1,0:T(8,128)(2,1)S(1)} %get-tuple-element.18), channel_id=1, source_target_pairs={{0,2},{1,3},{2,0},{3,1},{4,6},{5,7},{6,4},{7,5},{8,10},{9,11},{10,... | collective-permute-start | bytes 1572872 | tf_op jit(solution)/shard_map/ppermute | solution.py:41
  9.7 22.6 %collective-permute-start = (bf16[256,1024]{1,0:T(8,128)(2,1)S(1)}, bf16[256,1024]{1,0:T(8,128)(2,1)}, u32[]{:S(2)}, u32[]{:S(2)}) collective-permute-start(bf16[256,1024]{1,0:T(8,128)(2,1)S(1)} %get-tuple-element.19), channel_id=1, source_target_pairs={{0,3},{1,0},{2,1},{3,2},{4,7},{5,4},{6,5},{7,6},{8,11},{9,8},{10,9... | collective-permute-start | bytes 1572872 | tf_op jit(solution)/shard_map/ppermute | solution.py:41
  11.3 23.9 %copy-start.3 = (bf16[128,1024]{1,0:T(8,128)(2,1)S(1)}, bf16[128,1024]{1,0:T(8,128)(2,1)}, u32[]{:S(2)}) copy-start(bf16[128,1024]{1,0:T(8,128)(2,1)} %param.7) | copy-start | bytes 786436
  34.1 0.8 copy-start.4
  34.1 1.0 copy-start.6
  34.1 1.1 copy-start.8
  63.2 3.6 %copy-start.15 = (s32[128]{0:T(128)S(1)}, s32[128]{0:T(128)}, u32[]{:S(2)}) copy-start(s32[128]{0:T(128)} %param.12) | copy-start | bytes 1540
  63.2 3.6 %copy-start.16 = (f32[128]{0:T(128)S(1)}, f32[128]{0:T(128)}, u32[]{:S(2)}) copy-start(f32[128]{0:T(128)} %param.13) | copy-start | bytes 1540
  64.1 5.3 %collective-permute-start.3 = (f32[32,1152]{1,0:T(8,128)S(1)}, f32[32,1152]{1,0:T(8,128)S(1)}, u32[]{:S(2)}, u32[]{:S(2)}) collective-permute-start(f32[32,1152]{1,0:T(8,128)S(1)} %copy.57), channel_id=1, source_target_pairs={{0,1},{1,2},{2,3},{3,0},{4,5},{5,6},{6,7},{7,4},{8,9},{9,10},{10,1... | collective-permute-start | bytes 442376 | tf_op jit(solution)/shard_map/ppermute | solution.py:67
  64.2 5.8 %collective-permute-start.5 = (f32[32,1152]{1,0:T(8,128)S(1)}, f32[32,1152]{1,0:T(8,128)S(1)}, u32[]{:S(2)}, u32[]{:S(2)}) collective-permute-start(f32[32,1152]{1,0:T(8,128)S(1)} %copy.61), channel_id=1, source_target_pairs={{0,3},{1,0},{2,1},{3,2},{4,7},{5,4},{6,5},{7,6},{8,11},{9,8},{10,9... | collective-permute-start | bytes 442376 | tf_op jit(solution)/shard_map/ppermute | solution.py:67
  66.1 7.4 %collective-permute-start.4 = (f32[32,1152]{1,0:T(8,128)S(1)}, f32[32,1152]{1,0:T(8,128)S(1)}, u32[]{:S(2)}, u32[]{:S(2)}) collective-permute-start(f32[32,1152]{1,0:T(8,128)S(1)} %copy.59), channel_id=1, source_target_pairs={{0,2},{1,3},{2,0},{3,1},{4,6},{5,7},{6,4},{7,5},{8,10},{9,11},{10,... | collective-permute-start | bytes 442376 | tf_op jit(solution)/shard_map/ppermute | solution.py:67
  75.5 8.7 %collective-permute-start.8 = (bf16[32,1152]{0,1:T(8,128)(2,1)S(1)}, bf16[32,1152]{0,1:T(8,128)(2,1)S(1)}, u32[]{:S(2)}, u32[]{:S(2)}) collective-permute-start(bf16[32,1152]{0,1:T(8,128)(2,1)S(1)} %concatenate.20), channel_id=1, source_target_pairs={{0,1},{1,2},{2,3},{3,0},{4,5},{5,6},{6,7},{7,4},{8,9},{9,10},{10,1... | collective-permute-start | bytes 221192 | tf_op jit(solution)/shard_map/ppermute | solution.py:90
  75.6 9.9 %collective-permute-start.7 = (bf16[32,1152]{0,1:T(8,128)(2,1)S(1)}, bf16[32,1152]{0,1:T(8,128)(2,1)S(1)}, u32[]{:S(2)}, u32[]{:S(2)}) collective-permute-start(bf16[32,1152]{0,1:T(8,128)(2,1)S(1)} %concatenate.20), channel_id=1, source_target_pairs={{0,2},{1,3},{2,0},{3,1},{4,6},{5,7},{6,4},{7,5},{8,10},{9,11},{10,... | collective-permute-start | bytes 221192 | tf_op jit(solution)/shard_map/ppermute | solution.py:90
  76.2 13.1 %collective-permute-start.6 = (bf16[32,1152]{0,1:T(8,128)(2,1)S(1)}, bf16[32,1152]{0,1:T(8,128)(2,1)S(1)}, u32[]{:S(2)}, u32[]{:S(2)}) collective-permute-start(bf16[32,1152]{0,1:T(8,128)(2,1)S(1)} %concatenate.20), channel_id=1, source_target_pairs={{0,3},{1,0},{2,1},{3,2},{4,7},{5,4},{6,5},{7,6},{8,11},{9,8},{10,9... | collective-permute-start | bytes 221192 | tf_op jit(solution)/shard_map/ppermute | solution.py:90
  89.8 4.9 %copy-start.5 = (bf16[256,1024]{1,0:T(8,128)(2,1)S(1)}, bf16[256,1024]{1,0:T(8,128)(2,1)}, u32[]{:S(2)}) copy-start(bf16[256,1024]{1,0:T(8,128)(2,1)} %copy-done.4) | copy-start | bytes 1572868
  89.8 4.9 %copy-start.7 = (bf16[256,1024]{1,0:T(8,128)(2,1)S(1)}, bf16[256,1024]{1,0:T(8,128)(2,1)}, u32[]{:S(2)}) copy-start(bf16[256,1024]{1,0:T(8,128)(2,1)} %copy-done.6) | copy-start | bytes 1572868
  89.8 4.9 %copy-start.9 = (bf16[256,1024]{1,0:T(8,128)(2,1)S(1)}, bf16[256,1024]{1,0:T(8,128)(2,1)}, u32[]{:S(2)}) copy-start(bf16[256,1024]{1,0:T(8,128)(2,1)} %copy-done.8) | copy-start | bytes 1572868
  90.8 14.3 %all-to-all-start = ((bf16[128,8,160]{0,2,1:T(8,128)(2,1)}), bf16[128,8,160]{0,2,1:T(8,128)(2,1)S(1)}, u32[]{:S(2)}, u32[]{:S(2)}) async-start(bf16[128,8,160]{0,2,1:T(8,128)(2,1)} %pad_maximum_fusion.1), calls=%async_computation | async-start | bytes 655360 | tf_op jit(solution)/shard_map/all_to_all | solution.py:120
  94.8 0.8 copy-start.10
  94.8 1.8 %copy-start.1 = (bf16[1024,1024]{1,0:T(8,128)(2,1)S(1)}, bf16[1024,1024]{1,0:T(8,128)(2,1)}, u32[]{:S(2)}) copy-start(bf16[1024,1024]{1,0:T(8,128)(2,1)} %all-gather.3.cloned.1.call-done) | copy-start | bytes 6291460
  126.0 3.9 %copy-start = (f32[1024,1024]{1,0:T(8,128)S(1)}, f32[1024,1024]{1,0:T(8,128)}, u32[]{:S(2)}) copy-start(f32[1024,1024]{1,0:T(8,128)} %select_reduce_fusion) | copy-start | bytes 12582916
  126.0 4.4 %copy-start.2 = (bf16[1024,1024]{1,0:T(8,128)(2,1)S(1)}, bf16[1024,1024]{1,0:T(8,128)(2,1)}, u32[]{:S(2)}) copy-start(bf16[1024,1024]{1,0:T(8,128)(2,1)} %all-gather.5.cloned.1.call-done) | copy-start | bytes 6291460
  131.7 3.0 %copy-start.11 = (f32[128,1024]{1,0:T(8,128)S(1)}, f32[128,1024]{1,0:T(8,128)}, u32[]{:S(2)}) copy-start(f32[128,1024]{1,0:T(8,128)} %copy-done.10) | copy-start | bytes 1572868
  131.7 3.0 %copy-start.12 = (f32[128,1024]{1,0:T(8,128)S(1)}, f32[128,1024]{1,0:T(8,128)}, u32[]{:S(2)}) copy-start(f32[128,1024]{1,0:T(8,128)} %convolution_add_fusion.1) | copy-start | bytes 1572868
  131.9 5.4 %collective-permute-start.9 = (f32[256,512]{1,0:T(8,128)S(1)}, f32[256,512]{1,0:T(8,128)S(1)}, u32[]{:S(2)}, u32[]{:S(2)}) collective-permute-start(f32[256,512]{1,0:T(8,128)S(1)} %get-tuple-element.14), channel_id=1, source_target_pairs={{0,1},{4,5},{9,10},{13,14},{18,19},{22,23},{27,24},{31,28}} | collective-permute-start | bytes 1572872 | tf_op jit(solution)/shard_map/ppermute | solution.py:153
  132.7 4.5 %collective-permute-start.11 = (f32[256,512]{1,0:T(8,128)S(1)}, f32[256,512]{1,0:T(8,128)S(1)}, u32[]{:S(2)}, u32[]{:S(2)}) collective-permute-start(f32[256,512]{1,0:T(8,128)S(1)} %get-tuple-element.15), channel_id=1, source_target_pairs={{0,3},{4,7},{9,8},{13,12},{18,17},{22,21},{27,26},{31,30}} | collective-permute-start | bytes 1572872 | tf_op jit(solution)/shard_map/ppermute | solution.py:153
  133.4 14.5 %collective-permute-start.10 = (f32[256,512]{1,0:T(8,128)S(1)}, f32[256,512]{1,0:T(8,128)S(1)}, u32[]{:S(2)}, u32[]{:S(2)}) collective-permute-start(f32[256,512]{1,0:T(8,128)S(1)} %get-tuple-element.16), channel_id=1, source_target_pairs={{0,2},{4,6},{9,11},{13,15},{18,16},{22,20},{27,25},{31,29}} | collective-permute-start | bytes 1572872 | tf_op jit(solution)/shard_map/ppermute | solution.py:153
Sparse Core Ops, SparseCore 0:
  10.1 50.2 all-gather.2
  77.7 48.1 all-gather.4

commit v7 on v6

--- a/solution.py
+++ b/solution.py
@@ -40,8 +40,17 @@
         shift = [(j, (j + k) % owner_count) for j in range(owner_count)]
         received.append(lax.ppermute(slice_of(k), "corpus", shift))
     table_cols = gather_blocks(slice_of(0), received, owner_index, owner_count)
-    all_passages = lax.all_gather(passages, "blk", axis=0, tiled=True)
-    all_queries = lax.all_gather(queries, "blk", axis=0, tiled=True)
+    received = []
+    for k in range(1, blk_count):
+        shift = [(j, (j + k) % blk_count) for j in range(blk_count)]
+        received.append(lax.ppermute(passages, "blk", shift))
+    all_passages = gather_blocks(passages, received, blk_index, blk_count)
+    all_passages, later = lax.optimization_barrier((all_passages, queries))
+    received = []
+    for k in range(1, blk_count):
+        shift = [(j, (j + k) % blk_count) for j in range(blk_count)]
+        received.append(lax.ppermute(later, "blk", shift))
+    all_queries = gather_blocks(later, received, blk_index, blk_count)
     ids = neg_owner * rows_shard + neg_row
     all_rows = all_passages.shape[0]
 
@@ -64,7 +73,8 @@
     summed = chunk_of(0)
     for k in range(1, owner_count):
         shift = [(j, (j + k) % owner_count) for j in range(owner_count)]
-        summed = summed + lax.ppermute(chunk_of(k), "corpus", shift)
+        got = lax.ppermute(chunk_of(k), "corpus", shift)
+        summed = summed + got
     logits = summed[:, :all_rows] * factor
     hard_logits = summed[:, all_rows:all_rows + negs] * factor
     my_positive = lax.dynamic_slice_in_dim(positive, owner_index * share, share)

time: 157 us -> 172 us (1.096)
  starting transfers between devices: 12.6 us -> 70.6 us
  waiting for transfers between devices: 95.5 us -> 57 us
  between operations: 14.6 us -> 1.45 us
  other arithmetic: 13.1 us -> 22.4 us
    ppermute x3 -> x17, starting transfers between devices: 2.39 us -> 49 us  [the longest x7 30.5 us: per_device_body(): received.append(lax.ppermute(later, 'blk', shift))]
    all_gather x2 -> x0, waiting for transfers between devices: 38.3 us -> none  [the longest x1 23.7 us: per_device_body(): all_passages = lax.all_gather(passages, 'blk', axis=0, tiled=True)]
    ppermute x3 -> x17, waiting for transfers between devices: 6.13 us -> 27.2 us  [the longest x7 16 us: per_device_body(): received.append(lax.ppermute(passages, 'blk', shift))]
    ppermute x3, waiting for transfers between devices: 20.9 us -> 0.01 us  [per_device_body(): received.append(lax.ppermute(slice_of(k), 'corpus', shift))]
    unnamed x0 -> x14, other arithmetic: none -> 9.96 us
    all_to_all x1, starting transfers between devices: 3.43 us -> 12.3 us  [per_device_body(): lax.all_to_all(packed, 'blk', split_axis=1, concat_axis=0, tiled=True)]
    ppermute x3, starting transfers between devices: 2.06 us -> 4.83 us  [per_device_body(): received.append(lax.ppermute(grads_part, 'corpus', shift))]
    reduce_sum x1, other arithmetic: 6.24 us -> 4.34 us  [per_device_body(): jnp.sum(jnp.where(all_picks, all_hard.astype(jnp.float32)[:, :, None], 0....]
  transfers between devices with their start and end apart: 15 -> 27, of which waited for: 13 -> 12; matrix products, arithmetic and copies ran while one was open for 12% -> 15% of each run, Pallas kernels for 0% -> 0%
where the time goes in v7:
time: 172 us; the launch traced here: 171 us
  starting transfers between devices  70.6 us (41%)
  waiting for transfers between devices  57 us (33%)
  other arithmetic  22.4 us (13%)
  matrix products  12.4 us (7%)
  local copies, waits for them, and re-layouts  7.32 us (4%)
    ppermute x7, starting transfers between devices, per_device_body(): received.append(lax.ppermute(later, 'blk', shift))  30.5 us
    ppermute x7, waiting for transfers between devices, per_device_body(): received.append(lax.ppermute(passages, 'blk', shift))  16 us
    ppermute x7, starting transfers between devices, per_device_body(): received.append(lax.ppermute(passages, 'blk', shift))  16 us
    all_to_all x1, starting transfers between devices, per_device_body(): lax.all_to_all(packed, 'blk', split_axis=1, concat_axis=0, tiled=True)  12.3 us
    ppermute x7, waiting for transfers between devices, per_device_body(): received.append(lax.ppermute(later, 'blk', shift))  11.2 us
    ppermute x3, waiting for transfers between devices, per_device_body(): received.append(lax.ppermute(grads_part, 'corpus', shift))  10.5 us
    ppermute x3, waiting for transfers between devices, per_device_body(): table_grad = table_grad + lax.ppermute(sent, ('blk', 'corpus'), pairs)  10.4 us
    unnamed x14, other arithmetic  9.96 us
  transfers between devices with their start and end apart: 27, of which 12 were waited for; matrix products, arithmetic and copies ran while one was open for 15% of the time, Pallas kernels for 0%

profile of v7, /device:TPU:2, one launch (start us, length us, event | category | flops | bytes accessed | tf_op | source)
XLA Modules:
  0.0 171.1 jit_solution(16695028504876594513)
XLA Ops:
  0.7 1.6 collective-permute-start.6
  2.3 1.6 collective-permute-start.5
  3.8 2.5 %collective-permute-start.4 = (bf16[128,1024]{1,0:T(8,128)(2,1)}, bf16[128,1024]{1,0:T(8,128)(2,1)S(1)}, u32[]{:S(2)}, u32[]{:S(2)}) collective-permute-start(bf16[128,1024]{1,0:T(8,128)(2,1)} %param.8), channel_id=1, source_target_pairs={{0,12},{4,16},{8,20},{12,24},{16,28},{20,0},{24,4},{28,8},{1,13},{... | collective-permute-start | bytes 786440 | tf_op jit(solution)/shard_map/ppermute | solution.py:46
  6.4 1.2 collective-permute-start.3
  7.6 2.6 %collective-permute-start.2 = (bf16[128,1024]{1,0:T(8,128)(2,1)}, bf16[128,1024]{1,0:T(8,128)(2,1)S(1)}, u32[]{:S(2)}, u32[]{:S(2)}) collective-permute-start(bf16[128,1024]{1,0:T(8,128)(2,1)} %param.8), channel_id=1, source_target_pairs={{0,20},{4,24},{8,28},{12,0},{16,4},{20,8},{24,12},{28,16},{1,21},{... | collective-permute-start | bytes 786440 | tf_op jit(solution)/shard_map/ppermute | solution.py:46
  10.2 2.4 %constant_dynamic-slice_fusion.6 = (bf16[256,1024]{1,0:T(8,128)(2,1)}, bf16[256,1024]{1,0:T(8,128)(2,1)}, bf16[256,1024]{1,0:T(8,128)(2,1)S(1)}) fusion(bf16[256,4096]{1,0:T(8,128)(2,1)} %param.9, s32[]{:T(128)S(6)} %select_n.1017, s32[]{:T(128)S(6)} %select_n.1014, s32[]{:T(128)S(6)} %select_n.1011), kind=kLoop, calls=%fused_computation.74 | loop fusion | bytes 3145740 | tf_op jit(solution)/shard_map/dynamic_slice | solution.py:35
  13.0 1.6 collective-permute-start.1
  14.6 4.9 %collective-permute-start = (bf16[128,1024]{1,0:T(8,128)(2,1)S(1)}, bf16[128,1024]{1,0:T(8,128)(2,1)S(1)}, u32[]{:S(2)}, u32[]{:S(2)}) collective-permute-start(bf16[128,1024]{1,0:T(8,128)(2,1)S(1)} %copy-done.1), channel_id=1, source_target_pairs={{0,28},{4,0},{8,4},{12,8},{16,12},{20,16},{24,20},{28,24},{1,29},{... | collective-permute-start | bytes 786440 | tf_op jit(solution)/shard_map/ppermute | solution.py:46
  20.1 14.3 %collective-permute-done.4 = bf16[128,1024]{1,0:T(8,128)(2,1)S(1)} collective-permute-done((bf16[128,1024]{1,0:T(8,128)(2,1)}, bf16[128,1024]{1,0:T(8,128)(2,1)S(1)}, u32[]{:S(2)}, u32[]{:S(2)}) %collective-permute-start.4) | collective-permute-done | bytes 262176 | tf_op jit(solution)/shard_map/ppermute | solution.py:46
  34.7 0.5 collective-permute-start.8
  35.3 1.2 collective-permute-start.7
  36.4 1.0 collective-permute-done
  37.5 0.4 select_dynamic-update-slice_fusion.15
  37.8 0.4 select_dynamic-update-slice_fusion.14
  38.2 0.4 select_dynamic-update-slice_fusion.13
  38.6 0.4 select_dynamic-update-slice_fusion.12
  40.6 4.4 %collective-permute-start.22 = (bf16[128,1024]{1,0:T(8,128)(2,1)S(1)}, bf16[128,1024]{1,0:T(8,128)(2,1)S(1)}, u32[]{:S(2)}, u32[]{:S(2)}) collective-permute-start(bf16[128,1024]{1,0:T(8,128)(2,1)S(1)} %copy-done), channel_id=1, source_target_pairs={{0,4},{4,8},{8,12},{12,16},{16,20},{20,24},{24,28},{28,0},{1,5},{5... | collective-permute-start | bytes 786440 | tf_op jit(solution)/shard_map/ppermute | solution.py:52
  45.0 11.6 %collective-permute-start.21 = (bf16[128,1024]{1,0:T(8,128)(2,1)S(1)}, bf16[128,1024]{1,0:T(8,128)(2,1)S(1)}, u32[]{:S(2)}, u32[]{:S(2)}) collective-permute-start(bf16[128,1024]{1,0:T(8,128)(2,1)S(1)} %copy-done), channel_id=1, source_target_pairs={{0,8},{4,12},{8,16},{12,20},{16,24},{20,28},{24,0},{28,4},{1,9},{5... | collective-permute-start | bytes 786440 | tf_op jit(solution)/shard_map/ppermute | solution.py:52
  56.7 0.8 convolution_bitcast_fusion.1
  57.6 2.1 %collective-permute-start.19 = (bf16[128,1024]{1,0:T(8,128)(2,1)S(1)}, bf16[128,1024]{1,0:T(8,128)(2,1)S(1)}, u32[]{:S(2)}, u32[]{:S(2)}) collective-permute-start(bf16[128,1024]{1,0:T(8,128)(2,1)S(1)} %copy-done), channel_id=1, source_target_pairs={{0,16},{4,20},{8,24},{12,28},{16,0},{20,4},{24,8},{28,12},{1,17},{... | collective-permute-start | bytes 786440 | tf_op jit(solution)/shard_map/ppermute | solution.py:52
  59.7 7.2 %collective-permute-start.18 = (bf16[128,1024]{1,0:T(8,128)(2,1)S(1)}, bf16[128,1024]{1,0:T(8,128)(2,1)S(1)}, u32[]{:S(2)}, u32[]{:S(2)}) collective-permute-start(bf16[128,1024]{1,0:T(8,128)(2,1)S(1)} %copy-done), channel_id=1, source_target_pairs={{0,20},{4,24},{8,28},{12,0},{16,4},{20,8},{24,12},{28,16},{1,21},{... | collective-permute-start | bytes 786440 | tf_op jit(solution)/shard_map/ppermute | solution.py:52
  66.9 1.7 select_select_fusion.3
  68.7 0.8 copy-done.4
  69.8 1.5 convolution_bitcast_fusion
  71.3 1.2 copy.49
  72.5 5.1 %collective-permute-start.17 = (bf16[128,1024]{1,0:T(8,128)(2,1)S(1)}, bf16[128,1024]{1,0:T(8,128)(2,1)S(1)}, u32[]{:S(2)}, u32[]{:S(2)}) collective-permute-start(bf16[128,1024]{1,0:T(8,128)(2,1)S(1)} %copy-done), channel_id=1, source_target_pairs={{0,24},{4,28},{8,0},{12,4},{16,8},{20,12},{24,16},{28,20},{1,25},{... | collective-permute-start | bytes 786440 | tf_op jit(solution)/shard_map/ppermute | solution.py:52
  77.6 0.6 select_reduce_fusion.2
  78.5 8.3 %collective-permute-done.20 = bf16[128,1024]{1,0:T(8,128)(2,1)S(1)} collective-permute-done((bf16[128,1024]{1,0:T(8,128)(2,1)S(1)}, bf16[128,1024]{1,0:T(8,128)(2,1)S(1)}, u32[]{:S(2)}, u32[]{:S(2)}) %collective-permute-start.20) | collective-permute-done | bytes 262176 | tf_op jit(solution)/shard_map/ppermute | solution.py:52
  86.8 1.7 collective-permute-start.12
  88.5 0.8 collective-permute-start.11
  89.3 2.8 %collective-permute-done.16 = bf16[128,1024]{1,0:T(8,128)(2,1)S(1)} collective-permute-done((bf16[128,1024]{1,0:T(8,128)(2,1)S(1)}, bf16[128,1024]{1,0:T(8,128)(2,1)S(1)}, u32[]{:S(2)}, u32[]{:S(2)}) %collective-permute-start.16) | collective-permute-done | bytes 262176 | tf_op jit(solution)/shard_map/ppermute | solution.py:52
  92.1 1.1 select_dynamic-update-slice_fusion.7
  93.1 1.1 select_dynamic-update-slice_fusion.6
  94.2 1.1 select_dynamic-update-slice_fusion.5
  95.3 1.1 select_dynamic-update-slice_fusion.4
  96.3 1.0 select_dynamic-update-slice_fusion.3
  97.4 1.1 select_dynamic-update-slice_fusion.2
  98.4 1.1 select_dynamic-update-slice_fusion.1
  100.2 0.5 fusion.16
  101.3 3.4 %collective-permute-start.15 = (bf16[32,1152]{0,1:T(8,128)(2,1)S(1)}, bf16[32,1152]{0,1:T(8,128)(2,1)S(1)}, u32[]{:S(2)}, u32[]{:S(2)}) collective-permute-start(bf16[32,1152]{0,1:T(8,128)(2,1)S(1)} %copy.51), channel_id=1, source_target_pairs={{0,1},{1,2},{2,3},{3,0},{4,5},{5,6},{6,7},{7,4},{8,9},{9,10},{10,1... | collective-permute-start | bytes 221192 | tf_op jit(solution)/shard_map/ppermute | solution.py:100
  104.7 1.0 collective-permute-start.14
  105.7 0.4 collective-permute-start.13
  106.1 1.1 select_dynamic-update-slice_fusion
  107.2 4.0 %collective-permute-done.15 = bf16[32,1152]{0,1:T(8,128)(2,1)S(1)} collective-permute-done((bf16[32,1152]{0,1:T(8,128)(2,1)S(1)}, bf16[32,1152]{0,1:T(8,128)(2,1)S(1)}, u32[]{:S(2)}, u32[]{:S(2)}) %collective-permute-start.15) | collective-permute-done | bytes 73760 | tf_op jit(solution)/shard_map/ppermute | solution.py:100
  111.1 3.4 %collective-permute-done.14 = bf16[32,1152]{0,1:T(8,128)(2,1)S(1)} collective-permute-done((bf16[32,1152]{0,1:T(8,128)(2,1)S(1)}, bf16[32,1152]{0,1:T(8,128)(2,1)S(1)}, u32[]{:S(2)}, u32[]{:S(2)}) %collective-permute-start.14) | collective-permute-done | bytes 73760 | tf_op jit(solution)/shard_map/ppermute | solution.py:100
  114.6 3.2 %collective-permute-done.13 = bf16[32,1152]{0,1:T(8,128)(2,1)S(1)} collective-permute-done((bf16[32,1152]{0,1:T(8,128)(2,1)S(1)}, bf16[32,1152]{0,1:T(8,128)(2,1)S(1)}, u32[]{:S(2)}, u32[]{:S(2)}) %collective-permute-start.13) | collective-permute-done | bytes 73760 | tf_op jit(solution)/shard_map/ppermute | solution.py:100
  117.9 0.4 pad_maximum_fusion.2
  118.5 0.7 pad_maximum_fusion.1
  119.2 12.3 %all-to-all-start = ((bf16[128,8,160]{0,2,1:T(8,128)(2,1)}), bf16[128,8,160]{0,2,1:T(8,128)(2,1)S(1)}, u32[]{:S(2)}, u32[]{:S(2)}) async-start(bf16[128,8,160]{0,2,1:T(8,128)(2,1)} %pad_maximum_fusion.1), calls=%async_computation | async-start | bytes 655360 | tf_op jit(solution)/shard_map/all_to_all | solution.py:130
  131.5 0.5 select_reduce_fusion.1
  132.1 0.5 fusion.8
  132.8 1.0 copy-done.3
  133.8 0.5 convolution_add_fusion.2
  134.3 8.8 %all-to-all-done = bf16[128,8,160]{0,2,1:T(8,128)(2,1)S(1)} async-done(((bf16[128,8,160]{0,2,1:T(8,128)(2,1)}), bf16[128,8,160]{0,2,1:T(8,128)(2,1)S(1)}, u32[]{:S(2)}, u32[]{:S(2)}) %all-to-all-start) | async-done | bytes 327712 | tf_op jit(solution)/shard_map/all_to_all | solution.py:130
  143.2 4.3 %select_reduce_fusion = f32[1024,1024]{1,0:T(8,128)S(1)} fusion(f32[1024,7]{0,1:T(8,128)S(1)} %slice_convert_fusion, s32[1024,7]{0,1:T(8,128)S(1)} %convert_add_fusion), kind=kLoop, calls=%fused_computation | loop fusion | flops 20971520 | bytes 4251648 | tf_op jit(solution)/shard_map/reduce_sum | solution.py:146
  147.5 2.5 %fusion = f32[1024,512]{1,0:T(8,128)S(1)} fusion(f32[1024,1024]{1,0:T(8,128)S(1)} %select_reduce_fusion, bf16[1024,1024]{1,0:T(8,128)(2,1)} %select_dynamic-update-slice_fusion, s32[]{:T(128)S(6)} %select_n.1135), kind=kOutput, calls=%fused_computation.6 | convolution fusion | flops 1077936128 | bytes 7340036 | tf_op jit(solution)/shard_map/dot_general | solution.py:152
  150.0 2.5 %convolution_add_fusion = f32[1024,512]{1,0:T(8,128)S(1)} fusion(f32[1024,512]{1,0:T(8,128)S(1)} %fusion, f32[1024,1024]{1,0:T(8,128)S(1)} %select_reduce_fusion, bf16[1024,1024]{1,0:T(8,128)(2,1)} %select_dynamic-update-slice_fusion, s32[]{:T(128)S(6)} %select_n.1135), kind=kOutput, calls=%fused_computation.8 | convolution fusion | flops 1075314688 | bytes 9437188 | tf_op jit(solution)/shard_map/dot_general | solution.py:150
  152.7 0.8 collective-permute-start.23
  153.6 0.7 collective-permute-start.25
  154.3 1.3 collective-permute-start.24
  155.6 1.3 convolution_add_fusion.1
  156.9 2.8 %fusion.5 = f32[128,1024]{1,0:T(8,128)} fusion(bf16[1024,1024]{1,0:T(8,128)(2,1)} %select_dynamic-update-slice_fusion, bf16[1024,160]{0,1:T(8,128)(2,1)S(1)} %copy_bitcast_fusion), kind=kOutput, calls=%fused_computation.30 | convolution fusion | flops 268435456 | bytes 2883584 | tf_op jit(solution)/shard_map/dot_general | solution.py:137
  159.7 10.4 %collective-permute-done.24 = f32[256,512]{1,0:T(8,128)S(1)} collective-permute-done((f32[256,512]{1,0:T(8,128)S(1)}, f32[256,512]{1,0:T(8,128)S(1)}, u32[]{:S(2)}, u32[]{:S(2)}) %collective-permute-start.24) | collective-permute-done | bytes 524320 | tf_op jit(solution)/shard_map/ppermute | solution.py:163
  170.1 1.0 add_add_fusion
  (93 shorter events, 5.4 us)
Async XLA Ops:
  0.6 12.4 %copy-start.1 = (bf16[128,1024]{1,0:T(8,128)(2,1)S(1)}, bf16[128,1024]{1,0:T(8,128)(2,1)}, u32[]{:S(2)}) copy-start(bf16[128,1024]{1,0:T(8,128)(2,1)} %param.8) | copy-start | bytes 786436
  0.6 18.8 %copy-start.18 = (f32[128]{0:T(128)S(1)}, f32[128]{0:T(128)}, u32[]{:S(2)}) copy-start(f32[128]{0:T(128)} %param.13) | copy-start | bytes 1540
  0.7 19.2 %copy-start.19 = (s32[128]{0:T(128)S(1)}, s32[128]{0:T(128)}, u32[]{:S(2)}) copy-start(s32[128]{0:T(128)} %param.12) | copy-start | bytes 1540
  0.7 19.4 %copy-start.17 = (s32[128,7]{0,1:T(8,128)S(1)}, s32[128,7]{0,1:T(8,128)}, u32[]{:S(2)}) copy-start(s32[128,7]{0,1:T(8,128)} %param.11) | copy-start | bytes 10756
  0.7 19.4 %copy-start.16 = (s32[128,7]{0,1:T(8,128)S(1)}, s32[128,7]{0,1:T(8,128)}, u32[]{:S(2)}) copy-start(s32[128,7]{0,1:T(8,128)} %param.10) | copy-start | bytes 10756
  0.7 12.3 %collective-permute-start.6 = (bf16[128,1024]{1,0:T(8,128)(2,1)}, bf16[128,1024]{1,0:T(8,128)(2,1)S(1)}, u32[]{:S(2)}, u32[]{:S(2)}) collective-permute-start(bf16[128,1024]{1,0:T(8,128)(2,1)} %param.8), channel_id=1, source_target_pairs={{0,4},{4,8},{8,12},{12,16},{16,20},{20,24},{24,28},{28,0},{1,5},{5... | collective-permute-start | bytes 786440 | tf_op jit(solution)/shard_map/ppermute | solution.py:46
  2.3 12.4 %collective-permute-start.5 = (bf16[128,1024]{1,0:T(8,128)(2,1)}, bf16[128,1024]{1,0:T(8,128)(2,1)S(1)}, u32[]{:S(2)}, u32[]{:S(2)}) collective-permute-start(bf16[128,1024]{1,0:T(8,128)(2,1)} %param.8), channel_id=1, source_target_pairs={{0,8},{4,12},{8,16},{12,20},{16,24},{20,28},{24,0},{28,4},{1,9},{5... | collective-permute-start | bytes 786440 | tf_op jit(solution)/shard_map/ppermute | solution.py:46
  3.8 30.6 %collective-permute-start.4 = (bf16[128,1024]{1,0:T(8,128)(2,1)}, bf16[128,1024]{1,0:T(8,128)(2,1)S(1)}, u32[]{:S(2)}, u32[]{:S(2)}) collective-permute-start(bf16[128,1024]{1,0:T(8,128)(2,1)} %param.8), channel_id=1, source_target_pairs={{0,12},{4,16},{8,20},{12,24},{16,28},{20,0},{24,4},{28,8},{1,13},{... | collective-permute-start | bytes 786440 | tf_op jit(solution)/shard_map/ppermute | solution.py:46
  6.4 28.4 %collective-permute-start.3 = (bf16[128,1024]{1,0:T(8,128)(2,1)}, bf16[128,1024]{1,0:T(8,128)(2,1)S(1)}, u32[]{:S(2)}, u32[]{:S(2)}) collective-permute-start(bf16[128,1024]{1,0:T(8,128)(2,1)} %param.8), channel_id=1, source_target_pairs={{0,16},{4,20},{8,24},{12,28},{16,0},{20,4},{24,8},{28,12},{1,17},{... | collective-permute-start | bytes 786440 | tf_op jit(solution)/shard_map/ppermute | solution.py:46
  7.6 27.7 %collective-permute-start.2 = (bf16[128,1024]{1,0:T(8,128)(2,1)}, bf16[128,1024]{1,0:T(8,128)(2,1)S(1)}, u32[]{:S(2)}, u32[]{:S(2)}) collective-permute-start(bf16[128,1024]{1,0:T(8,128)(2,1)} %param.8), channel_id=1, source_target_pairs={{0,20},{4,24},{8,28},{12,0},{16,4},{20,8},{24,12},{28,16},{1,21},{... | collective-permute-start | bytes 786440 | tf_op jit(solution)/shard_map/ppermute | solution.py:46
  13.0 23.4 %collective-permute-start.1 = (bf16[128,1024]{1,0:T(8,128)(2,1)S(1)}, bf16[128,1024]{1,0:T(8,128)(2,1)S(1)}, u32[]{:S(2)}, u32[]{:S(2)}) collective-permute-start(bf16[128,1024]{1,0:T(8,128)(2,1)S(1)} %copy-done.1), channel_id=1, source_target_pairs={{0,24},{4,28},{8,0},{12,4},{16,8},{20,12},{24,16},{28,20},{1,25},{... | collective-permute-start | bytes 786440 | tf_op jit(solution)/shard_map/ppermute | solution.py:46
  14.6 22.8 %collective-permute-start = (bf16[128,1024]{1,0:T(8,128)(2,1)S(1)}, bf16[128,1024]{1,0:T(8,128)(2,1)S(1)}, u32[]{:S(2)}, u32[]{:S(2)}) collective-permute-start(bf16[128,1024]{1,0:T(8,128)(2,1)S(1)} %copy-done.1), channel_id=1, source_target_pairs={{0,28},{4,0},{8,4},{12,8},{16,12},{20,16},{24,20},{28,24},{1,29},{... | collective-permute-start | bytes 786440 | tf_op jit(solution)/shard_map/ppermute | solution.py:46
  34.4 23.1 %collective-permute-start.9 = (bf16[256,1024]{1,0:T(8,128)(2,1)}, bf16[256,1024]{1,0:T(8,128)(2,1)S(1)}, u32[]{:S(2)}, u32[]{:S(2)}) collective-permute-start(bf16[256,1024]{1,0:T(8,128)(2,1)} %get-tuple-element.21), channel_id=1, source_target_pairs={{0,1},{1,2},{2,3},{3,0},{4,5},{5,6},{6,7},{7,4},{8,9},{9,10},{10,1... | collective-permute-start | bytes 1572872 | tf_op jit(solution)/shard_map/ppermute | solution.py:41
  34.7 22.9 %collective-permute-start.8 = (bf16[256,1024]{1,0:T(8,128)(2,1)}, bf16[256,1024]{1,0:T(8,128)(2,1)S(1)}, u32[]{:S(2)}, u32[]{:S(2)}) collective-permute-start(bf16[256,1024]{1,0:T(8,128)(2,1)} %get-tuple-element.22), channel_id=1, source_target_pairs={{0,2},{1,3},{2,0},{3,1},{4,6},{5,7},{6,4},{7,5},{8,10},{9,11},{10,... | collective-permute-start | bytes 1572872 | tf_op jit(solution)/shard_map/ppermute | solution.py:41
  35.3 24.4 %collective-permute-start.7 = (bf16[256,1024]{1,0:T(8,128)(2,1)S(1)}, bf16[256,1024]{1,0:T(8,128)(2,1)S(1)}, u32[]{:S(2)}, u32[]{:S(2)}) collective-permute-start(bf16[256,1024]{1,0:T(8,128)(2,1)S(1)} %get-tuple-element.23), channel_id=1, source_target_pairs={{0,3},{1,0},{2,1},{3,2},{4,7},{5,4},{6,5},{7,6},{8,11},{9,8},{10,9... | collective-permute-start | bytes 1572872 | tf_op jit(solution)/shard_map/ppermute | solution.py:41
  39.7 1.0 copy-start
  40.6 19.1 %copy-start.2 = (bf16[1024,1024]{1,0:T(8,128)(2,1)}, bf16[1024,1024]{1,0:T(8,128)(2,1)S(1)}, u32[]{:S(2)}) copy-start(bf16[1024,1024]{1,0:T(8,128)(2,1)S(1)} %select_dynamic-update-slice_fusion.8) | copy-start | bytes 6291460
  40.6 31.9 %collective-permute-start.22 = (bf16[128,1024]{1,0:T(8,128)(2,1)S(1)}, bf16[128,1024]{1,0:T(8,128)(2,1)S(1)}, u32[]{:S(2)}, u32[]{:S(2)}) collective-permute-start(bf16[128,1024]{1,0:T(8,128)(2,1)S(1)} %copy-done), channel_id=1, source_target_pairs={{0,4},{4,8},{8,12},{12,16},{16,20},{20,24},{24,28},{28,0},{1,5},{5... | collective-permute-start | bytes 786440 | tf_op jit(solution)/shard_map/ppermute | solution.py:52
  45.0 32.5 %collective-permute-start.21 = (bf16[128,1024]{1,0:T(8,128)(2,1)S(1)}, bf16[128,1024]{1,0:T(8,128)(2,1)S(1)}, u32[]{:S(2)}, u32[]{:S(2)}) collective-permute-start(bf16[128,1024]{1,0:T(8,128)(2,1)S(1)} %copy-done), channel_id=1, source_target_pairs={{0,8},{4,12},{8,16},{12,20},{16,24},{20,28},{24,0},{28,4},{1,9},{5... | collective-permute-start | bytes 786440 | tf_op jit(solution)/shard_map/ppermute | solution.py:52
  57.5 29.2 %collective-permute-start.20 = (bf16[128,1024]{1,0:T(8,128)(2,1)S(1)}, bf16[128,1024]{1,0:T(8,128)(2,1)S(1)}, u32[]{:S(2)}, u32[]{:S(2)}) collective-permute-start(bf16[128,1024]{1,0:T(8,128)(2,1)S(1)} %copy-done), channel_id=1, source_target_pairs={{0,12},{4,16},{8,20},{12,24},{16,28},{20,0},{24,4},{28,8},{1,13},{... | collective-permute-start | bytes 786440 | tf_op jit(solution)/shard_map/ppermute | solution.py:52
  57.6 29.3 %collective-permute-start.19 = (bf16[128,1024]{1,0:T(8,128)(2,1)S(1)}, bf16[128,1024]{1,0:T(8,128)(2,1)S(1)}, u32[]{:S(2)}, u32[]{:S(2)}) collective-permute-start(bf16[128,1024]{1,0:T(8,128)(2,1)S(1)} %copy-done), channel_id=1, source_target_pairs={{0,16},{4,20},{8,24},{12,28},{16,0},{20,4},{24,8},{28,12},{1,17},{... | collective-permute-start | bytes 786440 | tf_op jit(solution)/shard_map/ppermute | solution.py:52
  59.7 28.8 %collective-permute-start.18 = (bf16[128,1024]{1,0:T(8,128)(2,1)S(1)}, bf16[128,1024]{1,0:T(8,128)(2,1)S(1)}, u32[]{:S(2)}, u32[]{:S(2)}) collective-permute-start(bf16[128,1024]{1,0:T(8,128)(2,1)S(1)} %copy-done), channel_id=1, source_target_pairs={{0,20},{4,24},{8,28},{12,0},{16,4},{20,8},{24,12},{28,16},{1,21},{... | collective-permute-start | bytes 786440 | tf_op jit(solution)/shard_map/ppermute | solution.py:52
  68.6 0.8 copy-start.4
  68.6 1.0 copy-start.8
  68.6 1.1 copy-start.11
  68.7 2.6 %copy-start.6 = (bf16[256,1024]{1,0:T(8,128)(2,1)}, bf16[256,1024]{1,0:T(8,128)(2,1)S(1)}, u32[]{:S(2)}) copy-start(bf16[256,1024]{1,0:T(8,128)(2,1)S(1)} %get-tuple-element.15) | copy-start | bytes 1572868
  72.5 16.8 %collective-permute-start.17 = (bf16[128,1024]{1,0:T(8,128)(2,1)S(1)}, bf16[128,1024]{1,0:T(8,128)(2,1)S(1)}, u32[]{:S(2)}, u32[]{:S(2)}) collective-permute-start(bf16[128,1024]{1,0:T(8,128)(2,1)S(1)} %copy-done), channel_id=1, source_target_pairs={{0,24},{4,28},{8,0},{12,4},{16,8},{20,12},{24,16},{28,20},{1,25},{... | collective-permute-start | bytes 786440 | tf_op jit(solution)/shard_map/ppermute | solution.py:52
  77.6 14.5 %collective-permute-start.16 = (bf16[128,1024]{1,0:T(8,128)(2,1)S(1)}, bf16[128,1024]{1,0:T(8,128)(2,1)S(1)}, u32[]{:S(2)}, u32[]{:S(2)}) collective-permute-start(bf16[128,1024]{1,0:T(8,128)(2,1)S(1)} %copy-done), channel_id=1, source_target_pairs={{0,28},{4,0},{8,4},{12,8},{16,12},{20,16},{24,20},{28,24},{1,29},{... | collective-permute-start | bytes 786440 | tf_op jit(solution)/shard_map/ppermute | solution.py:52
  86.8 12.8 %collective-permute-start.10 = (f32[32,1152]{1,0:T(8,128)S(1)}, f32[32,1152]{1,0:T(8,128)S(1)}, u32[]{:S(2)}, u32[]{:S(2)}) collective-permute-start(f32[32,1152]{1,0:T(8,128)S(1)} %get-tuple-element.28), channel_id=1, source_target_pairs={{0,1},{1,2},{2,3},{3,0},{4,5},{5,6},{6,7},{7,4},{8,9},{9,10},{10,1... | collective-permute-start | bytes 442376 | tf_op jit(solution)/shard_map/ppermute | solution.py:76
  86.8 12.7 %collective-permute-start.12 = (f32[32,1152]{1,0:T(8,128)S(1)}, f32[32,1152]{1,0:T(8,128)S(1)}, u32[]{:S(2)}, u32[]{:S(2)}) collective-permute-start(f32[32,1152]{1,0:T(8,128)S(1)} %get-tuple-element.29), channel_id=1, source_target_pairs={{0,3},{1,0},{2,1},{3,2},{4,7},{5,4},{6,5},{7,6},{8,11},{9,8},{10,9... | collective-permute-start | bytes 442376 | tf_op jit(solution)/shard_map/ppermute | solution.py:76
  88.5 11.0 %collective-permute-start.11 = (f32[32,1152]{1,0:T(8,128)S(1)}, f32[32,1152]{1,0:T(8,128)S(1)}, u32[]{:S(2)}, u32[]{:S(2)}) collective-permute-start(f32[32,1152]{1,0:T(8,128)S(1)} %get-tuple-element.30), channel_id=1, source_target_pairs={{0,2},{1,3},{2,0},{3,1},{4,6},{5,7},{6,4},{7,5},{8,10},{9,11},{10,... | collective-permute-start | bytes 442376 | tf_op jit(solution)/shard_map/ppermute | solution.py:76
  101.3 9.9 %collective-permute-start.15 = (bf16[32,1152]{0,1:T(8,128)(2,1)S(1)}, bf16[32,1152]{0,1:T(8,128)(2,1)S(1)}, u32[]{:S(2)}, u32[]{:S(2)}) collective-permute-start(bf16[32,1152]{0,1:T(8,128)(2,1)S(1)} %copy.51), channel_id=1, source_target_pairs={{0,1},{1,2},{2,3},{3,0},{4,5},{5,6},{6,7},{7,4},{8,9},{9,10},{10,1... | collective-permute-start | bytes 221192 | tf_op jit(solution)/shard_map/ppermute | solution.py:100
  104.7 9.9 %collective-permute-start.14 = (bf16[32,1152]{0,1:T(8,128)(2,1)S(1)}, bf16[32,1152]{0,1:T(8,128)(2,1)S(1)}, u32[]{:S(2)}, u32[]{:S(2)}) collective-permute-start(bf16[32,1152]{0,1:T(8,128)(2,1)S(1)} %copy.51), channel_id=1, source_target_pairs={{0,2},{1,3},{2,0},{3,1},{4,6},{5,7},{6,4},{7,5},{8,10},{9,11},{10,... | collective-permute-start | bytes 221192 | tf_op jit(solution)/shard_map/ppermute | solution.py:100
  105.7 12.0 %collective-permute-start.13 = (bf16[32,1152]{0,1:T(8,128)(2,1)S(1)}, bf16[32,1152]{0,1:T(8,128)(2,1)S(1)}, u32[]{:S(2)}, u32[]{:S(2)}) collective-permute-start(bf16[32,1152]{0,1:T(8,128)(2,1)S(1)} %copy.51), channel_id=1, source_target_pairs={{0,3},{1,0},{2,1},{3,2},{4,7},{5,4},{6,5},{7,6},{8,11},{9,8},{10,9... | collective-permute-start | bytes 221192 | tf_op jit(solution)/shard_map/ppermute | solution.py:100
  117.9 14.1 %copy-start.5 = (bf16[256,1024]{1,0:T(8,128)(2,1)S(1)}, bf16[256,1024]{1,0:T(8,128)(2,1)}, u32[]{:S(2)}) copy-start(bf16[256,1024]{1,0:T(8,128)(2,1)} %copy-done.4) | copy-start | bytes 1572868
  117.9 14.1 %copy-start.7 = (bf16[256,1024]{1,0:T(8,128)(2,1)S(1)}, bf16[256,1024]{1,0:T(8,128)(2,1)}, u32[]{:S(2)}) copy-start(bf16[256,1024]{1,0:T(8,128)(2,1)} %copy-done.6) | copy-start | bytes 1572868
  117.9 14.1 %copy-start.9 = (bf16[256,1024]{1,0:T(8,128)(2,1)S(1)}, bf16[256,1024]{1,0:T(8,128)(2,1)}, u32[]{:S(2)}) copy-start(bf16[256,1024]{1,0:T(8,128)(2,1)} %copy-done.8) | copy-start | bytes 1572868
  118.3 13.7 %copy-start.12 = (bf16[256,1024]{1,0:T(8,128)(2,1)S(1)}, bf16[256,1024]{1,0:T(8,128)(2,1)}, u32[]{:S(2)}) copy-start(bf16[256,1024]{1,0:T(8,128)(2,1)} %copy-done.11) | copy-start | bytes 1572868
  119.2 23.9 %all-to-all-start = ((bf16[128,8,160]{0,2,1:T(8,128)(2,1)}), bf16[128,8,160]{0,2,1:T(8,128)(2,1)S(1)}, u32[]{:S(2)}, u32[]{:S(2)}) async-start(bf16[128,8,160]{0,2,1:T(8,128)(2,1)} %pad_maximum_fusion.1), calls=%async_computation | async-start | bytes 655360 | tf_op jit(solution)/shard_map/all_to_all | solution.py:130
  132.0 0.8 copy-start.14
  132.1 1.8 %copy-start.3 = (bf16[1024,1024]{1,0:T(8,128)(2,1)S(1)}, bf16[1024,1024]{1,0:T(8,128)(2,1)}, u32[]{:S(2)}) copy-start(bf16[1024,1024]{1,0:T(8,128)(2,1)} %copy-done.2) | copy-start | bytes 6291460
  152.6 3.0 %copy-start.10 = (bf16[256,1024]{1,0:T(8,128)(2,1)S(1)}, bf16[256,1024]{1,0:T(8,128)(2,1)}, u32[]{:S(2)}) copy-start(bf16[256,1024]{1,0:T(8,128)(2,1)} %copy-done.8) | copy-start | bytes 1572868
  152.6 3.0 %copy-start.13 = (bf16[256,1024]{1,0:T(8,128)(2,1)S(1)}, bf16[256,1024]{1,0:T(8,128)(2,1)}, u32[]{:S(2)}) copy-start(bf16[256,1024]{1,0:T(8,128)(2,1)} %copy-done.11) | copy-start | bytes 1572868
  152.6 3.0 %copy-start.15 = (f32[128,1024]{1,0:T(8,128)S(1)}, f32[128,1024]{1,0:T(8,128)}, u32[]{:S(2)}) copy-start(f32[128,1024]{1,0:T(8,128)} %copy-done.14) | copy-start | bytes 1572868
  152.7 7.0 %collective-permute-start.23 = (f32[256,512]{1,0:T(8,128)S(1)}, f32[256,512]{1,0:T(8,128)S(1)}, u32[]{:S(2)}, u32[]{:S(2)}) collective-permute-start(f32[256,512]{1,0:T(8,128)S(1)} %get-tuple-element.18), channel_id=1, source_target_pairs={{0,1},{4,5},{9,10},{13,14},{18,19},{22,23},{27,24},{31,28}} | collective-permute-start | bytes 1572872 | tf_op jit(solution)/shard_map/ppermute | solution.py:163
  153.6 6.1 %collective-permute-start.25 = (f32[256,512]{1,0:T(8,128)S(1)}, f32[256,512]{1,0:T(8,128)S(1)}, u32[]{:S(2)}, u32[]{:S(2)}) collective-permute-start(f32[256,512]{1,0:T(8,128)S(1)} %get-tuple-element.19), channel_id=1, source_target_pairs={{0,3},{4,7},{9,8},{13,12},{18,17},{22,21},{27,26},{31,30}} | collective-permute-start | bytes 1572872 | tf_op jit(solution)/shard_map/ppermute | solution.py:163
  154.3 15.8 %collective-permute-start.24 = (f32[256,512]{1,0:T(8,128)S(1)}, f32[256,512]{1,0:T(8,128)S(1)}, u32[]{:S(2)}, u32[]{:S(2)}) collective-permute-start(f32[256,512]{1,0:T(8,128)S(1)} %get-tuple-element.20), channel_id=1, source_target_pairs={{0,2},{4,6},{9,11},{13,15},{18,16},{22,20},{27,25},{31,29}} | collective-permute-start | bytes 1572872 | tf_op jit(solution)/shard_map/ppermute | solution.py:163

commit v8 on v7

--- a/solution.py
+++ b/solution.py
@@ -39,18 +39,18 @@
     for k in range(1, owner_count):
         shift = [(j, (j + k) % owner_count) for j in range(owner_count)]
         received.append(lax.ppermute(slice_of(k), "corpus", shift))
-    table_cols = gather_blocks(slice_of(0), received, owner_index, owner_count)
+    table_cols = jnp.concatenate([slice_of(0)] + received, axis=0)
     received = []
     for k in range(1, blk_count):
         shift = [(j, (j + k) % blk_count) for j in range(blk_count)]
         received.append(lax.ppermute(passages, "blk", shift))
-    all_passages = gather_blocks(passages, received, blk_index, blk_count)
+    all_passages = jnp.concatenate([passages] + received, axis=0)
     all_passages, later = lax.optimization_barrier((all_passages, queries))
     received = []
     for k in range(1, blk_count):
         shift = [(j, (j + k) % blk_count) for j in range(blk_count)]
         received.append(lax.ppermute(later, "blk", shift))
-    all_queries = gather_blocks(later, received, blk_index, blk_count)
+    all_queries = jnp.concatenate([later] + received, axis=0)
     ids = neg_owner * rows_shard + neg_row
     all_rows = all_passages.shape[0]
 
@@ -61,7 +61,8 @@
         queries, table_cols, (((1,), (1,)), ((), ())), preferred_element_type=jnp.float32
     )
     row_iota = jnp.arange(table_rows, dtype=jnp.int32)
-    picks = ids[:, :, None] == row_iota[None, None, :]
+    local_ids = ((owner_index - neg_owner) % owner_count) * rows_shard + neg_row
+    picks = local_ids[:, :, None] == row_iota[None, None, :]
     hard_logits = jnp.sum(jnp.where(picks, table_scores[:, None, :], 0.0), axis=2)
     negs = ids.shape[1]
     pad = jnp.zeros((q_rows, 128 - negs), jnp.float32)
@@ -78,6 +79,10 @@
     logits = summed[:, :all_rows] * factor
     hard_logits = summed[:, all_rows:all_rows + negs] * factor
     my_positive = lax.dynamic_slice_in_dim(positive, owner_index * share, share)
+    block_rows = all_rows // blk_count
+    my_positive = ((blk_index - my_positive // block_rows) % blk_count) * block_rows + (
+        my_positive % block_rows
+    )
     my_weight = lax.dynamic_slice_in_dim(loss_weight, owner_index * share, share)
     row_top = jnp.maximum(jnp.max(logits, axis=1), jnp.max(hard_logits, axis=1))
     log_total = row_top + jnp.log(
@@ -126,8 +131,13 @@
             jnp.broadcast_to(extra[:, None, :], (q_rows, blk_count, 32)),
         ],
         axis=2,
-    ).reshape(q_rows, blk_count * (cols_per + 32))
+    )
+    back = (blk_index - jnp.arange(blk_count, dtype=jnp.int32)) % blk_count
+    packed = jnp.take(packed, back, axis=1).reshape(q_rows, blk_count * (cols_per + 32))
     moved = lax.all_to_all(packed, "blk", split_axis=1, concat_axis=0, tiled=True)
+    moved = jnp.take(moved.reshape(blk_count, q_rows, cols_per + 32), back, axis=0).reshape(
+        blk_count * q_rows, cols_per + 32
+    )
     soft_cols = moved[:, :cols_per]
     all_hard = moved[:, cols_per:cols_per + negs]
     all_ids = (

time: 172 us -> 193 us (1.12)
  waiting for transfers between devices: 57 us -> 78.7 us
  local copies, waits for them, and re-layouts: 7.32 us -> 24.4 us
  other arithmetic: 22.4 us -> 11.5 us
  starting transfers between devices: 70.6 us -> 65.2 us
    unnamed x40 -> x54, local copies, waits for them, and re-layouts: 2.71 us -> 14 us
    unnamed x14 -> x0, other arithmetic: 9.96 us -> none
    ppermute x3, waiting for transfers between devices: 0.01 us -> 9.34 us  [per_device_body(): received.append(lax.ppermute(slice_of(k), 'corpus', shift))]
    ppermute x7, waiting for transfers between devices: 16 us -> 24.1 us  [per_device_body(): received.append(lax.ppermute(passages, 'blk', shift))]
    ppermute x7, starting transfers between devices: 16 us -> 23.2 us  [per_device_body(): received.append(lax.ppermute(passages, 'blk', shift))]
    ppermute x7, starting transfers between devices: 30.5 us -> 26.5 us  [per_device_body(): received.append(lax.ppermute(later, 'blk', shift))]
    all_to_all x1, starting transfers between devices: 12.3 us -> 8.66 us  [per_device_body(): lax.all_to_all(packed, 'blk', split_axis=1, concat_axis=0, tiled=True)]
    ppermute x3, waiting for transfers between devices: 0.01 us -> 3.29 us  [per_device_body(): got = lax.ppermute(chunk_of(k), 'corpus', shift)]
  transfers between devices with their start and end apart: 27 -> 27, of which waited for: 12 -> 13; matrix products, arithmetic and copies ran while one was open for 15% -> 19% of each run, Pallas kernels for 0% -> 0%
where the time goes in v8:
time: 193 us; the launch traced here: 192 us
  waiting for transfers between devices  78.7 us (41%)
  starting transfers between devices  65.2 us (34%)
  local copies, waits for them, and re-layouts  24.4 us (13%)
  other arithmetic  11.5 us (6%)
  matrix products  10.7 us (6%)
    ppermute x7, starting transfers between devices, per_device_body(): received.append(lax.ppermute(later, 'blk', shift))  26.5 us
    ppermute x7, waiting for transfers between devices, per_device_body(): received.append(lax.ppermute(passages, 'blk', shift))  24.1 us
    ppermute x7, starting transfers between devices, per_device_body(): received.append(lax.ppermute(passages, 'blk', shift))  23.2 us
    unnamed x54, local copies, waits for them, and re-layouts  14 us
    ppermute x7, waiting for transfers between devices, per_device_body(): received.append(lax.ppermute(later, 'blk', shift))  12.6 us
    ppermute x3, waiting for transfers between devices, per_device_body(): table_grad = table_grad + lax.ppermute(sent, ('blk', 'corpus'), pairs)  12 us
    ppermute x3, waiting for transfers between devices, per_device_body(): received.append(lax.ppermute(grads_part, 'corpus', shift))  9.99 us
    ppermute x3, waiting for transfers between devices, per_device_body(): received.append(lax.ppermute(slice_of(k), 'corpus', shift))  9.34 us
  transfers between devices with their start and end apart: 27, of which 13 were waited for; matrix products, arithmetic and copies ran while one was open for 19% of the time, Pallas kernels for 0%

profile of v8, /device:TPU:2, one launch (start us, length us, event | category | flops | bytes accessed | tf_op | source)
XLA Modules:
  0.0 191.7 jit_solution(16611251141115454076)
XLA Ops:
  0.6 3.7 %collective-permute-start.5 = (bf16[128,1024]{1,0:T(8,128)(2,1)}, bf16[128,1024]{1,0:T(8,128)(2,1)S(1)}, u32[]{:S(2)}, u32[]{:S(2)}) collective-permute-start(bf16[128,1024]{1,0:T(8,128)(2,1)} %param.8), channel_id=1, source_target_pairs={{0,24},{4,28},{8,0},{12,4},{16,8},{20,12},{24,16},{28,20},{1,25},{... | collective-permute-start | bytes 786440 | tf_op jit(solution)/shard_map/ppermute | solution.py:46
  4.7 2.5 %collective-permute-start.2 = (bf16[128,1024]{1,0:T(8,128)(2,1)}, bf16[128,1024]{1,0:T(8,128)(2,1)}, u32[]{:S(2)}, u32[]{:S(2)}) collective-permute-start(bf16[128,1024]{1,0:T(8,128)(2,1)} %param.8), channel_id=1, source_target_pairs={{0,12},{4,16},{8,20},{12,24},{16,28},{20,0},{24,4},{28,8},{1,13},{... | collective-permute-start | bytes 786440 | tf_op jit(solution)/shard_map/ppermute | solution.py:46
  7.2 2.4 %collective-permute-start = (bf16[128,1024]{1,0:T(8,128)(2,1)}, bf16[128,1024]{1,0:T(8,128)(2,1)}, u32[]{:S(2)}, u32[]{:S(2)}) collective-permute-start(bf16[128,1024]{1,0:T(8,128)(2,1)} %param.8), channel_id=1, source_target_pairs={{0,4},{4,8},{8,12},{12,16},{16,20},{20,24},{24,28},{28,0},{1,5},{5... | collective-permute-start | bytes 786440 | tf_op jit(solution)/shard_map/ppermute | solution.py:46
  9.7 1.0 constant_dynamic-update-slice_fusion.7
  10.7 0.6 broadcast_bitcast_fusion
  11.3 0.8 fusion.26
  12.1 2.7 %constant_dynamic-slice_fusion.9 = (bf16[256,1024]{1,0:T(8,128)(2,1)S(1)}, bf16[256,1024]{1,0:T(8,128)(2,1)}, bf16[256,1024]{1,0:T(8,128)(2,1)}, bf16[256,1024]{1,0:T(8,128)(2,1)}) fusion(bf16[256,4096]{1,0:T(8,128)(2,1)} %param.9, s32[]{:T(128)S(6)} %select_n.265, s32[]{:T(128)S(6)} %select_n.267, s32[]{:T(128)S(6)} %select_n.271, s32[]{:T(128)S(6)} %select_n.269), kind=kLoop, calls=%fused_computation.82 | loop fusion | bytes 4194320 | tf_op jit(solution)/shard_map/dynamic_slice | solution.py:35
  14.9 0.6 fusion.17
  15.5 0.7 dynamic-slice_multiply_fusion
  16.2 0.6 pad.5.clone
  16.8 17.8 %collective-permute-done = bf16[128,1024]{1,0:T(8,128)(2,1)} collective-permute-done((bf16[128,1024]{1,0:T(8,128)(2,1)}, bf16[128,1024]{1,0:T(8,128)(2,1)}, u32[]{:S(2)}, u32[]{:S(2)}) %collective-permute-start) | collective-permute-done | bytes 262176 | tf_op jit(solution)/shard_map/ppermute | solution.py:46
  34.6 13.7 %collective-permute-start.3 = (bf16[128,1024]{1,0:T(8,128)(2,1)S(1)}, bf16[128,1024]{1,0:T(8,128)(2,1)S(1)}, u32[]{:S(2)}, u32[]{:S(2)}) collective-permute-start(bf16[128,1024]{1,0:T(8,128)(2,1)S(1)} %copy-done.5), channel_id=1, source_target_pairs={{0,16},{4,20},{8,24},{12,28},{16,0},{20,4},{24,8},{28,12},{1,17},{... | collective-permute-start | bytes 786440 | tf_op jit(solution)/shard_map/ppermute | solution.py:46
  48.3 1.0 constant_dynamic-update-slice_fusion.6
  49.8 1.0 constant_dynamic-update-slice_fusion.5
  50.8 1.0 constant_dynamic-update-slice_fusion.4
  51.8 3.7 %collective-permute-done.3 = bf16[128,1024]{1,0:T(8,128)(2,1)S(1)} collective-permute-done((bf16[128,1024]{1,0:T(8,128)(2,1)S(1)}, bf16[128,1024]{1,0:T(8,128)(2,1)S(1)}, u32[]{:S(2)}, u32[]{:S(2)}) %collective-permute-start.3) | collective-permute-done | bytes 262176 | tf_op jit(solution)/shard_map/ppermute | solution.py:46
  55.5 0.6 collective-permute-start.8
  56.1 1.0 constant_dynamic-update-slice_fusion.2
  57.1 2.6 %collective-permute-done.6 = bf16[128,1024]{1,0:T(8,128)(2,1)S(1)} collective-permute-done((bf16[128,1024]{1,0:T(8,128)(2,1)S(1)}, bf16[128,1024]{1,0:T(8,128)(2,1)S(1)}, u32[]{:S(2)}, u32[]{:S(2)}) %collective-permute-start.6) | collective-permute-done | bytes 262176 | tf_op jit(solution)/shard_map/ppermute | solution.py:46
  59.7 5.2 %collective-permute-start.22 = (bf16[128,1024]{1,0:T(8,128)(2,1)S(1)}, bf16[128,1024]{1,0:T(8,128)(2,1)}, u32[]{:S(2)}, u32[]{:S(2)}) collective-permute-start(bf16[128,1024]{1,0:T(8,128)(2,1)S(1)} %copy-done.1), channel_id=1, source_target_pairs={{0,28},{4,0},{8,4},{12,8},{16,12},{20,16},{24,20},{28,24},{1,29},{... | collective-permute-start | bytes 786440 | tf_op jit(solution)/shard_map/ppermute | solution.py:52
  64.9 0.7 constant_dynamic-update-slice_fusion.15
  65.6 0.8 convolution_bitcast_fusion.1
  66.6 1.5 collective-permute-done.9
  68.1 0.6 collective-permute-start.17
  68.7 7.8 %collective-permute-done.8 = bf16[256,1024]{1,0:T(8,128)(2,1)S(1)} collective-permute-done((bf16[256,1024]{1,0:T(8,128)(2,1)}, bf16[256,1024]{1,0:T(8,128)(2,1)S(1)}, u32[]{:S(2)}, u32[]{:S(2)}) %collective-permute-start.8) | collective-permute-done | bytes 524320 | tf_op jit(solution)/shard_map/ppermute | solution.py:41
  76.5 1.6 collective-permute-start.16
  78.1 1.5 convolution_bitcast_fusion
  79.6 1.2 copy.69
  80.8 0.6 select_reduce_fusion.2
  81.5 0.6 broadcast_in_dim.97
  82.2 1.0 concatenate.26
  83.2 4.8 %collective-permute-done.16 = bf16[128,1024]{1,0:T(8,128)(2,1)} collective-permute-done((bf16[128,1024]{1,0:T(8,128)(2,1)S(1)}, bf16[128,1024]{1,0:T(8,128)(2,1)}, u32[]{:S(2)}, u32[]{:S(2)}) %collective-permute-start.16) | collective-permute-done | bytes 262176 | tf_op jit(solution)/shard_map/ppermute | solution.py:52
  88.1 19.1 %collective-permute-start.19 = (bf16[128,1024]{1,0:T(8,128)(2,1)S(1)}, bf16[128,1024]{1,0:T(8,128)(2,1)S(1)}, u32[]{:S(2)}, u32[]{:S(2)}) collective-permute-start(bf16[128,1024]{1,0:T(8,128)(2,1)S(1)} %copy-done.1), channel_id=1, source_target_pairs={{0,16},{4,20},{8,24},{12,28},{16,0},{20,4},{24,8},{28,12},{1,17},{... | collective-permute-start | bytes 786440 | tf_op jit(solution)/shard_map/ppermute | solution.py:52
  107.1 1.7 constant_dynamic-update-slice_fusion.14
  108.8 1.7 constant_dynamic-update-slice_fusion.13
  110.5 1.7 constant_dynamic-update-slice_fusion.12
  112.2 7.7 %collective-permute-done.19 = bf16[128,1024]{1,0:T(8,128)(2,1)S(1)} collective-permute-done((bf16[128,1024]{1,0:T(8,128)(2,1)S(1)}, bf16[128,1024]{1,0:T(8,128)(2,1)S(1)}, u32[]{:S(2)}, u32[]{:S(2)}) %collective-permute-start.19) | collective-permute-done | bytes 262176 | tf_op jit(solution)/shard_map/ppermute | solution.py:52
  119.9 0.7 constant_dynamic-update-slice_fusion.11
  121.2 0.7 constant_dynamic-update-slice_fusion.10
  121.9 1.7 constant_dynamic-update-slice_fusion.9
  123.6 3.3 %collective-permute-done.11 = f32[32,1152]{1,0:T(8,128)S(1)} collective-permute-done((f32[32,1152]{1,0:T(8,128)S(1)}, f32[32,1152]{1,0:T(8,128)S(1)}, u32[]{:S(2)}, u32[]{:S(2)}) %collective-permute-start.11) | collective-permute-done | bytes 147488 | tf_op jit(solution)/shard_map/ppermute | solution.py:77
  128.7 1.4 collective-permute-start.14
  130.1 1.4 collective-permute-start.13
  131.5 1.7 constant_dynamic-update-slice_fusion.8
  133.2 4.2 %collective-permute-done.15 = bf16[32,1152]{0,1:T(8,128)(2,1)S(1)} collective-permute-done((bf16[32,1152]{0,1:T(8,128)(2,1)S(1)}, bf16[32,1152]{0,1:T(8,128)(2,1)S(1)}, u32[]{:S(2)}, u32[]{:S(2)}) %collective-permute-start.15) | collective-permute-done | bytes 73760 | tf_op jit(solution)/shard_map/ppermute | solution.py:105
  137.3 1.3 collective-permute-done.14
  138.7 4.5 %collective-permute-done.13 = bf16[32,1152]{0,1:T(8,128)(2,1)S(1)} collective-permute-done((bf16[32,1152]{0,1:T(8,128)(2,1)S(1)}, bf16[32,1152]{0,1:T(8,128)(2,1)S(1)}, u32[]{:S(2)}, u32[]{:S(2)}) %collective-permute-start.13) | collective-permute-done | bytes 73760 | tf_op jit(solution)/shard_map/ppermute | solution.py:105
  144.0 0.6 gather_fusion
  144.6 0.8 select_bitcast_fusion
  145.4 8.7 %all-to-all-start = ((bf16[128,8,160]{0,2,1:T(8,128)(2,1)}), bf16[128,8,160]{0,2,1:T(8,128)(2,1)S(1)}, u32[]{:S(2)}, u32[]{:S(2)}) async-start(bf16[128,8,160]{0,2,1:T(8,128)(2,1)} %select_bitcast_fusion), calls=%async_computation | async-start | bytes 655360 | tf_op jit(solution)/shard_map/all_to_all | solution.py:137
  154.6 2.0 %fusion.8 = f32[128,1024]{1,0:T(8,128)S(1)} fusion(f32[128,1024]{1,0:T(8,128)S(1)} %select_reduce_fusion.1, bf16[256,1024]{1,0:T(8,128)(2,1)} %copy-done.15, bf16[256,1024]{1,0:T(8,128)(2,1)} %copy-done.17, bf16[256,1024]{1,0:T(8,128)(2,1)} %copy-done.13, bf16[256,1024]{1,0:T(8,128)(2,1)} %copy-done.3), kind=kOutput, calls=%fused_computation.34 | convolution fusion | flops 276955136 | bytes 3145728 | tf_op jit(solution)/shard_map/dot_general | solution.py:114
  156.6 1.3 convolution_add_fusion.2
  157.9 7.4 %all-to-all-done = bf16[128,8,160]{0,2,1:T(8,128)(2,1)S(1)} async-done(((bf16[128,8,160]{0,2,1:T(8,128)(2,1)}), bf16[128,8,160]{0,2,1:T(8,128)(2,1)S(1)}, u32[]{:S(2)}, u32[]{:S(2)}) %all-to-all-start) | async-done | bytes 327712 | tf_op jit(solution)/shard_map/all_to_all | solution.py:137
  165.3 0.6 gather_fusion.1
  166.0 4.3 %select_reduce_fusion = f32[1024,1024]{1,0:T(8,128)S(1)} fusion(f32[1024,7]{0,1:T(8,128)S(1)} %slice_convert_fusion, s32[1024,7]{0,1:T(8,128)S(1)} %convert_add_fusion), kind=kLoop, calls=%fused_computation.2 | loop fusion | flops 20971520 | bytes 4251648 | tf_op jit(solution)/shard_map/reduce_sum | solution.py:156
  170.4 1.3 fusion
  171.7 1.3 convolution_add_fusion
  173.2 0.8 collective-permute-start.23
  174.0 0.7 collective-permute-start.25
  174.7 1.3 collective-permute-start.24
  176.1 1.3 convolution_add_fusion.1
  177.3 1.2 fusion.5
  178.6 12.0 %collective-permute-done.24 = f32[256,512]{1,0:T(8,128)S(1)} collective-permute-done((f32[256,512]{1,0:T(8,128)S(1)}, f32[256,512]{1,0:T(8,128)S(1)}, u32[]{:S(2)}, u32[]{:S(2)}) %collective-permute-start.24) | collective-permute-done | bytes 524320 | tf_op jit(solution)/shard_map/ppermute | solution.py:173
  190.6 1.0 add_add_fusion
  (99 shorter events, 5.2 us)
Async XLA Ops:
  0.6 56.4 %collective-permute-start.5 = (bf16[128,1024]{1,0:T(8,128)(2,1)}, bf16[128,1024]{1,0:T(8,128)(2,1)S(1)}, u32[]{:S(2)}, u32[]{:S(2)}) collective-permute-start(bf16[128,1024]{1,0:T(8,128)(2,1)} %param.8), channel_id=1, source_target_pairs={{0,24},{4,28},{8,0},{12,4},{16,8},{20,12},{24,16},{28,20},{1,25},{... | collective-permute-start | bytes 786440 | tf_op jit(solution)/shard_map/ppermute | solution.py:46
  4.3 51.2 %collective-permute-start.4 = (bf16[128,1024]{1,0:T(8,128)(2,1)}, bf16[128,1024]{1,0:T(8,128)(2,1)}, u32[]{:S(2)}, u32[]{:S(2)}) collective-permute-start(bf16[128,1024]{1,0:T(8,128)(2,1)} %param.8), channel_id=1, source_target_pairs={{0,20},{4,24},{8,28},{12,0},{16,4},{20,8},{24,12},{28,16},{1,21},{... | collective-permute-start | bytes 786440 | tf_op jit(solution)/shard_map/ppermute | solution.py:46
  4.7 46.1 %collective-permute-start.2 = (bf16[128,1024]{1,0:T(8,128)(2,1)}, bf16[128,1024]{1,0:T(8,128)(2,1)}, u32[]{:S(2)}, u32[]{:S(2)}) collective-permute-start(bf16[128,1024]{1,0:T(8,128)(2,1)} %param.8), channel_id=1, source_target_pairs={{0,12},{4,16},{8,20},{12,24},{16,28},{20,0},{24,4},{28,8},{1,13},{... | collective-permute-start | bytes 786440 | tf_op jit(solution)/shard_map/ppermute | solution.py:46
  7.2 42.1 %collective-permute-start.1 = (bf16[128,1024]{1,0:T(8,128)(2,1)}, bf16[128,1024]{1,0:T(8,128)(2,1)}, u32[]{:S(2)}, u32[]{:S(2)}) collective-permute-start(bf16[128,1024]{1,0:T(8,128)(2,1)} %param.8), channel_id=1, source_target_pairs={{0,8},{4,12},{8,16},{12,20},{16,24},{20,28},{24,0},{28,4},{1,9},{5... | collective-permute-start | bytes 786440 | tf_op jit(solution)/shard_map/ppermute | solution.py:46
  7.2 27.4 %collective-permute-start = (bf16[128,1024]{1,0:T(8,128)(2,1)}, bf16[128,1024]{1,0:T(8,128)(2,1)}, u32[]{:S(2)}, u32[]{:S(2)}) collective-permute-start(bf16[128,1024]{1,0:T(8,128)(2,1)} %param.8), channel_id=1, source_target_pairs={{0,4},{4,8},{8,12},{12,16},{16,20},{20,24},{24,28},{28,0},{1,5},{5... | collective-permute-start | bytes 786440 | tf_op jit(solution)/shard_map/ppermute | solution.py:46
  9.6 2.4 %copy-start.11 = (pred[8]{0:T(512)(128)(4,1)}, pred[8]{0:T(512)(128)(4,1)S(1)}, u32[]{:S(2)}) copy-start(pred[8]{0:T(512)(128)(4,1)S(1)} %compare_and_fusion) | copy-start | bytes 28
  12.1 2.8 %copy-start.9 = (s32[128]{0:T(128)S(1)}, s32[128]{0:T(128)}, u32[]{:S(2)}) copy-start(s32[128]{0:T(128)} %param.12) | copy-start | bytes 1540
  12.1 3.4 %copy-start.19 = (f32[128]{0:T(128)S(1)}, f32[128]{0:T(128)}, u32[]{:S(2)}) copy-start(f32[128]{0:T(128)} %param.13) | copy-start | bytes 1540
  12.1 22.5 %copy-start.5 = (bf16[128,1024]{1,0:T(8,128)(2,1)S(1)}, bf16[128,1024]{1,0:T(8,128)(2,1)}, u32[]{:S(2)}) copy-start(bf16[128,1024]{1,0:T(8,128)(2,1)} %param.8) | copy-start | bytes 786436
  14.9 63.2 %copy-start.3 = (bf16[256,1024]{1,0:T(8,128)(2,1)}, bf16[256,1024]{1,0:T(8,128)(2,1)S(1)}, u32[]{:S(2)}) copy-start(bf16[256,1024]{1,0:T(8,128)(2,1)S(1)} %get-tuple-element.17) | copy-start | bytes 1572868
  14.9 44.8 %copy-start.1 = (bf16[128,1024]{1,0:T(8,128)(2,1)S(1)}, bf16[128,1024]{1,0:T(8,128)(2,1)}, u32[]{:S(2)}) copy-start(bf16[128,1024]{1,0:T(8,128)(2,1)} %param.7) | copy-start | bytes 786436
  34.6 20.9 %collective-permute-start.3 = (bf16[128,1024]{1,0:T(8,128)(2,1)S(1)}, bf16[128,1024]{1,0:T(8,128)(2,1)S(1)}, u32[]{:S(2)}, u32[]{:S(2)}) collective-permute-start(bf16[128,1024]{1,0:T(8,128)(2,1)S(1)} %copy-done.5), channel_id=1, source_target_pairs={{0,16},{4,20},{8,24},{12,28},{16,0},{20,4},{24,8},{28,12},{1,17},{... | collective-permute-start | bytes 786440 | tf_op jit(solution)/shard_map/ppermute | solution.py:46
  49.3 10.4 %collective-permute-start.6 = (bf16[128,1024]{1,0:T(8,128)(2,1)S(1)}, bf16[128,1024]{1,0:T(8,128)(2,1)S(1)}, u32[]{:S(2)}, u32[]{:S(2)}) collective-permute-start(bf16[128,1024]{1,0:T(8,128)(2,1)S(1)} %copy-done.5), channel_id=1, source_target_pairs={{0,28},{4,0},{8,4},{12,8},{16,12},{20,16},{24,20},{28,24},{1,29},{... | collective-permute-start | bytes 786440 | tf_op jit(solution)/shard_map/ppermute | solution.py:46
  50.8 15.7 %collective-permute-start.7 = (bf16[256,1024]{1,0:T(8,128)(2,1)}, bf16[256,1024]{1,0:T(8,128)(2,1)S(1)}, u32[]{:S(2)}, u32[]{:S(2)}) collective-permute-start(bf16[256,1024]{1,0:T(8,128)(2,1)} %get-tuple-element.18), channel_id=1, source_target_pairs={{0,1},{1,2},{2,3},{3,0},{4,5},{5,6},{6,7},{7,4},{8,9},{9,10},{10,1... | collective-permute-start | bytes 1572872 | tf_op jit(solution)/shard_map/ppermute | solution.py:41
  55.5 12.6 %collective-permute-start.9 = (bf16[256,1024]{1,0:T(8,128)(2,1)}, bf16[256,1024]{1,0:T(8,128)(2,1)S(1)}, u32[]{:S(2)}, u32[]{:S(2)}) collective-permute-start(bf16[256,1024]{1,0:T(8,128)(2,1)} %get-tuple-element.19), channel_id=1, source_target_pairs={{0,3},{1,0},{2,1},{3,2},{4,7},{5,4},{6,5},{7,6},{8,11},{9,8},{10,9... | collective-permute-start | bytes 1572872 | tf_op jit(solution)/shard_map/ppermute | solution.py:41
  55.5 21.0 %collective-permute-start.8 = (bf16[256,1024]{1,0:T(8,128)(2,1)}, bf16[256,1024]{1,0:T(8,128)(2,1)S(1)}, u32[]{:S(2)}, u32[]{:S(2)}) collective-permute-start(bf16[256,1024]{1,0:T(8,128)(2,1)} %get-tuple-element.20), channel_id=1, source_target_pairs={{0,2},{1,3},{2,0},{3,1},{4,6},{5,7},{6,4},{7,5},{8,10},{9,11},{10,... | collective-permute-start | bytes 1572872 | tf_op jit(solution)/shard_map/ppermute | solution.py:41
  59.7 71.8 %collective-permute-start.22 = (bf16[128,1024]{1,0:T(8,128)(2,1)S(1)}, bf16[128,1024]{1,0:T(8,128)(2,1)}, u32[]{:S(2)}, u32[]{:S(2)}) collective-permute-start(bf16[128,1024]{1,0:T(8,128)(2,1)S(1)} %copy-done.1), channel_id=1, source_target_pairs={{0,28},{4,0},{8,4},{12,8},{16,12},{20,16},{24,20},{28,24},{1,29},{... | collective-permute-start | bytes 786440 | tf_op jit(solution)/shard_map/ppermute | solution.py:52
  64.9 57.0 %collective-permute-start.21 = (bf16[128,1024]{1,0:T(8,128)(2,1)S(1)}, bf16[128,1024]{1,0:T(8,128)(2,1)}, u32[]{:S(2)}, u32[]{:S(2)}) collective-permute-start(bf16[128,1024]{1,0:T(8,128)(2,1)S(1)} %copy-done.1), channel_id=1, source_target_pairs={{0,24},{4,28},{8,0},{12,4},{16,8},{20,12},{24,16},{28,20},{1,25},{... | collective-permute-start | bytes 786440 | tf_op jit(solution)/shard_map/ppermute | solution.py:52
  66.5 11.6 %copy-start.13 = (bf16[256,1024]{1,0:T(8,128)(2,1)}, bf16[256,1024]{1,0:T(8,128)(2,1)S(1)}, u32[]{:S(2)}) copy-start(bf16[256,1024]{1,0:T(8,128)(2,1)S(1)} %collective-permute-done.7) | copy-start | bytes 1572868
  66.5 44.0 %collective-permute-start.18 = (bf16[128,1024]{1,0:T(8,128)(2,1)S(1)}, bf16[128,1024]{1,0:T(8,128)(2,1)}, u32[]{:S(2)}, u32[]{:S(2)}) collective-permute-start(bf16[128,1024]{1,0:T(8,128)(2,1)S(1)} %copy-done.1), channel_id=1, source_target_pairs={{0,12},{4,16},{8,20},{12,24},{16,28},{20,0},{24,4},{28,8},{1,13},{... | collective-permute-start | bytes 786440 | tf_op jit(solution)/shard_map/ppermute | solution.py:52
  68.1 10.0 %copy-start.15 = (bf16[256,1024]{1,0:T(8,128)(2,1)}, bf16[256,1024]{1,0:T(8,128)(2,1)S(1)}, u32[]{:S(2)}) copy-start(bf16[256,1024]{1,0:T(8,128)(2,1)S(1)} %collective-permute-done.9) | copy-start | bytes 1572868
  68.1 40.7 %collective-permute-start.17 = (bf16[128,1024]{1,0:T(8,128)(2,1)S(1)}, bf16[128,1024]{1,0:T(8,128)(2,1)}, u32[]{:S(2)}, u32[]{:S(2)}) collective-permute-start(bf16[128,1024]{1,0:T(8,128)(2,1)S(1)} %copy-done.1), channel_id=1, source_target_pairs={{0,8},{4,12},{8,16},{12,20},{16,24},{20,28},{24,0},{28,4},{1,9},{5... | collective-permute-start | bytes 786440 | tf_op jit(solution)/shard_map/ppermute | solution.py:52
  76.5 1.6 copy-start.17
  76.5 11.6 %collective-permute-start.16 = (bf16[128,1024]{1,0:T(8,128)(2,1)S(1)}, bf16[128,1024]{1,0:T(8,128)(2,1)}, u32[]{:S(2)}, u32[]{:S(2)}) collective-permute-start(bf16[128,1024]{1,0:T(8,128)(2,1)S(1)} %copy-done.1), channel_id=1, source_target_pairs={{0,4},{4,8},{8,12},{12,16},{16,20},{20,24},{24,28},{28,0},{1,5},{5... | collective-permute-start | bytes 786440 | tf_op jit(solution)/shard_map/ppermute | solution.py:52
  83.2 44.1 %copy-start.6 = (s32[32]{0:T(128)S(1)}, s32[32]{0:T(128)}, u32[]{:S(2)}) copy-start(s32[32]{0:T(128)} %fusion.17) | copy-start | bytes 388
  83.2 44.9 %copy-start.7 = (f32[32]{0:T(128)S(1)}, f32[32]{0:T(128)}, u32[]{:S(2)}) copy-start(f32[32]{0:T(128)} %dynamic-slice_multiply_fusion) | copy-start | bytes 388
  88.1 31.8 %collective-permute-start.19 = (bf16[128,1024]{1,0:T(8,128)(2,1)S(1)}, bf16[128,1024]{1,0:T(8,128)(2,1)S(1)}, u32[]{:S(2)}, u32[]{:S(2)}) collective-permute-start(bf16[128,1024]{1,0:T(8,128)(2,1)S(1)} %copy-done.1), channel_id=1, source_target_pairs={{0,16},{4,20},{8,24},{12,28},{16,0},{20,4},{24,8},{28,12},{1,17},{... | collective-permute-start | bytes 786440 | tf_op jit(solution)/shard_map/ppermute | solution.py:52
  108.8 11.8 %collective-permute-start.20 = (bf16[128,1024]{1,0:T(8,128)(2,1)S(1)}, bf16[128,1024]{1,0:T(8,128)(2,1)S(1)}, u32[]{:S(2)}, u32[]{:S(2)}) collective-permute-start(bf16[128,1024]{1,0:T(8,128)(2,1)S(1)} %copy-done.1), channel_id=1, source_target_pairs={{0,20},{4,24},{8,28},{12,0},{16,4},{20,8},{24,12},{28,16},{1,21},{... | collective-permute-start | bytes 786440 | tf_op jit(solution)/shard_map/ppermute | solution.py:52
  110.5 13.1 %collective-permute-start.10 = (f32[32,1152]{1,0:T(8,128)S(1)}, f32[32,1152]{1,0:T(8,128)S(1)}, u32[]{:S(2)}, u32[]{:S(2)}) collective-permute-start(f32[32,1152]{1,0:T(8,128)S(1)} %get-tuple-element.25), channel_id=1, source_target_pairs={{0,1},{1,2},{2,3},{3,0},{4,5},{5,6},{6,7},{7,4},{8,9},{9,10},{10,1... | collective-permute-start | bytes 442376 | tf_op jit(solution)/shard_map/ppermute | solution.py:77
  119.9 3.7 %collective-permute-start.12 = (f32[32,1152]{1,0:T(8,128)S(1)}, f32[32,1152]{1,0:T(8,128)S(1)}, u32[]{:S(2)}, u32[]{:S(2)}) collective-permute-start(f32[32,1152]{1,0:T(8,128)S(1)} %get-tuple-element.26), channel_id=1, source_target_pairs={{0,3},{1,0},{2,1},{3,2},{4,7},{5,4},{6,5},{7,6},{8,11},{9,8},{10,9... | collective-permute-start | bytes 442376 | tf_op jit(solution)/shard_map/ppermute | solution.py:77
  120.6 6.3 %collective-permute-start.11 = (f32[32,1152]{1,0:T(8,128)S(1)}, f32[32,1152]{1,0:T(8,128)S(1)}, u32[]{:S(2)}, u32[]{:S(2)}) collective-permute-start(f32[32,1152]{1,0:T(8,128)S(1)} %get-tuple-element.27), channel_id=1, source_target_pairs={{0,2},{1,3},{2,0},{3,1},{4,6},{5,7},{6,4},{7,5},{8,10},{9,11},{10,... | collective-permute-start | bytes 442376 | tf_op jit(solution)/shard_map/ppermute | solution.py:77
  128.6 8.7 %collective-permute-start.15 = (bf16[32,1152]{0,1:T(8,128)(2,1)S(1)}, bf16[32,1152]{0,1:T(8,128)(2,1)S(1)}, u32[]{:S(2)}, u32[]{:S(2)}) collective-permute-start(bf16[32,1152]{0,1:T(8,128)(2,1)S(1)} %copy.71), channel_id=1, source_target_pairs={{0,1},{1,2},{2,3},{3,0},{4,5},{5,6},{6,7},{7,4},{8,9},{9,10},{10,1... | collective-permute-start | bytes 221192 | tf_op jit(solution)/shard_map/ppermute | solution.py:105
  128.7 9.9 %collective-permute-start.14 = (bf16[32,1152]{0,1:T(8,128)(2,1)S(1)}, bf16[32,1152]{0,1:T(8,128)(2,1)S(1)}, u32[]{:S(2)}, u32[]{:S(2)}) collective-permute-start(bf16[32,1152]{0,1:T(8,128)(2,1)S(1)} %copy.71), channel_id=1, source_target_pairs={{0,2},{1,3},{2,0},{3,1},{4,6},{5,7},{6,4},{7,5},{8,10},{9,11},{10,... | collective-permute-start | bytes 221192 | tf_op jit(solution)/shard_map/ppermute | solution.py:105
  130.1 13.1 %collective-permute-start.13 = (bf16[32,1152]{0,1:T(8,128)(2,1)S(1)}, bf16[32,1152]{0,1:T(8,128)(2,1)S(1)}, u32[]{:S(2)}, u32[]{:S(2)}) collective-permute-start(bf16[32,1152]{0,1:T(8,128)(2,1)S(1)} %copy.71), channel_id=1, source_target_pairs={{0,3},{1,0},{2,1},{3,2},{4,7},{5,4},{6,5},{7,6},{8,11},{9,8},{10,9... | collective-permute-start | bytes 221192 | tf_op jit(solution)/shard_map/ppermute | solution.py:105
  143.3 0.6 copy-start.10
  143.4 1.2 copy-start.12
  145.4 19.8 %all-to-all-start = ((bf16[128,8,160]{0,2,1:T(8,128)(2,1)}), bf16[128,8,160]{0,2,1:T(8,128)(2,1)S(1)}, u32[]{:S(2)}, u32[]{:S(2)}) async-start(bf16[128,8,160]{0,2,1:T(8,128)(2,1)} %select_bitcast_fusion), calls=%async_computation | async-start | bytes 655360 | tf_op jit(solution)/shard_map/all_to_all | solution.py:137
  156.6 9.3 %copy-start.8 = (pred[1024]{0:T(1024)(128)(4,1)S(1)}, pred[1024]{0:T(1024)(128)(4,1)}, u32[]{:S(2)}) copy-start(pred[1024]{0:T(1024)(128)(4,1)} %broadcast_bitcast_fusion) | copy-start | bytes 3076
  166.0 4.4 %copy-start = (bf16[1024,1024]{1,0:T(8,128)(2,1)S(1)}, bf16[1024,1024]{1,0:T(8,128)(2,1)}, u32[]{:S(2)}) copy-start(bf16[1024,1024]{1,0:T(8,128)(2,1)} %constant_dynamic-update-slice_fusion.8) | copy-start | bytes 6291460
  173.0 3.0 %copy-start.2 = (f32[128,1024]{1,0:T(8,128)S(1)}, f32[128,1024]{1,0:T(8,128)}, u32[]{:S(2)}) copy-start(f32[128,1024]{1,0:T(8,128)} %convolution_add_fusion.2) | copy-start | bytes 1572868
  173.0 3.0 %copy-start.4 = (bf16[256,1024]{1,0:T(8,128)(2,1)S(1)}, bf16[256,1024]{1,0:T(8,128)(2,1)}, u32[]{:S(2)}) copy-start(bf16[256,1024]{1,0:T(8,128)(2,1)} %copy-done.3) | copy-start | bytes 1572868
  173.0 3.0 %copy-start.14 = (bf16[256,1024]{1,0:T(8,128)(2,1)S(1)}, bf16[256,1024]{1,0:T(8,128)(2,1)}, u32[]{:S(2)}) copy-start(bf16[256,1024]{1,0:T(8,128)(2,1)} %copy-done.13) | copy-start | bytes 1572868
  173.0 3.0 %copy-start.16 = (bf16[256,1024]{1,0:T(8,128)(2,1)S(1)}, bf16[256,1024]{1,0:T(8,128)(2,1)}, u32[]{:S(2)}) copy-start(bf16[256,1024]{1,0:T(8,128)(2,1)} %copy-done.15) | copy-start | bytes 1572868
  173.0 3.0 %copy-start.18 = (bf16[256,1024]{1,0:T(8,128)(2,1)S(1)}, bf16[256,1024]{1,0:T(8,128)(2,1)}, u32[]{:S(2)}) copy-start(bf16[256,1024]{1,0:T(8,128)(2,1)} %copy-done.17) | copy-start | bytes 1572868
  173.2 5.4 %collective-permute-start.23 = (f32[256,512]{1,0:T(8,128)S(1)}, f32[256,512]{1,0:T(8,128)S(1)}, u32[]{:S(2)}, u32[]{:S(2)}) collective-permute-start(f32[256,512]{1,0:T(8,128)S(1)} %get-tuple-element.14), channel_id=1, source_target_pairs={{0,1},{4,5},{9,10},{13,14},{18,19},{22,23},{27,24},{31,28}} | collective-permute-start | bytes 1572872 | tf_op jit(solution)/shard_map/ppermute | solution.py:173
  174.0 4.6 %collective-permute-start.25 = (f32[256,512]{1,0:T(8,128)S(1)}, f32[256,512]{1,0:T(8,128)S(1)}, u32[]{:S(2)}, u32[]{:S(2)}) collective-permute-start(f32[256,512]{1,0:T(8,128)S(1)} %get-tuple-element.15), channel_id=1, source_target_pairs={{0,3},{4,7},{9,8},{13,12},{18,17},{22,21},{27,26},{31,30}} | collective-permute-start | bytes 1572872 | tf_op jit(solution)/shard_map/ppermute | solution.py:173
  174.7 15.9 %collective-permute-start.24 = (f32[256,512]{1,0:T(8,128)S(1)}, f32[256,512]{1,0:T(8,128)S(1)}, u32[]{:S(2)}, u32[]{:S(2)}) collective-permute-start(f32[256,512]{1,0:T(8,128)S(1)} %get-tuple-element.16), channel_id=1, source_target_pairs={{0,2},{4,6},{9,11},{13,15},{18,16},{22,20},{27,25},{31,29}} | collective-permute-start | bytes 1572872 | tf_op jit(solution)/shard_map/ppermute | solution.py:173

commit v9 on v8

--- a/solution.py
+++ b/solution.py
@@ -44,18 +44,25 @@
     for k in range(1, blk_count):
         shift = [(j, (j + k) % blk_count) for j in range(blk_count)]
         received.append(lax.ppermute(passages, "blk", shift))
-    all_passages = jnp.concatenate([passages] + received, axis=0)
-    all_passages, later = lax.optimization_barrier((all_passages, queries))
+    passage_blocks = [passages] + received
+    passage_blocks, later = lax.optimization_barrier((passage_blocks, queries))
     received = []
     for k in range(1, blk_count):
         shift = [(j, (j + k) % blk_count) for j in range(blk_count)]
         received.append(lax.ppermute(later, "blk", shift))
-    all_queries = jnp.concatenate([later] + received, axis=0)
+    query_blocks = [later] + received
     ids = neg_owner * rows_shard + neg_row
-    all_rows = all_passages.shape[0]
-
-    logits = lax.dot_general(
-        queries, all_passages, (((1,), (1,)), ((), ())), preferred_element_type=jnp.float32
+    all_rows = q_rows * blk_count
+    block_rows = q_rows
+
+    logits = jnp.concatenate(
+        [
+            lax.dot_general(
+                queries, block, (((1,), (1,)), ((), ())), preferred_element_type=jnp.float32
+            )
+            for block in passage_blocks
+        ],
+        axis=1,
     )
     table_scores = lax.dot_general(
         queries, table_cols, (((1,), (1,)), ((), ())), preferred_element_type=jnp.float32
@@ -79,7 +86,6 @@
     logits = summed[:, :all_rows] * factor
     hard_logits = summed[:, all_rows:all_rows + negs] * factor
     my_positive = lax.dynamic_slice_in_dim(positive, owner_index * share, share)
-    block_rows = all_rows // blk_count
     my_positive = ((blk_index - my_positive // block_rows) % blk_count) * block_rows + (
         my_positive % block_rows
     )
@@ -110,7 +116,14 @@
     mixing = jnp.sum(jnp.where(picks, hard_grad.astype(jnp.float32)[:, :, None], 0.0), axis=1)
     mix_hi, mix_lo = hi_lo(mixing)
     query_grad = (
-        jnp.dot(soft_grad, all_passages, preferred_element_type=jnp.float32)
+        sum(
+            jnp.dot(
+                soft_grad[:, k * block_rows:(k + 1) * block_rows],
+                block,
+                preferred_element_type=jnp.float32,
+            )
+            for k, block in enumerate(passage_blocks)
+        )
         + jnp.dot(mix_hi, table_cols, preferred_element_type=jnp.float32)
         + jnp.dot(mix_lo, table_cols, preferred_element_type=jnp.float32)
     )
@@ -144,8 +157,12 @@
         moved[:, cols_per + negs:cols_per + 2 * negs].astype(jnp.int32) * rows_shard
         + moved[:, cols_per + 2 * negs:cols_per + 3 * negs].astype(jnp.int32)
     )
-    passage_grad = lax.dot_general(
-        soft_cols, all_queries, (((0,), (0,)), ((), ())), preferred_element_type=jnp.float32
+    dims = (((0,), (0,)), ((), ()))
+    passage_grad = sum(
+        lax.dot_general(
+            soft_cols[k * q_rows:(k + 1) * q_rows], block, dims, preferred_element_type=jnp.float32
+        )
+        for k, block in enumerate(query_blocks)
     )
 
     per_col = blk_count // owner_count
@@ -155,11 +172,13 @@
     all_picks = all_ids[:, :, None] == row_iota[None, None, :]
     all_mix = jnp.sum(jnp.where(all_picks, all_hard.astype(jnp.float32)[:, :, None], 0.0), axis=1)
     all_hi, all_lo = hi_lo(all_mix)
-    query_part = lax.dynamic_slice_in_dim(all_queries, part * piece_width, piece_width, axis=1)
-    dims = (((0,), (0,)), ((), ()))
-    pieces = lax.dot_general(
-        all_hi, query_part, dims, preferred_element_type=jnp.float32
-    ) + lax.dot_general(all_lo, query_part, dims, preferred_element_type=jnp.float32)
+    pieces = 0.0
+    for k, block in enumerate(query_blocks):
+        query_part = lax.dynamic_slice_in_dim(block, part * piece_width, piece_width, axis=1)
+        rows = slice(k * q_rows, (k + 1) * q_rows)
+        pieces = pieces + lax.dot_general(
+            all_hi[rows], query_part, dims, preferred_element_type=jnp.float32
+        ) + lax.dot_general(all_lo[rows], query_part, dims, preferred_element_type=jnp.float32)
     own = lax.dynamic_slice_in_dim(pieces, owner_index * rows_shard, rows_shard, axis=0)
     table_grad = jnp.where(owner_index == holder, own, 0.0)
     for k in range(1, owner_count):

time: 193 us -> 192 us (level)
  matrix products: 10.7 us -> 47.8 us
  local copies, waits for them, and re-layouts: 24.4 us -> 6.85 us
  waiting for transfers between devices: 78.7 us -> 67.5 us
  starting transfers between devices: 65.2 us -> 54.2 us
    dot_general x5 -> x40, matrix products: 5.92 us -> 44.2 us  [the longest x8 16.8 us: per_device_body(): lax.dot_general(all_lo[rows], query_part, dims, preferred_element_type=jn...]
    ppermute x7, waiting for transfers between devices: 12.6 us -> 0.02 us  [per_device_body(): received.append(lax.ppermute(later, 'blk', shift))]
    unnamed x54 -> x50, local copies, waits for them, and re-layouts: 14 us -> 1.76 us
    ppermute x3, waiting for transfers between devices: 9.34 us -> 20.8 us  [per_device_body(): received.append(lax.ppermute(slice_of(k), 'corpus', shift))]
    ppermute x3, waiting for transfers between devices: 9.99 us -> 0.01 us  [per_device_body(): received.append(lax.ppermute(grads_part, 'corpus', shift))]
    all_to_all x1, waiting for transfers between devices: 7.43 us -> 16.2 us  [per_device_body(): lax.all_to_all(packed, 'blk', split_axis=1, concat_axis=0, tiled=True)]
    ppermute x7, waiting for transfers between devices: 24.1 us -> 16.6 us  [per_device_body(): received.append(lax.ppermute(passages, 'blk', shift))]
    ppermute x7, starting transfers between devices: 23.2 us -> 15.9 us  [per_device_body(): received.append(lax.ppermute(passages, 'blk', shift))]
  transfers between devices with their start and end apart: 27 -> 27, of which waited for: 13 -> 10; matrix products, arithmetic and copies ran while one was open for 19% -> 26% of each run, Pallas kernels for 0% -> 0%
where the time goes in v9:
time: 192 us; the launch traced here: 189 us
  waiting for transfers between devices  67.5 us (35%)
  starting transfers between devices  54.2 us (28%)
  matrix products  47.8 us (25%)
  other arithmetic  11.3 us (6%)
  local copies, waits for them, and re-layouts  6.85 us (4%)
    ppermute x7, starting transfers between devices, per_device_body(): received.append(lax.ppermute(later, 'blk', shift))  26.4 us
    ppermute x3, waiting for transfers between devices, per_device_body(): received.append(lax.ppermute(slice_of(k), 'corpus', shift))  20.8 us
    dot_general x8, matrix products, per_device_body(): lax.dot_general(all_lo[rows], query_part, dims, preferred_element_type=jn...  16.8 us
    ppermute x7, waiting for transfers between devices, per_device_body(): received.append(lax.ppermute(passages, 'blk', shift))  16.6 us
    all_to_all x1, waiting for transfers between devices, per_device_body(): lax.all_to_all(packed, 'blk', split_axis=1, concat_axis=0, tiled=True)  16.2 us
    ppermute x7, starting transfers between devices, per_device_body(): received.append(lax.ppermute(passages, 'blk', shift))  15.9 us
    dot_general x8, matrix products, per_device_body(): lax.dot_general(all_hi[rows], query_part, dims, preferred_element_type=jn...  13.7 us
    dot_general x8, matrix products, per_device_body(): lax.dot_general(soft_cols[k * q_rows:(k + 1) * q_rows], block, dims, pref...  7.34 us
  transfers between devices with their start and end apart: 27, of which 10 were waited for; matrix products, arithmetic and copies ran while one was open for 26% of the time, Pallas kernels for 0%

profile of v9, /device:TPU:2, one launch (start us, length us, event | category | flops | bytes accessed | tf_op | source)
XLA Modules:
  0.0 189.1 jit_solution(14095533260488177652)
XLA Ops:
  0.6 1.6 collective-permute-start
  2.2 1.6 collective-permute-start.1
  3.8 2.5 %collective-permute-start.2 = (bf16[128,1024]{1,0:T(8,128)(2,1)}, bf16[128,1024]{1,0:T(8,128)(2,1)S(1)}, u32[]{:S(2)}, u32[]{:S(2)}) collective-permute-start(bf16[128,1024]{1,0:T(8,128)(2,1)} %param.8), channel_id=1, source_target_pairs={{0,12},{4,16},{8,20},{12,24},{16,28},{20,0},{24,4},{28,8},{1,13},{... | collective-permute-start | bytes 786440 | tf_op jit(solution)/shard_map/ppermute | solution.py:46
  6.3 1.2 collective-permute-start.3
  7.5 2.6 %collective-permute-start.4 = (bf16[128,1024]{1,0:T(8,128)(2,1)}, bf16[128,1024]{1,0:T(8,128)(2,1)S(1)}, u32[]{:S(2)}, u32[]{:S(2)}) collective-permute-start(bf16[128,1024]{1,0:T(8,128)(2,1)} %param.8), channel_id=1, source_target_pairs={{0,20},{4,24},{8,28},{12,0},{16,4},{20,8},{24,12},{28,16},{1,21},{... | collective-permute-start | bytes 786440 | tf_op jit(solution)/shard_map/ppermute | solution.py:46
  10.2 2.8 %constant_dynamic-slice_fusion.9 = (bf16[256,1024]{1,0:T(8,128)(2,1)S(1)}, bf16[256,1024]{1,0:T(8,128)(2,1)}, bf16[256,1024]{1,0:T(8,128)(2,1)}, bf16[256,1024]{1,0:T(8,128)(2,1)}) fusion(bf16[256,4096]{1,0:T(8,128)(2,1)} %param.9, s32[]{:T(128)S(6)} %select_n.272, s32[]{:T(128)S(6)} %select_n.274, s32[]{:T(128)S(6)} %select_n.278, s32[]{:T(128)S(6)} %select_n.276), kind=kLoop, calls=%fused_computation.169 | loop fusion | bytes 4194320 | tf_op jit(solution)/shard_map/dynamic_slice | solution.py:35
  13.1 1.5 collective-permute-start.5
  14.6 4.9 %collective-permute-start.6 = (bf16[128,1024]{1,0:T(8,128)(2,1)S(1)}, bf16[128,1024]{1,0:T(8,128)(2,1)S(1)}, u32[]{:S(2)}, u32[]{:S(2)}) collective-permute-start(bf16[128,1024]{1,0:T(8,128)(2,1)S(1)} %copy-done.10), channel_id=1, source_target_pairs={{0,28},{4,0},{8,4},{12,8},{16,12},{20,16},{24,20},{28,24},{1,29},{... | collective-permute-start | bytes 786440 | tf_op jit(solution)/shard_map/ppermute | solution.py:46
  19.5 14.9 %collective-permute-done.2 = bf16[128,1024]{1,0:T(8,128)(2,1)S(1)} collective-permute-done((bf16[128,1024]{1,0:T(8,128)(2,1)}, bf16[128,1024]{1,0:T(8,128)(2,1)S(1)}, u32[]{:S(2)}, u32[]{:S(2)}) %collective-permute-start.2) | collective-permute-done | bytes 262176 | tf_op jit(solution)/shard_map/ppermute | solution.py:46
  34.7 1.2 collective-permute-start.8
  35.9 1.5 collective-permute-done.6
  39.3 7.7 %collective-permute-done.9 = bf16[256,1024]{1,0:T(8,128)(2,1)S(1)} collective-permute-done((bf16[256,1024]{1,0:T(8,128)(2,1)}, bf16[256,1024]{1,0:T(8,128)(2,1)S(1)}, u32[]{:S(2)}, u32[]{:S(2)}) %collective-permute-start.9) | collective-permute-done | bytes 524320 | tf_op jit(solution)/shard_map/ppermute | solution.py:41
  47.0 13.1 %collective-permute-done.8 = bf16[256,1024]{1,0:T(8,128)(2,1)S(1)} collective-permute-done((bf16[256,1024]{1,0:T(8,128)(2,1)}, bf16[256,1024]{1,0:T(8,128)(2,1)S(1)}, u32[]{:S(2)}, u32[]{:S(2)}) %collective-permute-start.8) | collective-permute-done | bytes 524320 | tf_op jit(solution)/shard_map/ppermute | solution.py:41
  60.2 0.8 copy-done.20
  61.1 0.7 convolution_bitcast_fusion
  62.0 0.6 select_reduce_fusion.2
  63.0 0.6 collective-permute-start.11
  64.1 3.0 %collective-permute-done.12 = f32[32,1152]{1,0:T(8,128)S(1)} collective-permute-done((f32[32,1152]{1,0:T(8,128)S(1)}, f32[32,1152]{1,0:T(8,128)S(1)}, u32[]{:S(2)}, u32[]{:S(2)}) %collective-permute-start.12) | collective-permute-done | bytes 147488 | tf_op jit(solution)/shard_map/ppermute | solution.py:84
  67.1 3.2 %collective-permute-done.11 = f32[32,1152]{1,0:T(8,128)S(1)} collective-permute-done((f32[32,1152]{1,0:T(8,128)S(1)}, f32[32,1152]{1,0:T(8,128)S(1)}, u32[]{:S(2)}, u32[]{:S(2)}) %collective-permute-start.11) | collective-permute-done | bytes 147488 | tf_op jit(solution)/shard_map/ppermute | solution.py:84
  70.3 1.0 collective-permute-done.10
  73.2 1.6 collective-permute-start.14
  74.9 11.0 %collective-permute-start.22 = (bf16[128,1024]{1,0:T(8,128)(2,1)S(1)}, bf16[128,1024]{1,0:T(8,128)(2,1)}, u32[]{:S(2)}, u32[]{:S(2)}) collective-permute-start(bf16[128,1024]{1,0:T(8,128)(2,1)S(1)} %copy-done), channel_id=1, source_target_pairs={{0,28},{4,0},{8,4},{12,8},{16,12},{20,16},{24,20},{28,24},{1,29},{... | collective-permute-start | bytes 786440 | tf_op jit(solution)/shard_map/ppermute | solution.py:52
  85.9 1.7 collective-permute-start.21
  87.6 1.6 collective-permute-start.20
  89.2 4.6 %collective-permute-start.19 = (bf16[128,1024]{1,0:T(8,128)(2,1)S(1)}, bf16[128,1024]{1,0:T(8,128)(2,1)}, u32[]{:S(2)}, u32[]{:S(2)}) collective-permute-start(bf16[128,1024]{1,0:T(8,128)(2,1)S(1)} %copy-done), channel_id=1, source_target_pairs={{0,16},{4,20},{8,24},{12,28},{16,0},{20,4},{24,8},{28,12},{1,17},{... | collective-permute-start | bytes 786440 | tf_op jit(solution)/shard_map/ppermute | solution.py:52
  93.8 6.5 %collective-permute-start.18 = (bf16[128,1024]{1,0:T(8,128)(2,1)S(1)}, bf16[128,1024]{1,0:T(8,128)(2,1)}, u32[]{:S(2)}, u32[]{:S(2)}) collective-permute-start(bf16[128,1024]{1,0:T(8,128)(2,1)S(1)} %copy-done), channel_id=1, source_target_pairs={{0,12},{4,16},{8,20},{12,24},{16,28},{20,0},{24,4},{28,8},{1,13},{... | collective-permute-start | bytes 786440 | tf_op jit(solution)/shard_map/ppermute | solution.py:52
  102.0 1.1 fusion.92
  103.0 1.1 fusion.94
  104.1 1.3 select_reduce_fusion.1
  105.5 0.6 gather_fusion
  106.1 0.8 select_bitcast_fusion
  107.0 5.3 %all-to-all-start = ((bf16[128,8,160]{0,2,1:T(8,128)(2,1)}), bf16[128,8,160]{0,2,1:T(8,128)(2,1)S(1)}, u32[]{:S(2)}, u32[]{:S(2)}) async-start(bf16[128,8,160]{0,2,1:T(8,128)(2,1)} %select_bitcast_fusion), calls=%async_computation | async-start | bytes 655360 | tf_op jit(solution)/shard_map/all_to_all | solution.py:150
  112.3 2.4 %fusion.14 = f32[128,1024]{1,0:T(8,128)S(1)} fusion(f32[128,1024]{1,0:T(8,128)} %select_reduce_fusion.1, bf16[256,1024]{1,0:T(8,128)(2,1)} %copy-done.18, bf16[256,1024]{1,0:T(8,128)(2,1)} %copy-done.20, bf16[256,1024]{1,0:T(8,128)(2,1)} %copy-done.22, bf16[256,1024]{1,0:T(8,128)(2,1)} %copy-done.13), kind=kOutput, calls=%fused_computation.45 | convolution fusion | flops 277348352 | bytes 3145728 | tf_op jit(solution)/shard_map/dot_general | solution.py:128
  116.2 1.3 fusion.7
  117.5 16.2 %all-to-all-done = bf16[128,8,160]{0,2,1:T(8,128)(2,1)S(1)} async-done(((bf16[128,8,160]{0,2,1:T(8,128)(2,1)}), bf16[128,8,160]{0,2,1:T(8,128)(2,1)S(1)}, u32[]{:S(2)}, u32[]{:S(2)}) %all-to-all-start) | async-done | bytes 327712 | tf_op jit(solution)/shard_map/all_to_all | solution.py:150
  133.7 0.6 gather_fusion.1
  134.5 4.3 %select_reduce_fusion = f32[1024,1024]{1,0:T(8,128)S(1)} fusion(f32[1024,7]{0,1:T(8,128)S(1)} %slice_convert_fusion, s32[1024,7]{0,1:T(8,128)S(1)} %convert_add_fusion), kind=kLoop, calls=%fused_computation.2 | loop fusion | flops 20971520 | bytes 4251648 | tf_op jit(solution)/shard_map/reduce_sum | solution.py:173
  138.8 0.9 subtract_convert_fusion
  140.6 0.7 collective-permute-start.17
  141.3 1.4 fusion.21
  142.7 1.4 fusion.23
  144.3 1.4 fusion.25
  145.7 1.4 fusion.27
  147.1 1.4 fusion.29
  148.5 1.4 fusion.31
  149.8 1.4 fusion.33
  151.2 2.7 %fusion.35 = f32[1024,512]{1,0:T(8,128)} fusion(bf16[1024,1024]{1,0:T(8,128)(2,1)S(1)} %get-tuple-element.25, bf16[128,1024]{1,0:T(8,128)(2,1)} %collective-permute-done.18, s32[]{:T(128)S(6)} %select_n.327), kind=kOutput, calls=%fused_computation.64 | convolution fusion | flops 134217728 | bytes 2490372 | tf_op jit(solution)/shard_map/dot_general | solution.py:179
  153.9 1.8 fusion.37
  155.8 1.8 fusion.39
  157.6 1.8 fusion.41
  159.5 1.8 fusion.43
  161.3 2.7 %fusion.19 = f32[1024,512]{1,0:T(8,128)} fusion(bf16[1024,1024]{1,0:T(8,128)(2,1)S(1)} %get-tuple-element.25, bf16[128,1024]{1,0:T(8,128)(2,1)} %collective-permute-done.22, s32[]{:T(128)S(6)} %select_n.327), kind=kOutput, calls=%fused_computation.48 | convolution fusion | flops 134217728 | bytes 2490372 | tf_op jit(solution)/shard_map/dot_general | solution.py:179
  164.0 7.2 %add_add_fusion = f32[1024,512]{1,0:T(8,128)S(1)} fusion(f32[1024,512]{1,0:T(8,128)} %fusion.19, f32[1024,512]{1,0:T(8,128)S(1)} %fusion.21, f32[1024,512]{1,0:T(8,128)S(1)} %fusion.23, f32[1024,512]{1,0:T(8,128)S(1)} %fusion.25, f32[1024,512]{1,0:T(8,128)S(1)} %fusion.27, f32[1024,512]{1,0:T(8,128)S(1)} %fusion.29, f32[1024,512]{1,0:T(8,128)S(1)} %fusion.31, ...), kind=kOutput, calls=%fused_computation.9 | convolution fusion | flops 142082048 | bytes 33947652 | tf_op jit(solution)/shard_map/dot_general | solution.py:181
  171.3 0.7 collective-permute-start.25
  172.0 1.3 collective-permute-start.24
  173.3 0.7 collective-permute-start.23
  174.0 1.2 fusion.69
  175.2 1.2 fusion.71
  176.4 1.2 fusion.73
  177.5 1.2 fusion.75
  178.7 1.2 fusion.77
  180.3 1.1 fusion.13
  181.4 6.6 %collective-permute-done.24 = f32[256,512]{1,0:T(8,128)S(1)} collective-permute-done((f32[256,512]{1,0:T(8,128)S(1)}, f32[256,512]{1,0:T(8,128)S(1)}, u32[]{:S(2)}, u32[]{:S(2)}) %collective-permute-start.24) | collective-permute-done | bytes 524320 | tf_op jit(solution)/shard_map/ppermute | solution.py:192
  188.0 1.0 add_add_fusion.1
  (129 shorter events, 10.4 us)
Async XLA Ops:
  0.6 12.4 %collective-permute-start = (bf16[128,1024]{1,0:T(8,128)(2,1)}, bf16[128,1024]{1,0:T(8,128)(2,1)S(1)}, u32[]{:S(2)}, u32[]{:S(2)}) collective-permute-start(bf16[128,1024]{1,0:T(8,128)(2,1)} %param.8), channel_id=1, source_target_pairs={{0,4},{4,8},{8,12},{12,16},{16,20},{20,24},{24,28},{28,0},{1,5},{5... | collective-permute-start | bytes 786440 | tf_op jit(solution)/shard_map/ppermute | solution.py:46
  2.2 12.4 %collective-permute-start.1 = (bf16[128,1024]{1,0:T(8,128)(2,1)}, bf16[128,1024]{1,0:T(8,128)(2,1)S(1)}, u32[]{:S(2)}, u32[]{:S(2)}) collective-permute-start(bf16[128,1024]{1,0:T(8,128)(2,1)} %param.8), channel_id=1, source_target_pairs={{0,8},{4,12},{8,16},{12,20},{16,24},{20,28},{24,0},{28,4},{1,9},{5... | collective-permute-start | bytes 786440 | tf_op jit(solution)/shard_map/ppermute | solution.py:46
  3.8 30.6 %collective-permute-start.2 = (bf16[128,1024]{1,0:T(8,128)(2,1)}, bf16[128,1024]{1,0:T(8,128)(2,1)S(1)}, u32[]{:S(2)}, u32[]{:S(2)}) collective-permute-start(bf16[128,1024]{1,0:T(8,128)(2,1)} %param.8), channel_id=1, source_target_pairs={{0,12},{4,16},{8,20},{12,24},{16,28},{20,0},{24,4},{28,8},{1,13},{... | collective-permute-start | bytes 786440 | tf_op jit(solution)/shard_map/ppermute | solution.py:46
  6.3 28.4 %collective-permute-start.3 = (bf16[128,1024]{1,0:T(8,128)(2,1)}, bf16[128,1024]{1,0:T(8,128)(2,1)S(1)}, u32[]{:S(2)}, u32[]{:S(2)}) collective-permute-start(bf16[128,1024]{1,0:T(8,128)(2,1)} %param.8), channel_id=1, source_target_pairs={{0,16},{4,20},{8,24},{12,28},{16,0},{20,4},{24,8},{28,12},{1,17},{... | collective-permute-start | bytes 786440 | tf_op jit(solution)/shard_map/ppermute | solution.py:46
  7.5 28.4 %collective-permute-start.4 = (bf16[128,1024]{1,0:T(8,128)(2,1)}, bf16[128,1024]{1,0:T(8,128)(2,1)S(1)}, u32[]{:S(2)}, u32[]{:S(2)}) collective-permute-start(bf16[128,1024]{1,0:T(8,128)(2,1)} %param.8), channel_id=1, source_target_pairs={{0,20},{4,24},{8,28},{12,0},{16,4},{20,8},{24,12},{28,16},{1,21},{... | collective-permute-start | bytes 786440 | tf_op jit(solution)/shard_map/ppermute | solution.py:46
  10.2 2.9 %copy-start.10 = (bf16[128,1024]{1,0:T(8,128)(2,1)S(1)}, bf16[128,1024]{1,0:T(8,128)(2,1)}, u32[]{:S(2)}) copy-start(bf16[128,1024]{1,0:T(8,128)(2,1)} %param.8) | copy-start | bytes 786436
  10.2 9.3 %copy-start.15 = (s32[128,7]{0,1:T(8,128)S(1)}, s32[128,7]{0,1:T(8,128)}, u32[]{:S(2)}) copy-start(s32[128,7]{0,1:T(8,128)} %param.10) | copy-start | bytes 10756
  10.2 9.3 %copy-start.16 = (s32[128,7]{0,1:T(8,128)S(1)}, s32[128,7]{0,1:T(8,128)}, u32[]{:S(2)}) copy-start(s32[128,7]{0,1:T(8,128)} %param.11) | copy-start | bytes 10756
  10.2 27.2 %copy-start = (bf16[128,1024]{1,0:T(8,128)(2,1)S(1)}, bf16[128,1024]{1,0:T(8,128)(2,1)}, u32[]{:S(2)}) copy-start(bf16[128,1024]{1,0:T(8,128)(2,1)} %param.7) | copy-start | bytes 786436
  13.0 47.2 %copy-start.13 = (bf16[256,1024]{1,0:T(8,128)(2,1)}, bf16[256,1024]{1,0:T(8,128)(2,1)S(1)}, u32[]{:S(2)}) copy-start(bf16[256,1024]{1,0:T(8,128)(2,1)S(1)} %get-tuple-element.33) | copy-start | bytes 1572868
  13.1 26.2 %copy-start.4 = (bf16[128,1024]{1,0:T(8,128)(2,1)}, bf16[128,1024]{1,0:T(8,128)(2,1)S(1)}, u32[]{:S(2)}) copy-start(bf16[128,1024]{1,0:T(8,128)(2,1)S(1)} %collective-permute-done) | copy-start | bytes 786436
  13.1 22.9 %collective-permute-start.5 = (bf16[128,1024]{1,0:T(8,128)(2,1)S(1)}, bf16[128,1024]{1,0:T(8,128)(2,1)S(1)}, u32[]{:S(2)}, u32[]{:S(2)}) collective-permute-start(bf16[128,1024]{1,0:T(8,128)(2,1)S(1)} %copy-done.10), channel_id=1, source_target_pairs={{0,24},{4,28},{8,0},{12,4},{16,8},{20,12},{24,16},{28,20},{1,25},{... | collective-permute-start | bytes 786440 | tf_op jit(solution)/shard_map/ppermute | solution.py:46
  14.6 22.8 %collective-permute-start.6 = (bf16[128,1024]{1,0:T(8,128)(2,1)S(1)}, bf16[128,1024]{1,0:T(8,128)(2,1)S(1)}, u32[]{:S(2)}, u32[]{:S(2)}) collective-permute-start(bf16[128,1024]{1,0:T(8,128)(2,1)S(1)} %copy-done.10), channel_id=1, source_target_pairs={{0,28},{4,0},{8,4},{12,8},{16,12},{20,16},{24,20},{28,24},{1,29},{... | collective-permute-start | bytes 786440 | tf_op jit(solution)/shard_map/ppermute | solution.py:46
  34.4 4.9 %copy-start.6 = (bf16[128,1024]{1,0:T(8,128)(2,1)}, bf16[128,1024]{1,0:T(8,128)(2,1)S(1)}, u32[]{:S(2)}) copy-start(bf16[128,1024]{1,0:T(8,128)(2,1)S(1)} %collective-permute-done.2) | copy-start | bytes 786436
  34.4 12.7 %collective-permute-start.9 = (bf16[256,1024]{1,0:T(8,128)(2,1)}, bf16[256,1024]{1,0:T(8,128)(2,1)S(1)}, u32[]{:S(2)}, u32[]{:S(2)}) collective-permute-start(bf16[256,1024]{1,0:T(8,128)(2,1)} %get-tuple-element.35), channel_id=1, source_target_pairs={{0,3},{1,0},{2,1},{3,2},{4,7},{5,4},{6,5},{7,6},{8,11},{9,8},{10,9... | collective-permute-start | bytes 1572872 | tf_op jit(solution)/shard_map/ppermute | solution.py:41
  34.7 4.6 %copy-start.8 = (bf16[128,1024]{1,0:T(8,128)(2,1)}, bf16[128,1024]{1,0:T(8,128)(2,1)S(1)}, u32[]{:S(2)}) copy-start(bf16[128,1024]{1,0:T(8,128)(2,1)S(1)} %collective-permute-done.3) | copy-start | bytes 786436
  34.7 25.4 %collective-permute-start.8 = (bf16[256,1024]{1,0:T(8,128)(2,1)}, bf16[256,1024]{1,0:T(8,128)(2,1)S(1)}, u32[]{:S(2)}, u32[]{:S(2)}) collective-permute-start(bf16[256,1024]{1,0:T(8,128)(2,1)} %get-tuple-element.36), channel_id=1, source_target_pairs={{0,2},{1,3},{2,0},{3,1},{4,6},{5,7},{6,4},{7,5},{8,10},{9,11},{10,... | collective-permute-start | bytes 1572872 | tf_op jit(solution)/shard_map/ppermute | solution.py:41
  35.9 24.2 %collective-permute-start.7 = (bf16[256,1024]{1,0:T(8,128)(2,1)}, bf16[256,1024]{1,0:T(8,128)(2,1)S(1)}, u32[]{:S(2)}, u32[]{:S(2)}) collective-permute-start(bf16[256,1024]{1,0:T(8,128)(2,1)} %get-tuple-element.34), channel_id=1, source_target_pairs={{0,1},{1,2},{2,3},{3,0},{4,5},{5,6},{6,7},{7,4},{8,9},{9,10},{10,1... | collective-permute-start | bytes 1572872 | tf_op jit(solution)/shard_map/ppermute | solution.py:41
  47.0 13.1 %copy-start.18 = (bf16[256,1024]{1,0:T(8,128)(2,1)}, bf16[256,1024]{1,0:T(8,128)(2,1)S(1)}, u32[]{:S(2)}) copy-start(bf16[256,1024]{1,0:T(8,128)(2,1)S(1)} %collective-permute-done.9) | copy-start | bytes 1572868
  60.1 0.8 copy-start.20
  60.1 1.0 copy-start.22
  61.8 1.9 %copy-start.17 = (s32[128]{0:T(128)S(1)}, s32[128]{0:T(128)}, u32[]{:S(2)}) copy-start(s32[128]{0:T(128)} %param.12) | copy-start | bytes 1540
  61.8 2.2 %copy-start.24 = (f32[128]{0:T(128)S(1)}, f32[128]{0:T(128)}, u32[]{:S(2)}) copy-start(f32[128]{0:T(128)} %param.13) | copy-start | bytes 1540
  62.9 4.2 %collective-permute-start.12 = (f32[32,1152]{1,0:T(8,128)S(1)}, f32[32,1152]{1,0:T(8,128)S(1)}, u32[]{:S(2)}, u32[]{:S(2)}) collective-permute-start(f32[32,1152]{1,0:T(8,128)S(1)} %get-tuple-element.42), channel_id=1, source_target_pairs={{0,3},{1,0},{2,1},{3,2},{4,7},{5,4},{6,5},{7,6},{8,11},{9,8},{10,9... | collective-permute-start | bytes 442376 | tf_op jit(solution)/shard_map/ppermute | solution.py:84
  63.0 7.3 %collective-permute-start.11 = (f32[32,1152]{1,0:T(8,128)S(1)}, f32[32,1152]{1,0:T(8,128)S(1)}, u32[]{:S(2)}, u32[]{:S(2)}) collective-permute-start(f32[32,1152]{1,0:T(8,128)S(1)} %get-tuple-element.43), channel_id=1, source_target_pairs={{0,2},{1,3},{2,0},{3,1},{4,6},{5,7},{6,4},{7,5},{8,10},{9,11},{10,... | collective-permute-start | bytes 442376 | tf_op jit(solution)/shard_map/ppermute | solution.py:84
  63.6 7.8 %collective-permute-start.10 = (f32[32,1152]{1,0:T(8,128)S(1)}, f32[32,1152]{1,0:T(8,128)S(1)}, u32[]{:S(2)}, u32[]{:S(2)}) collective-permute-start(f32[32,1152]{1,0:T(8,128)S(1)} %get-tuple-element.41), channel_id=1, source_target_pairs={{0,1},{1,2},{2,3},{3,0},{4,5},{5,6},{6,7},{7,4},{8,9},{9,10},{10,1... | collective-permute-start | bytes 442376 | tf_op jit(solution)/shard_map/ppermute | solution.py:84
  73.1 14.5 %collective-permute-start.13 = (bf16[32,1152]{0,1:T(8,128)(2,1)S(1)}, bf16[32,1152]{0,1:T(8,128)(2,1)S(1)}, u32[]{:S(2)}, u32[]{:S(2)}) collective-permute-start(bf16[32,1152]{0,1:T(8,128)(2,1)S(1)} %copy.78), channel_id=1, source_target_pairs={{0,3},{1,0},{2,1},{3,2},{4,7},{5,4},{6,5},{7,6},{8,11},{9,8},{10,9... | collective-permute-start | bytes 221192 | tf_op jit(solution)/shard_map/ppermute | solution.py:111
  73.2 16.1 %collective-permute-start.14 = (bf16[32,1152]{0,1:T(8,128)(2,1)S(1)}, bf16[32,1152]{0,1:T(8,128)(2,1)S(1)}, u32[]{:S(2)}, u32[]{:S(2)}) collective-permute-start(bf16[32,1152]{0,1:T(8,128)(2,1)S(1)} %copy.78), channel_id=1, source_target_pairs={{0,2},{1,3},{2,0},{3,1},{4,6},{5,7},{6,4},{7,5},{8,10},{9,11},{10,... | collective-permute-start | bytes 221192 | tf_op jit(solution)/shard_map/ppermute | solution.py:111
  74.7 19.1 %collective-permute-start.15 = (bf16[32,1152]{0,1:T(8,128)(2,1)S(1)}, bf16[32,1152]{0,1:T(8,128)(2,1)S(1)}, u32[]{:S(2)}, u32[]{:S(2)}) collective-permute-start(bf16[32,1152]{0,1:T(8,128)(2,1)S(1)} %copy.78), channel_id=1, source_target_pairs={{0,1},{1,2},{2,3},{3,0},{4,5},{5,6},{6,7},{7,4},{8,9},{9,10},{10,1... | collective-permute-start | bytes 221192 | tf_op jit(solution)/shard_map/ppermute | solution.py:111
  74.9 86.4 %collective-permute-start.22 = (bf16[128,1024]{1,0:T(8,128)(2,1)S(1)}, bf16[128,1024]{1,0:T(8,128)(2,1)}, u32[]{:S(2)}, u32[]{:S(2)}) collective-permute-start(bf16[128,1024]{1,0:T(8,128)(2,1)S(1)} %copy-done), channel_id=1, source_target_pairs={{0,28},{4,0},{8,4},{12,8},{16,12},{20,16},{24,20},{28,24},{1,29},{... | collective-permute-start | bytes 786440 | tf_op jit(solution)/shard_map/ppermute | solution.py:52
  85.9 54.8 %collective-permute-start.21 = (bf16[128,1024]{1,0:T(8,128)(2,1)S(1)}, bf16[128,1024]{1,0:T(8,128)(2,1)}, u32[]{:S(2)}, u32[]{:S(2)}) collective-permute-start(bf16[128,1024]{1,0:T(8,128)(2,1)S(1)} %copy-done), channel_id=1, source_target_pairs={{0,24},{4,28},{8,0},{12,4},{16,8},{20,12},{24,16},{28,20},{1,25},{... | collective-permute-start | bytes 786440 | tf_op jit(solution)/shard_map/ppermute | solution.py:52
  87.6 56.5 %collective-permute-start.20 = (bf16[128,1024]{1,0:T(8,128)(2,1)S(1)}, bf16[128,1024]{1,0:T(8,128)(2,1)}, u32[]{:S(2)}, u32[]{:S(2)}) collective-permute-start(bf16[128,1024]{1,0:T(8,128)(2,1)S(1)} %copy-done), channel_id=1, source_target_pairs={{0,20},{4,24},{8,28},{12,0},{16,4},{20,8},{24,12},{28,16},{1,21},{... | collective-permute-start | bytes 786440 | tf_op jit(solution)/shard_map/ppermute | solution.py:52
  89.2 57.9 %collective-permute-start.19 = (bf16[128,1024]{1,0:T(8,128)(2,1)S(1)}, bf16[128,1024]{1,0:T(8,128)(2,1)}, u32[]{:S(2)}, u32[]{:S(2)}) collective-permute-start(bf16[128,1024]{1,0:T(8,128)(2,1)S(1)} %copy-done), channel_id=1, source_target_pairs={{0,16},{4,20},{8,24},{12,28},{16,0},{20,4},{24,8},{28,12},{1,17},{... | collective-permute-start | bytes 786440 | tf_op jit(solution)/shard_map/ppermute | solution.py:52
  93.8 56.0 %collective-permute-start.18 = (bf16[128,1024]{1,0:T(8,128)(2,1)S(1)}, bf16[128,1024]{1,0:T(8,128)(2,1)}, u32[]{:S(2)}, u32[]{:S(2)}) collective-permute-start(bf16[128,1024]{1,0:T(8,128)(2,1)S(1)} %copy-done), channel_id=1, source_target_pairs={{0,12},{4,16},{8,20},{12,24},{16,28},{20,0},{24,4},{28,8},{1,13},{... | collective-permute-start | bytes 786440 | tf_op jit(solution)/shard_map/ppermute | solution.py:52
  100.5 1.2 copy-start.9
  100.5 1.4 copy-start.7
  107.0 26.8 %all-to-all-start = ((bf16[128,8,160]{0,2,1:T(8,128)(2,1)}), bf16[128,8,160]{0,2,1:T(8,128)(2,1)S(1)}, u32[]{:S(2)}, u32[]{:S(2)}) async-start(bf16[128,8,160]{0,2,1:T(8,128)(2,1)} %select_bitcast_fusion), calls=%async_computation | async-start | bytes 655360 | tf_op jit(solution)/shard_map/all_to_all | solution.py:150
  112.3 2.5 %copy-start.12 = (f32[128,1024]{1,0:T(8,128)S(1)}, f32[128,1024]{1,0:T(8,128)}, u32[]{:S(2)}) copy-start(f32[128,1024]{1,0:T(8,128)} %select_reduce_fusion.1) | copy-start | bytes 1572868
  112.3 2.5 %copy-start.14 = (bf16[256,1024]{1,0:T(8,128)(2,1)S(1)}, bf16[256,1024]{1,0:T(8,128)(2,1)}, u32[]{:S(2)}) copy-start(bf16[256,1024]{1,0:T(8,128)(2,1)} %copy-done.13) | copy-start | bytes 1572868
  112.3 2.5 %copy-start.19 = (bf16[256,1024]{1,0:T(8,128)(2,1)S(1)}, bf16[256,1024]{1,0:T(8,128)(2,1)}, u32[]{:S(2)}) copy-start(bf16[256,1024]{1,0:T(8,128)(2,1)} %copy-done.18) | copy-start | bytes 1572868
  112.3 2.5 %copy-start.21 = (bf16[256,1024]{1,0:T(8,128)(2,1)S(1)}, bf16[256,1024]{1,0:T(8,128)(2,1)}, u32[]{:S(2)}) copy-start(bf16[256,1024]{1,0:T(8,128)(2,1)} %copy-done.20) | copy-start | bytes 1572868
  112.3 2.6 %copy-start.23 = (bf16[256,1024]{1,0:T(8,128)(2,1)S(1)}, bf16[256,1024]{1,0:T(8,128)(2,1)}, u32[]{:S(2)}) copy-start(bf16[256,1024]{1,0:T(8,128)(2,1)} %copy-done.22) | copy-start | bytes 1572868
  114.9 0.9 copy-start.5
  114.9 1.2 copy-start.2
  114.9 1.3 copy-start.3
  114.9 1.3 copy-start.11
  139.7 17.9 %copy-start.1 = (bf16[1024,1024]{1,0:T(8,128)(2,1)}, bf16[1024,1024]{1,0:T(8,128)(2,1)S(1)}, u32[]{:S(2)}) copy-start(bf16[1024,1024]{1,0:T(8,128)(2,1)S(1)} %get-tuple-element.24) | copy-start | bytes 6291460
  140.6 13.3 %collective-permute-start.17 = (bf16[128,1024]{1,0:T(8,128)(2,1)S(1)}, bf16[128,1024]{1,0:T(8,128)(2,1)S(1)}, u32[]{:S(2)}, u32[]{:S(2)}) collective-permute-start(bf16[128,1024]{1,0:T(8,128)(2,1)S(1)} %copy-done), channel_id=1, source_target_pairs={{0,8},{4,12},{8,16},{12,20},{16,24},{20,28},{24,0},{28,4},{1,9},{5... | collective-permute-start | bytes 786440 | tf_op jit(solution)/shard_map/ppermute | solution.py:52
  144.1 13.5 %collective-permute-start.16 = (bf16[128,1024]{1,0:T(8,128)(2,1)S(1)}, bf16[128,1024]{1,0:T(8,128)(2,1)S(1)}, u32[]{:S(2)}, u32[]{:S(2)}) collective-permute-start(bf16[128,1024]{1,0:T(8,128)(2,1)S(1)} %copy-done), channel_id=1, source_target_pairs={{0,4},{4,8},{8,12},{12,16},{16,20},{20,24},{24,28},{28,0},{1,5},{5... | collective-permute-start | bytes 786440 | tf_op jit(solution)/shard_map/ppermute | solution.py:52
  171.3 10.1 %collective-permute-start.25 = (f32[256,512]{1,0:T(8,128)S(1)}, f32[256,512]{1,0:T(8,128)S(1)}, u32[]{:S(2)}, u32[]{:S(2)}) collective-permute-start(f32[256,512]{1,0:T(8,128)S(1)} %get-tuple-element.31), channel_id=1, source_target_pairs={{0,3},{4,7},{9,8},{13,12},{18,17},{22,21},{27,26},{31,30}} | collective-permute-start | bytes 1572872 | tf_op jit(solution)/shard_map/ppermute | solution.py:192
  172.0 16.0 %collective-permute-start.24 = (f32[256,512]{1,0:T(8,128)S(1)}, f32[256,512]{1,0:T(8,128)S(1)}, u32[]{:S(2)}, u32[]{:S(2)}) collective-permute-start(f32[256,512]{1,0:T(8,128)S(1)} %get-tuple-element.32), channel_id=1, source_target_pairs={{0,2},{4,6},{9,11},{13,15},{18,16},{22,20},{27,25},{31,29}} | collective-permute-start | bytes 1572872 | tf_op jit(solution)/shard_map/ppermute | solution.py:192
  173.3 14.7 %collective-permute-start.23 = (f32[256,512]{1,0:T(8,128)S(1)}, f32[256,512]{1,0:T(8,128)S(1)}, u32[]{:S(2)}, u32[]{:S(2)}) collective-permute-start(f32[256,512]{1,0:T(8,128)S(1)} %get-tuple-element.30), channel_id=1, source_target_pairs={{0,1},{4,5},{9,10},{13,14},{18,19},{22,23},{27,24},{31,28}} | collective-permute-start | bytes 1572872 | tf_op jit(solution)/shard_map/ppermute | solution.py:192

commit v10 on v7

--- a/solution.py
+++ b/solution.py
@@ -51,6 +51,11 @@
         shift = [(j, (j + k) % blk_count) for j in range(blk_count)]
         received.append(lax.ppermute(later, "blk", shift))
     all_queries = gather_blocks(later, received, blk_index, blk_count)
+    per_col = blk_count // owner_count
+    piece_width = col_width // per_col
+    part = blk_index % per_col
+    cut = lambda block: lax.dynamic_slice_in_dim(block, part * piece_width, piece_width, axis=1)
+    query_part = gather_blocks(cut(later), [cut(r) for r in received], blk_index, blk_count)
     ids = neg_owner * rows_shard + neg_row
     all_rows = all_passages.shape[0]
 
@@ -138,20 +143,17 @@
         soft_cols, all_queries, (((0,), (0,)), ((), ())), preferred_element_type=jnp.float32
     )
 
-    per_col = blk_count // owner_count
-    piece_width = col_width // per_col
-    part = blk_index % per_col
     holder = blk_index // per_col
     all_picks = all_ids[:, :, None] == row_iota[None, None, :]
     all_mix = jnp.sum(jnp.where(all_picks, all_hard.astype(jnp.float32)[:, :, None], 0.0), axis=1)
     all_hi, all_lo = hi_lo(all_mix)
-    query_part = lax.dynamic_slice_in_dim(all_queries, part * piece_width, piece_width, axis=1)
     dims = (((0,), (0,)), ((), ()))
     pieces = lax.dot_general(
         all_hi, query_part, dims, preferred_element_type=jnp.float32
     ) + lax.dot_general(all_lo, query_part, dims, preferred_element_type=jnp.float32)
     own = lax.dynamic_slice_in_dim(pieces, owner_index * rows_shard, rows_shard, axis=0)
     table_grad = jnp.where(owner_index == holder, own, 0.0)
+    pieces = pieces.astype(jnp.bfloat16)
     for k in range(1, owner_count):
         pairs = [
             (b * owner_count + b // per_col, b * owner_count + (b // per_col + k) % owner_count)
@@ -160,7 +162,7 @@
         sent = lax.dynamic_slice_in_dim(
             pieces, ((owner_index + k) % owner_count) * rows_shard, rows_shard, axis=0
         )
-        table_grad = table_grad + lax.ppermute(sent, ("blk", "corpus"), pairs)
+        table_grad = table_grad + lax.ppermute(sent, ("blk", "corpus"), pairs).astype(jnp.float32)
     return (loss_share, query_grad, passage_grad, table_grad)
 
 

time: 172 us -> 166 us (0.965)
  waiting for transfers between devices: 57 us -> 51.8 us
  matrix products: 12.4 us -> 9.92 us
  other arithmetic: 22.4 us -> 24.6 us
    ppermute x3, waiting for transfers between devices: 10.4 us -> 6.1 us  [per_device_body(): lax.ppermute(sent, ('blk', 'corpus'), pairs).astype(jnp.float32)]
    unnamed x14 -> x21, other arithmetic: 9.96 us -> 11.4 us
  transfers between devices with their start and end apart: 27 -> 27, of which waited for: 12 -> 12; matrix products, arithmetic and copies ran while one was open for 15% -> 17% of each run, Pallas kernels for 0% -> 0%
where the time goes in v10:
time: 166 us; the launch traced here: 165 us
  starting transfers between devices  70.5 us (42%)
  waiting for transfers between devices  51.8 us (31%)
  other arithmetic  24.6 us (15%)
  matrix products  9.92 us (6%)
  local copies, waits for them, and re-layouts  7.05 us (4%)
    ppermute x7, starting transfers between devices, per_device_body(): received.append(lax.ppermute(later, 'blk', shift))  30.5 us
    ppermute x7, waiting for transfers between devices, per_device_body(): received.append(lax.ppermute(passages, 'blk', shift))  16 us
    ppermute x7, starting transfers between devices, per_device_body(): received.append(lax.ppermute(passages, 'blk', shift))  16 us
    all_to_all x1, starting transfers between devices, per_device_body(): lax.all_to_all(packed, 'blk', split_axis=1, concat_axis=0, tiled=True)  12.3 us
    unnamed x21, other arithmetic  11.4 us
    ppermute x7, waiting for transfers between devices, per_device_body(): received.append(lax.ppermute(later, 'blk', shift))  11.2 us
    ppermute x3, waiting for transfers between devices, per_device_body(): received.append(lax.ppermute(grads_part, 'corpus', shift))  10.8 us
    all_to_all x1, waiting for transfers between devices, per_device_body(): lax.all_to_all(packed, 'blk', split_axis=1, concat_axis=0, tiled=True)  7.72 us
  transfers between devices with their start and end apart: 27, of which 12 were waited for; matrix products, arithmetic and copies ran while one was open for 17% of the time, Pallas kernels for 0%

profile of v10, /device:TPU:2, one launch (start us, length us, event | category | flops | bytes accessed | tf_op | source)
XLA Modules:
  0.0 165.3 jit_solution(2877140458475583814)
XLA Ops:
  0.7 1.6 collective-permute-start.6
  2.3 1.6 collective-permute-start.5
  3.8 2.5 %collective-permute-start.4 = (bf16[128,1024]{1,0:T(8,128)(2,1)}, bf16[128,1024]{1,0:T(8,128)(2,1)S(1)}, u32[]{:S(2)}, u32[]{:S(2)}) collective-permute-start(bf16[128,1024]{1,0:T(8,128)(2,1)} %param.8), channel_id=1, source_target_pairs={{0,12},{4,16},{8,20},{12,24},{16,28},{20,0},{24,4},{28,8},{1,13},{... | collective-permute-start | bytes 786440 | tf_op jit(solution)/shard_map/ppermute | solution.py:46
  6.4 1.2 collective-permute-start.3
  7.6 2.6 %collective-permute-start.2 = (bf16[128,1024]{1,0:T(8,128)(2,1)}, bf16[128,1024]{1,0:T(8,128)(2,1)S(1)}, u32[]{:S(2)}, u32[]{:S(2)}) collective-permute-start(bf16[128,1024]{1,0:T(8,128)(2,1)} %param.8), channel_id=1, source_target_pairs={{0,20},{4,24},{8,28},{12,0},{16,4},{20,8},{24,12},{28,16},{1,21},{... | collective-permute-start | bytes 786440 | tf_op jit(solution)/shard_map/ppermute | solution.py:46
  10.2 2.4 %constant_dynamic-slice_fusion.6 = (bf16[256,1024]{1,0:T(8,128)(2,1)}, bf16[256,1024]{1,0:T(8,128)(2,1)}, bf16[256,1024]{1,0:T(8,128)(2,1)S(1)}) fusion(bf16[256,4096]{1,0:T(8,128)(2,1)} %param.9, s32[]{:T(128)S(6)} %select_n.1378, s32[]{:T(128)S(6)} %select_n.1375, s32[]{:T(128)S(6)} %select_n.1372), kind=kLoop, calls=%fused_computation.77 | loop fusion | bytes 3145740 | tf_op jit(solution)/shard_map/dynamic_slice | solution.py:35
  13.0 1.6 collective-permute-start.1
  14.6 4.9 %collective-permute-start = (bf16[128,1024]{1,0:T(8,128)(2,1)S(1)}, bf16[128,1024]{1,0:T(8,128)(2,1)S(1)}, u32[]{:S(2)}, u32[]{:S(2)}) collective-permute-start(bf16[128,1024]{1,0:T(8,128)(2,1)S(1)} %copy-done.1), channel_id=1, source_target_pairs={{0,28},{4,0},{8,4},{12,8},{16,12},{20,16},{24,20},{28,24},{1,29},{... | collective-permute-start | bytes 786440 | tf_op jit(solution)/shard_map/ppermute | solution.py:46
  20.1 14.3 %collective-permute-done.4 = bf16[128,1024]{1,0:T(8,128)(2,1)S(1)} collective-permute-done((bf16[128,1024]{1,0:T(8,128)(2,1)}, bf16[128,1024]{1,0:T(8,128)(2,1)S(1)}, u32[]{:S(2)}, u32[]{:S(2)}) %collective-permute-start.4) | collective-permute-done | bytes 262176 | tf_op jit(solution)/shard_map/ppermute | solution.py:46
  34.7 0.5 collective-permute-start.8
  35.3 1.2 collective-permute-start.7
  36.4 1.0 collective-permute-done
  37.5 0.4 select_dynamic-update-slice_fusion.15
  37.8 0.4 select_dynamic-update-slice_fusion.14
  38.2 0.4 select_dynamic-update-slice_fusion.13
  40.6 4.4 %collective-permute-start.22 = (bf16[128,1024]{1,0:T(8,128)(2,1)S(1)}, bf16[128,1024]{1,0:T(8,128)(2,1)S(1)}, u32[]{:S(2)}, u32[]{:S(2)}) collective-permute-start(bf16[128,1024]{1,0:T(8,128)(2,1)S(1)} %copy-done), channel_id=1, source_target_pairs={{0,4},{4,8},{8,12},{12,16},{16,20},{20,24},{24,28},{28,0},{1,5},{5... | collective-permute-start | bytes 786440 | tf_op jit(solution)/shard_map/ppermute | solution.py:52
  45.0 11.6 %collective-permute-start.21 = (bf16[128,1024]{1,0:T(8,128)(2,1)S(1)}, bf16[128,1024]{1,0:T(8,128)(2,1)S(1)}, u32[]{:S(2)}, u32[]{:S(2)}) collective-permute-start(bf16[128,1024]{1,0:T(8,128)(2,1)S(1)} %copy-done), channel_id=1, source_target_pairs={{0,8},{4,12},{8,16},{12,20},{16,24},{20,28},{24,0},{28,4},{1,9},{5... | collective-permute-start | bytes 786440 | tf_op jit(solution)/shard_map/ppermute | solution.py:52
  56.7 0.8 convolution_bitcast_fusion.1
  57.6 2.1 %collective-permute-start.19 = (bf16[128,1024]{1,0:T(8,128)(2,1)S(1)}, bf16[128,1024]{1,0:T(8,128)(2,1)S(1)}, u32[]{:S(2)}, u32[]{:S(2)}) collective-permute-start(bf16[128,1024]{1,0:T(8,128)(2,1)S(1)} %copy-done), channel_id=1, source_target_pairs={{0,16},{4,20},{8,24},{12,28},{16,0},{20,4},{24,8},{28,12},{1,17},{... | collective-permute-start | bytes 786440 | tf_op jit(solution)/shard_map/ppermute | solution.py:52
  59.7 7.2 %collective-permute-start.18 = (bf16[128,1024]{1,0:T(8,128)(2,1)S(1)}, bf16[128,1024]{1,0:T(8,128)(2,1)S(1)}, u32[]{:S(2)}, u32[]{:S(2)}) collective-permute-start(bf16[128,1024]{1,0:T(8,128)(2,1)S(1)} %copy-done), channel_id=1, source_target_pairs={{0,20},{4,24},{8,28},{12,0},{16,4},{20,8},{24,12},{28,16},{1,21},{... | collective-permute-start | bytes 786440 | tf_op jit(solution)/shard_map/ppermute | solution.py:52
  66.9 1.7 %select_select_fusion.3 = (bf16[256,1024]{1,0:T(8,128)(2,1)S(1)}, bf16[256,1024]{1,0:T(8,128)(2,1)S(1)}, bf16[256,1024]{1,0:T(8,128)(2,1)S(1)}, bf16[256,1024]{1,0:T(8,128)(2,1)S(1)}) fusion(bf16[256,1024]{1,0:T(8,128)(2,1)S(1)} %collective-permute-done.7, bf16[256,1024]{1,0:T(8,128)(2,1)S(1)} %collective-permute-done.8, ...), kind=kLoop, calls=%fused_computation.20 | loop fusion | flops 3145728 | bytes 4194320 | tf_op jit(solution)/shard_map/jit(_where)/select_n | solution.py:20
  68.7 0.8 copy-done.6
  69.8 1.5 convolution_bitcast_fusion
  71.3 1.2 copy.49
  72.5 5.1 %collective-permute-start.17 = (bf16[128,1024]{1,0:T(8,128)(2,1)S(1)}, bf16[128,1024]{1,0:T(8,128)(2,1)S(1)}, u32[]{:S(2)}, u32[]{:S(2)}) collective-permute-start(bf16[128,1024]{1,0:T(8,128)(2,1)S(1)} %copy-done), channel_id=1, source_target_pairs={{0,24},{4,28},{8,0},{12,4},{16,8},{20,12},{24,16},{28,20},{1,25},{... | collective-permute-start | bytes 786440 | tf_op jit(solution)/shard_map/ppermute | solution.py:52
  77.6 0.6 select_reduce_fusion.2
  78.5 8.3 %collective-permute-done.20 = bf16[128,1024]{1,0:T(8,128)(2,1)S(1)} collective-permute-done((bf16[128,1024]{1,0:T(8,128)(2,1)S(1)}, bf16[128,1024]{1,0:T(8,128)(2,1)S(1)}, u32[]{:S(2)}, u32[]{:S(2)}) %collective-permute-start.20) | collective-permute-done | bytes 262176 | tf_op jit(solution)/shard_map/ppermute | solution.py:52
  86.8 1.7 %collective-permute-start.12 = (f32[32,1152]{1,0:T(8,128)S(1)}, f32[32,1152]{1,0:T(8,128)S(1)}, u32[]{:S(2)}, u32[]{:S(2)}) collective-permute-start(f32[32,1152]{1,0:T(8,128)S(1)} %get-tuple-element.29), channel_id=1, source_target_pairs={{0,3},{1,0},{2,1},{3,2},{4,7},{5,4},{6,5},{7,6},{8,11},{9,8},{10,9... | collective-permute-start | bytes 442376 | tf_op jit(solution)/shard_map/ppermute | solution.py:81
  88.5 0.8 collective-permute-start.11
  89.3 2.8 %collective-permute-done.16 = bf16[128,1024]{1,0:T(8,128)(2,1)S(1)} collective-permute-done((bf16[128,1024]{1,0:T(8,128)(2,1)S(1)}, bf16[128,1024]{1,0:T(8,128)(2,1)S(1)}, u32[]{:S(2)}, u32[]{:S(2)}) %collective-permute-start.16) | collective-permute-done | bytes 262176 | tf_op jit(solution)/shard_map/ppermute | solution.py:52
  92.1 1.1 select_dynamic-update-slice_fusion.7
  94.2 1.1 select_dynamic-update-slice_fusion.6
  95.3 1.1 select_dynamic-update-slice_fusion.5
  96.4 1.1 select_dynamic-update-slice_fusion.4
  97.4 1.0 select_dynamic-update-slice_fusion.3
  98.5 1.1 select_dynamic-update-slice_fusion.2
  99.5 1.0 select_dynamic-update-slice_fusion.1
  100.6 1.1 select_dynamic-update-slice_fusion
  102.8 0.5 fusion.12
  103.9 3.4 %collective-permute-start.15 = (bf16[32,1152]{0,1:T(8,128)(2,1)S(1)}, bf16[32,1152]{0,1:T(8,128)(2,1)S(1)}, u32[]{:S(2)}, u32[]{:S(2)}) collective-permute-start(bf16[32,1152]{0,1:T(8,128)(2,1)S(1)} %copy.51), channel_id=1, source_target_pairs={{0,1},{1,2},{2,3},{3,0},{4,5},{5,6},{6,7},{7,4},{8,9},{9,10},{10,1... | collective-permute-start | bytes 221192 | tf_op jit(solution)/shard_map/ppermute | solution.py:105
  107.3 1.0 collective-permute-start.14
  108.3 0.4 collective-permute-start.13
  108.7 0.8 select_dynamic-update-slice_fusion.16
  109.6 4.2 %collective-permute-done.15 = bf16[32,1152]{0,1:T(8,128)(2,1)S(1)} collective-permute-done((bf16[32,1152]{0,1:T(8,128)(2,1)S(1)}, bf16[32,1152]{0,1:T(8,128)(2,1)S(1)}, u32[]{:S(2)}, u32[]{:S(2)}) %collective-permute-start.15) | collective-permute-done | bytes 73760 | tf_op jit(solution)/shard_map/ppermute | solution.py:105
  113.7 3.5 %collective-permute-done.14 = bf16[32,1152]{0,1:T(8,128)(2,1)S(1)} collective-permute-done((bf16[32,1152]{0,1:T(8,128)(2,1)S(1)}, bf16[32,1152]{0,1:T(8,128)(2,1)S(1)}, u32[]{:S(2)}, u32[]{:S(2)}) %collective-permute-start.14) | collective-permute-done | bytes 73760 | tf_op jit(solution)/shard_map/ppermute | solution.py:105
  117.2 3.2 %collective-permute-done.13 = bf16[32,1152]{0,1:T(8,128)(2,1)S(1)} collective-permute-done((bf16[32,1152]{0,1:T(8,128)(2,1)S(1)}, bf16[32,1152]{0,1:T(8,128)(2,1)S(1)}, u32[]{:S(2)}, u32[]{:S(2)}) %collective-permute-start.13) | collective-permute-done | bytes 73760 | tf_op jit(solution)/shard_map/ppermute | solution.py:105
  120.5 0.4 pad_maximum_fusion.2
  121.1 0.7 pad_maximum_fusion.1
  121.8 12.3 %all-to-all-start = ((bf16[128,8,160]{0,2,1:T(8,128)(2,1)}), bf16[128,8,160]{0,2,1:T(8,128)(2,1)S(1)}, u32[]{:S(2)}, u32[]{:S(2)}) async-start(bf16[128,8,160]{0,2,1:T(8,128)(2,1)} %pad_maximum_fusion.1), calls=%async_computation | async-start | bytes 655360 | tf_op jit(solution)/shard_map/all_to_all | solution.py:135
  134.1 0.5 select_reduce_fusion.1
  134.7 0.5 fusion.6
  135.1 1.1 copy-done.3
  136.2 0.5 convolution_add_fusion.2
  136.7 1.3 convolution_add_fusion.1
  138.0 7.7 %all-to-all-done = bf16[128,8,160]{0,2,1:T(8,128)(2,1)S(1)} async-done(((bf16[128,8,160]{0,2,1:T(8,128)(2,1)}), bf16[128,8,160]{0,2,1:T(8,128)(2,1)S(1)}, u32[]{:S(2)}, u32[]{:S(2)}) %all-to-all-start) | async-done | bytes 327712 | tf_op jit(solution)/shard_map/all_to_all | solution.py:135
  145.8 4.3 %select_reduce_fusion = f32[1024,1024]{1,0:T(8,128)S(1)} fusion(f32[1024,7]{0,1:T(8,128)S(1)} %slice_convert_fusion, s32[1024,7]{0,1:T(8,128)S(1)} %convert_add_fusion.1), kind=kLoop, calls=%fused_computation | loop fusion | flops 20971520 | bytes 4251648 | tf_op jit(solution)/shard_map/reduce_sum | solution.py:148
  150.1 1.3 fusion
  151.4 1.3 fusion.14
  152.8 0.7 collective-permute-start.23
  153.5 0.7 collective-permute-start.25
  154.2 1.3 collective-permute-start.24
  155.5 2.8 %fusion.3 = f32[128,1024]{1,0:T(8,128)} fusion(bf16[1024,1024]{1,0:T(8,128)(2,1)} %select_dynamic-update-slice_fusion, bf16[1024,160]{0,1:T(8,128)(2,1)S(1)} %copy_bitcast_fusion), kind=kOutput, calls=%fused_computation.28 | convolution fusion | flops 268435456 | bytes 2883584 | tf_op jit(solution)/shard_map/dot_general | solution.py:142
  158.3 6.1 %collective-permute-done.24 = bf16[256,512]{1,0:T(8,128)(2,1)S(1)} collective-permute-done((bf16[256,512]{1,0:T(8,128)(2,1)S(1)}, bf16[256,512]{1,0:T(8,128)(2,1)S(1)}, u32[]{:S(2)}, u32[]{:S(2)}) %collective-permute-start.24) | collective-permute-done | bytes 262176 | tf_op jit(solution)/shard_map/ppermute | solution.py:165
  164.4 0.9 convert_add_fusion
  (97 shorter events, 6.8 us)
Async XLA Ops:
  0.6 12.4 %copy-start.1 = (bf16[128,1024]{1,0:T(8,128)(2,1)S(1)}, bf16[128,1024]{1,0:T(8,128)(2,1)}, u32[]{:S(2)}) copy-start(bf16[128,1024]{1,0:T(8,128)(2,1)} %param.8) | copy-start | bytes 786436
  0.6 18.8 %copy-start.16 = (f32[128]{0:T(128)S(1)}, f32[128]{0:T(128)}, u32[]{:S(2)}) copy-start(f32[128]{0:T(128)} %param.13) | copy-start | bytes 1540
  0.7 19.2 %copy-start.17 = (s32[128]{0:T(128)S(1)}, s32[128]{0:T(128)}, u32[]{:S(2)}) copy-start(s32[128]{0:T(128)} %param.12) | copy-start | bytes 1540
  0.7 19.4 %copy-start.15 = (s32[128,7]{0,1:T(8,128)S(1)}, s32[128,7]{0,1:T(8,128)}, u32[]{:S(2)}) copy-start(s32[128,7]{0,1:T(8,128)} %param.11) | copy-start | bytes 10756
  0.7 19.4 %copy-start.14 = (s32[128,7]{0,1:T(8,128)S(1)}, s32[128,7]{0,1:T(8,128)}, u32[]{:S(2)}) copy-start(s32[128,7]{0,1:T(8,128)} %param.10) | copy-start | bytes 10756
  0.7 12.3 %collective-permute-start.6 = (bf16[128,1024]{1,0:T(8,128)(2,1)}, bf16[128,1024]{1,0:T(8,128)(2,1)S(1)}, u32[]{:S(2)}, u32[]{:S(2)}) collective-permute-start(bf16[128,1024]{1,0:T(8,128)(2,1)} %param.8), channel_id=1, source_target_pairs={{0,4},{4,8},{8,12},{12,16},{16,20},{20,24},{24,28},{28,0},{1,5},{5... | collective-permute-start | bytes 786440 | tf_op jit(solution)/shard_map/ppermute | solution.py:46
  2.3 12.4 %collective-permute-start.5 = (bf16[128,1024]{1,0:T(8,128)(2,1)}, bf16[128,1024]{1,0:T(8,128)(2,1)S(1)}, u32[]{:S(2)}, u32[]{:S(2)}) collective-permute-start(bf16[128,1024]{1,0:T(8,128)(2,1)} %param.8), channel_id=1, source_target_pairs={{0,8},{4,12},{8,16},{12,20},{16,24},{20,28},{24,0},{28,4},{1,9},{5... | collective-permute-start | bytes 786440 | tf_op jit(solution)/shard_map/ppermute | solution.py:46
  3.8 30.6 %collective-permute-start.4 = (bf16[128,1024]{1,0:T(8,128)(2,1)}, bf16[128,1024]{1,0:T(8,128)(2,1)S(1)}, u32[]{:S(2)}, u32[]{:S(2)}) collective-permute-start(bf16[128,1024]{1,0:T(8,128)(2,1)} %param.8), channel_id=1, source_target_pairs={{0,12},{4,16},{8,20},{12,24},{16,28},{20,0},{24,4},{28,8},{1,13},{... | collective-permute-start | bytes 786440 | tf_op jit(solution)/shard_map/ppermute | solution.py:46
  6.4 28.4 %collective-permute-start.3 = (bf16[128,1024]{1,0:T(8,128)(2,1)}, bf16[128,1024]{1,0:T(8,128)(2,1)S(1)}, u32[]{:S(2)}, u32[]{:S(2)}) collective-permute-start(bf16[128,1024]{1,0:T(8,128)(2,1)} %param.8), channel_id=1, source_target_pairs={{0,16},{4,20},{8,24},{12,28},{16,0},{20,4},{24,8},{28,12},{1,17},{... | collective-permute-start | bytes 786440 | tf_op jit(solution)/shard_map/ppermute | solution.py:46
  7.6 27.7 %collective-permute-start.2 = (bf16[128,1024]{1,0:T(8,128)(2,1)}, bf16[128,1024]{1,0:T(8,128)(2,1)S(1)}, u32[]{:S(2)}, u32[]{:S(2)}) collective-permute-start(bf16[128,1024]{1,0:T(8,128)(2,1)} %param.8), channel_id=1, source_target_pairs={{0,20},{4,24},{8,28},{12,0},{16,4},{20,8},{24,12},{28,16},{1,21},{... | collective-permute-start | bytes 786440 | tf_op jit(solution)/shard_map/ppermute | solution.py:46
  13.0 23.4 %collective-permute-start.1 = (bf16[128,1024]{1,0:T(8,128)(2,1)S(1)}, bf16[128,1024]{1,0:T(8,128)(2,1)S(1)}, u32[]{:S(2)}, u32[]{:S(2)}) collective-permute-start(bf16[128,1024]{1,0:T(8,128)(2,1)S(1)} %copy-done.1), channel_id=1, source_target_pairs={{0,24},{4,28},{8,0},{12,4},{16,8},{20,12},{24,16},{28,20},{1,25},{... | collective-permute-start | bytes 786440 | tf_op jit(solution)/shard_map/ppermute | solution.py:46
  14.6 22.8 %collective-permute-start = (bf16[128,1024]{1,0:T(8,128)(2,1)S(1)}, bf16[128,1024]{1,0:T(8,128)(2,1)S(1)}, u32[]{:S(2)}, u32[]{:S(2)}) collective-permute-start(bf16[128,1024]{1,0:T(8,128)(2,1)S(1)} %copy-done.1), channel_id=1, source_target_pairs={{0,28},{4,0},{8,4},{12,8},{16,12},{20,16},{24,20},{28,24},{1,29},{... | collective-permute-start | bytes 786440 | tf_op jit(solution)/shard_map/ppermute | solution.py:46
  34.4 23.1 %collective-permute-start.9 = (bf16[256,1024]{1,0:T(8,128)(2,1)}, bf16[256,1024]{1,0:T(8,128)(2,1)S(1)}, u32[]{:S(2)}, u32[]{:S(2)}) collective-permute-start(bf16[256,1024]{1,0:T(8,128)(2,1)} %get-tuple-element.18), channel_id=1, source_target_pairs={{0,1},{1,2},{2,3},{3,0},{4,5},{5,6},{6,7},{7,4},{8,9},{9,10},{10,1... | collective-permute-start | bytes 1572872 | tf_op jit(solution)/shard_map/ppermute | solution.py:41
  34.7 22.9 %collective-permute-start.8 = (bf16[256,1024]{1,0:T(8,128)(2,1)}, bf16[256,1024]{1,0:T(8,128)(2,1)S(1)}, u32[]{:S(2)}, u32[]{:S(2)}) collective-permute-start(bf16[256,1024]{1,0:T(8,128)(2,1)} %get-tuple-element.19), channel_id=1, source_target_pairs={{0,2},{1,3},{2,0},{3,1},{4,6},{5,7},{6,4},{7,5},{8,10},{9,11},{10,... | collective-permute-start | bytes 1572872 | tf_op jit(solution)/shard_map/ppermute | solution.py:41
  35.3 24.4 %collective-permute-start.7 = (bf16[256,1024]{1,0:T(8,128)(2,1)S(1)}, bf16[256,1024]{1,0:T(8,128)(2,1)S(1)}, u32[]{:S(2)}, u32[]{:S(2)}) collective-permute-start(bf16[256,1024]{1,0:T(8,128)(2,1)S(1)} %get-tuple-element.20), channel_id=1, source_target_pairs={{0,3},{1,0},{2,1},{3,2},{4,7},{5,4},{6,5},{7,6},{8,11},{9,8},{10,9... | collective-permute-start | bytes 1572872 | tf_op jit(solution)/shard_map/ppermute | solution.py:41
  39.7 1.0 copy-start
  40.6 19.1 %copy-start.2 = (bf16[1024,1024]{1,0:T(8,128)(2,1)}, bf16[1024,1024]{1,0:T(8,128)(2,1)S(1)}, u32[]{:S(2)}) copy-start(bf16[1024,1024]{1,0:T(8,128)(2,1)S(1)} %select_dynamic-update-slice_fusion.8) | copy-start | bytes 6291460
  40.6 31.9 %collective-permute-start.22 = (bf16[128,1024]{1,0:T(8,128)(2,1)S(1)}, bf16[128,1024]{1,0:T(8,128)(2,1)S(1)}, u32[]{:S(2)}, u32[]{:S(2)}) collective-permute-start(bf16[128,1024]{1,0:T(8,128)(2,1)S(1)} %copy-done), channel_id=1, source_target_pairs={{0,4},{4,8},{8,12},{12,16},{16,20},{20,24},{24,28},{28,0},{1,5},{5... | collective-permute-start | bytes 786440 | tf_op jit(solution)/shard_map/ppermute | solution.py:52
  45.0 32.6 %collective-permute-start.21 = (bf16[128,1024]{1,0:T(8,128)(2,1)S(1)}, bf16[128,1024]{1,0:T(8,128)(2,1)S(1)}, u32[]{:S(2)}, u32[]{:S(2)}) collective-permute-start(bf16[128,1024]{1,0:T(8,128)(2,1)S(1)} %copy-done), channel_id=1, source_target_pairs={{0,8},{4,12},{8,16},{12,20},{16,24},{20,28},{24,0},{28,4},{1,9},{5... | collective-permute-start | bytes 786440 | tf_op jit(solution)/shard_map/ppermute | solution.py:52
  57.5 29.2 %collective-permute-start.20 = (bf16[128,1024]{1,0:T(8,128)(2,1)S(1)}, bf16[128,1024]{1,0:T(8,128)(2,1)S(1)}, u32[]{:S(2)}, u32[]{:S(2)}) collective-permute-start(bf16[128,1024]{1,0:T(8,128)(2,1)S(1)} %copy-done), channel_id=1, source_target_pairs={{0,12},{4,16},{8,20},{12,24},{16,28},{20,0},{24,4},{28,8},{1,13},{... | collective-permute-start | bytes 786440 | tf_op jit(solution)/shard_map/ppermute | solution.py:52
  57.6 29.3 %collective-permute-start.19 = (bf16[128,1024]{1,0:T(8,128)(2,1)S(1)}, bf16[128,1024]{1,0:T(8,128)(2,1)S(1)}, u32[]{:S(2)}, u32[]{:S(2)}) collective-permute-start(bf16[128,1024]{1,0:T(8,128)(2,1)S(1)} %copy-done), channel_id=1, source_target_pairs={{0,16},{4,20},{8,24},{12,28},{16,0},{20,4},{24,8},{28,12},{1,17},{... | collective-permute-start | bytes 786440 | tf_op jit(solution)/shard_map/ppermute | solution.py:52
  59.7 28.8 %collective-permute-start.18 = (bf16[128,1024]{1,0:T(8,128)(2,1)S(1)}, bf16[128,1024]{1,0:T(8,128)(2,1)S(1)}, u32[]{:S(2)}, u32[]{:S(2)}) collective-permute-start(bf16[128,1024]{1,0:T(8,128)(2,1)S(1)} %copy-done), channel_id=1, source_target_pairs={{0,20},{4,24},{8,28},{12,0},{16,4},{20,8},{24,12},{28,16},{1,21},{... | collective-permute-start | bytes 786440 | tf_op jit(solution)/shard_map/ppermute | solution.py:52
  68.6 0.8 copy-start.6
  68.6 1.0 copy-start.10
  68.6 1.1 copy-start.12
  68.7 2.6 %copy-start.8 = (bf16[256,1024]{1,0:T(8,128)(2,1)}, bf16[256,1024]{1,0:T(8,128)(2,1)S(1)}, u32[]{:S(2)}) copy-start(bf16[256,1024]{1,0:T(8,128)(2,1)S(1)} %get-tuple-element.15) | copy-start | bytes 1572868
  72.5 16.8 %collective-permute-start.17 = (bf16[128,1024]{1,0:T(8,128)(2,1)S(1)}, bf16[128,1024]{1,0:T(8,128)(2,1)S(1)}, u32[]{:S(2)}, u32[]{:S(2)}) collective-permute-start(bf16[128,1024]{1,0:T(8,128)(2,1)S(1)} %copy-done), channel_id=1, source_target_pairs={{0,24},{4,28},{8,0},{12,4},{16,8},{20,12},{24,16},{28,20},{1,25},{... | collective-permute-start | bytes 786440 | tf_op jit(solution)/shard_map/ppermute | solution.py:52
  77.6 14.5 %collective-permute-start.16 = (bf16[128,1024]{1,0:T(8,128)(2,1)S(1)}, bf16[128,1024]{1,0:T(8,128)(2,1)S(1)}, u32[]{:S(2)}, u32[]{:S(2)}) collective-permute-start(bf16[128,1024]{1,0:T(8,128)(2,1)S(1)} %copy-done), channel_id=1, source_target_pairs={{0,28},{4,0},{8,4},{12,8},{16,12},{20,16},{24,20},{28,24},{1,29},{... | collective-permute-start | bytes 786440 | tf_op jit(solution)/shard_map/ppermute | solution.py:52
  86.8 15.3 %collective-permute-start.10 = (f32[32,1152]{1,0:T(8,128)S(1)}, f32[32,1152]{1,0:T(8,128)S(1)}, u32[]{:S(2)}, u32[]{:S(2)}) collective-permute-start(f32[32,1152]{1,0:T(8,128)S(1)} %get-tuple-element.28), channel_id=1, source_target_pairs={{0,1},{1,2},{2,3},{3,0},{4,5},{5,6},{6,7},{7,4},{8,9},{9,10},{10,1... | collective-permute-start | bytes 442376 | tf_op jit(solution)/shard_map/ppermute | solution.py:81
  86.8 15.2 %collective-permute-start.12 = (f32[32,1152]{1,0:T(8,128)S(1)}, f32[32,1152]{1,0:T(8,128)S(1)}, u32[]{:S(2)}, u32[]{:S(2)}) collective-permute-start(f32[32,1152]{1,0:T(8,128)S(1)} %get-tuple-element.29), channel_id=1, source_target_pairs={{0,3},{1,0},{2,1},{3,2},{4,7},{5,4},{6,5},{7,6},{8,11},{9,8},{10,9... | collective-permute-start | bytes 442376 | tf_op jit(solution)/shard_map/ppermute | solution.py:81
  88.5 13.6 %collective-permute-start.11 = (f32[32,1152]{1,0:T(8,128)S(1)}, f32[32,1152]{1,0:T(8,128)S(1)}, u32[]{:S(2)}, u32[]{:S(2)}) collective-permute-start(f32[32,1152]{1,0:T(8,128)S(1)} %get-tuple-element.30), channel_id=1, source_target_pairs={{0,2},{1,3},{2,0},{3,1},{4,6},{5,7},{6,4},{7,5},{8,10},{9,11},{10,... | collective-permute-start | bytes 442376 | tf_op jit(solution)/shard_map/ppermute | solution.py:81
  102.1 1.5 copy-start.4
  103.9 9.8 %collective-permute-start.15 = (bf16[32,1152]{0,1:T(8,128)(2,1)S(1)}, bf16[32,1152]{0,1:T(8,128)(2,1)S(1)}, u32[]{:S(2)}, u32[]{:S(2)}) collective-permute-start(bf16[32,1152]{0,1:T(8,128)(2,1)S(1)} %copy.51), channel_id=1, source_target_pairs={{0,1},{1,2},{2,3},{3,0},{4,5},{5,6},{6,7},{7,4},{8,9},{9,10},{10,1... | collective-permute-start | bytes 221192 | tf_op jit(solution)/shard_map/ppermute | solution.py:105
  107.3 9.9 %collective-permute-start.14 = (bf16[32,1152]{0,1:T(8,128)(2,1)S(1)}, bf16[32,1152]{0,1:T(8,128)(2,1)S(1)}, u32[]{:S(2)}, u32[]{:S(2)}) collective-permute-start(bf16[32,1152]{0,1:T(8,128)(2,1)S(1)} %copy.51), channel_id=1, source_target_pairs={{0,2},{1,3},{2,0},{3,1},{4,6},{5,7},{6,4},{7,5},{8,10},{9,11},{10,... | collective-permute-start | bytes 221192 | tf_op jit(solution)/shard_map/ppermute | solution.py:105
  108.3 12.1 %collective-permute-start.13 = (bf16[32,1152]{0,1:T(8,128)(2,1)S(1)}, bf16[32,1152]{0,1:T(8,128)(2,1)S(1)}, u32[]{:S(2)}, u32[]{:S(2)}) collective-permute-start(bf16[32,1152]{0,1:T(8,128)(2,1)S(1)} %copy.51), channel_id=1, source_target_pairs={{0,3},{1,0},{2,1},{3,2},{4,7},{5,4},{6,5},{7,6},{8,11},{9,8},{10,9... | collective-permute-start | bytes 221192 | tf_op jit(solution)/shard_map/ppermute | solution.py:105
  120.5 14.1 %copy-start.7 = (bf16[256,1024]{1,0:T(8,128)(2,1)S(1)}, bf16[256,1024]{1,0:T(8,128)(2,1)}, u32[]{:S(2)}) copy-start(bf16[256,1024]{1,0:T(8,128)(2,1)} %copy-done.6) | copy-start | bytes 1572868
  120.5 14.1 %copy-start.9 = (bf16[256,1024]{1,0:T(8,128)(2,1)S(1)}, bf16[256,1024]{1,0:T(8,128)(2,1)}, u32[]{:S(2)}) copy-start(bf16[256,1024]{1,0:T(8,128)(2,1)} %copy-done.8) | copy-start | bytes 1572868
  120.5 14.1 %copy-start.11 = (bf16[256,1024]{1,0:T(8,128)(2,1)S(1)}, bf16[256,1024]{1,0:T(8,128)(2,1)}, u32[]{:S(2)}) copy-start(bf16[256,1024]{1,0:T(8,128)(2,1)} %copy-done.10) | copy-start | bytes 1572868
  120.9 13.7 %copy-start.13 = (bf16[256,1024]{1,0:T(8,128)(2,1)S(1)}, bf16[256,1024]{1,0:T(8,128)(2,1)}, u32[]{:S(2)}) copy-start(bf16[256,1024]{1,0:T(8,128)(2,1)} %copy-done.12) | copy-start | bytes 1572868
  121.8 23.9 %all-to-all-start = ((bf16[128,8,160]{0,2,1:T(8,128)(2,1)}), bf16[128,8,160]{0,2,1:T(8,128)(2,1)S(1)}, u32[]{:S(2)}, u32[]{:S(2)}) async-start(bf16[128,8,160]{0,2,1:T(8,128)(2,1)} %pad_maximum_fusion.1), calls=%async_computation | async-start | bytes 655360 | tf_op jit(solution)/shard_map/all_to_all | solution.py:135
  134.6 1.6 copy-start.3
  145.8 4.4 %copy-start.5 = (bf16[1024,512]{1,0:T(8,128)(2,1)S(1)}, bf16[1024,512]{1,0:T(8,128)(2,1)}, u32[]{:S(2)}) copy-start(bf16[1024,512]{1,0:T(8,128)(2,1)} %select_dynamic-update-slice_fusion.16) | copy-start | bytes 3145732
  152.8 5.5 %collective-permute-start.23 = (bf16[256,512]{1,0:T(8,128)(2,1)S(1)}, bf16[256,512]{1,0:T(8,128)(2,1)S(1)}, u32[]{:S(2)}, u32[]{:S(2)}) collective-permute-start(bf16[256,512]{1,0:T(8,128)(2,1)S(1)} %get-tuple-element.25), channel_id=1, source_target_pairs={{0,1},{4,5},{9,10},{13,14},{18,19},{22,23},{27,24},{31,28}} | collective-permute-start | bytes 786440 | tf_op jit(solution)/shard_map/ppermute | solution.py:165
  153.5 4.8 %collective-permute-start.25 = (bf16[256,512]{1,0:T(8,128)(2,1)S(1)}, bf16[256,512]{1,0:T(8,128)(2,1)S(1)}, u32[]{:S(2)}, u32[]{:S(2)}) collective-permute-start(bf16[256,512]{1,0:T(8,128)(2,1)S(1)} %get-tuple-element.26), channel_id=1, source_target_pairs={{0,3},{4,7},{9,8},{13,12},{18,17},{22,21},{27,26},{31,30}} | collective-permute-start | bytes 786440 | tf_op jit(solution)/shard_map/ppermute | solution.py:165
  154.2 10.2 %collective-permute-start.24 = (bf16[256,512]{1,0:T(8,128)(2,1)S(1)}, bf16[256,512]{1,0:T(8,128)(2,1)S(1)}, u32[]{:S(2)}, u32[]{:S(2)}) collective-permute-start(bf16[256,512]{1,0:T(8,128)(2,1)S(1)} %get-tuple-element.27), channel_id=1, source_target_pairs={{0,2},{4,6},{9,11},{13,15},{18,16},{22,20},{27,25},{31,29}} | collective-permute-start | bytes 786440 | tf_op jit(solution)/shard_map/ppermute | solution.py:165

commit v11 on v10

--- a/solution.py
+++ b/solution.py
@@ -50,12 +50,11 @@
     for k in range(1, blk_count):
         shift = [(j, (j + k) % blk_count) for j in range(blk_count)]
         received.append(lax.ppermute(later, "blk", shift))
-    all_queries = gather_blocks(later, received, blk_index, blk_count)
+    query_received = received
     per_col = blk_count // owner_count
     piece_width = col_width // per_col
     part = blk_index % per_col
     cut = lambda block: lax.dynamic_slice_in_dim(block, part * piece_width, piece_width, axis=1)
-    query_part = gather_blocks(cut(later), [cut(r) for r in received], blk_index, blk_count)
     ids = neg_owner * rows_shard + neg_row
     all_rows = all_passages.shape[0]
 
@@ -139,18 +138,26 @@
         moved[:, cols_per + negs:cols_per + 2 * negs].astype(jnp.int32) * rows_shard
         + moved[:, cols_per + 2 * negs:cols_per + 3 * negs].astype(jnp.int32)
     )
-    passage_grad = lax.dot_general(
-        soft_cols, all_queries, (((0,), (0,)), ((), ())), preferred_element_type=jnp.float32
-    )
 
     holder = blk_index // per_col
     all_picks = all_ids[:, :, None] == row_iota[None, None, :]
     all_mix = jnp.sum(jnp.where(all_picks, all_hard.astype(jnp.float32)[:, :, None], 0.0), axis=1)
     all_hi, all_lo = hi_lo(all_mix)
+    all_hi, all_lo, part_own, part_received = lax.optimization_barrier(
+        (all_hi, all_lo, later, query_received)
+    )
+    query_part = gather_blocks(
+        cut(part_own), [cut(r) for r in part_received], blk_index, blk_count
+    )
     dims = (((0,), (0,)), ((), ()))
     pieces = lax.dot_general(
         all_hi, query_part, dims, preferred_element_type=jnp.float32
     ) + lax.dot_general(all_lo, query_part, dims, preferred_element_type=jnp.float32)
+    pieces, later, query_received = lax.optimization_barrier((pieces, later, query_received))
+    all_queries = gather_blocks(later, query_received, blk_index, blk_count)
+    passage_grad = lax.dot_general(
+        soft_cols, all_queries, (((0,), (0,)), ((), ())), preferred_element_type=jnp.float32
+    )
     own = lax.dynamic_slice_in_dim(pieces, owner_index * rows_shard, rows_shard, axis=0)
     table_grad = jnp.where(owner_index == holder, own, 0.0)
     pieces = pieces.astype(jnp.bfloat16)

time: 166 us -> 174 us (1.048); the launches traced: 165 us -> 171 us
  waiting for transfers between devices: 51.8 us -> 104 us
  starting transfers between devices: 70.5 us -> 29.5 us
  other arithmetic: 24.6 us -> 19.4 us
    ppermute x7, waiting for transfers between devices: 16 us -> 39.2 us  [per_device_body(): received.append(lax.ppermute(passages, 'blk', shift))]
    ppermute x7, starting transfers between devices: 30.5 us -> 11.9 us  [per_device_body(): received.append(lax.ppermute(later, 'blk', shift))]
    ppermute x3, waiting for transfers between devices: 0.01 us -> 12.7 us  [per_device_body(): received.append(lax.ppermute(slice_of(k), 'corpus', shift))]
    all_to_all x1, waiting for transfers between devices: 7.72 us -> 19.6 us  [per_device_body(): lax.all_to_all(packed, 'blk', split_axis=1, concat_axis=0, tiled=True)]
    all_to_all x1, starting transfers between devices: 12.3 us -> 3.74 us  [per_device_body(): lax.all_to_all(packed, 'blk', split_axis=1, concat_axis=0, tiled=True)]
    ppermute x7, starting transfers between devices: 16 us -> 8.05 us  [per_device_body(): received.append(lax.ppermute(passages, 'blk', shift))]
    ppermute x3, waiting for transfers between devices: 0.01 us -> 7.48 us  [per_device_body(): got = lax.ppermute(chunk_of(k), 'corpus', shift)]
    unnamed x21, other arithmetic: 11.4 us -> 6.49 us
  transfers between devices with their start and end apart: 27 -> 27, of which waited for: 12 -> 15; matrix products, arithmetic and copies ran while one was open for 17% -> 11% of each run, Pallas kernels for 0% -> 0%
where the time goes in v11:
time: 174 us; the launch traced here: 171 us
  waiting for transfers between devices  104 us (60%)
  starting transfers between devices  29.5 us (17%)
  other arithmetic  19.4 us (11%)
  matrix products  10.1 us (6%)
  local copies, waits for them, and re-layouts  6.05 us (3%)
    ppermute x7, waiting for transfers between devices, per_device_body(): received.append(lax.ppermute(passages, 'blk', shift))  39.2 us
    all_to_all x1, waiting for transfers between devices, per_device_body(): lax.all_to_all(packed, 'blk', split_axis=1, concat_axis=0, tiled=True)  19.6 us
    ppermute x3, waiting for transfers between devices, per_device_body(): received.append(lax.ppermute(slice_of(k), 'corpus', shift))  12.7 us
    ppermute x7, starting transfers between devices, per_device_body(): received.append(lax.ppermute(later, 'blk', shift))  11.9 us
    ppermute x3, waiting for transfers between devices, per_device_body(): received.append(lax.ppermute(grads_part, 'corpus', shift))  10.5 us
    ppermute x7, waiting for transfers between devices, per_device_body(): received.append(lax.ppermute(later, 'blk', shift))  8.17 us
    ppermute x7, starting transfers between devices, per_device_body(): received.append(lax.ppermute(passages, 'blk', shift))  8.05 us
    ppermute x3, waiting for transfers between devices, per_device_body(): got = lax.ppermute(chunk_of(k), 'corpus', shift)  7.48 us
  transfers between devices with their start and end apart: 27, of which 15 were waited for; matrix products, arithmetic and copies ran while one was open for 11% of the time, Pallas kernels for 0%

profile of v11, /device:TPU:2, one launch (start us, length us, event | category | flops | bytes accessed | tf_op | source)
XLA Modules:
  0.0 170.8 jit_solution(14347657420539267246)
XLA Ops:
  0.7 4.6 %collective-permute-start = (bf16[128,1024]{1,0:T(8,128)(2,1)}, bf16[128,1024]{1,0:T(8,128)(2,1)S(1)}, u32[]{:S(2)}, u32[]{:S(2)}) collective-permute-start(bf16[128,1024]{1,0:T(8,128)(2,1)} %param.8), channel_id=1, source_target_pairs={{0,28},{4,0},{8,4},{12,8},{16,12},{20,16},{24,20},{28,24},{1,29},{... | collective-permute-start | bytes 786440 | tf_op jit(solution)/shard_map/ppermute | solution.py:46
  5.3 0.4 collective-permute-start.1
  5.7 3.0 %collective-permute-start.3 = (bf16[128,1024]{1,0:T(8,128)(2,1)}, bf16[128,1024]{1,0:T(8,128)(2,1)S(1)}, u32[]{:S(2)}, u32[]{:S(2)}) collective-permute-start(bf16[128,1024]{1,0:T(8,128)(2,1)} %param.8), channel_id=1, source_target_pairs={{0,16},{4,20},{8,24},{12,28},{16,0},{20,4},{24,8},{28,12},{1,17},{... | collective-permute-start | bytes 786440 | tf_op jit(solution)/shard_map/ppermute | solution.py:46
  8.7 3.7 %collective-permute-done = bf16[128,1024]{1,0:T(8,128)(2,1)S(1)} collective-permute-done((bf16[128,1024]{1,0:T(8,128)(2,1)}, bf16[128,1024]{1,0:T(8,128)(2,1)S(1)}, u32[]{:S(2)}, u32[]{:S(2)}) %collective-permute-start) | collective-permute-done | bytes 262176 | tf_op jit(solution)/shard_map/ppermute | solution.py:46
  12.4 5.6 %collective-permute-done.1 = bf16[128,1024]{1,0:T(8,128)(2,1)S(1)} collective-permute-done((bf16[128,1024]{1,0:T(8,128)(2,1)}, bf16[128,1024]{1,0:T(8,128)(2,1)S(1)}, u32[]{:S(2)}, u32[]{:S(2)}) %collective-permute-start.1) | collective-permute-done | bytes 262176 | tf_op jit(solution)/shard_map/ppermute | solution.py:46
  18.0 2.3 %constant_dynamic-slice_fusion.6 = (bf16[256,1024]{1,0:T(8,128)(2,1)S(1)}, bf16[256,1024]{1,0:T(8,128)(2,1)S(1)}, bf16[256,1024]{1,0:T(8,128)(2,1)}) fusion(bf16[256,4096]{1,0:T(8,128)(2,1)} %param.9, s32[]{:T(128)S(6)} %select_n.1378, s32[]{:T(128)S(6)} %select_n.1375, s32[]{:T(128)S(6)} %select_n.1372), kind=kLoop, calls=%fused_computation.74 | loop fusion | bytes 3145740 | tf_op jit(solution)/shard_map/dynamic_slice | solution.py:35
  20.3 3.3 %collective-permute-done.2 = bf16[128,1024]{1,0:T(8,128)(2,1)S(1)} collective-permute-done((bf16[128,1024]{1,0:T(8,128)(2,1)}, bf16[128,1024]{1,0:T(8,128)(2,1)S(1)}, u32[]{:S(2)}, u32[]{:S(2)}) %collective-permute-start.2) | collective-permute-done | bytes 262176 | tf_op jit(solution)/shard_map/ppermute | solution.py:46
  23.7 26.6 %collective-permute-done.3 = bf16[128,1024]{1,0:T(8,128)(2,1)S(1)} collective-permute-done((bf16[128,1024]{1,0:T(8,128)(2,1)}, bf16[128,1024]{1,0:T(8,128)(2,1)S(1)}, u32[]{:S(2)}, u32[]{:S(2)}) %collective-permute-start.3) | collective-permute-done | bytes 262176 | tf_op jit(solution)/shard_map/ppermute | solution.py:46
  50.3 0.5 collective-permute-start.8
  50.8 0.4 select_dynamic-update-slice_fusion.15
  51.2 0.4 select_dynamic-update-slice_fusion.14
  51.6 0.4 select_dynamic-update-slice_fusion.13
  52.0 0.4 select_dynamic-update-slice_fusion.12
  52.3 0.4 select_dynamic-update-slice_fusion.11
  52.7 0.4 select_dynamic-update-slice_fusion.10
  53.1 0.4 select_dynamic-update-slice_fusion.9
  53.4 0.4 select_dynamic-update-slice_fusion.8
  53.8 1.3 copy-done.2
  55.1 0.8 convolution_bitcast_fusion.1
  56.0 9.1 %collective-permute-done.8 = bf16[256,1024]{1,0:T(8,128)(2,1)S(1)} collective-permute-done((bf16[256,1024]{1,0:T(8,128)(2,1)S(1)}, bf16[256,1024]{1,0:T(8,128)(2,1)S(1)}, u32[]{:S(2)}, u32[]{:S(2)}) %collective-permute-start.8) | collective-permute-done | bytes 524320 | tf_op jit(solution)/shard_map/ppermute | solution.py:41
  65.1 3.6 %collective-permute-done.9 = bf16[256,1024]{1,0:T(8,128)(2,1)S(1)} collective-permute-done((bf16[256,1024]{1,0:T(8,128)(2,1)S(1)}, bf16[256,1024]{1,0:T(8,128)(2,1)S(1)}, u32[]{:S(2)}, u32[]{:S(2)}) %collective-permute-start.9) | collective-permute-done | bytes 524320 | tf_op jit(solution)/shard_map/ppermute | solution.py:41
  68.7 1.7 select_select_fusion.3
  70.4 0.7 copy-done.12
  71.2 0.7 convolution_bitcast_fusion
  72.2 0.6 select_reduce_fusion.2
  73.1 0.6 collective-permute-start.11
  74.0 3.3 %collective-permute-done.12 = f32[32,1152]{1,0:T(8,128)S(1)} collective-permute-done((f32[32,1152]{1,0:T(8,128)S(1)}, f32[32,1152]{1,0:T(8,128)S(1)}, u32[]{:S(2)}, u32[]{:S(2)}) %collective-permute-start.12) | collective-permute-done | bytes 147488 | tf_op jit(solution)/shard_map/ppermute | solution.py:80
  77.3 3.2 %collective-permute-done.11 = f32[32,1152]{1,0:T(8,128)S(1)} collective-permute-done((f32[32,1152]{1,0:T(8,128)S(1)}, f32[32,1152]{1,0:T(8,128)S(1)}, u32[]{:S(2)}, u32[]{:S(2)}) %collective-permute-start.11) | collective-permute-done | bytes 147488 | tf_op jit(solution)/shard_map/ppermute | solution.py:80
  80.4 1.0 collective-permute-done.10
  82.2 0.5 fusion.9
  83.3 1.6 collective-permute-start.14
  85.1 3.3 %collective-permute-start.16 = (bf16[128,1024]{1,0:T(8,128)(2,1)S(1)}, bf16[128,1024]{1,0:T(8,128)(2,1)S(1)}, u32[]{:S(2)}, u32[]{:S(2)}) collective-permute-start(bf16[128,1024]{1,0:T(8,128)(2,1)S(1)} %copy-done), channel_id=1, source_target_pairs={{0,4},{4,8},{8,12},{12,16},{16,20},{20,24},{24,28},{28,0},{1,5},{5... | collective-permute-start | bytes 786440 | tf_op jit(solution)/shard_map/ppermute | solution.py:52
  88.4 1.3 collective-permute-done.13
  89.6 9.2 %collective-permute-done.14 = bf16[32,1152]{0,1:T(8,128)(2,1)S(1)} collective-permute-done((bf16[32,1152]{0,1:T(8,128)(2,1)S(1)}, bf16[32,1152]{0,1:T(8,128)(2,1)S(1)}, u32[]{:S(2)}, u32[]{:S(2)}) %collective-permute-start.14) | collective-permute-done | bytes 73760 | tf_op jit(solution)/shard_map/ppermute | solution.py:104
  98.9 0.5 collective-permute-start.19
  99.4 4.3 %collective-permute-start.20 = (bf16[128,1024]{1,0:T(8,128)(2,1)S(1)}, bf16[128,1024]{1,0:T(8,128)(2,1)S(1)}, u32[]{:S(2)}, u32[]{:S(2)}) collective-permute-start(bf16[128,1024]{1,0:T(8,128)(2,1)S(1)} %copy-done), channel_id=1, source_target_pairs={{0,20},{4,24},{8,28},{12,0},{16,4},{20,8},{24,12},{28,16},{1,21},{... | collective-permute-start | bytes 786440 | tf_op jit(solution)/shard_map/ppermute | solution.py:52
  104.0 0.4 pad_maximum_fusion.2
  104.4 0.5 select_reduce_fusion.1
  105.4 1.2 fusion.3
  106.7 0.7 pad_maximum_fusion.1
  107.5 3.7 %all-to-all-start = ((bf16[128,8,160]{0,2,1:T(8,128)(2,1)}), bf16[128,8,160]{0,2,1:T(8,128)(2,1)S(1)}, u32[]{:S(2)}, u32[]{:S(2)}) async-start(bf16[128,8,160]{0,2,1:T(8,128)(2,1)} %pad_maximum_fusion.1), calls=%async_computation | async-start | bytes 655360 | tf_op jit(solution)/shard_map/all_to_all | solution.py:134
  111.3 2.3 %convolution_add_fusion.2 = f32[128,1024]{1,0:T(8,128)S(1)} fusion(f32[128,1024]{1,0:T(8,128)} %fusion.3, bf16[1024,1024]{1,0:T(8,128)(2,1)} %copy-done.2, bf16[128,1152]{0,1:T(8,128)(2,1)S(1)} %pad_maximum_fusion.2), kind=kOutput, calls=%fused_computation.11 | convolution fusion | flops 268566528 | bytes 3407872 | tf_op jit(solution)/shard_map/dot_general | solution.py:112
  113.6 1.2 convolution_add_fusion.1
  114.9 19.6 %all-to-all-done = bf16[128,8,160]{0,2,1:T(8,128)(2,1)S(1)} async-done(((bf16[128,8,160]{0,2,1:T(8,128)(2,1)}), bf16[128,8,160]{0,2,1:T(8,128)(2,1)S(1)}, u32[]{:S(2)}, u32[]{:S(2)}) %all-to-all-start) | async-done | bytes 327712 | tf_op jit(solution)/shard_map/all_to_all | solution.py:134
  134.6 4.3 %select_reduce_fusion = f32[1024,1024]{1,0:T(8,128)S(1)} fusion(f32[1024,7]{0,1:T(8,128)S(1)} %slice_convert_fusion, s32[1024,7]{0,1:T(8,128)S(1)} %convert_add_fusion.1), kind=kLoop, calls=%fused_computation | loop fusion | flops 20971520 | bytes 4251648 | tf_op jit(solution)/shard_map/reduce_sum | solution.py:144
  138.9 0.7 collective-permute-start.21
  139.7 3.1 %collective-permute-start.22 = (bf16[128,1024]{1,0:T(8,128)(2,1)S(1)}, bf16[128,1024]{1,0:T(8,128)(2,1)S(1)}, u32[]{:S(2)}, u32[]{:S(2)}) collective-permute-start(bf16[128,1024]{1,0:T(8,128)(2,1)S(1)} %copy-done), channel_id=1, source_target_pairs={{0,28},{4,0},{8,4},{12,8},{16,12},{20,16},{24,20},{28,24},{1,29},{... | collective-permute-start | bytes 786440 | tf_op jit(solution)/shard_map/ppermute | solution.py:52
  142.7 0.9 subtract_convert_fusion
  143.6 4.8 %collective-permute-done.21 = bf16[128,1024]{1,0:T(8,128)(2,1)S(1)} collective-permute-done((bf16[128,1024]{1,0:T(8,128)(2,1)S(1)}, bf16[128,1024]{1,0:T(8,128)(2,1)S(1)}, u32[]{:S(2)}, u32[]{:S(2)}) %collective-permute-start.21) | collective-permute-done | bytes 262176 | tf_op jit(solution)/shard_map/ppermute | solution.py:52
  148.5 3.3 %collective-permute-done.22 = bf16[128,1024]{1,0:T(8,128)(2,1)S(1)} collective-permute-done((bf16[128,1024]{1,0:T(8,128)(2,1)S(1)}, bf16[128,1024]{1,0:T(8,128)(2,1)S(1)}, u32[]{:S(2)}, u32[]{:S(2)}) %collective-permute-start.22) | collective-permute-done | bytes 262176 | tf_op jit(solution)/shard_map/ppermute | solution.py:52
  153.5 1.3 fusion.11
  154.8 1.3 convolution_add_fusion
  156.1 0.4 select_dynamic-update-slice_fusion.7
  156.5 0.4 select_dynamic-update-slice_fusion.6
  156.8 0.4 select_dynamic-update-slice_fusion.5
  157.9 0.4 select_dynamic-update-slice_fusion.2
  158.3 0.4 select_dynamic-update-slice_fusion.1
  158.6 0.4 select_dynamic-update-slice_fusion
  159.2 0.7 collective-permute-start.25
  159.9 1.3 collective-permute-start.24
  161.2 0.7 collective-permute-start.23
  161.9 1.2 fusion
  163.1 6.7 %collective-permute-done.24 = bf16[256,512]{1,0:T(8,128)(2,1)S(1)} collective-permute-done((bf16[256,512]{1,0:T(8,128)(2,1)S(1)}, bf16[256,512]{1,0:T(8,128)(2,1)S(1)}, u32[]{:S(2)}, u32[]{:S(2)}) %collective-permute-start.24) | collective-permute-done | bytes 262176 | tf_op jit(solution)/shard_map/ppermute | solution.py:172
  169.8 1.0 convert_add_fusion
  (105 shorter events, 5.9 us)
Async XLA Ops:
  0.6 50.2 %copy-start.1 = (bf16[128,1024]{1,0:T(8,128)(2,1)S(1)}, bf16[128,1024]{1,0:T(8,128)(2,1)}, u32[]{:S(2)}) copy-start(bf16[128,1024]{1,0:T(8,128)(2,1)} %param.8) | copy-start | bytes 786436
  0.6 19.7 %copy-start.17 = (s32[128,7]{0,1:T(8,128)S(1)}, s32[128,7]{0,1:T(8,128)}, u32[]{:S(2)}) copy-start(s32[128,7]{0,1:T(8,128)} %param.10) | copy-start | bytes 10756
  0.7 19.6 %copy-start.18 = (s32[128,7]{0,1:T(8,128)S(1)}, s32[128,7]{0,1:T(8,128)}, u32[]{:S(2)}) copy-start(s32[128,7]{0,1:T(8,128)} %param.11) | copy-start | bytes 10756
  0.7 11.7 %collective-permute-start = (bf16[128,1024]{1,0:T(8,128)(2,1)}, bf16[128,1024]{1,0:T(8,128)(2,1)S(1)}, u32[]{:S(2)}, u32[]{:S(2)}) collective-permute-start(bf16[128,1024]{1,0:T(8,128)(2,1)} %param.8), channel_id=1, source_target_pairs={{0,28},{4,0},{8,4},{12,8},{16,12},{20,16},{24,20},{28,24},{1,29},{... | collective-permute-start | bytes 786440 | tf_op jit(solution)/shard_map/ppermute | solution.py:46
  5.3 12.7 %collective-permute-start.1 = (bf16[128,1024]{1,0:T(8,128)(2,1)}, bf16[128,1024]{1,0:T(8,128)(2,1)S(1)}, u32[]{:S(2)}, u32[]{:S(2)}) collective-permute-start(bf16[128,1024]{1,0:T(8,128)(2,1)} %param.8), channel_id=1, source_target_pairs={{0,24},{4,28},{8,0},{12,4},{16,8},{20,12},{24,16},{28,20},{1,25},{... | collective-permute-start | bytes 786440 | tf_op jit(solution)/shard_map/ppermute | solution.py:46
  5.7 17.9 %collective-permute-start.2 = (bf16[128,1024]{1,0:T(8,128)(2,1)}, bf16[128,1024]{1,0:T(8,128)(2,1)S(1)}, u32[]{:S(2)}, u32[]{:S(2)}) collective-permute-start(bf16[128,1024]{1,0:T(8,128)(2,1)} %param.8), channel_id=1, source_target_pairs={{0,20},{4,24},{8,28},{12,0},{16,4},{20,8},{24,12},{28,16},{1,21},{... | collective-permute-start | bytes 786440 | tf_op jit(solution)/shard_map/ppermute | solution.py:46
  5.7 44.5 %collective-permute-start.3 = (bf16[128,1024]{1,0:T(8,128)(2,1)}, bf16[128,1024]{1,0:T(8,128)(2,1)S(1)}, u32[]{:S(2)}, u32[]{:S(2)}) collective-permute-start(bf16[128,1024]{1,0:T(8,128)(2,1)} %param.8), channel_id=1, source_target_pairs={{0,16},{4,20},{8,24},{12,28},{16,0},{20,4},{24,8},{28,12},{1,17},{... | collective-permute-start | bytes 786440 | tf_op jit(solution)/shard_map/ppermute | solution.py:46
  8.7 42.1 %collective-permute-start.4 = (bf16[128,1024]{1,0:T(8,128)(2,1)}, bf16[128,1024]{1,0:T(8,128)(2,1)S(1)}, u32[]{:S(2)}, u32[]{:S(2)}) collective-permute-start(bf16[128,1024]{1,0:T(8,128)(2,1)} %param.8), channel_id=1, source_target_pairs={{0,12},{4,16},{8,20},{12,24},{16,28},{20,0},{24,4},{28,8},{1,13},{... | collective-permute-start | bytes 786440 | tf_op jit(solution)/shard_map/ppermute | solution.py:46
  12.4 38.4 %collective-permute-start.5 = (bf16[128,1024]{1,0:T(8,128)(2,1)}, bf16[128,1024]{1,0:T(8,128)(2,1)S(1)}, u32[]{:S(2)}, u32[]{:S(2)}) collective-permute-start(bf16[128,1024]{1,0:T(8,128)(2,1)} %param.8), channel_id=1, source_target_pairs={{0,8},{4,12},{8,16},{12,20},{16,24},{20,28},{24,0},{28,4},{1,9},{5... | collective-permute-start | bytes 786440 | tf_op jit(solution)/shard_map/ppermute | solution.py:46
  18.0 32.8 %collective-permute-start.6 = (bf16[128,1024]{1,0:T(8,128)(2,1)}, bf16[128,1024]{1,0:T(8,128)(2,1)S(1)}, u32[]{:S(2)}, u32[]{:S(2)}) collective-permute-start(bf16[128,1024]{1,0:T(8,128)(2,1)} %param.8), channel_id=1, source_target_pairs={{0,4},{4,8},{8,12},{12,16},{16,20},{20,24},{24,28},{28,0},{1,5},{5... | collective-permute-start | bytes 786440 | tf_op jit(solution)/shard_map/ppermute | solution.py:46
  23.7 32.3 %collective-permute-start.7 = (bf16[256,1024]{1,0:T(8,128)(2,1)}, bf16[256,1024]{1,0:T(8,128)(2,1)S(1)}, u32[]{:S(2)}, u32[]{:S(2)}) collective-permute-start(bf16[256,1024]{1,0:T(8,128)(2,1)} %get-tuple-element.60), channel_id=1, source_target_pairs={{0,3},{1,0},{2,1},{3,2},{4,7},{5,4},{6,5},{7,6},{8,11},{9,8},{10,9... | collective-permute-start | bytes 1572872 | tf_op jit(solution)/shard_map/ppermute | solution.py:41
  50.3 14.8 %collective-permute-start.8 = (bf16[256,1024]{1,0:T(8,128)(2,1)S(1)}, bf16[256,1024]{1,0:T(8,128)(2,1)S(1)}, u32[]{:S(2)}, u32[]{:S(2)}) collective-permute-start(bf16[256,1024]{1,0:T(8,128)(2,1)S(1)} %get-tuple-element.59), channel_id=1, source_target_pairs={{0,2},{1,3},{2,0},{3,1},{4,6},{5,7},{6,4},{7,5},{8,10},{9,11},{10,... | collective-permute-start | bytes 1572872 | tf_op jit(solution)/shard_map/ppermute | solution.py:41
  50.8 17.9 %collective-permute-start.9 = (bf16[256,1024]{1,0:T(8,128)(2,1)S(1)}, bf16[256,1024]{1,0:T(8,128)(2,1)S(1)}, u32[]{:S(2)}, u32[]{:S(2)}) collective-permute-start(bf16[256,1024]{1,0:T(8,128)(2,1)S(1)} %get-tuple-element.58), channel_id=1, source_target_pairs={{0,1},{1,2},{2,3},{3,0},{4,5},{5,6},{6,7},{7,4},{8,9},{9,10},{10,1... | collective-permute-start | bytes 1572872 | tf_op jit(solution)/shard_map/ppermute | solution.py:41
  53.0 2.1 %copy-start = (bf16[128,1024]{1,0:T(8,128)(2,1)S(1)}, bf16[128,1024]{1,0:T(8,128)(2,1)}, u32[]{:S(2)}) copy-start(bf16[128,1024]{1,0:T(8,128)(2,1)} %param.7) | copy-start | bytes 786436
  53.8 1.3 copy-start.2
  70.4 0.8 copy-start.12
  70.4 1.5 copy-start.3
  70.4 1.5 copy-start.6
  70.4 1.5 copy-start.9
  71.9 1.9 %copy-start.19 = (s32[128]{0:T(128)S(1)}, s32[128]{0:T(128)}, u32[]{:S(2)}) copy-start(s32[128]{0:T(128)} %param.12) | copy-start | bytes 1540
  71.9 2.0 %copy-start.20 = (f32[128]{0:T(128)S(1)}, f32[128]{0:T(128)}, u32[]{:S(2)}) copy-start(f32[128]{0:T(128)} %param.13) | copy-start | bytes 1540
  73.0 4.2 %collective-permute-start.12 = (f32[32,1152]{1,0:T(8,128)S(1)}, f32[32,1152]{1,0:T(8,128)S(1)}, u32[]{:S(2)}, u32[]{:S(2)}) collective-permute-start(f32[32,1152]{1,0:T(8,128)S(1)} %get-tuple-element.69), channel_id=1, source_target_pairs={{0,3},{1,0},{2,1},{3,2},{4,7},{5,4},{6,5},{7,6},{8,11},{9,8},{10,9... | collective-permute-start | bytes 442376 | tf_op jit(solution)/shard_map/ppermute | solution.py:80
  73.1 7.4 %collective-permute-start.11 = (f32[32,1152]{1,0:T(8,128)S(1)}, f32[32,1152]{1,0:T(8,128)S(1)}, u32[]{:S(2)}, u32[]{:S(2)}) collective-permute-start(f32[32,1152]{1,0:T(8,128)S(1)} %get-tuple-element.70), channel_id=1, source_target_pairs={{0,2},{1,3},{2,0},{3,1},{4,6},{5,7},{6,4},{7,5},{8,10},{9,11},{10,... | collective-permute-start | bytes 442376 | tf_op jit(solution)/shard_map/ppermute | solution.py:80
  73.7 7.8 %collective-permute-start.10 = (f32[32,1152]{1,0:T(8,128)S(1)}, f32[32,1152]{1,0:T(8,128)S(1)}, u32[]{:S(2)}, u32[]{:S(2)}) collective-permute-start(f32[32,1152]{1,0:T(8,128)S(1)} %get-tuple-element.68), channel_id=1, source_target_pairs={{0,1},{1,2},{2,3},{3,0},{4,5},{5,6},{6,7},{7,4},{8,9},{9,10},{10,1... | collective-permute-start | bytes 442376 | tf_op jit(solution)/shard_map/ppermute | solution.py:80
  83.2 6.4 %collective-permute-start.13 = (bf16[32,1152]{0,1:T(8,128)(2,1)S(1)}, bf16[32,1152]{0,1:T(8,128)(2,1)S(1)}, u32[]{:S(2)}, u32[]{:S(2)}) collective-permute-start(bf16[32,1152]{0,1:T(8,128)(2,1)S(1)} %copy.51), channel_id=1, source_target_pairs={{0,3},{1,0},{2,1},{3,2},{4,7},{5,4},{6,5},{7,6},{8,11},{9,8},{10,9... | collective-permute-start | bytes 221192 | tf_op jit(solution)/shard_map/ppermute | solution.py:104
  83.3 15.6 %collective-permute-start.14 = (bf16[32,1152]{0,1:T(8,128)(2,1)S(1)}, bf16[32,1152]{0,1:T(8,128)(2,1)S(1)}, u32[]{:S(2)}, u32[]{:S(2)}) collective-permute-start(bf16[32,1152]{0,1:T(8,128)(2,1)S(1)} %copy.51), channel_id=1, source_target_pairs={{0,2},{1,3},{2,0},{3,1},{4,6},{5,7},{6,4},{7,5},{8,10},{9,11},{10,... | collective-permute-start | bytes 221192 | tf_op jit(solution)/shard_map/ppermute | solution.py:104
  84.8 14.6 %collective-permute-start.15 = (bf16[32,1152]{0,1:T(8,128)(2,1)S(1)}, bf16[32,1152]{0,1:T(8,128)(2,1)S(1)}, u32[]{:S(2)}, u32[]{:S(2)}) collective-permute-start(bf16[32,1152]{0,1:T(8,128)(2,1)S(1)} %copy.51), channel_id=1, source_target_pairs={{0,1},{1,2},{2,3},{3,0},{4,5},{5,6},{6,7},{7,4},{8,9},{9,10},{10,1... | collective-permute-start | bytes 221192 | tf_op jit(solution)/shard_map/ppermute | solution.py:104
  85.1 53.9 %collective-permute-start.16 = (bf16[128,1024]{1,0:T(8,128)(2,1)S(1)}, bf16[128,1024]{1,0:T(8,128)(2,1)S(1)}, u32[]{:S(2)}, u32[]{:S(2)}) collective-permute-start(bf16[128,1024]{1,0:T(8,128)(2,1)S(1)} %copy-done), channel_id=1, source_target_pairs={{0,4},{4,8},{8,12},{12,16},{16,20},{20,24},{24,28},{28,0},{1,5},{5... | collective-permute-start | bytes 786440 | tf_op jit(solution)/shard_map/ppermute | solution.py:52
  88.4 51.3 %collective-permute-start.17 = (bf16[128,1024]{1,0:T(8,128)(2,1)S(1)}, bf16[128,1024]{1,0:T(8,128)(2,1)S(1)}, u32[]{:S(2)}, u32[]{:S(2)}) collective-permute-start(bf16[128,1024]{1,0:T(8,128)(2,1)S(1)} %copy-done), channel_id=1, source_target_pairs={{0,8},{4,12},{8,16},{12,20},{16,24},{20,28},{24,0},{28,4},{1,9},{5... | collective-permute-start | bytes 786440 | tf_op jit(solution)/shard_map/ppermute | solution.py:52
  89.6 54.0 %collective-permute-start.18 = (bf16[128,1024]{1,0:T(8,128)(2,1)S(1)}, bf16[128,1024]{1,0:T(8,128)(2,1)S(1)}, u32[]{:S(2)}, u32[]{:S(2)}) collective-permute-start(bf16[128,1024]{1,0:T(8,128)(2,1)S(1)} %copy-done), channel_id=1, source_target_pairs={{0,12},{4,16},{8,20},{12,24},{16,28},{20,0},{24,4},{28,8},{1,13},{... | collective-permute-start | bytes 786440 | tf_op jit(solution)/shard_map/ppermute | solution.py:52
  98.9 44.8 %collective-permute-start.19 = (bf16[128,1024]{1,0:T(8,128)(2,1)S(1)}, bf16[128,1024]{1,0:T(8,128)(2,1)S(1)}, u32[]{:S(2)}, u32[]{:S(2)}) collective-permute-start(bf16[128,1024]{1,0:T(8,128)(2,1)S(1)} %copy-done), channel_id=1, source_target_pairs={{0,16},{4,20},{8,24},{12,28},{16,0},{20,4},{24,8},{28,12},{1,17},{... | collective-permute-start | bytes 786440 | tf_op jit(solution)/shard_map/ppermute | solution.py:52
  99.4 44.2 %collective-permute-start.20 = (bf16[128,1024]{1,0:T(8,128)(2,1)S(1)}, bf16[128,1024]{1,0:T(8,128)(2,1)S(1)}, u32[]{:S(2)}, u32[]{:S(2)}) collective-permute-start(bf16[128,1024]{1,0:T(8,128)(2,1)S(1)} %copy-done), channel_id=1, source_target_pairs={{0,20},{4,24},{8,28},{12,0},{16,4},{20,8},{24,12},{28,16},{1,21},{... | collective-permute-start | bytes 786440 | tf_op jit(solution)/shard_map/ppermute | solution.py:52
  103.9 1.0 copy-start.4
  103.9 1.2 copy-start.7
  103.9 1.3 copy-start.10
  103.9 1.5 copy-start.13
  105.4 1.3 copy-start.15
  107.5 6.1 %copy-start.5 = (bf16[256,1024]{1,0:T(8,128)(2,1)S(1)}, bf16[256,1024]{1,0:T(8,128)(2,1)}, u32[]{:S(2)}) copy-start(bf16[256,1024]{1,0:T(8,128)(2,1)} %copy-done.3) | copy-start | bytes 1572868
  107.5 27.0 %all-to-all-start = ((bf16[128,8,160]{0,2,1:T(8,128)(2,1)}), bf16[128,8,160]{0,2,1:T(8,128)(2,1)S(1)}, u32[]{:S(2)}, u32[]{:S(2)}) async-start(bf16[128,8,160]{0,2,1:T(8,128)(2,1)} %pad_maximum_fusion.1), calls=%async_computation | async-start | bytes 655360 | tf_op jit(solution)/shard_map/all_to_all | solution.py:134
  111.2 2.3 %copy-start.8 = (bf16[256,1024]{1,0:T(8,128)(2,1)S(1)}, bf16[256,1024]{1,0:T(8,128)(2,1)}, u32[]{:S(2)}) copy-start(bf16[256,1024]{1,0:T(8,128)(2,1)} %copy-done.6) | copy-start | bytes 1572868
  111.3 2.3 %copy-start.11 = (bf16[256,1024]{1,0:T(8,128)(2,1)S(1)}, bf16[256,1024]{1,0:T(8,128)(2,1)}, u32[]{:S(2)}) copy-start(bf16[256,1024]{1,0:T(8,128)(2,1)} %copy-done.9) | copy-start | bytes 1572868
  111.3 2.3 %copy-start.14 = (bf16[256,1024]{1,0:T(8,128)(2,1)S(1)}, bf16[256,1024]{1,0:T(8,128)(2,1)}, u32[]{:S(2)}) copy-start(bf16[256,1024]{1,0:T(8,128)(2,1)} %copy-done.12) | copy-start | bytes 1572868
  111.3 2.3 %copy-start.16 = (f32[128,1024]{1,0:T(8,128)S(1)}, f32[128,1024]{1,0:T(8,128)}, u32[]{:S(2)}) copy-start(f32[128,1024]{1,0:T(8,128)} %copy-done.15) | copy-start | bytes 1572868
  138.9 9.5 %collective-permute-start.21 = (bf16[128,1024]{1,0:T(8,128)(2,1)S(1)}, bf16[128,1024]{1,0:T(8,128)(2,1)S(1)}, u32[]{:S(2)}, u32[]{:S(2)}) collective-permute-start(bf16[128,1024]{1,0:T(8,128)(2,1)S(1)} %copy-done), channel_id=1, source_target_pairs={{0,24},{4,28},{8,0},{12,4},{16,8},{20,12},{24,16},{28,20},{1,25},{... | collective-permute-start | bytes 786440 | tf_op jit(solution)/shard_map/ppermute | solution.py:52
  139.7 12.1 %collective-permute-start.22 = (bf16[128,1024]{1,0:T(8,128)(2,1)S(1)}, bf16[128,1024]{1,0:T(8,128)(2,1)S(1)}, u32[]{:S(2)}, u32[]{:S(2)}) collective-permute-start(bf16[128,1024]{1,0:T(8,128)(2,1)S(1)} %copy-done), channel_id=1, source_target_pairs={{0,28},{4,0},{8,4},{12,8},{16,12},{20,16},{24,20},{28,24},{1,29},{... | collective-permute-start | bytes 786440 | tf_op jit(solution)/shard_map/ppermute | solution.py:52
  159.2 3.9 %collective-permute-start.25 = (bf16[256,512]{1,0:T(8,128)(2,1)S(1)}, bf16[256,512]{1,0:T(8,128)(2,1)S(1)}, u32[]{:S(2)}, u32[]{:S(2)}) collective-permute-start(bf16[256,512]{1,0:T(8,128)(2,1)S(1)} %get-tuple-element.66), channel_id=1, source_target_pairs={{0,3},{4,7},{9,8},{13,12},{18,17},{22,21},{27,26},{31,30}} | collective-permute-start | bytes 786440 | tf_op jit(solution)/shard_map/ppermute | solution.py:172
  159.9 9.9 %collective-permute-start.24 = (bf16[256,512]{1,0:T(8,128)(2,1)S(1)}, bf16[256,512]{1,0:T(8,128)(2,1)S(1)}, u32[]{:S(2)}, u32[]{:S(2)}) collective-permute-start(bf16[256,512]{1,0:T(8,128)(2,1)S(1)} %get-tuple-element.67), channel_id=1, source_target_pairs={{0,2},{4,6},{9,11},{13,15},{18,16},{22,20},{27,25},{31,29}} | collective-permute-start | bytes 786440 | tf_op jit(solution)/shard_map/ppermute | solution.py:172
  161.2 8.6 %collective-permute-start.23 = (bf16[256,512]{1,0:T(8,128)(2,1)S(1)}, bf16[256,512]{1,0:T(8,128)(2,1)S(1)}, u32[]{:S(2)}, u32[]{:S(2)}) collective-permute-start(bf16[256,512]{1,0:T(8,128)(2,1)S(1)} %get-tuple-element.65), channel_id=1, source_target_pairs={{0,1},{4,5},{9,10},{13,14},{18,19},{22,23},{27,24},{31,28}} | collective-permute-start | bytes 786440 | tf_op jit(solution)/shard_map/ppermute | solution.py:172

commit v12 on v11

--- a/solution.py
+++ b/solution.py
@@ -55,6 +55,7 @@
     piece_width = col_width // per_col
     part = blk_index % per_col
     cut = lambda block: lax.dynamic_slice_in_dim(block, part * piece_width, piece_width, axis=1)
+    query_part = gather_blocks(cut(later), [cut(r) for r in received], blk_index, blk_count)
     ids = neg_owner * rows_shard + neg_row
     all_rows = all_passages.shape[0]
 
@@ -68,7 +69,7 @@
     picks = ids[:, :, None] == row_iota[None, None, :]
     hard_logits = jnp.sum(jnp.where(picks, table_scores[:, None, :], 0.0), axis=2)
     negs = ids.shape[1]
-    pad = jnp.zeros((q_rows, 128 - negs), jnp.float32)
+    pad = jnp.zeros((q_rows, 8 - negs), jnp.float32)
     partial = jnp.concatenate([logits, hard_logits, pad], axis=1)
     share = q_rows // owner_count
     chunk_of = lambda k: lax.dynamic_slice_in_dim(
@@ -96,7 +97,7 @@
     ).astype(jnp.bfloat16)
     hard_part = (weighting * jnp.exp(hard_logits - log_total[:, None])).astype(jnp.bfloat16)
     grads_part = jnp.concatenate(
-        [soft_part, hard_part, jnp.zeros((share, 128 - negs), jnp.bfloat16)], axis=1
+        [soft_part, hard_part, jnp.zeros((share, 8 - negs), jnp.bfloat16)], axis=1
     )
     received = []
     for k in range(1, owner_count):
@@ -143,12 +144,6 @@
     all_picks = all_ids[:, :, None] == row_iota[None, None, :]
     all_mix = jnp.sum(jnp.where(all_picks, all_hard.astype(jnp.float32)[:, :, None], 0.0), axis=1)
     all_hi, all_lo = hi_lo(all_mix)
-    all_hi, all_lo, part_own, part_received = lax.optimization_barrier(
-        (all_hi, all_lo, later, query_received)
-    )
-    query_part = gather_blocks(
-        cut(part_own), [cut(r) for r in part_received], blk_index, blk_count
-    )
     dims = (((0,), (0,)), ((), ()))
     pieces = lax.dot_general(
         all_hi, query_part, dims, preferred_element_type=jnp.float32

time: 174 us -> 161 us (0.925); the launches traced: 171 us -> 160 us
  waiting for transfers between devices: 104 us -> 50.1 us
  starting transfers between devices: 29.5 us -> 72.7 us
    ppermute x7, waiting for transfers between devices: 39.2 us -> 16 us  [per_device_body(): received.append(lax.ppermute(passages, 'blk', shift))]
    ppermute x7, starting transfers between devices: 11.9 us -> 30.5 us  [per_device_body(): received.append(lax.ppermute(later, 'blk', shift))]
    all_to_all x1, waiting for transfers between devices: 19.6 us -> 6.42 us  [per_device_body(): lax.all_to_all(packed, 'blk', split_axis=1, concat_axis=0, tiled=True)]
    all_to_all x1, starting transfers between devices: 3.74 us -> 16.8 us  [per_device_body(): lax.all_to_all(packed, 'blk', split_axis=1, concat_axis=0, tiled=True)]
    ppermute x3, waiting for transfers between devices: 12.7 us -> 0.01 us  [per_device_body(): received.append(lax.ppermute(slice_of(k), 'corpus', shift))]
    ppermute x7, starting transfers between devices: 8.05 us -> 16 us  [per_device_body(): received.append(lax.ppermute(passages, 'blk', shift))]
    ppermute x3, waiting for transfers between devices: 7.48 us -> 2.46 us  [per_device_body(): got = lax.ppermute(chunk_of(k), 'corpus', shift)]
    ppermute x7, waiting for transfers between devices: 8.17 us -> 11 us  [per_device_body(): received.append(lax.ppermute(later, 'blk', shift))]
  transfers between devices with their start and end apart: 27 -> 27, of which waited for: 15 -> 13; matrix products, arithmetic and copies ran while one was open for 11% -> 14% of each run, Pallas kernels for 0% -> 0%
where the time goes in v12:
time: 161 us; the launch traced here: 160 us
  starting transfers between devices  72.7 us (45%)
  waiting for transfers between devices  50.1 us (31%)
  other arithmetic  19.3 us (12%)
  matrix products  9.81 us (6%)
  local copies, waits for them, and re-layouts  7.01 us (4%)
    ppermute x7, starting transfers between devices, per_device_body(): received.append(lax.ppermute(later, 'blk', shift))  30.5 us
    all_to_all x1, starting transfers between devices, per_device_body(): lax.all_to_all(packed, 'blk', split_axis=1, concat_axis=0, tiled=True)  16.8 us
    ppermute x7, waiting for transfers between devices, per_device_body(): received.append(lax.ppermute(passages, 'blk', shift))  16 us
    ppermute x7, starting transfers between devices, per_device_body(): received.append(lax.ppermute(passages, 'blk', shift))  16 us
    ppermute x7, waiting for transfers between devices, per_device_body(): received.append(lax.ppermute(later, 'blk', shift))  11 us
    ppermute x3, waiting for transfers between devices, per_device_body(): received.append(lax.ppermute(grads_part, 'corpus', shift))  9.45 us
    unnamed x21, other arithmetic  6.48 us
    all_to_all x1, waiting for transfers between devices, per_device_body(): lax.all_to_all(packed, 'blk', split_axis=1, concat_axis=0, tiled=True)  6.42 us
  transfers between devices with their start and end apart: 27, of which 13 were waited for; matrix products, arithmetic and copies ran while one was open for 14% of the time, Pallas kernels for 0%

profile of v12, /device:TPU:2, one launch (start us, length us, event | category | flops | bytes accessed | tf_op | source)
XLA Modules:
  0.0 160.5 jit_solution(12442115490520106856)
XLA Ops:
  0.7 1.6 collective-permute-start.6
  2.3 1.6 collective-permute-start.5
  3.8 2.5 %collective-permute-start.4 = (bf16[128,1024]{1,0:T(8,128)(2,1)}, bf16[128,1024]{1,0:T(8,128)(2,1)S(1)}, u32[]{:S(2)}, u32[]{:S(2)}) collective-permute-start(bf16[128,1024]{1,0:T(8,128)(2,1)} %param.8), channel_id=1, source_target_pairs={{0,12},{4,16},{8,20},{12,24},{16,28},{20,0},{24,4},{28,8},{1,13},{... | collective-permute-start | bytes 786440 | tf_op jit(solution)/shard_map/ppermute | solution.py:46
  6.4 1.2 collective-permute-start.3
  7.6 2.6 %collective-permute-start.2 = (bf16[128,1024]{1,0:T(8,128)(2,1)}, bf16[128,1024]{1,0:T(8,128)(2,1)S(1)}, u32[]{:S(2)}, u32[]{:S(2)}) collective-permute-start(bf16[128,1024]{1,0:T(8,128)(2,1)} %param.8), channel_id=1, source_target_pairs={{0,20},{4,24},{8,28},{12,0},{16,4},{20,8},{24,12},{28,16},{1,21},{... | collective-permute-start | bytes 786440 | tf_op jit(solution)/shard_map/ppermute | solution.py:46
  10.2 2.4 %constant_dynamic-slice_fusion.6 = (bf16[256,1024]{1,0:T(8,128)(2,1)}, bf16[256,1024]{1,0:T(8,128)(2,1)}, bf16[256,1024]{1,0:T(8,128)(2,1)S(1)}) fusion(bf16[256,4096]{1,0:T(8,128)(2,1)} %param.9, s32[]{:T(128)S(6)} %select_n.1378, s32[]{:T(128)S(6)} %select_n.1375, s32[]{:T(128)S(6)} %select_n.1372), kind=kLoop, calls=%fused_computation.77 | loop fusion | bytes 3145740 | tf_op jit(solution)/shard_map/dynamic_slice | solution.py:35
  13.0 1.6 collective-permute-start.1
  14.6 4.9 %collective-permute-start = (bf16[128,1024]{1,0:T(8,128)(2,1)S(1)}, bf16[128,1024]{1,0:T(8,128)(2,1)S(1)}, u32[]{:S(2)}, u32[]{:S(2)}) collective-permute-start(bf16[128,1024]{1,0:T(8,128)(2,1)S(1)} %copy-done.1), channel_id=1, source_target_pairs={{0,28},{4,0},{8,4},{12,8},{16,12},{20,16},{24,20},{28,24},{1,29},{... | collective-permute-start | bytes 786440 | tf_op jit(solution)/shard_map/ppermute | solution.py:46
  20.1 14.3 %collective-permute-done.4 = bf16[128,1024]{1,0:T(8,128)(2,1)S(1)} collective-permute-done((bf16[128,1024]{1,0:T(8,128)(2,1)}, bf16[128,1024]{1,0:T(8,128)(2,1)S(1)}, u32[]{:S(2)}, u32[]{:S(2)}) %collective-permute-start.4) | collective-permute-done | bytes 262176 | tf_op jit(solution)/shard_map/ppermute | solution.py:46
  34.7 0.5 collective-permute-start.8
  35.3 1.2 collective-permute-start.7
  36.4 1.0 collective-permute-done
  37.5 0.4 select_dynamic-update-slice_fusion.15
  37.8 0.4 select_dynamic-update-slice_fusion.14
  38.2 0.4 select_dynamic-update-slice_fusion.13
  38.6 0.4 select_dynamic-update-slice_fusion.12
  38.9 0.4 select_dynamic-update-slice_fusion.11
  40.6 4.4 %collective-permute-start.22 = (bf16[128,1024]{1,0:T(8,128)(2,1)S(1)}, bf16[128,1024]{1,0:T(8,128)(2,1)S(1)}, u32[]{:S(2)}, u32[]{:S(2)}) collective-permute-start(bf16[128,1024]{1,0:T(8,128)(2,1)S(1)} %copy-done), channel_id=1, source_target_pairs={{0,4},{4,8},{8,12},{12,16},{16,20},{20,24},{24,28},{28,0},{1,5},{5... | collective-permute-start | bytes 786440 | tf_op jit(solution)/shard_map/ppermute | solution.py:52
  45.0 11.6 %collective-permute-start.21 = (bf16[128,1024]{1,0:T(8,128)(2,1)S(1)}, bf16[128,1024]{1,0:T(8,128)(2,1)S(1)}, u32[]{:S(2)}, u32[]{:S(2)}) collective-permute-start(bf16[128,1024]{1,0:T(8,128)(2,1)S(1)} %copy-done), channel_id=1, source_target_pairs={{0,8},{4,12},{8,16},{12,20},{16,24},{20,28},{24,0},{28,4},{1,9},{5... | collective-permute-start | bytes 786440 | tf_op jit(solution)/shard_map/ppermute | solution.py:52
  56.7 0.8 convolution_bitcast_fusion.1
  57.6 2.1 %collective-permute-start.19 = (bf16[128,1024]{1,0:T(8,128)(2,1)S(1)}, bf16[128,1024]{1,0:T(8,128)(2,1)S(1)}, u32[]{:S(2)}, u32[]{:S(2)}) collective-permute-start(bf16[128,1024]{1,0:T(8,128)(2,1)S(1)} %copy-done), channel_id=1, source_target_pairs={{0,16},{4,20},{8,24},{12,28},{16,0},{20,4},{24,8},{28,12},{1,17},{... | collective-permute-start | bytes 786440 | tf_op jit(solution)/shard_map/ppermute | solution.py:52
  59.7 7.2 %collective-permute-start.18 = (bf16[128,1024]{1,0:T(8,128)(2,1)S(1)}, bf16[128,1024]{1,0:T(8,128)(2,1)S(1)}, u32[]{:S(2)}, u32[]{:S(2)}) collective-permute-start(bf16[128,1024]{1,0:T(8,128)(2,1)S(1)} %copy-done), channel_id=1, source_target_pairs={{0,20},{4,24},{8,28},{12,0},{16,4},{20,8},{24,12},{28,16},{1,21},{... | collective-permute-start | bytes 786440 | tf_op jit(solution)/shard_map/ppermute | solution.py:52
  66.9 1.7 %select_select_fusion.3 = (bf16[256,1024]{1,0:T(8,128)(2,1)S(1)}, bf16[256,1024]{1,0:T(8,128)(2,1)S(1)}, bf16[256,1024]{1,0:T(8,128)(2,1)S(1)}, bf16[256,1024]{1,0:T(8,128)(2,1)S(1)}) fusion(bf16[256,1024]{1,0:T(8,128)(2,1)S(1)} %collective-permute-done.7, bf16[256,1024]{1,0:T(8,128)(2,1)S(1)} %collective-permute-done.8, ...), kind=kLoop, calls=%fused_computation.20 | loop fusion | flops 3145728 | bytes 4194320 | tf_op jit(solution)/shard_map/jit(_where)/select_n | solution.py:20
  68.7 0.7 copy-done.6
  69.9 1.5 convolution_bitcast_fusion
  71.4 1.2 copy.49
  72.7 5.1 %collective-permute-start.17 = (bf16[128,1024]{1,0:T(8,128)(2,1)S(1)}, bf16[128,1024]{1,0:T(8,128)(2,1)S(1)}, u32[]{:S(2)}, u32[]{:S(2)}) collective-permute-start(bf16[128,1024]{1,0:T(8,128)(2,1)S(1)} %copy-done), channel_id=1, source_target_pairs={{0,24},{4,28},{8,0},{12,4},{16,8},{20,12},{24,16},{28,20},{1,25},{... | collective-permute-start | bytes 786440 | tf_op jit(solution)/shard_map/ppermute | solution.py:52
  77.8 0.6 select_reduce_fusion.2
  78.6 8.1 %collective-permute-done.20 = bf16[128,1024]{1,0:T(8,128)(2,1)S(1)} collective-permute-done((bf16[128,1024]{1,0:T(8,128)(2,1)S(1)}, bf16[128,1024]{1,0:T(8,128)(2,1)S(1)}, u32[]{:S(2)}, u32[]{:S(2)}) %collective-permute-start.20) | collective-permute-done | bytes 262176 | tf_op jit(solution)/shard_map/ppermute | solution.py:52
  86.8 1.7 %collective-permute-start.12 = (f32[32,1032]{1,0:T(8,128)S(1)}, f32[32,1032]{1,0:T(8,128)S(1)}, u32[]{:S(2)}, u32[]{:S(2)}) collective-permute-start(f32[32,1032]{1,0:T(8,128)S(1)} %get-tuple-element.47), channel_id=1, source_target_pairs={{0,3},{1,0},{2,1},{3,2},{4,7},{5,4},{6,5},{7,6},{8,11},{9,8},{10,9... | collective-permute-start | bytes 396296 | tf_op jit(solution)/shard_map/ppermute | solution.py:81
  88.5 0.8 collective-permute-start.11
  89.3 2.8 %collective-permute-done.16 = bf16[128,1024]{1,0:T(8,128)(2,1)S(1)} collective-permute-done((bf16[128,1024]{1,0:T(8,128)(2,1)S(1)}, bf16[128,1024]{1,0:T(8,128)(2,1)S(1)}, u32[]{:S(2)}, u32[]{:S(2)}) %collective-permute-start.16) | collective-permute-done | bytes 262176 | tf_op jit(solution)/shard_map/ppermute | solution.py:52
  93.6 2.5 %collective-permute-done.11 = f32[32,1032]{1,0:T(8,128)S(1)} collective-permute-done((f32[32,1032]{1,0:T(8,128)S(1)}, f32[32,1032]{1,0:T(8,128)S(1)}, u32[]{:S(2)}, u32[]{:S(2)}) %collective-permute-start.11) | collective-permute-done | bytes 132128 | tf_op jit(solution)/shard_map/ppermute | solution.py:81
  96.8 0.5 fusion.12
  97.8 1.1 collective-permute-start.15
  98.9 1.0 collective-permute-start.14
  99.9 0.4 collective-permute-start.13
  100.3 0.8 select_dynamic-update-slice_fusion.16
  101.2 3.7 %collective-permute-done.15 = bf16[32,1032]{0,1:T(8,128)(2,1)S(1)} collective-permute-done((bf16[32,1032]{0,1:T(8,128)(2,1)S(1)}, bf16[32,1032]{0,1:T(8,128)(2,1)S(1)}, u32[]{:S(2)}, u32[]{:S(2)}) %collective-permute-start.15) | collective-permute-done | bytes 66080 | tf_op jit(solution)/shard_map/ppermute | solution.py:105
  104.8 3.3 %collective-permute-done.14 = bf16[32,1032]{0,1:T(8,128)(2,1)S(1)} collective-permute-done((bf16[32,1032]{0,1:T(8,128)(2,1)S(1)}, bf16[32,1032]{0,1:T(8,128)(2,1)S(1)}, u32[]{:S(2)}, u32[]{:S(2)}) %collective-permute-start.14) | collective-permute-done | bytes 66080 | tf_op jit(solution)/shard_map/ppermute | solution.py:105
  108.1 2.5 %collective-permute-done.13 = bf16[32,1032]{0,1:T(8,128)(2,1)S(1)} collective-permute-done((bf16[32,1032]{0,1:T(8,128)(2,1)S(1)}, bf16[32,1032]{0,1:T(8,128)(2,1)S(1)}, u32[]{:S(2)}, u32[]{:S(2)}) %collective-permute-start.13) | collective-permute-done | bytes 66080 | tf_op jit(solution)/shard_map/ppermute | solution.py:105
  111.1 0.4 pad_maximum_fusion.2
  111.5 0.7 pad_maximum_fusion.1
  112.3 16.8 %all-to-all-start = ((bf16[128,8,160]{0,2,1:T(8,128)(2,1)}), bf16[128,8,160]{0,2,1:T(8,128)(2,1)S(1)}, u32[]{:S(2)}, u32[]{:S(2)}) async-start(bf16[128,8,160]{0,2,1:T(8,128)(2,1)} %pad_maximum_fusion.1), calls=%async_computation | async-start | bytes 655360 | tf_op jit(solution)/shard_map/all_to_all | solution.py:135
  129.1 0.5 select_reduce_fusion.1
  129.6 2.0 %fusion.6 = f32[128,1024]{1,0:T(8,128)S(1)} fusion(f32[128,1024]{1,0:T(8,128)S(1)} %select_reduce_fusion.1, bf16[256,1024]{1,0:T(8,128)(2,1)} %copy-done.8, bf16[256,1024]{1,0:T(8,128)(2,1)} %copy-done.10, bf16[256,1024]{1,0:T(8,128)(2,1)} %copy-done.12, bf16[256,1024]{1,0:T(8,128)(2,1)S(1)} %copy-done.7), kind=kOutput, calls=%fused_computation.57 | convolution fusion | flops 276955136 | bytes 3145728 | tf_op jit(solution)/shard_map/dot_general | solution.py:114
  131.7 0.5 convolution_add_fusion.2
  132.2 0.6 copy-done.9
  133.1 1.2 convolution_add_fusion.1
  134.3 6.4 %all-to-all-done = bf16[128,8,160]{0,2,1:T(8,128)(2,1)S(1)} async-done(((bf16[128,8,160]{0,2,1:T(8,128)(2,1)}), bf16[128,8,160]{0,2,1:T(8,128)(2,1)S(1)}, u32[]{:S(2)}, u32[]{:S(2)}) %all-to-all-start) | async-done | bytes 327712 | tf_op jit(solution)/shard_map/all_to_all | solution.py:135
  140.8 4.3 %select_reduce_fusion = f32[1024,1024]{1,0:T(8,128)S(1)} fusion(f32[1024,7]{0,1:T(8,128)S(1)} %slice_convert_fusion, s32[1024,7]{0,1:T(8,128)S(1)} %convert_add_fusion.1), kind=kLoop, calls=%fused_computation | loop fusion | flops 20971520 | bytes 4251648 | tf_op jit(solution)/shard_map/reduce_sum | solution.py:145
  145.1 1.3 fusion
  146.4 1.3 convolution_add_fusion
  147.9 0.7 collective-permute-start.23
  148.6 0.7 collective-permute-start.25
  149.3 1.3 collective-permute-start.24
  150.6 0.4 select_dynamic-update-slice_fusion.7
  151.7 0.4 select_dynamic-update-slice_fusion.4
  152.1 0.4 select_dynamic-update-slice_fusion.3
  152.4 0.4 select_dynamic-update-slice_fusion.2
  152.8 0.4 select_dynamic-update-slice_fusion.1
  153.5 1.2 fusion.3
  154.8 4.8 %collective-permute-done.24 = bf16[256,512]{1,0:T(8,128)(2,1)S(1)} collective-permute-done((bf16[256,512]{1,0:T(8,128)(2,1)S(1)}, bf16[256,512]{1,0:T(8,128)(2,1)S(1)}, u32[]{:S(2)}, u32[]{:S(2)}) %collective-permute-start.24) | collective-permute-done | bytes 262176 | tf_op jit(solution)/shard_map/ppermute | solution.py:167
  159.5 0.9 convert_add_fusion
  (98 shorter events, 8.0 us)
Async XLA Ops:
  0.6 12.4 %copy-start.1 = (bf16[128,1024]{1,0:T(8,128)(2,1)S(1)}, bf16[128,1024]{1,0:T(8,128)(2,1)}, u32[]{:S(2)}) copy-start(bf16[128,1024]{1,0:T(8,128)(2,1)} %param.8) | copy-start | bytes 786436
  0.6 18.8 %copy-start.16 = (f32[128]{0:T(128)S(1)}, f32[128]{0:T(128)}, u32[]{:S(2)}) copy-start(f32[128]{0:T(128)} %param.13) | copy-start | bytes 1540
  0.7 19.2 %copy-start.17 = (s32[128]{0:T(128)S(1)}, s32[128]{0:T(128)}, u32[]{:S(2)}) copy-start(s32[128]{0:T(128)} %param.12) | copy-start | bytes 1540
  0.7 19.4 %copy-start.15 = (s32[128,7]{0,1:T(8,128)S(1)}, s32[128,7]{0,1:T(8,128)}, u32[]{:S(2)}) copy-start(s32[128,7]{0,1:T(8,128)} %param.11) | copy-start | bytes 10756
  0.7 19.4 %copy-start.14 = (s32[128,7]{0,1:T(8,128)S(1)}, s32[128,7]{0,1:T(8,128)}, u32[]{:S(2)}) copy-start(s32[128,7]{0,1:T(8,128)} %param.10) | copy-start | bytes 10756
  0.7 12.3 %collective-permute-start.6 = (bf16[128,1024]{1,0:T(8,128)(2,1)}, bf16[128,1024]{1,0:T(8,128)(2,1)S(1)}, u32[]{:S(2)}, u32[]{:S(2)}) collective-permute-start(bf16[128,1024]{1,0:T(8,128)(2,1)} %param.8), channel_id=1, source_target_pairs={{0,4},{4,8},{8,12},{12,16},{16,20},{20,24},{24,28},{28,0},{1,5},{5... | collective-permute-start | bytes 786440 | tf_op jit(solution)/shard_map/ppermute | solution.py:46
  2.3 12.4 %collective-permute-start.5 = (bf16[128,1024]{1,0:T(8,128)(2,1)}, bf16[128,1024]{1,0:T(8,128)(2,1)S(1)}, u32[]{:S(2)}, u32[]{:S(2)}) collective-permute-start(bf16[128,1024]{1,0:T(8,128)(2,1)} %param.8), channel_id=1, source_target_pairs={{0,8},{4,12},{8,16},{12,20},{16,24},{20,28},{24,0},{28,4},{1,9},{5... | collective-permute-start | bytes 786440 | tf_op jit(solution)/shard_map/ppermute | solution.py:46
  3.8 30.6 %collective-permute-start.4 = (bf16[128,1024]{1,0:T(8,128)(2,1)}, bf16[128,1024]{1,0:T(8,128)(2,1)S(1)}, u32[]{:S(2)}, u32[]{:S(2)}) collective-permute-start(bf16[128,1024]{1,0:T(8,128)(2,1)} %param.8), channel_id=1, source_target_pairs={{0,12},{4,16},{8,20},{12,24},{16,28},{20,0},{24,4},{28,8},{1,13},{... | collective-permute-start | bytes 786440 | tf_op jit(solution)/shard_map/ppermute | solution.py:46
  6.4 28.4 %collective-permute-start.3 = (bf16[128,1024]{1,0:T(8,128)(2,1)}, bf16[128,1024]{1,0:T(8,128)(2,1)S(1)}, u32[]{:S(2)}, u32[]{:S(2)}) collective-permute-start(bf16[128,1024]{1,0:T(8,128)(2,1)} %param.8), channel_id=1, source_target_pairs={{0,16},{4,20},{8,24},{12,28},{16,0},{20,4},{24,8},{28,12},{1,17},{... | collective-permute-start | bytes 786440 | tf_op jit(solution)/shard_map/ppermute | solution.py:46
  7.6 27.7 %collective-permute-start.2 = (bf16[128,1024]{1,0:T(8,128)(2,1)}, bf16[128,1024]{1,0:T(8,128)(2,1)S(1)}, u32[]{:S(2)}, u32[]{:S(2)}) collective-permute-start(bf16[128,1024]{1,0:T(8,128)(2,1)} %param.8), channel_id=1, source_target_pairs={{0,20},{4,24},{8,28},{12,0},{16,4},{20,8},{24,12},{28,16},{1,21},{... | collective-permute-start | bytes 786440 | tf_op jit(solution)/shard_map/ppermute | solution.py:46
  13.0 23.4 %collective-permute-start.1 = (bf16[128,1024]{1,0:T(8,128)(2,1)S(1)}, bf16[128,1024]{1,0:T(8,128)(2,1)S(1)}, u32[]{:S(2)}, u32[]{:S(2)}) collective-permute-start(bf16[128,1024]{1,0:T(8,128)(2,1)S(1)} %copy-done.1), channel_id=1, source_target_pairs={{0,24},{4,28},{8,0},{12,4},{16,8},{20,12},{24,16},{28,20},{1,25},{... | collective-permute-start | bytes 786440 | tf_op jit(solution)/shard_map/ppermute | solution.py:46
  14.6 22.8 %collective-permute-start = (bf16[128,1024]{1,0:T(8,128)(2,1)S(1)}, bf16[128,1024]{1,0:T(8,128)(2,1)S(1)}, u32[]{:S(2)}, u32[]{:S(2)}) collective-permute-start(bf16[128,1024]{1,0:T(8,128)(2,1)S(1)} %copy-done.1), channel_id=1, source_target_pairs={{0,28},{4,0},{8,4},{12,8},{16,12},{20,16},{24,20},{28,24},{1,29},{... | collective-permute-start | bytes 786440 | tf_op jit(solution)/shard_map/ppermute | solution.py:46
  34.4 23.1 %collective-permute-start.9 = (bf16[256,1024]{1,0:T(8,128)(2,1)}, bf16[256,1024]{1,0:T(8,128)(2,1)S(1)}, u32[]{:S(2)}, u32[]{:S(2)}) collective-permute-start(bf16[256,1024]{1,0:T(8,128)(2,1)} %get-tuple-element.36), channel_id=1, source_target_pairs={{0,1},{1,2},{2,3},{3,0},{4,5},{5,6},{6,7},{7,4},{8,9},{9,10},{10,1... | collective-permute-start | bytes 1572872 | tf_op jit(solution)/shard_map/ppermute | solution.py:41
  34.7 22.9 %collective-permute-start.8 = (bf16[256,1024]{1,0:T(8,128)(2,1)}, bf16[256,1024]{1,0:T(8,128)(2,1)S(1)}, u32[]{:S(2)}, u32[]{:S(2)}) collective-permute-start(bf16[256,1024]{1,0:T(8,128)(2,1)} %get-tuple-element.37), channel_id=1, source_target_pairs={{0,2},{1,3},{2,0},{3,1},{4,6},{5,7},{6,4},{7,5},{8,10},{9,11},{10,... | collective-permute-start | bytes 1572872 | tf_op jit(solution)/shard_map/ppermute | solution.py:41
  35.3 24.4 %collective-permute-start.7 = (bf16[256,1024]{1,0:T(8,128)(2,1)S(1)}, bf16[256,1024]{1,0:T(8,128)(2,1)S(1)}, u32[]{:S(2)}, u32[]{:S(2)}) collective-permute-start(bf16[256,1024]{1,0:T(8,128)(2,1)S(1)} %get-tuple-element.38), channel_id=1, source_target_pairs={{0,3},{1,0},{2,1},{3,2},{4,7},{5,4},{6,5},{7,6},{8,11},{9,8},{10,9... | collective-permute-start | bytes 1572872 | tf_op jit(solution)/shard_map/ppermute | solution.py:41
  39.7 1.0 copy-start
  40.6 19.1 %copy-start.2 = (bf16[1024,1024]{1,0:T(8,128)(2,1)}, bf16[1024,1024]{1,0:T(8,128)(2,1)S(1)}, u32[]{:S(2)}) copy-start(bf16[1024,1024]{1,0:T(8,128)(2,1)S(1)} %select_dynamic-update-slice_fusion.8) | copy-start | bytes 6291460
  40.6 32.1 %collective-permute-start.22 = (bf16[128,1024]{1,0:T(8,128)(2,1)S(1)}, bf16[128,1024]{1,0:T(8,128)(2,1)S(1)}, u32[]{:S(2)}, u32[]{:S(2)}) collective-permute-start(bf16[128,1024]{1,0:T(8,128)(2,1)S(1)} %copy-done), channel_id=1, source_target_pairs={{0,4},{4,8},{8,12},{12,16},{16,20},{20,24},{24,28},{28,0},{1,5},{5... | collective-permute-start | bytes 786440 | tf_op jit(solution)/shard_map/ppermute | solution.py:52
  45.0 32.7 %collective-permute-start.21 = (bf16[128,1024]{1,0:T(8,128)(2,1)S(1)}, bf16[128,1024]{1,0:T(8,128)(2,1)S(1)}, u32[]{:S(2)}, u32[]{:S(2)}) collective-permute-start(bf16[128,1024]{1,0:T(8,128)(2,1)S(1)} %copy-done), channel_id=1, source_target_pairs={{0,8},{4,12},{8,16},{12,20},{16,24},{20,28},{24,0},{28,4},{1,9},{5... | collective-permute-start | bytes 786440 | tf_op jit(solution)/shard_map/ppermute | solution.py:52
  57.5 29.2 %collective-permute-start.20 = (bf16[128,1024]{1,0:T(8,128)(2,1)S(1)}, bf16[128,1024]{1,0:T(8,128)(2,1)S(1)}, u32[]{:S(2)}, u32[]{:S(2)}) collective-permute-start(bf16[128,1024]{1,0:T(8,128)(2,1)S(1)} %copy-done), channel_id=1, source_target_pairs={{0,12},{4,16},{8,20},{12,24},{16,28},{20,0},{24,4},{28,8},{1,13},{... | collective-permute-start | bytes 786440 | tf_op jit(solution)/shard_map/ppermute | solution.py:52
  57.6 29.3 %collective-permute-start.19 = (bf16[128,1024]{1,0:T(8,128)(2,1)S(1)}, bf16[128,1024]{1,0:T(8,128)(2,1)S(1)}, u32[]{:S(2)}, u32[]{:S(2)}) collective-permute-start(bf16[128,1024]{1,0:T(8,128)(2,1)S(1)} %copy-done), channel_id=1, source_target_pairs={{0,16},{4,20},{8,24},{12,28},{16,0},{20,4},{24,8},{28,12},{1,17},{... | collective-permute-start | bytes 786440 | tf_op jit(solution)/shard_map/ppermute | solution.py:52
  59.7 28.8 %collective-permute-start.18 = (bf16[128,1024]{1,0:T(8,128)(2,1)S(1)}, bf16[128,1024]{1,0:T(8,128)(2,1)S(1)}, u32[]{:S(2)}, u32[]{:S(2)}) collective-permute-start(bf16[128,1024]{1,0:T(8,128)(2,1)S(1)} %copy-done), channel_id=1, source_target_pairs={{0,20},{4,24},{8,28},{12,0},{16,4},{20,8},{24,12},{28,16},{1,21},{... | collective-permute-start | bytes 786440 | tf_op jit(solution)/shard_map/ppermute | solution.py:52
  68.6 0.8 copy-start.6
  68.6 1.0 copy-start.8
  68.6 1.1 copy-start.10
  68.7 1.3 copy-start.12
  72.7 16.6 %collective-permute-start.17 = (bf16[128,1024]{1,0:T(8,128)(2,1)S(1)}, bf16[128,1024]{1,0:T(8,128)(2,1)S(1)}, u32[]{:S(2)}, u32[]{:S(2)}) collective-permute-start(bf16[128,1024]{1,0:T(8,128)(2,1)S(1)} %copy-done), channel_id=1, source_target_pairs={{0,24},{4,28},{8,0},{12,4},{16,8},{20,12},{24,16},{28,20},{1,25},{... | collective-permute-start | bytes 786440 | tf_op jit(solution)/shard_map/ppermute | solution.py:52
  77.8 14.3 %collective-permute-start.16 = (bf16[128,1024]{1,0:T(8,128)(2,1)S(1)}, bf16[128,1024]{1,0:T(8,128)(2,1)S(1)}, u32[]{:S(2)}, u32[]{:S(2)}) collective-permute-start(bf16[128,1024]{1,0:T(8,128)(2,1)S(1)} %copy-done), channel_id=1, source_target_pairs={{0,28},{4,0},{8,4},{12,8},{16,12},{20,16},{24,20},{28,24},{1,29},{... | collective-permute-start | bytes 786440 | tf_op jit(solution)/shard_map/ppermute | solution.py:52
  86.8 6.8 %collective-permute-start.10 = (f32[32,1032]{1,0:T(8,128)S(1)}, f32[32,1032]{1,0:T(8,128)S(1)}, u32[]{:S(2)}, u32[]{:S(2)}) collective-permute-start(f32[32,1032]{1,0:T(8,128)S(1)} %get-tuple-element.46), channel_id=1, source_target_pairs={{0,1},{1,2},{2,3},{3,0},{4,5},{5,6},{6,7},{7,4},{8,9},{9,10},{10,1... | collective-permute-start | bytes 396296 | tf_op jit(solution)/shard_map/ppermute | solution.py:81
  86.8 6.8 %collective-permute-start.12 = (f32[32,1032]{1,0:T(8,128)S(1)}, f32[32,1032]{1,0:T(8,128)S(1)}, u32[]{:S(2)}, u32[]{:S(2)}) collective-permute-start(f32[32,1032]{1,0:T(8,128)S(1)} %get-tuple-element.47), channel_id=1, source_target_pairs={{0,3},{1,0},{2,1},{3,2},{4,7},{5,4},{6,5},{7,6},{8,11},{9,8},{10,9... | collective-permute-start | bytes 396296 | tf_op jit(solution)/shard_map/ppermute | solution.py:81
  88.5 7.6 %collective-permute-start.11 = (f32[32,1032]{1,0:T(8,128)S(1)}, f32[32,1032]{1,0:T(8,128)S(1)}, u32[]{:S(2)}, u32[]{:S(2)}) collective-permute-start(f32[32,1032]{1,0:T(8,128)S(1)} %get-tuple-element.48), channel_id=1, source_target_pairs={{0,2},{1,3},{2,0},{3,1},{4,6},{5,7},{6,4},{7,5},{8,10},{9,11},{10,... | collective-permute-start | bytes 396296 | tf_op jit(solution)/shard_map/ppermute | solution.py:81
  93.6 3.9 %copy-start.4 = (bf16[1024,512]{1,0:T(8,128)(2,1)}, bf16[1024,512]{1,0:T(8,128)(2,1)S(1)}, u32[]{:S(2)}) copy-start(bf16[1024,512]{1,0:T(8,128)(2,1)S(1)} %select_dynamic-update-slice_fusion.17) | copy-start | bytes 3145732
  97.8 7.1 %collective-permute-start.15 = (bf16[32,1032]{0,1:T(8,128)(2,1)S(1)}, bf16[32,1032]{0,1:T(8,128)(2,1)S(1)}, u32[]{:S(2)}, u32[]{:S(2)}) collective-permute-start(bf16[32,1032]{0,1:T(8,128)(2,1)S(1)} %copy.51), channel_id=1, source_target_pairs={{0,1},{1,2},{2,3},{3,0},{4,5},{5,6},{6,7},{7,4},{8,9},{9,10},{10,1... | collective-permute-start | bytes 198152 | tf_op jit(solution)/shard_map/ppermute | solution.py:105
  98.9 9.2 %collective-permute-start.14 = (bf16[32,1032]{0,1:T(8,128)(2,1)S(1)}, bf16[32,1032]{0,1:T(8,128)(2,1)S(1)}, u32[]{:S(2)}, u32[]{:S(2)}) collective-permute-start(bf16[32,1032]{0,1:T(8,128)(2,1)S(1)} %copy.51), channel_id=1, source_target_pairs={{0,2},{1,3},{2,0},{3,1},{4,6},{5,7},{6,4},{7,5},{8,10},{9,11},{10,... | collective-permute-start | bytes 198152 | tf_op jit(solution)/shard_map/ppermute | solution.py:105
  99.9 10.7 %collective-permute-start.13 = (bf16[32,1032]{0,1:T(8,128)(2,1)S(1)}, bf16[32,1032]{0,1:T(8,128)(2,1)S(1)}, u32[]{:S(2)}, u32[]{:S(2)}) collective-permute-start(bf16[32,1032]{0,1:T(8,128)(2,1)S(1)} %copy.51), channel_id=1, source_target_pairs={{0,3},{1,0},{2,1},{3,2},{4,7},{5,4},{6,5},{7,6},{8,11},{9,8},{10,9... | collective-permute-start | bytes 198152 | tf_op jit(solution)/shard_map/ppermute | solution.py:105
  111.1 18.6 %copy-start.7 = (bf16[256,1024]{1,0:T(8,128)(2,1)S(1)}, bf16[256,1024]{1,0:T(8,128)(2,1)}, u32[]{:S(2)}) copy-start(bf16[256,1024]{1,0:T(8,128)(2,1)} %copy-done.6) | copy-start | bytes 1572868
  112.3 28.4 %all-to-all-start = ((bf16[128,8,160]{0,2,1:T(8,128)(2,1)}), bf16[128,8,160]{0,2,1:T(8,128)(2,1)S(1)}, u32[]{:S(2)}, u32[]{:S(2)}) async-start(bf16[128,8,160]{0,2,1:T(8,128)(2,1)} %pad_maximum_fusion.1), calls=%async_computation | async-start | bytes 655360 | tf_op jit(solution)/shard_map/all_to_all | solution.py:135
  129.6 2.1 %copy-start.3 = (bf16[1024,1024]{1,0:T(8,128)(2,1)S(1)}, bf16[1024,1024]{1,0:T(8,128)(2,1)}, u32[]{:S(2)}) copy-start(bf16[1024,1024]{1,0:T(8,128)(2,1)} %copy-done.2) | copy-start | bytes 6291460
  131.7 1.0 copy-start.9
  131.7 1.2 copy-start.11
  131.7 1.4 copy-start.13
  140.8 4.3 %copy-start.5 = (bf16[1024,512]{1,0:T(8,128)(2,1)S(1)}, bf16[1024,512]{1,0:T(8,128)(2,1)}, u32[]{:S(2)}) copy-start(bf16[1024,512]{1,0:T(8,128)(2,1)} %select_dynamic-update-slice_fusion.16) | copy-start | bytes 3145732
  147.9 6.8 %collective-permute-start.23 = (bf16[256,512]{1,0:T(8,128)(2,1)S(1)}, bf16[256,512]{1,0:T(8,128)(2,1)S(1)}, u32[]{:S(2)}, u32[]{:S(2)}) collective-permute-start(bf16[256,512]{1,0:T(8,128)(2,1)S(1)} %get-tuple-element.43), channel_id=1, source_target_pairs={{0,1},{4,5},{9,10},{13,14},{18,19},{22,23},{27,24},{31,28}} | collective-permute-start | bytes 786440 | tf_op jit(solution)/shard_map/ppermute | solution.py:167
  148.6 6.2 %collective-permute-start.25 = (bf16[256,512]{1,0:T(8,128)(2,1)S(1)}, bf16[256,512]{1,0:T(8,128)(2,1)S(1)}, u32[]{:S(2)}, u32[]{:S(2)}) collective-permute-start(bf16[256,512]{1,0:T(8,128)(2,1)S(1)} %get-tuple-element.44), channel_id=1, source_target_pairs={{0,3},{4,7},{9,8},{13,12},{18,17},{22,21},{27,26},{31,30}} | collective-permute-start | bytes 786440 | tf_op jit(solution)/shard_map/ppermute | solution.py:167
  149.3 10.2 %collective-permute-start.24 = (bf16[256,512]{1,0:T(8,128)(2,1)S(1)}, bf16[256,512]{1,0:T(8,128)(2,1)S(1)}, u32[]{:S(2)}, u32[]{:S(2)}) collective-permute-start(bf16[256,512]{1,0:T(8,128)(2,1)S(1)} %get-tuple-element.45), channel_id=1, source_target_pairs={{0,2},{4,6},{9,11},{13,15},{18,16},{22,20},{27,25},{31,29}} | collective-permute-start | bytes 786440 | tf_op jit(solution)/shard_map/ppermute | solution.py:167
